TPU v7x, 128 devices: a whole 4x4x4 slice. The times are simulated.
128 devices in a mesh: gx: 16 (over y, z_lo, core), gy: 2 (over z_hi), gz: 4 (over x).
Axes of the slice: x: 4, y: 4, z: 4 (z_hi: 2, z_lo: 2; z = z_hi * 2 + z_lo), core: 2. Of those that a mesh axis runs over, the one named last changes fastest.
Arguments:
- check_pops: float32 [27, 64, 32, 512], P(None, 'gx', 'gy', 'gz'), as said below
- adjoint_end: float32 [27, 64, 32, 512], P(None, 'gx', 'gy', 'gz'), may hold values from -6 to 6
- relax_rate: float32 [64, 32, 512], P('gx', 'gy', 'gz'), may hold values from 0.6 to 1.7
- wall_flag: int32 [64, 32, 512], P('gx', 'gy', 'gz'), may hold values from 0 to 1
- patch_of_cell: int32 [64, 32, 512], P('gx', 'gy', 'gz'), may hold values from 0 to 1023, as said below
- porosity: float32 [1024], replicated, may hold values from 0.1 to 0.9
- patch_slot: int32 [1024], replicated, may hold values from 0 to 1023, each once
Outputs:
- adjoint_start: float32 [27, 64, 32, 512], P(None, 'gx', 'gy', 'gz')
- patch_sens: float32 [1024], P(('gx', 'gy', 'gz'))
Inputs may be any that keep to these rules, and one draw needn't show every extreme that they name: `patch_of_cell`: the cells of one patch form one box of 2 x 16/2 x 128/2 cells, boxes shifted by 1 cells along the first dimension (periodically); every patch id is used. `check_pops`: all populations are positive.
All inputs are finite; a program needn't handle non-finite values.
Results may differ from a plain program's by a relative error of at most 0.0003.
Values sent between devices are 32-bit elements; how exact they have to be, the bound alone decides.
No kernel may reach another device: no remote copies, remote signals or barrier semaphores. Data moves between devices by JAX's collectives and lax.ppermute only.
A program may use at most 64 MiB of HBM per device.

v0:
```python
import jax
import jax.numpy as jnp
import numpy as np
from jax import lax
from jax.sharding import PartitionSpec as P


def extended(cells, sides, width):
    for axis, dim in sides:
        count = lax.axis_size(axis)
        head = lax.slice_in_dim(cells, 0, width, axis=dim)
        tail = lax.slice_in_dim(cells, cells.shape[dim] - width, cells.shape[dim], axis=dim)
        cells = jnp.concatenate(
            [
                lax.ppermute(tail, axis, [(i, (i + 1) % count) for i in range(count)]),
                cells,
                lax.ppermute(head, axis, [((i + 1) % count, i) for i in range(count)]),
            ],
            axis=dim,
        )
    return cells


def lattice_table():
    steps = np.array(
        [
            [first, second, third]
            for first in (-1, 0, 1)
            for second in (-1, 0, 1)
            for third in (-1, 0, 1)
        ],
        dtype=np.int64,
    )
    moved = np.abs(steps).sum(axis=1)
    weights = np.array([8.0 / 27.0, 2.0 / 27.0, 1.0 / 54.0, 1.0 / 216.0])[moved]
    return (steps, weights)


def collide(pops, rate, gamma):
    steps, weights = lattice_table()
    cube = pops.reshape((3, 3, 3) + pops.shape[1:])
    density = jnp.sum(pops, axis=0)
    mom_x = jnp.sum(cube[2], axis=(0, 1)) - jnp.sum(cube[0], axis=(0, 1))
    mom_y = jnp.sum(cube[:, 2], axis=(0, 1)) - jnp.sum(cube[:, 0], axis=(0, 1))
    mom_z = jnp.sum(cube[:, :, 2], axis=(0, 1)) - jnp.sum(cube[:, :, 0], axis=(0, 1))
    vel_x = mom_x / density
    vel_y = mom_y / density
    vel_z = mom_z / density
    cx = jnp.asarray(steps[:, 0], jnp.float32)[:, None, None, None]
    cy = jnp.asarray(steps[:, 1], jnp.float32)[:, None, None, None]
    cz = jnp.asarray(steps[:, 2], jnp.float32)[:, None, None, None]
    wts = jnp.asarray(weights, jnp.float32)[:, None, None, None]
    along = cx * vel_x + cy * vel_y + cz * vel_z
    speed = vel_x * vel_x + vel_y * vel_y + vel_z * vel_z
    equil = wts * density * (1.0 + 3.0 * along + 4.5 * along * along - 1.5 * speed)
    relaxed = pops - rate * (pops - equil)
    flipped = pops[::-1]
    return ((1.0 - gamma) * relaxed + gamma * flipped, flipped - relaxed)


def adjoint_collide(pops, rate, gamma, adj_post):

    def forward(values):
        return collide(values, rate, gamma)

    post, pullback, deriv = jax.vjp(forward, pops, has_aux=True)
    (adj_pre,) = pullback(adj_post)
    return (adj_pre, jnp.sum(adj_post * deriv, axis=0))


def local_move(field, sign):
    steps, _ = lattice_table()
    size_x = field.shape[1] - 2
    size_y = field.shape[2] - 2
    size_z = field.shape[3] - 2
    moved = []
    for index in range(27):
        start_x = 1 - int(sign * steps[index, 0])
        start_y = 1 - int(sign * steps[index, 1])
        start_z = 1 - int(sign * steps[index, 2])
        moved.append(
            field[
                index,
                start_x : start_x + size_x,
                start_y : start_y + size_y,
                start_z : start_z + size_z,
            ]
        )
    return jnp.stack(moved, 0)


def propagate(fields, signs):
    stacked = fields[0]
    padded = extended(stacked, (("gx", 1), ("gy", 2), ("gz", 3)), 1)
    results = []
    for member, sign in enumerate(signs):
        results.append(local_move(padded[27 * member : 27 * member + 27], sign))
    return tuple(results)


def shards(check_pops, adjoint_end, relax_rate, wall_flag, patch_of_cell, porosity, patch_slot):
    walls = wall_flag.astype(jnp.float32)
    gamma = walls * porosity[patch_of_cell]
    post_now, _ = collide(check_pops, relax_rate, gamma)
    (pops_next,) = propagate((post_now,), (1,))
    (post_adj_next,) = propagate((adjoint_end,), (-1,))
    adj_next, sens_next = adjoint_collide(pops_next, relax_rate, gamma, post_adj_next)
    (post_adj,) = propagate((adj_next,), (-1,))
    adjoint_start, sens_now = adjoint_collide(check_pops, relax_rate, gamma, post_adj)
    density = walls * (sens_next + sens_now)
    count = porosity.shape[0]
    totals = jax.ops.segment_sum(density.reshape(-1), patch_of_cell.reshape(-1), num_segments=count)
    placed = jnp.zeros((count,), jnp.float32).at[patch_slot].set(totals)
    patch_sens = lax.psum_scatter(placed, ("gx", "gy", "gz"), scatter_dimension=0, tiled=True)
    return (adjoint_start, patch_sens)


def solution(mesh):
    in_specs = (
        P(None, "gx", "gy", "gz"),
        P(None, "gx", "gy", "gz"),
        P("gx", "gy", "gz"),
        P("gx", "gy", "gz"),
        P("gx", "gy", "gz"),
        P(),
        P(),
    )
    out_specs = (P(None, "gx", "gy", "gz"), P(("gx", "gy", "gz")))
    return jax.shard_map(shards, mesh=mesh, in_specs=in_specs, out_specs=out_specs, check_vma=False)
```

profile of v0, /device:TPU:1, one launch (start us, length us, event | category | flops | bytes accessed | tf_op | source)
XLA Modules:
  0.0 331.2 jit_solution(12144818372469360270)
XLA Ops:
  0.7 1.2 slice_reduce_fusion.8
  1.8 1.1 slice_reduce_fusion.6
  2.9 1.1 slice_reduce_fusion.4
  4.3 32.9 %gather_fusion = f32[8192]{0:T(1024)S(1)} fusion(f32[1024]{0:T(1024)S(1)} %copy-done, s32[8192]{0:T(1024)S(1)} %broadcast_clamp_fusion), kind=kCustom, calls=%fused_computation | custom fusion | bytes 98304 | tf_op jit(solution)/shard_map/gather | solution.py:103
  37.9 1.4 multiply_add_fusion.1
  39.4 1.5 collective-permute-start.7
  40.8 1.7 collective-permute-start.6
  43.1 1.9 collective-permute-start.1
  45.0 1.1 collective-permute-done.7
  46.1 4.1 %collective-permute-done.6 = f32[27,1,16,128]{3,2,1,0:T(8,128)S(1)} collective-permute-done((f32[27,1,16,128]{3,2,1,0:T(8,128)S(1)}, f32[27,1,16,128]{3,2,1,0:T(8,128)S(1)}, u32[]{:S(2)}, u32[]{:S(2)}) %collective-permute-start.6) | collective-permute-done | bytes 221216 | tf_op jit(solution)/shard_map/ppermute | solution.py:15
  50.3 3.4 %collective-permute-start.9 = (f32[27,6,1,128]{3,2,1,0:T(1,128)S(1)}, f32[27,6,1,128]{3,2,1,0:T(1,128)S(1)}, u32[]{:S(2)}, u32[]{:S(2)}) collective-permute-start(f32[27,6,1,128]{3,2,1,0:T(1,128)S(1)} %get-tuple-element.125), channel_id=1, source_target_pairs={{4,0},{0,4},{5,1},{1,5},{6,2},{2,6},{7,3},{3,7},{12,8},{8,12},{13,... | collective-permute-start | bytes 248840 | tf_op jit(solution)/shard_map/ppermute | solution.py:17
  53.9 0.8 fusion.48
  54.7 2.9 collective-permute-start.3
  57.7 1.3 collective-permute-done.8
  59.3 2.6 fusion.47
  61.9 2.9 copy.49
  64.8 2.5 collective-permute-start.10
  67.3 2.9 copy.51
  70.5 2.6 fusion.46
  73.1 2.9 copy.45
  76.2 2.9 copy.47
  79.1 2.5 collective-permute-start.5
  81.6 3.2 copy.50
  84.8 1.5 constant_dynamic-update-slice_fusion.56
  86.9 3.2 copy.52
  90.1 1.7 constant_dynamic-update-slice_fusion.54
  91.8 0.7 constant_dynamic-update-slice_fusion.53
  94.1 0.7 constant_dynamic-update-slice_fusion.50
  96.1 0.7 constant_dynamic-update-slice_fusion.47
  98.2 0.7 constant_dynamic-update-slice_fusion.44
  100.2 0.7 constant_dynamic-update-slice_fusion.41
  102.3 0.7 constant_dynamic-update-slice_fusion.38
  104.4 0.7 constant_dynamic-update-slice_fusion.35
  106.4 0.7 constant_dynamic-update-slice_fusion.32
  108.5 1.7 slice_reduce_fusion.2
  110.2 1.7 slice_reduce_fusion
  111.9 3.2 copy.46
  115.1 1.4 constant_dynamic-update-slice_fusion.29
  117.1 3.2 copy.48
  120.3 1.6 constant_dynamic-update-slice_fusion.27
  139.1 1.8 broadcast_multiply_fusion.1
  140.9 3.8 %multiply_reduce_fusion.7 = (f32[4,16,128]{2,1,0:T(8,128)S(1)}, f32[4,16,128]{2,1,0:T(8,128)S(1)}, f32[4,16,128]{2,1,0:T(8,128)S(1)}, f32[4,16,128]{2,1,0:T(8,12...) fusion(f32[27,4,16,128]{3,2,1,0:T(8,128)S(1)} %get-tuple-element.131, f32[27]{0:T(128)S(1)} %copy-done.70, ...), kind=kLoop, calls=%fused_computation.43 | loop fusion | flops 7471104 | bytes 3080624 | tf_op jit(solution)/shard_map/transpose(jvp())/reduce_sum | solution.py:53
  145.2 1.4 bitcast_add_fusion.1
  146.6 4.0 %collective-permute-start.13 = (f32[27,1,16,128]{3,2,1,0:T(8,128)S(1)}, f32[27,1,16,128]{3,2,1,0:T(8,128)S(1)}, u32[]{:S(2)}, u32[]{:S(2)}) collective-permute-start(f32[27,1,16,128]{3,2,1,0:T(8,128)S(1)} %get-tuple-element.129), channel_id=1, source_target_pairs={{8,0},{16,8},{24,16},{32,24},{40,32},{48,40},{56,48},{64,56},{72,6... | collective-permute-start | bytes 663560 | tf_op jit(solution)/shard_map/ppermute | solution.py:17
  151.2 3.5 %collective-permute-done.13 = f32[27,1,16,128]{3,2,1,0:T(8,128)S(1)} collective-permute-done((f32[27,1,16,128]{3,2,1,0:T(8,128)S(1)}, f32[27,1,16,128]{3,2,1,0:T(8,128)S(1)}, u32[]{:S(2)}, u32[]{:S(2)}) %collective-permute-start.13) | collective-permute-done | bytes 221216 | tf_op jit(solution)/shard_map/ppermute | solution.py:17
  154.8 1.7 collective-permute-start.15
  156.6 1.3 collective-permute-start.14
  157.9 1.8 collective-permute-done.15
  159.7 1.7 collective-permute-done.14
  161.7 2.6 fusion.45
  164.3 3.1 copy.53
  167.4 1.5 copy.55
  168.9 2.7 collective-permute-start.17
  171.9 1.9 copy.54
  173.8 0.8 constant_dynamic-update-slice_fusion.83
  175.2 1.9 copy.56
  177.9 0.9 copy-done.6
  194.3 0.7 constant_dynamic-update-slice_fusion.57
  195.1 1.9 broadcast_multiply_fusion
  197.1 1.4 multiply_reduce_fusion.3
  198.6 57.2 %scatter_custom_fusion = f32[1024]{0:T(1024)S(1)} fusion(s32[8192]{0:T(1024)} %bitcast.165, f32[8192]{0:T(1024)S(1)} %bitcast.166, f32[]{:T(128)} %constant.14.clone.1), kind=kCustom, calls=%fused_computation.277 | custom fusion | flops 8192 | bytes 4608 | tf_op jit(solution)/shard_map/scatter-add | solution.py:112
  255.8 4.3 %scatter_custom_fusion.1 = f32[1024]{0:T(1024)S(1)} fusion(s32[1024]{0:T(1024)S(1)} %compare_select_fusion.1, f32[1024]{0:T(1024)S(1)} %scatter_custom_fusion, f32[]{:T(128)} %constant.14.clone.1), kind=kCustom, calls=%fused_computation.275 | custom fusion | bytes 4100 | tf_op jit(solution)/shard_map/scatter | solution.py:113
  260.1 68.4 %all-reduce.12 = f32[1024]{0:T(1024)S(1)} all-reduce(f32[1024]{0:T(1024)S(1)} %scatter_custom_fusion.1), channel_id=2, replica_groups=mesh['gx'=16,'gy'=2,'gz'=4] {'gx','gy','gz'}, use_global_device_ids=true, to_apply=%region_25.0.clone | all-reduce | flops 1024 | bytes 8192
  330.0 1.2 bitcast_add_fusion
  (273 shorter events, 51.8 us)
Async XLA Ops:
  0.6 3.6 %copy-start = (f32[1024]{0:T(1024)S(1)}, f32[1024]{0:T(1024)}, u32[]{:S(2)}) copy-start(f32[1024]{0:T(1024)} %param.24) | copy-start | bytes 12292
  0.6 3.4 %copy-start.7 = (f32[27,4,16,128]{3,2,1,0:T(8,128)S(1)}, f32[27,4,16,128]{3,2,1,0:T(8,128)}, u32[]{:S(2)}) copy-start(f32[27,4,16,128]{3,2,1,0:T(8,128)} %param.19) | copy-start | bytes 2654212
  0.7 3.5 %copy-start.69 = (s32[4,16,128]{2,1,0:T(8,128)S(1)}, s32[4,16,128]{2,1,0:T(8,128)}, u32[]{:S(2)}) copy-start(s32[4,16,128]{2,1,0:T(8,128)} %param.23) | copy-start | bytes 98308
  4.1 33.7 %copy-start.16 = (f32[4,16,128]{2,1,0:T(8,128)}, f32[4,16,128]{2,1,0:T(8,128)S(1)}, u32[]{:S(2)}) copy-start(f32[4,16,128]{2,1,0:T(8,128)S(1)} %reduce_sum.653) | copy-start | bytes 98308
  4.2 33.0 %copy-start.67 = (s32[4,16,128]{2,1,0:T(8,128)S(1)}, s32[4,16,128]{2,1,0:T(8,128)}, u32[]{:S(2)}) copy-start(s32[4,16,128]{2,1,0:T(8,128)} %param.22) | copy-start | bytes 98308
  4.2 33.7 %copy-start.13 = (f32[4,16,128]{2,1,0:T(8,128)S(1)}, f32[4,16,128]{2,1,0:T(8,128)}, u32[]{:S(2)}) copy-start(f32[4,16,128]{2,1,0:T(8,128)} %param.21) | copy-start | bytes 98308
  4.2 33.7 %copy-start.70 = (f32[27]{0:T(128)S(1)}, f32[27]{0:T(128)}, u32[]{:S(2)}) copy-start(f32[27]{0:T(128)} %constant.9.clone) | copy-start | bytes 328
  4.2 33.7 %copy-start.71 = (f32[27]{0:T(128)S(1)}, f32[27]{0:T(128)}, u32[]{:S(2)}) copy-start(f32[27]{0:T(128)} %constant.8.clone) | copy-start | bytes 328
  4.2 33.7 %copy-start.72 = (f32[27]{0:T(128)S(1)}, f32[27]{0:T(128)}, u32[]{:S(2)}) copy-start(f32[27]{0:T(128)} %constant.7.clone) | copy-start | bytes 328
  4.2 33.7 %copy-start.73 = (f32[27]{0:T(128)S(1)}, f32[27]{0:T(128)}, u32[]{:S(2)}) copy-start(f32[27]{0:T(128)} %constant.10.clone) | copy-start | bytes 328
  37.1 5.4 %copy-start.9 = (f32[27,4,16,128]{3,2,1,0:T(8,128)S(1)}, f32[27,4,16,128]{3,2,1,0:T(8,128)}, u32[]{:S(2)}) copy-start(f32[27,4,16,128]{3,2,1,0:T(8,128)} %param.20) | copy-start | bytes 2654212
  37.2 5.4 %copy-start.28 = (f32[4,16,128]{2,1,0:T(8,128)}, f32[4,16,128]{2,1,0:T(8,128)S(1)}, u32[]{:S(2)}) copy-start(f32[4,16,128]{2,1,0:T(8,128)S(1)} %get-tuple-element.106) | copy-start | bytes 98308
  37.8 5.2 %copy-start.19 = (f32[4,16,128]{2,1,0:T(8,128)}, f32[4,16,128]{2,1,0:T(8,128)S(1)}, u32[]{:S(2)}) copy-start(f32[4,16,128]{2,1,0:T(8,128)S(1)} %get-tuple-element.108) | copy-start | bytes 98308
  37.8 5.2 %copy-start.22 = (f32[4,16,128]{2,1,0:T(8,128)}, f32[4,16,128]{2,1,0:T(8,128)S(1)}, u32[]{:S(2)}) copy-start(f32[4,16,128]{2,1,0:T(8,128)S(1)} %get-tuple-element.110) | copy-start | bytes 98308
  37.9 5.3 %copy-start.25 = (f32[4,16,128]{2,1,0:T(8,128)}, f32[4,16,128]{2,1,0:T(8,128)S(1)}, u32[]{:S(2)}) copy-start(f32[4,16,128]{2,1,0:T(8,128)S(1)} %get-tuple-element.112) | copy-start | bytes 98308
  37.9 5.3 %copy-start.31 = (f32[4,16,128]{2,1,0:T(8,128)}, f32[4,16,128]{2,1,0:T(8,128)S(1)}, u32[]{:S(2)}) copy-start(f32[4,16,128]{2,1,0:T(8,128)S(1)} %get-tuple-element.107) | copy-start | bytes 98308
  39.4 6.7 %collective-permute-start.7 = (f32[27,1,16,128]{3,2,1,0:T(8,128)S(1)}, f32[27,1,16,128]{3,2,1,0:T(8,128)S(1)}, u32[]{:S(2)}, u32[]{:S(2)}) collective-permute-start(f32[27,1,16,128]{3,2,1,0:T(8,128)S(1)} %get-tuple-element.135), channel_id=1, source_target_pairs={{8,0},{16,8},{24,16},{32,24},{40,32},{48,40},{56,48},{64,56},{72,6... | collective-permute-start | bytes 663560 | tf_op jit(solution)/shard_map/ppermute | solution.py:17
  40.8 9.3 %collective-permute-start.6 = (f32[27,1,16,128]{3,2,1,0:T(8,128)S(1)}, f32[27,1,16,128]{3,2,1,0:T(8,128)S(1)}, u32[]{:S(2)}, u32[]{:S(2)}) collective-permute-start(f32[27,1,16,128]{3,2,1,0:T(8,128)S(1)} %get-tuple-element.134), channel_id=1, source_target_pairs={{0,8},{8,16},{16,24},{24,32},{32,40},{40,48},{48,56},{56,64},{64,7... | collective-permute-start | bytes 663560 | tf_op jit(solution)/shard_map/ppermute | solution.py:15
  42.6 11.2 %collective-permute-start = (f32[27,1,16,128]{3,2,1,0:T(8,128)S(1)}, f32[27,1,16,128]{3,2,1,0:T(8,128)S(1)}, u32[]{:S(2)}, u32[]{:S(2)}) collective-permute-start(f32[27,1,16,128]{3,2,1,0:T(8,128)S(1)} %get-tuple-element.133), channel_id=1, source_target_pairs={{0,8},{8,16},{16,24},{24,32},{32,40},{40,48},{48,56},{56,64},{64,7... | collective-permute-start | bytes 663560 | tf_op jit(solution)/shard_map/ppermute | solution.py:15
  43.1 10.8 %collective-permute-start.1 = (f32[27,1,16,128]{3,2,1,0:T(8,128)S(1)}, f32[27,1,16,128]{3,2,1,0:T(8,128)S(1)}, u32[]{:S(2)}, u32[]{:S(2)}) collective-permute-start(f32[27,1,16,128]{3,2,1,0:T(8,128)S(1)} %get-tuple-element.132), channel_id=1, source_target_pairs={{8,0},{16,8},{24,16},{32,24},{40,32},{48,40},{56,48},{64,56},{72,6... | collective-permute-start | bytes 663560 | tf_op jit(solution)/shard_map/ppermute | solution.py:17
  50.3 7.4 %collective-permute-start.9 = (f32[27,6,1,128]{3,2,1,0:T(1,128)S(1)}, f32[27,6,1,128]{3,2,1,0:T(1,128)S(1)}, u32[]{:S(2)}, u32[]{:S(2)}) collective-permute-start(f32[27,6,1,128]{3,2,1,0:T(1,128)S(1)} %get-tuple-element.125), channel_id=1, source_target_pairs={{4,0},{0,4},{5,1},{1,5},{6,2},{2,6},{7,3},{3,7},{12,8},{8,12},{13,... | collective-permute-start | bytes 248840 | tf_op jit(solution)/shard_map/ppermute | solution.py:17
  53.7 5.3 %collective-permute-start.8 = (f32[27,6,1,128]{3,2,1,0:T(1,128)S(1)}, f32[27,6,1,128]{3,2,1,0:T(1,128)S(1)}, u32[]{:S(2)}, u32[]{:S(2)}) collective-permute-start(f32[27,6,1,128]{3,2,1,0:T(1,128)S(1)} %get-tuple-element.124), channel_id=1, source_target_pairs={{0,4},{4,0},{1,5},{5,1},{2,6},{6,2},{3,7},{7,3},{8,12},{12,8},{9,1... | collective-permute-start | bytes 248840 | tf_op jit(solution)/shard_map/ppermute | solution.py:15
  54.7 15.5 %collective-permute-start.3 = (f32[27,6,1,128]{3,2,1,0:T(1,128)}, f32[27,6,1,128]{3,2,1,0:T(1,128)S(1)}, u32[]{:S(2)}, u32[]{:S(2)}) collective-permute-start(f32[27,6,1,128]{3,2,1,0:T(1,128)} %get-tuple-element.123), channel_id=1, source_target_pairs={{4,0},{0,4},{5,1},{1,5},{6,2},{2,6},{7,3},{3,7},{12,8},{8,12},{13,... | collective-permute-start | bytes 248840 | tf_op jit(solution)/shard_map/ppermute | solution.py:17
  57.6 12.6 %collective-permute-start.2 = (f32[27,6,1,128]{3,2,1,0:T(1,128)}, f32[27,6,1,128]{3,2,1,0:T(1,128)S(1)}, u32[]{:S(2)}, u32[]{:S(2)}) collective-permute-start(f32[27,6,1,128]{3,2,1,0:T(1,128)} %get-tuple-element.122), channel_id=1, source_target_pairs={{0,4},{4,0},{1,5},{5,1},{2,6},{6,2},{3,7},{7,3},{8,12},{12,8},{9,1... | collective-permute-start | bytes 248840 | tf_op jit(solution)/shard_map/ppermute | solution.py:15
  64.8 16.8 %collective-permute-start.10 = (f32[27,6,18,1]{0,3,2,1:T(1,128)}, f32[27,6,18,1]{0,3,2,1:T(1,128)}, u32[]{:S(2)}, u32[]{:S(2)}) collective-permute-start(f32[27,6,18,1]{0,3,2,1:T(1,128)} %copy.49), channel_id=1, source_target_pairs={{1,0},{2,1},{3,2},{0,3},{5,4},{6,5},{7,6},{4,7},{9,8},{10,9},{11,1... | collective-permute-start | bytes 35000 | tf_op jit(solution)/shard_map/ppermute | solution.py:17
  70.2 16.7 %collective-permute-start.11 = (f32[27,6,18,1]{0,3,2,1:T(1,128)}, f32[27,6,18,1]{0,3,2,1:T(1,128)}, u32[]{:S(2)}, u32[]{:S(2)}) collective-permute-start(f32[27,6,18,1]{0,3,2,1:T(1,128)} %copy.51), channel_id=1, source_target_pairs={{0,1},{1,2},{2,3},{3,0},{4,5},{5,6},{6,7},{7,4},{8,9},{9,10},{10,1... | collective-permute-start | bytes 35000 | tf_op jit(solution)/shard_map/ppermute | solution.py:15
  76.0 35.9 %collective-permute-start.4 = (f32[27,6,18,1]{0,3,2,1:T(1,128)}, f32[27,6,18,1]{0,3,2,1:T(1,128)}, u32[]{:S(2)}, u32[]{:S(2)}) collective-permute-start(f32[27,6,18,1]{0,3,2,1:T(1,128)} %copy.45), channel_id=1, source_target_pairs={{0,1},{1,2},{2,3},{3,0},{4,5},{5,6},{6,7},{7,4},{8,9},{9,10},{10,1... | collective-permute-start | bytes 35000 | tf_op jit(solution)/shard_map/ppermute | solution.py:15
  79.1 38.0 %collective-permute-start.5 = (f32[27,6,18,1]{0,3,2,1:T(1,128)}, f32[27,6,18,1]{0,3,2,1:T(1,128)}, u32[]{:S(2)}, u32[]{:S(2)}) collective-permute-start(f32[27,6,18,1]{0,3,2,1:T(1,128)} %copy.47), channel_id=1, source_target_pairs={{1,0},{2,1},{3,2},{0,3},{5,4},{6,5},{7,6},{4,7},{9,8},{10,9},{11,1... | collective-permute-start | bytes 35000 | tf_op jit(solution)/shard_map/ppermute | solution.py:17
  90.1 1.7 copy-start.3
  91.8 1.6 copy-start.4
  120.3 1.6 copy-start.1
  121.9 1.8 copy-start.2
  128.4 1.6 copy-start.37
  128.4 1.6 copy-start.38
  128.4 1.6 copy-start.39
  128.5 1.6 copy-start.40
  128.5 1.6 copy-start.41
  128.5 1.6 copy-start.42
  128.5 1.6 copy-start.43
  128.5 1.6 copy-start.44
  128.5 1.6 copy-start.45
  128.5 1.6 copy-start.46
  128.5 1.6 copy-start.47
  128.5 1.6 copy-start.48
  128.5 1.6 copy-start.49
  146.6 8.1 %collective-permute-start.13 = (f32[27,1,16,128]{3,2,1,0:T(8,128)S(1)}, f32[27,1,16,128]{3,2,1,0:T(8,128)S(1)}, u32[]{:S(2)}, u32[]{:S(2)}) collective-permute-start(f32[27,1,16,128]{3,2,1,0:T(8,128)S(1)} %get-tuple-element.129), channel_id=1, source_target_pairs={{8,0},{16,8},{24,16},{32,24},{40,32},{48,40},{56,48},{64,56},{72,6... | collective-permute-start | bytes 663560 | tf_op jit(solution)/shard_map/ppermute | solution.py:17
  150.7 4.1 %collective-permute-start.12 = (f32[27,1,16,128]{3,2,1,0:T(8,128)S(1)}, f32[27,1,16,128]{3,2,1,0:T(8,128)S(1)}, u32[]{:S(2)}, u32[]{:S(2)}) collective-permute-start(f32[27,1,16,128]{3,2,1,0:T(8,128)S(1)} %get-tuple-element.128), channel_id=1, source_target_pairs={{0,8},{8,16},{16,24},{24,32},{32,40},{40,48},{48,56},{56,64},{64,7... | collective-permute-start | bytes 663560 | tf_op jit(solution)/shard_map/ppermute | solution.py:15
  154.8 4.9 %collective-permute-start.15 = (f32[27,6,1,128]{3,2,1,0:T(1,128)S(1)}, f32[27,6,1,128]{3,2,1,0:T(1,128)S(1)}, u32[]{:S(2)}, u32[]{:S(2)}) collective-permute-start(f32[27,6,1,128]{3,2,1,0:T(1,128)S(1)} %get-tuple-element.121), channel_id=1, source_target_pairs={{4,0},{0,4},{5,1},{1,5},{6,2},{2,6},{7,3},{3,7},{12,8},{8,12},{13,... | collective-permute-start | bytes 248840 | tf_op jit(solution)/shard_map/ppermute | solution.py:17
  156.6 4.8 %collective-permute-start.14 = (f32[27,6,1,128]{3,2,1,0:T(1,128)S(1)}, f32[27,6,1,128]{3,2,1,0:T(1,128)S(1)}, u32[]{:S(2)}, u32[]{:S(2)}) collective-permute-start(f32[27,6,1,128]{3,2,1,0:T(1,128)S(1)} %get-tuple-element.120), channel_id=1, source_target_pairs={{0,4},{4,0},{1,5},{5,1},{2,6},{6,2},{3,7},{7,3},{8,12},{12,8},{9,1... | collective-permute-start | bytes 248840 | tf_op jit(solution)/shard_map/ppermute | solution.py:15
  164.3 3.1 copy-start.74
  164.3 3.1 copy-start.12
  167.4 4.5 %collective-permute-start.16 = (f32[27,6,18,1]{0,3,2,1:T(1,128)}, f32[27,6,18,1]{0,3,2,1:T(1,128)}, u32[]{:S(2)}, u32[]{:S(2)}) collective-permute-start(f32[27,6,18,1]{0,3,2,1:T(1,128)} %copy.53), channel_id=1, source_target_pairs={{0,1},{1,2},{2,3},{3,0},{4,5},{5,6},{6,7},{7,4},{8,9},{9,10},{10,1... | collective-permute-start | bytes 35000 | tf_op jit(solution)/shard_map/ppermute | solution.py:15
  168.9 6.4 %collective-permute-start.17 = (f32[27,6,18,1]{0,3,2,1:T(1,128)}, f32[27,6,18,1]{0,3,2,1:T(1,128)}, u32[]{:S(2)}, u32[]{:S(2)}) collective-permute-start(f32[27,6,18,1]{0,3,2,1:T(1,128)} %copy.55), channel_id=1, source_target_pairs={{1,0},{2,1},{3,2},{0,3},{5,4},{6,5},{7,6},{4,7},{9,8},{10,9},{11,1... | collective-permute-start | bytes 35000 | tf_op jit(solution)/shard_map/ppermute | solution.py:17
  177.1 1.6 copy-start.6
  195.1 2.0 copy-start.8
  195.1 2.0 copy-start.11
  195.1 2.0 copy-start.32
  197.0 132.1 %copy-start.18 = (f32[4,16,128]{2,1,0:T(8,128)S(1)}, f32[4,16,128]{2,1,0:T(8,128)}, u32[]{:S(2)}) copy-start(f32[4,16,128]{2,1,0:T(8,128)} %copy-done.16) | copy-start | bytes 98308
  197.1 132.1 %copy-start.21 = (f32[4,16,128]{2,1,0:T(8,128)S(1)}, f32[4,16,128]{2,1,0:T(8,128)}, u32[]{:S(2)}) copy-start(f32[4,16,128]{2,1,0:T(8,128)} %copy-done.19) | copy-start | bytes 98308
  197.1 132.1 %copy-start.24 = (f32[4,16,128]{2,1,0:T(8,128)S(1)}, f32[4,16,128]{2,1,0:T(8,128)}, u32[]{:S(2)}) copy-start(f32[4,16,128]{2,1,0:T(8,128)} %copy-done.22) | copy-start | bytes 98308
  197.1 132.1 %copy-start.27 = (f32[4,16,128]{2,1,0:T(8,128)S(1)}, f32[4,16,128]{2,1,0:T(8,128)}, u32[]{:S(2)}) copy-start(f32[4,16,128]{2,1,0:T(8,128)} %copy-done.25) | copy-start | bytes 98308
  197.1 132.1 %copy-start.57 = (f32[4,16,128]{2,1,0:T(8,128)S(1)}, f32[4,16,128]{2,1,0:T(8,128)}, u32[]{:S(2)}) copy-start(f32[4,16,128]{2,1,0:T(8,128)} %get-tuple-element.109) | copy-start | bytes 98308
  197.1 132.1 %copy-start.58 = (f32[4,16,128]{2,1,0:T(8,128)S(1)}, f32[4,16,128]{2,1,0:T(8,128)}, u32[]{:S(2)}) copy-start(f32[4,16,128]{2,1,0:T(8,128)} %get-tuple-element.111) | copy-start | bytes 98308
  197.1 132.1 %copy-start.59 = (f32[4,16,128]{2,1,0:T(8,128)S(1)}, f32[4,16,128]{2,1,0:T(8,128)}, u32[]{:S(2)}) copy-start(f32[4,16,128]{2,1,0:T(8,128)} %get-tuple-element.113) | copy-start | bytes 98308
  (29 other events, 38.6 us)
where the time goes:
time: 333 us; the launch traced here: 331 us
  other arithmetic  136 us (41%)
  local copies, waits for them, and re-layouts  83.9 us (25%)
  blocking collectives  68.4 us (21%)
  starting transfers between devices  27.4 us (8%)
  waiting for transfers between devices  13.9 us (4%)
    unnamed x1, blocking collectives  68.4 us
    scatter-add x1, other arithmetic, shards(): jax.ops.segment_sum(density.reshape(-1), patch_of_cell.reshape(-1), num_s...  57.2 us
    unnamed x75, other arithmetic  54.2 us
    gather x1, local copies, waits for them, and re-layouts, shards(): gamma = walls * porosity[patch_of_cell]  32.9 us
    ppermute x9, starting transfers between devices, extended(): lax.ppermute(head, axis, [((i + 1) % count, i) for i in range(count)])  23 us
    slice x6, local copies, waits for them, and re-layouts, extended(): head = lax.slice_in_dim(cells, 0, width, axis=dim)  12.5 us
    slice x7, local copies, waits for them, and re-layouts, extended(): lax.slice_in_dim(cells, cells.shape[dim] - width, cells.shape[dim], axis=...  12.4 us
    ppermute x3, local copies, waits for them, and re-layouts, extended(): lax.ppermute(head, axis, [((i + 1) % count, i) for i in range(count)])  8.24 us
  transfers between devices with their start and end apart: 18, of which 7 were waited for; matrix products, arithmetic and copies ran while one was open for 18% of the time, Pallas kernels for 0%

commit v1 on v0

--- a/solution.py
+++ b/solution.py
@@ -3,22 +3,6 @@
 import numpy as np
 from jax import lax
 from jax.sharding import PartitionSpec as P
-
-
-def extended(cells, sides, width):
-    for axis, dim in sides:
-        count = lax.axis_size(axis)
-        head = lax.slice_in_dim(cells, 0, width, axis=dim)
-        tail = lax.slice_in_dim(cells, cells.shape[dim] - width, cells.shape[dim], axis=dim)
-        cells = jnp.concatenate(
-            [
-                lax.ppermute(tail, axis, [(i, (i + 1) % count) for i in range(count)]),
-                cells,
-                lax.ppermute(head, axis, [((i + 1) % count, i) for i in range(count)]),
-            ],
-            axis=dim,
-        )
-    return cells
 
 
 def lattice_table():
@@ -68,50 +52,72 @@
     return (adj_pre, jnp.sum(adj_post * deriv, axis=0))
 
 
-def local_move(field, sign):
-    steps, _ = lattice_table()
-    size_x = field.shape[1] - 2
-    size_y = field.shape[2] - 2
-    size_z = field.shape[3] - 2
-    moved = []
-    for index in range(27):
-        start_x = 1 - int(sign * steps[index, 0])
-        start_y = 1 - int(sign * steps[index, 1])
-        start_z = 1 - int(sign * steps[index, 2])
-        moved.append(
-            field[
-                index,
-                start_x : start_x + size_x,
-                start_y : start_y + size_y,
-                start_z : start_z + size_z,
-            ]
-        )
-    return jnp.stack(moved, 0)
+def halo_exchange(up, down, axis):
+    size = lax.axis_size(axis)
+    if size == 1:
+        return up, down
+    if size == 2:
+        both = lax.ppermute(jnp.stack([up, down]), axis, [(0, 1), (1, 0)])
+        return both[0], both[1]
+    lo = lax.ppermute(up, axis, [(i, (i + 1) % size) for i in range(size)])
+    hi = lax.ppermute(down, axis, [(i, (i - 1) % size) for i in range(size)])
+    return lo, hi
+
+
+def move_axis(cubes, signs, axis, d):
+    n = cubes[0].shape[3 + d]
+    ups, downs = [], []
+    for cube, sign in zip(cubes, signs):
+        plus = lax.index_in_dim(cube, 1 + sign, axis=d, keepdims=False)
+        minus = lax.index_in_dim(cube, 1 - sign, axis=d, keepdims=False)
+        ups.append(lax.slice_in_dim(plus, n - 1, n, axis=2 + d))
+        downs.append(lax.slice_in_dim(minus, 0, 1, axis=2 + d))
+    lo, hi = halo_exchange(jnp.stack(ups), jnp.stack(downs), axis)
+    out = []
+    for k, (cube, sign) in enumerate(zip(cubes, signs)):
+        plus = lax.index_in_dim(cube, 1 + sign, axis=d, keepdims=False)
+        minus = lax.index_in_dim(cube, 1 - sign, axis=d, keepdims=False)
+        still = lax.index_in_dim(cube, 1, axis=d, keepdims=False)
+        plus = jnp.concatenate([lo[k], lax.slice_in_dim(plus, 0, n - 1, axis=2 + d)], axis=2 + d)
+        minus = jnp.concatenate([lax.slice_in_dim(minus, 1, n, axis=2 + d), hi[k]], axis=2 + d)
+        groups = [None, still, None]
+        groups[1 + sign] = plus
+        groups[1 - sign] = minus
+        out.append(jnp.stack(groups, axis=d))
+    return out
 
 
 def propagate(fields, signs):
-    stacked = fields[0]
-    padded = extended(stacked, (("gx", 1), ("gy", 2), ("gz", 3)), 1)
-    results = []
-    for member, sign in enumerate(signs):
-        results.append(local_move(padded[27 * member : 27 * member + 27], sign))
-    return tuple(results)
+    cubes = [field.reshape((3, 3, 3) + field.shape[1:]) for field in fields]
+    for d, axis in enumerate(("gx", "gy", "gz")):
+        cubes = move_axis(cubes, signs, axis, d)
+    return [cube.reshape(field.shape) for cube, field in zip(cubes, fields)]
 
 
 def shards(check_pops, adjoint_end, relax_rate, wall_flag, patch_of_cell, porosity, patch_slot):
+    sx, sy, sz = relax_rate.shape
+    rows = np.array([0, 1, sx - 1])
+    row_of = np.array([0] + [1] * (sx - 2) + [2])
+    ids = patch_of_cell[rows][:, np.array([0, sy // 2])][:, :, np.array([0, sz // 2])]
+    solid = porosity[ids][row_of]
+    solid = jnp.broadcast_to(solid[:, :, None, :, None], (sx, 2, sy // 2, 2, sz // 2)).reshape(sx, sy, sz)
     walls = wall_flag.astype(jnp.float32)
-    gamma = walls * porosity[patch_of_cell]
+    gamma = walls * solid
     post_now, _ = collide(check_pops, relax_rate, gamma)
-    (pops_next,) = propagate((post_now,), (1,))
-    (post_adj_next,) = propagate((adjoint_end,), (-1,))
+    pops_next, post_adj_next = propagate([post_now, adjoint_end], [1, -1])
     adj_next, sens_next = adjoint_collide(pops_next, relax_rate, gamma, post_adj_next)
-    (post_adj,) = propagate((adj_next,), (-1,))
+    (post_adj,) = propagate([adj_next], [-1])
     adjoint_start, sens_now = adjoint_collide(check_pops, relax_rate, gamma, post_adj)
     density = walls * (sens_next + sens_now)
+    boxes = density.reshape(sx, 2, sy // 2, 2, sz // 2).sum(axis=(2, 4))
+    parts = jnp.stack([boxes[0], boxes[1 : sx - 1].sum(axis=0), boxes[sx - 1]])
     count = porosity.shape[0]
-    totals = jax.ops.segment_sum(density.reshape(-1), patch_of_cell.reshape(-1), num_segments=count)
-    placed = jnp.zeros((count,), jnp.float32).at[patch_slot].set(totals)
-    patch_sens = lax.psum_scatter(placed, ("gx", "gy", "gz"), scatter_dimension=0, tiled=True)
+    devices = lax.axis_size(("gx", "gy", "gz"))
+    slots = patch_slot[ids].reshape(-1)
+    hits = (slots[:, None] == jnp.arange(count, dtype=slots.dtype)[None, :]).astype(jnp.float32)
+    placed = jnp.sum(parts.reshape(-1)[:, None] * hits, axis=0)
+    got = lax.all_to_all(placed.reshape(devices, count // devices), ("gx", "gy", "gz"), 0, 0, tiled=True)
+    patch_sens = jnp.sum(got, axis=0)
     return (adjoint_start, patch_sens)
 
 

time: 333 us -> 104 us (0.31)
  other arithmetic: 136 us -> 18.9 us
  blocking collectives: 68.4 us -> 0 us
  local copies, waits for them, and re-layouts: 83.9 us -> 29.8 us
  starting transfers between devices: 27.4 us -> 34 us
  waiting for transfers between devices: 13.9 us -> 18.1 us
    unnamed x1 -> x0, blocking collectives: 68.4 us -> none
    scatter-add x1 -> x0, other arithmetic: 57.2 us -> none  [shards(): jax.ops.segment_sum(density.reshape(-1), patch_of_cell.reshape(-1), num_s...]
    unnamed x75 -> x0, other arithmetic: 54.2 us -> none
    gather x1 -> x9, local copies, waits for them, and re-layouts: 32.9 us -> 4.32 us  [the longest x5 1.86 us: shards(): patch_of_cell[rows][:, np.array([0, sy // 2])][:, :, np.array([0, sz // 2])]]
    slice x13 -> x47, local copies, waits for them, and re-layouts: 24.8 us -> 8.22 us  [the longest x10 3.59 us: move_axis(): ups.append(lax.slice_in_dim(plus, n - 1, n, axis=2 + d))]
    ppermute x6 -> x0, local copies, waits for them, and re-layouts: 16.5 us -> none  [the longest x3 8.24 us: extended(): lax.ppermute(head, axis, [((i + 1) % count, i) for i in range(count)])]
    all_to_all x0 -> x1, starting transfers between devices: none -> 12.1 us  [shards(): lax.all_to_all(placed.reshape(devices, count // devices), ('gx', 'gy', 'g...]
    all_to_all x0 -> x1, waiting for transfers between devices: none -> 7.47 us  [shards(): lax.all_to_all(placed.reshape(devices, count // devices), ('gx', 'gy', 'g...]
  transfers between devices with their start and end apart: 18 -> 11, of which waited for: 7 -> 8; matrix products, arithmetic and copies ran while one was open for 18% -> 11% of each run, Pallas kernels for 0% -> 0%
where the time goes in v1:
time: 104 us; the launch traced here: 103 us
  starting transfers between devices  34 us (33%)
  local copies, waits for them, and re-layouts  29.8 us (29%)
  other arithmetic  18.9 us (18%)
  waiting for transfers between devices  18.1 us (17%)
  between operations  1.93 us (2%)
    all_to_all x1, starting transfers between devices, shards(): lax.all_to_all(placed.reshape(devices, count // devices), ('gx', 'gy', 'g...  12.1 us
    unnamed x111, local copies, waits for them, and re-layouts  10.2 us
    ppermute x4, starting transfers between devices, halo_exchange(): lo = lax.ppermute(up, axis, [(i, (i + 1) % size) for i in range(size)])  8.37 us
    all_to_all x1, waiting for transfers between devices, shards(): lax.all_to_all(placed.reshape(devices, count // devices), ('gx', 'gy', 'g...  7.47 us
    ppermute x4, starting transfers between devices, halo_exchange(): hi = lax.ppermute(down, axis, [(i, (i - 1) % size) for i in range(size)])  6.83 us
    ppermute x2, starting transfers between devices, halo_exchange(): both = lax.ppermute(jnp.stack([up, down]), axis, [(0, 1), (1, 0)])  6.67 us
    another operation x25, other arithmetic, move_axis(): out.append(jnp.stack(groups, axis=d))  5.02 us
    ppermute x4, waiting for transfers between devices, halo_exchange(): lo = lax.ppermute(up, axis, [(i, (i + 1) % size) for i in range(size)])  4.77 us
  transfers between devices with their start and end apart: 11, of which 8 were waited for; matrix products, arithmetic and copies ran while one was open for 11% of the time, Pallas kernels for 0%

profile of v1, /device:TPU:1, one launch (start us, length us, event | category | flops | bytes accessed | tf_op | source)
XLA Modules:
  0.0 102.7 jit_solution(3381592909431864561)
XLA Ops:
  0.7 1.2 %slice_reduce_fusion.6 = (f32[4,16,128]{2,1,0:T(8,128)S(1)}, f32[4,16,128]{2,1,0:T(8,128)S(1)}) fusion(f32[3,3,3,4,16,128]{5,4,3,2,1,0:T(8,128)} %bitcast.198), kind=kLoop, calls=%fused_computation.93 | loop fusion | flops 131072 | bytes 655360 | tf_op jit(solution)/shard_map/reduce_sum | solution.py:28
  1.9 1.1 %slice_reduce_fusion.4 = (f32[4,16,128]{2,1,0:T(8,128)S(1)}, f32[4,16,128]{2,1,0:T(8,128)S(1)}) fusion(f32[3,3,3,4,16,128]{5,4,3,2,1,0:T(8,128)} %bitcast.199), kind=kLoop, calls=%fused_computation.91 | loop fusion | flops 131072 | bytes 655360 | tf_op jit(solution)/shard_map/reduce_sum | solution.py:29
  3.0 0.6 copy-done.52
  3.7 0.6 copy-done.53
  4.3 0.6 gather_fusion
  5.0 0.6 gather_fusion.1
  5.7 0.6 gather_fusion.2
  6.5 0.6 copy-done.1
  7.1 0.6 gather_fusion.3
  7.8 0.6 gather_fusion.4
  8.6 0.6 copy-done.29
  9.3 0.6 add_multiply_fusion.2
  9.9 0.6 copy-done.18
  10.6 1.4 %multiply_add_fusion.2 = f32[27,4,16,128]{3,2,1,0:T(8,128)S(1)} fusion(f32[27,4,16,128]{3,2,1,0:T(8,128)S(1)} %copy-done.3, f32[4,16,128]{2,1,0:T(8,128)S(1)} %get-tuple-element.48, f32[4,16,128]{2,1,0:T(8,128)S(1)} %get-tuple-element.53, f32[27]{0:T(128)S(1)} %copy-done.46, f32[4,16,128]{2,1,0:T(8,128)S(1)} %get-tuple-element.51, f32[27]{0:T(128)S(1)} %copy-done.48, ...), kind=kLoop, calls=%fused_computation.71 | loop fusion | flops 4202496 | bytes 2032048 | tf_op jit(solution)/shard_map/add | solution.py:42
  12.1 1.0 %copy-done.13 = f32[27,4,16,128]{3,2,1,0:T(8,128)S(1)} copy-done((f32[27,4,16,128]{3,2,1,0:T(8,128)S(1)}, f32[27,4,16,128]{3,2,1,0:T(8,128)}, u32[]{:S(2)}) %copy-start.13) | copy-done | bytes 884760
  13.3 1.5 %collective-permute-start = (f32[2,3,3,1,16,128]{5,4,2,1,3,0:T(8,128)S(1)}, f32[2,3,3,1,16,128]{5,4,2,1,3,0:T(8,128)S(1)}, u32[]{:S(2)}, u32[]{:S(2)}) collective-permute-start(f32[2,3,3,1,16,128]{5,4,2,1,3,0:T(8,128)S(1)} %pad_maximum_fusion.11), channel_id=1, source_target_pairs={{0,120},{8,0},{16,8},{24,16},{32,24},{40,32},{48,40},{56,48},{64,5... | collective-permute-start | bytes 442376 | tf_op jit(solution)/shard_map/ppermute | solution.py:63
  14.9 1.7 %collective-permute-start.1 = (f32[2,3,3,1,16,128]{5,4,2,1,3,0:T(8,128)S(1)}, f32[2,3,3,1,16,128]{5,4,2,1,3,0:T(8,128)S(1)}, u32[]{:S(2)}, u32[]{:S(2)}) collective-permute-start(f32[2,3,3,1,16,128]{5,4,2,1,3,0:T(8,128)S(1)} %pad_maximum_fusion.12), channel_id=1, source_target_pairs={{0,8},{8,16},{16,24},{24,32},{32,40},{40,48},{48,56},{56,64},{64,7... | collective-permute-start | bytes 442376 | tf_op jit(solution)/shard_map/ppermute | solution.py:62
  16.7 2.5 %collective-permute-done = f32[2,3,3,1,16,128]{5,4,2,1,3,0:T(8,128)S(1)} collective-permute-done((f32[2,3,3,1,16,128]{5,4,2,1,3,0:T(8,128)S(1)}, f32[2,3,3,1,16,128]{5,4,2,1,3,0:T(8,128)S(1)}, u32[]{:S(2)}, u32[]{:S(2)}) %collective-permute-start) | collective-permute-done | bytes 147488 | tf_op jit(solution)/shard_map/ppermute | solution.py:63
  19.3 1.0 collective-permute-done.1
  20.9 3.4 %collective-permute-start.2 = (f32[2,2,3,3,4,1,128]{6,4,3,2,1,5,0:T(4,128)S(1)}, f32[2,2,3,3,4,1,128]{6,4,3,2,1,5,0:T(4,128)S(1)}, u32[]{:S(2)}, u32[]{:S(2)}) collective-permute-start(f32[2,2,3,3,4,1,128]{6,4,3,2,1,5,0:T(4,128)S(1)} %pad_maximum_fusion.13), channel_id=1, source_target_pairs={{0,4},{4,0},{1,5},{5,1},{2,6},{6,2},{3,7},{7,3},{8,12},{12,8},{9,1... | collective-permute-start | bytes 221192 | tf_op jit(solution)/shard_map/ppermute | solution.py:60
  24.3 1.7 %collective-permute-done.2 = f32[2,2,3,3,4,1,128]{6,4,3,2,1,5,0:T(4,128)S(1)} collective-permute-done((f32[2,2,3,3,4,1,128]{6,4,3,2,1,5,0:T(4,128)S(1)}, f32[2,2,3,3,4,1,128]{6,4,3,2,1,5,0:T(4,128)S(1)}, u32[]{:S(2)}, u32[]{:S(2)}) %collective-permute-start.2) | collective-permute-done | bytes 73760 | tf_op jit(solution)/shard_map/ppermute | solution.py:60
  27.2 2.5 %collective-permute-start.4 = (f32[2,3,3,4,16,1]{4,3,2,1,5,0:T(4,128)S(1)}, f32[2,3,3,4,16,1]{4,3,2,1,5,0:T(4,128)S(1)}, u32[]{:S(2)}, u32[]{:S(2)}) collective-permute-start(f32[2,3,3,4,16,1]{4,3,2,1,5,0:T(4,128)S(1)} %pad_maximum_fusion.15), channel_id=1, source_target_pairs={{0,3},{1,0},{2,1},{3,2},{4,7},{5,4},{6,5},{7,6},{8,11},{9,8},{10,9... | collective-permute-start | bytes 13832 | tf_op jit(solution)/shard_map/ppermute | solution.py:63
  29.9 0.3 copy.582
  30.8 0.9 slice.471
  31.7 0.3 copy.594
  32.0 3.7 %collective-permute-done.3 = f32[2,3,3,4,16,1]{4,3,2,1,5,0:T(4,128)S(1)} collective-permute-done((f32[2,3,3,4,16,1]{4,3,2,1,5,0:T(4,128)S(1)}, f32[2,3,3,4,16,1]{4,3,2,1,5,0:T(4,128)S(1)}, u32[]{:S(2)}, u32[]{:S(2)}) %collective-permute-start.3) | collective-permute-done | bytes 4640 | tf_op jit(solution)/shard_map/ppermute | solution.py:62
  35.7 0.3 copy.595
  36.4 0.7 slice_reduce_fusion.2
  37.1 0.3 copy.592
  37.4 0.3 copy.587
  37.8 0.8 copy-done.12
  38.8 0.6 copy-done.31
  39.5 0.6 copy-done.34
  40.2 0.7 pad_maximum_fusion.4
  41.1 1.1 %multiply_reduce_fusion.5 = (f32[4,16,128]{2,1,0:T(8,128)S(1)}, f32[4,16,128]{2,1,0:T(8,128)S(1)}, f32[4,16,128]{2,1,0:T(8,128)S(1)}, f32[4,16,128]{2,1,0:T(8,128)S(1)}, f32[4,16,128]{2,1,0:T(8,128)S(1)}) fusion(f32[3,3,3,4,16,128]{5,4,1,3,0,2:T(8,128)S(1)} %get-tuple-element.69, f32[3,3,3]{1,0,2:T(4,128)S(1)} %copy-done.33, f32[3,3,3]{1,0,2:T(4,128)S(1)} %copy-done.37, ...), kind=kLoop, calls=%fused_computation.67 | loop fusion | flops 6373376 | bytes 2163120 | tf_op jit(solution)/shard_map/transpose(jvp())/reduce_sum | solution.py:37
  42.6 0.3 bitcast_add_fusion.1
  42.9 5.2 %collective-permute-start.5 = (f32[1,3,3,1,16,128]{5,4,2,1,3,0:T(8,128)S(1)}, f32[1,3,3,1,16,128]{5,4,2,1,3,0:T(8,128)S(1)}, u32[]{:S(2)}, u32[]{:S(2)}) collective-permute-start(f32[1,3,3,1,16,128]{5,4,2,1,3,0:T(8,128)S(1)} %slice_bitcast_fusion.13), channel_id=1, source_target_pairs={{0,8},{8,16},{16,24},{24,32},{32,40},{40,48},{48,56},{56,64},{64,7... | collective-permute-start | bytes 221192 | tf_op jit(solution)/shard_map/ppermute | solution.py:62
  48.1 2.8 %collective-permute-start.6 = (f32[1,3,3,1,16,128]{5,4,2,1,3,0:T(8,128)S(1)}, f32[1,3,3,1,16,128]{5,4,2,1,3,0:T(8,128)S(1)}, u32[]{:S(2)}, u32[]{:S(2)}) collective-permute-start(f32[1,3,3,1,16,128]{5,4,2,1,3,0:T(8,128)S(1)} %slice_bitcast_fusion.12), channel_id=1, source_target_pairs={{0,120},{8,0},{16,8},{24,16},{32,24},{40,32},{48,40},{56,48},{64,5... | collective-permute-start | bytes 221192 | tf_op jit(solution)/shard_map/ppermute | solution.py:63
  51.5 0.4 collective-permute-done.6
  52.7 3.3 %collective-permute-start.7 = (f32[2,1,3,3,4,1,128]{6,4,2,3,5,1,0:T(4,128)S(1)}, f32[2,1,3,3,4,1,128]{6,4,2,3,5,1,0:T(4,128)S(1)}, u32[]{:S(2)}, u32[]{:S(2)}) collective-permute-start(f32[2,1,3,3,4,1,128]{6,4,2,3,5,1,0:T(4,128)S(1)} %pad_maximum_fusion.16), channel_id=1, source_target_pairs={{0,4},{4,0},{1,5},{5,1},{2,6},{6,2},{3,7},{7,3},{8,12},{12,8},{9,1... | collective-permute-start | bytes 110600 | tf_op jit(solution)/shard_map/ppermute | solution.py:60
  56.1 1.3 %collective-permute-done.7 = f32[2,1,3,3,4,1,128]{6,4,2,3,5,1,0:T(4,128)S(1)} collective-permute-done((f32[2,1,3,3,4,1,128]{6,4,2,3,5,1,0:T(4,128)S(1)}, f32[2,1,3,3,4,1,128]{6,4,2,3,5,1,0:T(4,128)S(1)}, u32[]{:S(2)}, u32[]{:S(2)}) %collective-permute-start.7) | collective-permute-done | bytes 36896 | tf_op jit(solution)/shard_map/ppermute | solution.py:60
  57.6 0.8 slice_bitcast_fusion.1
  58.4 1.9 %copy.608 = f32[3,3,4,16,1]{3,2,1,0,4:T(4,128)} copy(f32[3,3,4,16,1]{4,3,1,2,0:T(8,128)} %bitcast.206) | data formatting | bytes 4608 | tf_op jit(solution)/shard_map/slice | solution.py:74
  60.3 0.9 slice.502
  61.2 1.9 %copy.606 = f32[3,3,4,16,1]{3,2,1,0,4:T(4,128)} copy(f32[3,3,4,16,1]{4,3,1,2,0:T(8,128)} %slice.502) | data formatting | bytes 4608 | tf_op jit(solution)/shard_map/slice | solution.py:73
  63.0 1.5 %collective-permute-start.8 = (f32[1,3,3,4,16,1]{4,3,2,1,5,0:T(4,128)}, f32[1,3,3,4,16,1]{4,3,2,1,5,0:T(4,128)S(1)}, u32[]{:S(2)}, u32[]{:S(2)}) collective-permute-start(f32[1,3,3,4,16,1]{4,3,2,1,5,0:T(4,128)} %bitcast.239), channel_id=1, source_target_pairs={{0,1},{1,2},{2,3},{3,0},{4,5},{5,6},{6,7},{7,4},{8,9},{9,10},{10,1... | collective-permute-start | bytes 6920 | tf_op jit(solution)/shard_map/ppermute | solution.py:62
  64.5 1.2 %gather_fusion.5 = s32[12]{0:T(128)} fusion(s32[1024]{0:T(1024)S(1)} %copy-done.2, s32[1024]{0:T(1024)S(1)} %pad_clamp_fusion.1), kind=kCustom, calls=%fused_computation.5 | custom fusion | bytes 144 | tf_op jit(solution)/shard_map/gather | solution.py:116
  65.7 1.0 %copy.611 = f32[3,3,3,4,16,128]{5,4,3,2,1,0:T(8,128)} copy(f32[3,3,3,4,16,128]{5,4,2,1,3,0:T(8,128)S(1)} %pad_maximum_fusion.5) | data formatting | bytes 1769472 | tf_op jit(solution)/shard_map/stack | solution.py:86
  66.9 1.0 %copy.609 = f32[3,3,4,16,1]{4,3,1,2,0:T(8,128)S(1)} copy(f32[3,3,4,16,1]{3,2,1,0,4:T(4,128)} %bitcast.83) | data formatting | bytes 4608 | tf_op jit(solution)/shard_map/squeeze | solution.py:82
  67.9 1.0 copy.607
  68.9 1.1 %maximum_bitcast_fusion.14 = f32[3,3,1,4,16,128]{5,4,1,3,0,2:T(8,128)S(1)} fusion(f32[3,3,4,16,127]{4,3,1,2,0:T(8,128)S(1)} %bitcast.203, f32[3,3,4,16,1]{4,3,1,2,0:T(8,128)} %copy.607), kind=kLoop, calls=%fused_computation.111 | loop fusion | flops 73728 | bytes 589824 | tf_op jit(solution)/shard_map/stack | solution.py:86
  70.3 1.5 %pad_maximum_fusion.8 = (f32[3,3,3,4,16,128]{5,4,1,3,0,2:T(8,128)S(1)}, f32[3,3,3,4,16,128]{5,4,1,3,0,2:T(8,128)}) fusion(f32[3,3,1,4,16,128]{5,4,1,3,0,2:T(8,128)S(1)} %maximum_bitcast_fusion.15, f32[3,3,1,4,16,128]{5,4,1,3,0,2:T(8,128)S(1)} %get-tuple-element.61, f32[3,3,1,4,16,128]{5,4,1,3,0,2:T(8,128)S(1)} %maximum_bitcast_fusion.14, ...), kind=kLoop, calls=%fused_computation.48 | loop fusion | flops 4423680 | bytes 2851248 | tf_op jit(solution)/shard_map/stack | solution.py:86
  72.0 1.0 copy-done.4
  73.0 1.7 %fusion.28 = (f32[4,16,128]{2,1,0:T(8,128)S(1)}, f32[4,16,128]{2,1,0:T(8,128)S(1)}) fusion(f32[3,3,3,4,16,128]{5,4,3,2,1,0:T(8,128)S(1)} %copy.610, f32[27,4,16,128]{3,2,1,0:T(8,128)S(1)} %copy-done.3, f32[4,16,128]{2,1,0:T(8,128)S(1)} %copy-done.19, f32[4,16,128]{2,1,0:T(8,128)S(1)} %get-tuple-element.53, f32[27]{0:T(128)S(1)} %copy-done.47, ...), kind=kLoop, calls=%fused_computation.53 | loop fusion | flops 8388608 | bytes 3965360 | tf_op jit(solution)/shard_map/reduce_sum | solution.py:52
  75.0 0.6 copy-done.22
  75.8 1.0 copy-done.5
  76.9 1.7 %multiply_reduce_fusion.2 = (f32[4,16,128]{2,1,0:T(8,128)S(1)}, f32[4,16,128]{2,1,0:T(8,128)S(1)}, f32[4,16,128]{2,1,0:T(8,128)}, f32[4,16,128]{2,1,0:T(8,128)}, f32[4,16,128]{2,1,0:T(8,128)}) fusion(f32[3,3,3,4,16,128]{5,4,1,3,0,2:T(8,128)S(1)} %copy-done.5, f32[3,3,3]{1,0,2:T(4,128)S(1)} %copy-done.33, f32[3,3,3]{1,0,2:T(4,128)S(1)} %copy-done.39, ...), kind=kLoop, calls=%fused_computation.60 | loop fusion | flops 6373376 | bytes 2163120 | tf_op jit(solution)/shard_map/transpose(jvp())/reduce_sum | solution.py:37
  78.6 0.6 copy-done.43
  79.3 0.7 all_to_all.6
  80.0 12.1 %all-to-all-start = ((f32[128,1,8]{2,1,0:T(1,128)}), f32[128,1,8]{2,1,0:T(1,128)S(1)}, u32[]{:S(2)}, u32[]{:S(2)}) async-start(f32[128,1,8]{2,1,0:T(1,128)} %bitcast.89), calls=%async_computation | async-start | bytes 131072 | tf_op jit(solution)/shard_map/all_to_all | solution.py:119
  92.2 0.8 fusion.42
  93.4 1.2 %bitcast_add_fusion = f32[27,4,16,128]{3,2,1,0:T(8,128)} fusion(f32[3,3,3,4,16,128]{5,4,3,2,1,0:T(8,128)S(1)} %pad_add_fusion, f32[3,3,3,4,16,128]{5,4,3,2,1,0:T(8,128)S(1)} %copy.610, f32[27,4,16,128]{3,2,1,0:T(8,128)S(1)} %bitcast_multiply_fusion.2, f32[4,16,128]{2,1,0:T(8,128)S(1)} %get-tuple-element.103, f32[4,16,128]{2,1,0:T(8,128)S(1)} %copy-done.11, ...), kind=kLoop, calls=%fused_computation.49 | loop fusion | flops 1548288 | bytes 3637248 | tf_op jit(solution)/shard_map/transpose(jvp())/add_any | solution.py:25
  94.5 7.5 %all-to-all-done = f32[128,1,8]{2,1,0:T(1,128)S(1)} async-done(((f32[128,1,8]{2,1,0:T(1,128)}), f32[128,1,8]{2,1,0:T(1,128)S(1)}, u32[]{:S(2)}, u32[]{:S(2)}) %all-to-all-start) | async-done | bytes 4128 | tf_op jit(solution)/shard_map/all_to_all | solution.py:119
  102.0 0.7 reduce_sum.391
  (244 shorter events, 8.1 us)
Async XLA Ops:
  0.6 3.7 %copy-start = (s32[4,16,128]{2,1,0:T(8,128)S(1)}, s32[4,16,128]{2,1,0:T(8,128)}, u32[]{:S(2)}) copy-start(s32[4,16,128]{2,1,0:T(8,128)} %param.31) | copy-start | bytes 98308
  0.6 2.3 %copy-start.3 = (f32[27,4,16,128]{3,2,1,0:T(8,128)S(1)}, f32[27,4,16,128]{3,2,1,0:T(8,128)}, u32[]{:S(2)}) copy-start(f32[27,4,16,128]{3,2,1,0:T(8,128)} %param.27) | copy-start | bytes 2654212
  3.0 0.7 copy-start.52
  3.7 0.7 copy-start.53
  6.4 0.7 copy-start.1
  8.5 0.8 copy-start.29
  9.3 1.3 %copy-start.11 = (f32[4,16,128]{2,1,0:T(8,128)S(1)}, f32[4,16,128]{2,1,0:T(8,128)}, u32[]{:S(2)}) copy-start(f32[4,16,128]{2,1,0:T(8,128)} %param.29) | copy-start | bytes 98308
  9.3 1.3 %copy-start.50 = (f32[27]{0:T(128)S(1)}, f32[27]{0:T(128)}, u32[]{:S(2)}) copy-start(f32[27]{0:T(128)} %constant.53.clone) | copy-start | bytes 328
  9.9 31.0 %copy-start.21 = (f32[4,16,128]{2,1,0:T(8,128)}, f32[4,16,128]{2,1,0:T(8,128)S(1)}, u32[]{:S(2)}) copy-start(f32[4,16,128]{2,1,0:T(8,128)S(1)} %get-tuple-element.122) | copy-start | bytes 98308
  9.9 0.7 copy-start.44
  9.9 0.7 copy-start.46
  9.9 0.7 copy-start.48
  12.0 1.2 %copy-start.13 = (f32[27,4,16,128]{3,2,1,0:T(8,128)S(1)}, f32[27,4,16,128]{3,2,1,0:T(8,128)}, u32[]{:S(2)}) copy-start(f32[27,4,16,128]{3,2,1,0:T(8,128)} %param.28) | copy-start | bytes 2654212
  13.3 5.9 %collective-permute-start = (f32[2,3,3,1,16,128]{5,4,2,1,3,0:T(8,128)S(1)}, f32[2,3,3,1,16,128]{5,4,2,1,3,0:T(8,128)S(1)}, u32[]{:S(2)}, u32[]{:S(2)}) collective-permute-start(f32[2,3,3,1,16,128]{5,4,2,1,3,0:T(8,128)S(1)} %pad_maximum_fusion.11), channel_id=1, source_target_pairs={{0,120},{8,0},{16,8},{24,16},{32,24},{40,32},{48,40},{56,48},{64,5... | collective-permute-start | bytes 442376 | tf_op jit(solution)/shard_map/ppermute | solution.py:63
  14.9 5.4 %collective-permute-start.1 = (f32[2,3,3,1,16,128]{5,4,2,1,3,0:T(8,128)S(1)}, f32[2,3,3,1,16,128]{5,4,2,1,3,0:T(8,128)S(1)}, u32[]{:S(2)}, u32[]{:S(2)}) collective-permute-start(f32[2,3,3,1,16,128]{5,4,2,1,3,0:T(8,128)S(1)} %pad_maximum_fusion.12), channel_id=1, source_target_pairs={{0,8},{8,16},{16,24},{24,32},{32,40},{40,48},{48,56},{56,64},{64,7... | collective-permute-start | bytes 442376 | tf_op jit(solution)/shard_map/ppermute | solution.py:62
  20.9 5.1 %collective-permute-start.2 = (f32[2,2,3,3,4,1,128]{6,4,3,2,1,5,0:T(4,128)S(1)}, f32[2,2,3,3,4,1,128]{6,4,3,2,1,5,0:T(4,128)S(1)}, u32[]{:S(2)}, u32[]{:S(2)}) collective-permute-start(f32[2,2,3,3,4,1,128]{6,4,3,2,1,5,0:T(4,128)S(1)} %pad_maximum_fusion.13), channel_id=1, source_target_pairs={{0,4},{4,0},{1,5},{5,1},{2,6},{6,2},{3,7},{7,3},{8,12},{12,8},{9,1... | collective-permute-start | bytes 221192 | tf_op jit(solution)/shard_map/ppermute | solution.py:60
  27.2 4.4 %collective-permute-start.4 = (f32[2,3,3,4,16,1]{4,3,2,1,5,0:T(4,128)S(1)}, f32[2,3,3,4,16,1]{4,3,2,1,5,0:T(4,128)S(1)}, u32[]{:S(2)}, u32[]{:S(2)}) collective-permute-start(f32[2,3,3,4,16,1]{4,3,2,1,5,0:T(4,128)S(1)} %pad_maximum_fusion.15), channel_id=1, source_target_pairs={{0,3},{1,0},{2,1},{3,2},{4,7},{5,4},{6,5},{7,6},{8,11},{9,8},{10,9... | collective-permute-start | bytes 13832 | tf_op jit(solution)/shard_map/ppermute | solution.py:63
  31.7 4.0 %collective-permute-start.3 = (f32[2,3,3,4,16,1]{4,3,2,1,5,0:T(4,128)S(1)}, f32[2,3,3,4,16,1]{4,3,2,1,5,0:T(4,128)S(1)}, u32[]{:S(2)}, u32[]{:S(2)}) collective-permute-start(f32[2,3,3,4,16,1]{4,3,2,1,5,0:T(4,128)S(1)} %pad_maximum_fusion.14), channel_id=1, source_target_pairs={{0,1},{1,2},{2,3},{3,0},{4,5},{5,6},{6,7},{7,4},{8,9},{9,10},{10,1... | collective-permute-start | bytes 13832 | tf_op jit(solution)/shard_map/ppermute | solution.py:62
  37.6 1.0 copy-start.12
  38.6 0.8 copy-start.31
  38.6 0.8 copy-start.32
  39.4 0.7 copy-start.34
  39.4 0.7 copy-start.37
  39.4 0.7 copy-start.40
  39.4 1.6 %copy-start.23 = (f32[4,16,128]{2,1,0:T(8,128)}, f32[4,16,128]{2,1,0:T(8,128)S(1)}, u32[]{:S(2)}) copy-start(f32[4,16,128]{2,1,0:T(8,128)S(1)} %get-tuple-element.40) | copy-start | bytes 98308
  39.4 2.7 %copy-start.14 = (f32[4,16,128]{2,1,0:T(8,128)}, f32[4,16,128]{2,1,0:T(8,128)S(1)}, u32[]{:S(2)}) copy-start(f32[4,16,128]{2,1,0:T(8,128)S(1)} %get-tuple-element.45) | copy-start | bytes 98308
  39.4 2.7 %copy-start.16 = (f32[4,16,128]{2,1,0:T(8,128)}, f32[4,16,128]{2,1,0:T(8,128)S(1)}, u32[]{:S(2)}) copy-start(f32[4,16,128]{2,1,0:T(8,128)S(1)} %get-tuple-element.47) | copy-start | bytes 98308
  39.4 0.7 copy-start.33
  42.9 8.5 %collective-permute-start.5 = (f32[1,3,3,1,16,128]{5,4,2,1,3,0:T(8,128)S(1)}, f32[1,3,3,1,16,128]{5,4,2,1,3,0:T(8,128)S(1)}, u32[]{:S(2)}, u32[]{:S(2)}) collective-permute-start(f32[1,3,3,1,16,128]{5,4,2,1,3,0:T(8,128)S(1)} %slice_bitcast_fusion.13), channel_id=1, source_target_pairs={{0,8},{8,16},{16,24},{24,32},{32,40},{40,48},{48,56},{56,64},{64,7... | collective-permute-start | bytes 221192 | tf_op jit(solution)/shard_map/ppermute | solution.py:62
  48.1 3.8 %collective-permute-start.6 = (f32[1,3,3,1,16,128]{5,4,2,1,3,0:T(8,128)S(1)}, f32[1,3,3,1,16,128]{5,4,2,1,3,0:T(8,128)S(1)}, u32[]{:S(2)}, u32[]{:S(2)}) collective-permute-start(f32[1,3,3,1,16,128]{5,4,2,1,3,0:T(8,128)S(1)} %slice_bitcast_fusion.12), channel_id=1, source_target_pairs={{0,120},{8,0},{16,8},{24,16},{32,24},{40,32},{48,40},{56,48},{64,5... | collective-permute-start | bytes 221192 | tf_op jit(solution)/shard_map/ppermute | solution.py:63
  52.7 4.6 %collective-permute-start.7 = (f32[2,1,3,3,4,1,128]{6,4,2,3,5,1,0:T(4,128)S(1)}, f32[2,1,3,3,4,1,128]{6,4,2,3,5,1,0:T(4,128)S(1)}, u32[]{:S(2)}, u32[]{:S(2)}) collective-permute-start(f32[2,1,3,3,4,1,128]{6,4,2,3,5,1,0:T(4,128)S(1)} %pad_maximum_fusion.16), channel_id=1, source_target_pairs={{0,4},{4,0},{1,5},{5,1},{2,6},{6,2},{3,7},{7,3},{8,12},{12,8},{9,1... | collective-permute-start | bytes 110600 | tf_op jit(solution)/shard_map/ppermute | solution.py:60
  58.4 2.8 %copy-start.8 = (f32[3,3,4,16,128]{4,3,1,2,0:T(8,128)}, f32[3,3,4,16,128]{4,3,1,2,0:T(8,128)S(1)}, u32[]{:S(2)}) copy-start(f32[3,3,4,16,128]{4,3,1,2,0:T(8,128)S(1)} %get-tuple-element.59) | copy-start | bytes 884740
  60.3 6.5 %collective-permute-start.9 = (f32[1,3,3,4,16,1]{4,3,2,1,5,0:T(4,128)}, f32[1,3,3,4,16,1]{4,3,2,1,5,0:T(4,128)}, u32[]{:S(2)}, u32[]{:S(2)}) collective-permute-start(f32[1,3,3,4,16,1]{4,3,2,1,5,0:T(4,128)} %bitcast.238), channel_id=1, source_target_pairs={{0,3},{1,0},{2,1},{3,2},{4,7},{5,4},{6,5},{7,6},{8,11},{9,8},{10,9... | collective-permute-start | bytes 6920 | tf_op jit(solution)/shard_map/ppermute | solution.py:63
  61.2 3.3 %copy-start.2 = (s32[1024]{0:T(1024)S(1)}, s32[1024]{0:T(1024)}, u32[]{:S(2)}) copy-start(s32[1024]{0:T(1024)} %param.33) | copy-start | bytes 12292
  63.0 4.9 %collective-permute-start.8 = (f32[1,3,3,4,16,1]{4,3,2,1,5,0:T(4,128)}, f32[1,3,3,4,16,1]{4,3,2,1,5,0:T(4,128)S(1)}, u32[]{:S(2)}, u32[]{:S(2)}) collective-permute-start(f32[1,3,3,4,16,1]{4,3,2,1,5,0:T(4,128)} %bitcast.239), channel_id=1, source_target_pairs={{0,1},{1,2},{2,3},{3,0},{4,5},{5,6},{6,7},{7,4},{8,9},{9,10},{10,1... | collective-permute-start | bytes 6920 | tf_op jit(solution)/shard_map/ppermute | solution.py:62
  65.7 1.1 %copy-start.10 = (f32[3,3,4,16,128]{4,3,1,2,0:T(8,128)S(1)}, f32[3,3,4,16,128]{4,3,1,2,0:T(8,128)}, u32[]{:S(2)}) copy-start(f32[3,3,4,16,128]{4,3,1,2,0:T(8,128)} %get-tuple-element.60) | copy-start | bytes 884740
  66.9 2.1 %copy-start.9 = (f32[3,3,4,16,128]{4,3,1,2,0:T(8,128)S(1)}, f32[3,3,4,16,128]{4,3,1,2,0:T(8,128)}, u32[]{:S(2)}) copy-start(f32[3,3,4,16,128]{4,3,1,2,0:T(8,128)} %copy-done.8) | copy-start | bytes 884740
  68.9 1.3 %copy-start.35 = (f32[3,3,3]{1,0,2:T(4,128)S(1)}, f32[3,3,3]{1,0,2:T(4,128)}, u32[]{:S(2)}) copy-start(f32[3,3,3]{1,0,2:T(4,128)} %constant.90) | copy-start | bytes 328
  68.9 1.3 %copy-start.38 = (f32[3,3,3]{1,0,2:T(4,128)S(1)}, f32[3,3,3]{1,0,2:T(4,128)}, u32[]{:S(2)}) copy-start(f32[3,3,3]{1,0,2:T(4,128)} %constant.89) | copy-start | bytes 328
  68.9 1.3 %copy-start.41 = (f32[3,3,3]{1,0,2:T(4,128)S(1)}, f32[3,3,3]{1,0,2:T(4,128)}, u32[]{:S(2)}) copy-start(f32[3,3,3]{1,0,2:T(4,128)} %constant.88) | copy-start | bytes 328
  70.2 1.6 %copy-start.6 = (f32[3,3,1,4,16,128]{5,4,1,3,0,2:T(8,128)}, f32[3,3,1,4,16,128]{5,4,1,3,0,2:T(8,128)S(1)}, u32[]{:S(2)}) copy-start(f32[3,3,1,4,16,128]{5,4,1,3,0,2:T(8,128)S(1)} %maximum_bitcast_fusion.15) | copy-start | bytes 884740
  71.8 1.2 %copy-start.4 = (f32[3,3,3,4,16,128]{5,4,3,2,1,0:T(8,128)S(1)}, f32[3,3,3,4,16,128]{5,4,3,2,1,0:T(8,128)}, u32[]{:S(2)}) copy-start(f32[3,3,3,4,16,128]{5,4,3,2,1,0:T(8,128)} %copy.611) | copy-start | bytes 2654212
  71.8 1.2 %copy-start.15 = (f32[4,16,128]{2,1,0:T(8,128)S(1)}, f32[4,16,128]{2,1,0:T(8,128)}, u32[]{:S(2)}) copy-start(f32[4,16,128]{2,1,0:T(8,128)} %copy-done.14) | copy-start | bytes 98308
  71.8 1.2 %copy-start.17 = (f32[4,16,128]{2,1,0:T(8,128)S(1)}, f32[4,16,128]{2,1,0:T(8,128)}, u32[]{:S(2)}) copy-start(f32[4,16,128]{2,1,0:T(8,128)} %copy-done.16) | copy-start | bytes 98308
  71.8 1.2 %copy-start.19 = (f32[4,16,128]{2,1,0:T(8,128)S(1)}, f32[4,16,128]{2,1,0:T(8,128)}, u32[]{:S(2)}) copy-start(f32[4,16,128]{2,1,0:T(8,128)} %copy-done.18) | copy-start | bytes 98308
  71.8 1.2 %copy-start.24 = (f32[4,16,128]{2,1,0:T(8,128)S(1)}, f32[4,16,128]{2,1,0:T(8,128)}, u32[]{:S(2)}) copy-start(f32[4,16,128]{2,1,0:T(8,128)} %copy-done.23) | copy-start | bytes 98308
  71.8 1.2 %copy-start.51 = (f32[27]{0:T(128)S(1)}, f32[27]{0:T(128)}, u32[]{:S(2)}) copy-start(f32[27]{0:T(128)} %constant.53.clone) | copy-start | bytes 328
  71.9 1.1 %copy-start.45 = (f32[27]{0:T(128)S(1)}, f32[27]{0:T(128)}, u32[]{:S(2)}) copy-start(f32[27]{0:T(128)} %constant.56.clone) | copy-start | bytes 328
  71.9 1.1 %copy-start.47 = (f32[27]{0:T(128)S(1)}, f32[27]{0:T(128)}, u32[]{:S(2)}) copy-start(f32[27]{0:T(128)} %constant.55.clone) | copy-start | bytes 328
  72.0 1.1 %copy-start.49 = (f32[27]{0:T(128)S(1)}, f32[27]{0:T(128)}, u32[]{:S(2)}) copy-start(f32[27]{0:T(128)} %constant.54.clone) | copy-start | bytes 328
  73.0 1.7 %copy-start.30 = (s32[4,16,128]{2,1,0:T(8,128)S(1)}, s32[4,16,128]{2,1,0:T(8,128)}, u32[]{:S(2)}) copy-start(s32[4,16,128]{2,1,0:T(8,128)} %param.30) | copy-start | bytes 98308
  74.9 0.8 copy-start.22
  75.7 1.2 %copy-start.5 = (f32[3,3,3,4,16,128]{5,4,1,3,0,2:T(8,128)S(1)}, f32[3,3,3,4,16,128]{5,4,1,3,0,2:T(8,128)}, u32[]{:S(2)}) copy-start(f32[3,3,3,4,16,128]{5,4,1,3,0,2:T(8,128)} %get-tuple-element.58) | copy-start | bytes 2654212
  75.7 1.2 %copy-start.7 = (f32[3,3,1,4,16,128]{5,4,1,3,0,2:T(8,128)S(1)}, f32[3,3,1,4,16,128]{5,4,1,3,0,2:T(8,128)}, u32[]{:S(2)}) copy-start(f32[3,3,1,4,16,128]{5,4,1,3,0,2:T(8,128)} %copy-done.6) | copy-start | bytes 884740
  75.7 1.2 %copy-start.20 = (f32[4,16,128]{2,1,0:T(8,128)S(1)}, f32[4,16,128]{2,1,0:T(8,128)}, u32[]{:S(2)}) copy-start(f32[4,16,128]{2,1,0:T(8,128)} %copy-done.18) | copy-start | bytes 98308
  75.7 1.2 %copy-start.36 = (f32[3,3,3]{1,0,2:T(4,128)S(1)}, f32[3,3,3]{1,0,2:T(4,128)}, u32[]{:S(2)}) copy-start(f32[3,3,3]{1,0,2:T(4,128)} %constant.90) | copy-start | bytes 328
  75.7 1.2 %copy-start.39 = (f32[3,3,3]{1,0,2:T(4,128)S(1)}, f32[3,3,3]{1,0,2:T(4,128)}, u32[]{:S(2)}) copy-start(f32[3,3,3]{1,0,2:T(4,128)} %constant.89) | copy-start | bytes 328
  75.7 1.2 %copy-start.42 = (f32[3,3,3]{1,0,2:T(4,128)S(1)}, f32[3,3,3]{1,0,2:T(4,128)}, u32[]{:S(2)}) copy-start(f32[3,3,3]{1,0,2:T(4,128)} %constant.88) | copy-start | bytes 328
  78.6 0.7 copy-start.43
  80.0 12.2 %copy-start.25 = (f32[4,16,128]{2,1,0:T(8,128)S(1)}, f32[4,16,128]{2,1,0:T(8,128)}, u32[]{:S(2)}) copy-start(f32[4,16,128]{2,1,0:T(8,128)} %get-tuple-element.8) | copy-start | bytes 98308
  80.0 12.2 %copy-start.26 = (f32[4,16,128]{2,1,0:T(8,128)S(1)}, f32[4,16,128]{2,1,0:T(8,128)}, u32[]{:S(2)}) copy-start(f32[4,16,128]{2,1,0:T(8,128)} %get-tuple-element.26) | copy-start | bytes 98308
  80.0 12.2 %copy-start.27 = (f32[4,16,128]{2,1,0:T(8,128)S(1)}, f32[4,16,128]{2,1,0:T(8,128)}, u32[]{:S(2)}) copy-start(f32[4,16,128]{2,1,0:T(8,128)} %get-tuple-element.27) | copy-start | bytes 98308
  80.0 12.2 %copy-start.28 = (f32[4,16,128]{2,1,0:T(8,128)S(1)}, f32[4,16,128]{2,1,0:T(8,128)}, u32[]{:S(2)}) copy-start(f32[4,16,128]{2,1,0:T(8,128)} %get-tuple-element.50) | copy-start | bytes 98308
  80.0 22.0 %all-to-all-start = ((f32[128,1,8]{2,1,0:T(1,128)}), f32[128,1,8]{2,1,0:T(1,128)S(1)}, u32[]{:S(2)}, u32[]{:S(2)}) async-start(f32[128,1,8]{2,1,0:T(1,128)} %bitcast.89), calls=%async_computation | async-start | bytes 131072 | tf_op jit(solution)/shard_map/all_to_all | solution.py:119
  (1 other events, 0.6 us)

commit v2 on v1

--- a/solution.py
+++ b/solution.py
@@ -96,11 +96,10 @@
 
 def shards(check_pops, adjoint_end, relax_rate, wall_flag, patch_of_cell, porosity, patch_slot):
     sx, sy, sz = relax_rate.shape
-    rows = np.array([0, 1, sx - 1])
-    row_of = np.array([0] + [1] * (sx - 2) + [2])
-    ids = patch_of_cell[rows][:, np.array([0, sy // 2])][:, :, np.array([0, sz // 2])]
-    solid = porosity[ids][row_of]
-    solid = jnp.broadcast_to(solid[:, :, None, :, None], (sx, 2, sy // 2, 2, sz // 2)).reshape(sx, sy, sz)
+    ids = patch_of_cell[:, :: sy // 2, :: sz // 2]
+    table = jnp.stack([porosity, patch_slot.astype(jnp.float32)], axis=1)
+    looked = table[ids]
+    solid = jnp.broadcast_to(looked[:, :, None, :, None, 0], (sx, 2, sy // 2, 2, sz // 2)).reshape(sx, sy, sz)
     walls = wall_flag.astype(jnp.float32)
     gamma = walls * solid
     post_now, _ = collide(check_pops, relax_rate, gamma)
@@ -113,8 +112,8 @@
     parts = jnp.stack([boxes[0], boxes[1 : sx - 1].sum(axis=0), boxes[sx - 1]])
     count = porosity.shape[0]
     devices = lax.axis_size(("gx", "gy", "gz"))
-    slots = patch_slot[ids].reshape(-1)
-    hits = (slots[:, None] == jnp.arange(count, dtype=slots.dtype)[None, :]).astype(jnp.float32)
+    slots = jnp.stack([looked[0, :, :, 1], looked[1, :, :, 1], looked[sx - 1, :, :, 1]]).reshape(-1)
+    hits = (slots[:, None] == jnp.arange(count, dtype=jnp.float32)[None, :]).astype(jnp.float32)
     placed = jnp.sum(parts.reshape(-1)[:, None] * hits, axis=0)
     got = lax.all_to_all(placed.reshape(devices, count // devices), ("gx", "gy", "gz"), 0, 0, tiled=True)
     patch_sens = jnp.sum(got, axis=0)

time: 104 us -> 106 us (1.019)
  local copies, waits for them, and re-layouts: 29.8 us -> 36 us
  starting transfers between devices: 34 us -> 31.6 us
  waiting for transfers between devices: 18.1 us -> 16.3 us
    unnamed x111 -> x165, local copies, waits for them, and re-layouts: 10.2 us -> 18.3 us
    gather x9 -> x1, local copies, waits for them, and re-layouts: 4.32 us -> 0.57 us  [shards(): looked = table[ids]]
    all_to_all x1, starting transfers between devices: 12.1 us -> 9.75 us  [shards(): lax.all_to_all(placed.reshape(devices, count // devices), ('gx', 'gy', 'g...]
    slice x10, local copies, waits for them, and re-layouts: 3.59 us -> 1.88 us  [move_axis(): ups.append(lax.slice_in_dim(plus, n - 1, n, axis=2 + d))]
    slice x0 -> x2, local copies, waits for them, and re-layouts: none -> 1.51 us  [the longest x1 0.85 us: shards(): ids = patch_of_cell[:, ::sy // 2, ::sz // 2]]
    squeeze x8, local copies, waits for them, and re-layouts: 1.75 us -> 3.06 us  [move_axis(): hi[k]]
    ppermute x2, waiting for transfers between devices: 2.94 us -> 1.68 us  [halo_exchange(): both = lax.ppermute(jnp.stack([up, down]), axis, [(0, 1), (1, 0)])]
  transfers between devices with their start and end apart: 11 -> 11, of which waited for: 8 -> 7; matrix products, arithmetic and copies ran while one was open for 11% -> 14% of each run, Pallas kernels for 0% -> 0%
where the time goes in v2:
time: 106 us; the launch traced here: 105 us
  local copies, waits for them, and re-layouts  36 us (34%)
  starting transfers between devices  31.6 us (30%)
  other arithmetic  18.6 us (18%)
  waiting for transfers between devices  16.3 us (15%)
  between operations  2.15 us (2%)
    unnamed x165, local copies, waits for them, and re-layouts  18.3 us
    all_to_all x1, starting transfers between devices, shards(): lax.all_to_all(placed.reshape(devices, count // devices), ('gx', 'gy', 'g...  9.75 us
    ppermute x4, starting transfers between devices, halo_exchange(): lo = lax.ppermute(up, axis, [(i, (i + 1) % size) for i in range(size)])  8.34 us
    all_to_all x1, waiting for transfers between devices, shards(): lax.all_to_all(placed.reshape(devices, count // devices), ('gx', 'gy', 'g...  7.59 us
    ppermute x4, starting transfers between devices, halo_exchange(): hi = lax.ppermute(down, axis, [(i, (i - 1) % size) for i in range(size)])  6.86 us
    ppermute x2, starting transfers between devices, halo_exchange(): both = lax.ppermute(jnp.stack([up, down]), axis, [(0, 1), (1, 0)])  6.62 us
    ppermute x4, waiting for transfers between devices, halo_exchange(): lo = lax.ppermute(up, axis, [(i, (i + 1) % size) for i in range(size)])  4.18 us
    another operation x25, other arithmetic, move_axis(): out.append(jnp.stack(groups, axis=d))  4.04 us
  transfers between devices with their start and end apart: 11, of which 7 were waited for; matrix products, arithmetic and copies ran while one was open for 14% of the time, Pallas kernels for 0%

profile of v2, /device:TPU:1, one launch (start us, length us, event | category | flops | bytes accessed | tf_op | source)
XLA Modules:
  0.0 104.7 jit_solution(5896556042180636587)
XLA Ops:
  0.6 1.2 %slice_reduce_fusion.6 = (f32[4,16,128]{2,1,0:T(8,128)S(1)}, f32[4,16,128]{2,1,0:T(8,128)S(1)}) fusion(f32[3,3,3,4,16,128]{5,4,3,2,1,0:T(8,128)} %bitcast.200), kind=kLoop, calls=%fused_computation.88 | loop fusion | flops 131072 | bytes 655360 | tf_op jit(solution)/shard_map/reduce_sum | solution.py:28
  1.8 1.1 %slice_reduce_fusion.4 = (f32[4,16,128]{2,1,0:T(8,128)S(1)}, f32[4,16,128]{2,1,0:T(8,128)S(1)}) fusion(f32[3,3,3,4,16,128]{5,4,3,2,1,0:T(8,128)} %bitcast.201), kind=kLoop, calls=%fused_computation.86 | loop fusion | flops 131072 | bytes 655360 | tf_op jit(solution)/shard_map/reduce_sum | solution.py:29
  3.0 0.8 slice.336
  3.9 0.6 copy-done.67
  4.6 0.6 copy-done.69
  5.4 0.6 gather_fusion
  6.2 0.4 copy-done.65
  6.8 0.6 copy-done.52
  7.5 0.6 add_multiply_fusion.2
  8.2 0.6 copy-done.70
  8.9 1.4 %multiply_add_fusion.2 = f32[27,4,16,128]{3,2,1,0:T(8,128)S(1)} fusion(f32[27,4,16,128]{3,2,1,0:T(8,128)S(1)} %copy-done, f32[4,16,128]{2,1,0:T(8,128)S(1)} %get-tuple-element.48, f32[4,16,128]{2,1,0:T(8,128)S(1)} %get-tuple-element.53, f32[27]{0:T(128)S(1)} %copy-done.72, f32[4,16,128]{2,1,0:T(8,128)S(1)} %get-tuple-element.51, f32[27]{0:T(128)S(1)} %copy-done.74, ...), kind=kLoop, calls=%fused_computation.66 | loop fusion | flops 4202496 | bytes 2032048 | tf_op jit(solution)/shard_map/add | solution.py:42
  10.5 1.0 copy-done.33
  11.6 1.5 %collective-permute-start = (f32[2,3,3,1,16,128]{5,4,2,1,3,0:T(8,128)S(1)}, f32[2,3,3,1,16,128]{5,4,2,1,3,0:T(8,128)S(1)}, u32[]{:S(2)}, u32[]{:S(2)}) collective-permute-start(f32[2,3,3,1,16,128]{5,4,2,1,3,0:T(8,128)S(1)} %pad_maximum_fusion.11), channel_id=1, source_target_pairs={{0,120},{8,0},{16,8},{24,16},{32,24},{40,32},{48,40},{56,48},{64,5... | collective-permute-start | bytes 442376 | tf_op jit(solution)/shard_map/ppermute | solution.py:63
  13.2 1.7 %collective-permute-start.1 = (f32[2,3,3,1,16,128]{5,4,2,1,3,0:T(8,128)S(1)}, f32[2,3,3,1,16,128]{5,4,2,1,3,0:T(8,128)S(1)}, u32[]{:S(2)}, u32[]{:S(2)}) collective-permute-start(f32[2,3,3,1,16,128]{5,4,2,1,3,0:T(8,128)S(1)} %pad_maximum_fusion.12), channel_id=1, source_target_pairs={{0,8},{8,16},{16,24},{24,32},{32,40},{40,48},{48,56},{56,64},{64,7... | collective-permute-start | bytes 442376 | tf_op jit(solution)/shard_map/ppermute | solution.py:62
  15.0 2.5 %collective-permute-done = f32[2,3,3,1,16,128]{5,4,2,1,3,0:T(8,128)S(1)} collective-permute-done((f32[2,3,3,1,16,128]{5,4,2,1,3,0:T(8,128)S(1)}, f32[2,3,3,1,16,128]{5,4,2,1,3,0:T(8,128)S(1)}, u32[]{:S(2)}, u32[]{:S(2)}) %collective-permute-start) | collective-permute-done | bytes 147488 | tf_op jit(solution)/shard_map/ppermute | solution.py:63
  17.6 1.0 collective-permute-done.1
  19.2 3.4 %collective-permute-start.2 = (f32[2,2,3,3,4,1,128]{6,4,3,2,1,5,0:T(4,128)S(1)}, f32[2,2,3,3,4,1,128]{6,4,3,2,1,5,0:T(4,128)S(1)}, u32[]{:S(2)}, u32[]{:S(2)}) collective-permute-start(f32[2,2,3,3,4,1,128]{6,4,3,2,1,5,0:T(4,128)S(1)} %pad_maximum_fusion.13), channel_id=1, source_target_pairs={{0,4},{4,0},{1,5},{5,1},{2,6},{6,2},{3,7},{7,3},{8,12},{12,8},{9,1... | collective-permute-start | bytes 221192 | tf_op jit(solution)/shard_map/ppermute | solution.py:60
  22.6 1.7 %collective-permute-done.2 = f32[2,2,3,3,4,1,128]{6,4,3,2,1,5,0:T(4,128)S(1)} collective-permute-done((f32[2,2,3,3,4,1,128]{6,4,3,2,1,5,0:T(4,128)S(1)}, f32[2,2,3,3,4,1,128]{6,4,3,2,1,5,0:T(4,128)S(1)}, u32[]{:S(2)}, u32[]{:S(2)}) %collective-permute-start.2) | collective-permute-done | bytes 73760 | tf_op jit(solution)/shard_map/ppermute | solution.py:60
  25.6 2.5 %collective-permute-start.4 = (f32[2,3,3,4,16,1]{4,3,2,1,5,0:T(4,128)S(1)}, f32[2,3,3,4,16,1]{4,3,2,1,5,0:T(4,128)S(1)}, u32[]{:S(2)}, u32[]{:S(2)}) collective-permute-start(f32[2,3,3,4,16,1]{4,3,2,1,5,0:T(4,128)S(1)} %pad_maximum_fusion.15), channel_id=1, source_target_pairs={{0,3},{1,0},{2,1},{3,2},{4,7},{5,4},{6,5},{7,6},{8,11},{9,8},{10,9... | collective-permute-start | bytes 13832 | tf_op jit(solution)/shard_map/ppermute | solution.py:63
  29.2 0.9 slice.482
  30.0 0.6 slice_bitcast_fusion.26
  30.9 3.1 %collective-permute-done.3 = f32[2,3,3,4,16,1]{4,3,2,1,5,0:T(4,128)S(1)} collective-permute-done((f32[2,3,3,4,16,1]{4,3,2,1,5,0:T(4,128)S(1)}, f32[2,3,3,4,16,1]{4,3,2,1,5,0:T(4,128)S(1)}, u32[]{:S(2)}, u32[]{:S(2)}) %collective-permute-start.3) | collective-permute-done | bytes 4640 | tf_op jit(solution)/shard_map/ppermute | solution.py:62
  34.0 0.6 slice_bitcast_fusion.27
  35.4 0.7 slice_reduce_fusion.2
  37.2 0.8 copy-done.30
  38.2 0.6 copy-done.54
  38.9 0.6 copy-done.56
  39.6 0.7 pad_maximum_fusion.4
  40.5 1.1 %multiply_reduce_fusion.5 = (f32[4,16,128]{2,1,0:T(8,128)S(1)}, f32[4,16,128]{2,1,0:T(8,128)S(1)}, f32[4,16,128]{2,1,0:T(8,128)S(1)}, f32[4,16,128]{2,1,0:T(8,128)S(1)}, f32[4,16,128]{2,1,0:T(8,128)S(1)}) fusion(f32[3,3,3,4,16,128]{5,4,1,3,0,2:T(8,128)S(1)} %get-tuple-element.69, f32[3,3,3]{1,0,2:T(4,128)S(1)} %copy-done.55, f32[3,3,3]{1,0,2:T(4,128)S(1)} %copy-done.57, ...), kind=kLoop, calls=%fused_computation.62 | loop fusion | flops 6373376 | bytes 2163120 | tf_op jit(solution)/shard_map/transpose(jvp())/reduce_sum | solution.py:37
  42.4 5.2 %collective-permute-start.5 = (f32[1,3,3,1,16,128]{5,4,2,1,3,0:T(8,128)S(1)}, f32[1,3,3,1,16,128]{5,4,2,1,3,0:T(8,128)S(1)}, u32[]{:S(2)}, u32[]{:S(2)}) collective-permute-start(f32[1,3,3,1,16,128]{5,4,2,1,3,0:T(8,128)S(1)} %slice_bitcast_fusion.13), channel_id=1, source_target_pairs={{0,8},{8,16},{16,24},{24,32},{32,40},{40,48},{48,56},{56,64},{64,7... | collective-permute-start | bytes 221192 | tf_op jit(solution)/shard_map/ppermute | solution.py:62
  47.6 2.9 %collective-permute-start.6 = (f32[1,3,3,1,16,128]{5,4,2,1,3,0:T(8,128)S(1)}, f32[1,3,3,1,16,128]{5,4,2,1,3,0:T(8,128)S(1)}, u32[]{:S(2)}, u32[]{:S(2)}) collective-permute-start(f32[1,3,3,1,16,128]{5,4,2,1,3,0:T(8,128)S(1)} %slice_bitcast_fusion.12), channel_id=1, source_target_pairs={{0,120},{8,0},{16,8},{24,16},{32,24},{40,32},{48,40},{56,48},{64,5... | collective-permute-start | bytes 221192 | tf_op jit(solution)/shard_map/ppermute | solution.py:63
  52.1 0.6 pad_maximum_fusion.16
  52.8 3.2 %collective-permute-start.7 = (f32[2,1,3,3,4,1,128]{6,4,2,3,5,1,0:T(4,128)}, f32[2,1,3,3,4,1,128]{6,4,2,3,5,1,0:T(4,128)}, u32[]{:S(2)}, u32[]{:S(2)}) collective-permute-start(f32[2,1,3,3,4,1,128]{6,4,2,3,5,1,0:T(4,128)} %pad_maximum_fusion.16), channel_id=1, source_target_pairs={{0,4},{4,0},{1,5},{5,1},{2,6},{6,2},{3,7},{7,3},{8,12},{12,8},{9,1... | collective-permute-start | bytes 110600 | tf_op jit(solution)/shard_map/ppermute | solution.py:60
  56.0 0.7 fusion.60
  56.7 1.3 %copy.630 = f32[1,2,2,1]{2,1,0,3:T(2,128)} copy(f32[1,2,2,1]{3,2,1,0:T(2,128)} %get-tuple-element.119) | data formatting | bytes 32
  58.0 1.3 %copy.631 = f32[1,2,2,1]{2,1,0,3:T(2,128)} copy(f32[1,2,2,1]{3,2,1,0:T(2,128)} %get-tuple-element.120) | data formatting | bytes 32
  59.3 1.3 %copy.632 = f32[1,2,2,1]{2,1,0,3:T(2,128)} copy(f32[1,2,2,1]{3,2,1,0:T(2,128)} %get-tuple-element.121) | data formatting | bytes 32
  60.7 0.7 slice_bitcast_fusion.22
  61.7 0.8 slice_bitcast_fusion.1
  62.5 0.9 copy.610
  63.5 0.9 copy.608
  64.4 1.5 %collective-permute-start.8 = (f32[1,3,3,4,16,1]{4,3,2,1,5,0:T(4,128)}, f32[1,3,3,4,16,1]{4,3,2,1,5,0:T(4,128)}, u32[]{:S(2)}, u32[]{:S(2)}) collective-permute-start(f32[1,3,3,4,16,1]{4,3,2,1,5,0:T(4,128)} %bitcast.242), channel_id=1, source_target_pairs={{0,1},{1,2},{2,3},{3,0},{4,5},{5,6},{6,7},{7,4},{8,9},{9,10},{10,1... | collective-permute-start | bytes 6920 | tf_op jit(solution)/shard_map/ppermute | solution.py:62
  65.9 0.7 copy-done.68
  66.5 0.7 pad_maximum_fusion.18
  67.2 0.6 eq.15
  67.9 0.8 copy-done.11
  68.8 0.9 slice.517
  69.6 1.8 %copy.611 = f32[3,3,4,16,1]{4,3,1,2,0:T(8,128)} copy(f32[3,3,4,16,1]{3,2,1,0,4:T(4,128)} %bitcast.84) | data formatting | bytes 4608 | tf_op jit(solution)/shard_map/squeeze | solution.py:82
  71.4 1.0 copy.609
  72.6 0.8 copy-done.31
  73.7 0.5 copy-done.4
  74.6 1.5 %pad_maximum_fusion.8 = (f32[3,3,3,4,16,128]{5,4,1,3,0,2:T(8,128)S(1)}, f32[3,3,3,4,16,128]{5,4,1,3,0,2:T(8,128)}) fusion(f32[3,3,1,4,16,128]{5,4,1,3,0,2:T(8,128)S(1)} %maximum_bitcast_fusion.15, f32[3,3,1,4,16,128]{5,4,1,3,0,2:T(8,128)S(1)} %copy-done.2, f32[3,3,1,4,16,128]{5,4,1,3,0,2:T(8,128)S(1)} %maximum_bitcast_fusion.14, ...), kind=kLoop, calls=%fused_computation.43 | loop fusion | flops 4423680 | bytes 2851248 | tf_op jit(solution)/shard_map/stack | solution.py:86
  76.3 0.6 copy-done.35
  77.0 1.7 %fusion.28 = (f32[4,16,128]{2,1,0:T(8,128)S(1)}, f32[4,16,128]{2,1,0:T(8,128)S(1)}) fusion(f32[3,3,3,4,16,128]{5,4,3,2,1,0:T(8,128)S(1)} %copy.612, f32[27,4,16,128]{3,2,1,0:T(8,128)S(1)} %copy-done, f32[4,16,128]{2,1,0:T(8,128)S(1)} %copy-done.43, f32[4,16,128]{2,1,0:T(8,128)S(1)} %copy-done.28, f32[27]{0:T(128)S(1)} %copy-done.73, ...), kind=kLoop, calls=%fused_computation.48 | loop fusion | flops 8388608 | bytes 3965360 | tf_op jit(solution)/shard_map/reduce_sum | solution.py:52
  79.0 0.6 copy-done.46
  79.8 1.0 copy-done.1
  81.0 1.9 %multiply_reduce_fusion.2 = (f32[4,16,128]{2,1,0:T(8,128)S(1)}, f32[4,16,128]{2,1,0:T(8,128)S(1)}, f32[4,16,128]{2,1,0:T(8,128)S(1)}, f32[4,16,128]{2,1,0:T(8,128)S(1)}, f32[4,16,128]{2,1,0:T(8,128)S(1)}) fusion(f32[3,3,3,4,16,128]{5,4,1,3,0,2:T(8,128)S(1)} %copy-done.1, f32[3,3,3]{1,0,2:T(4,128)S(1)} %copy-done.55, f32[3,3,3]{1,0,2:T(4,128)S(1)} %copy-done.59, ...), kind=kLoop, calls=%fused_computation.55 | loop fusion | flops 6373376 | bytes 2163120 | tf_op jit(solution)/shard_map/transpose(jvp())/reduce_sum | solution.py:37
  83.1 0.6 copy-done.78
  83.7 0.7 all_to_all.6
  84.4 9.8 %all-to-all-start = ((f32[128,1,8]{2,1,0:T(1,128)}), f32[128,1,8]{2,1,0:T(1,128)S(1)}, u32[]{:S(2)}, u32[]{:S(2)}) async-start(f32[128,1,8]{2,1,0:T(1,128)} %bitcast.93), calls=%async_computation | async-start | bytes 131072 | tf_op jit(solution)/shard_map/all_to_all | solution.py:118
  94.6 0.6 copy-done.17
  95.2 1.2 %bitcast_add_fusion = f32[27,4,16,128]{3,2,1,0:T(8,128)} fusion(f32[3,3,3,4,16,128]{5,4,3,2,1,0:T(8,128)S(1)} %pad_add_fusion, f32[3,3,3,4,16,128]{5,4,3,2,1,0:T(8,128)S(1)} %copy.612, f32[27,4,16,128]{3,2,1,0:T(8,128)S(1)} %bitcast_multiply_fusion.2, f32[4,16,128]{2,1,0:T(8,128)S(1)} %get-tuple-element.103, f32[4,16,128]{2,1,0:T(8,128)S(1)} %copy-done.14, ...), kind=kLoop, calls=%fused_computation.44 | loop fusion | flops 1548288 | bytes 3637248 | tf_op jit(solution)/shard_map/transpose(jvp())/add_any | solution.py:25
  96.4 7.6 %all-to-all-done = f32[128,1,8]{2,1,0:T(1,128)S(1)} async-done(((f32[128,1,8]{2,1,0:T(1,128)}), f32[128,1,8]{2,1,0:T(1,128)S(1)}, u32[]{:S(2)}, u32[]{:S(2)}) %all-to-all-start) | async-done | bytes 4128 | tf_op jit(solution)/shard_map/all_to_all | solution.py:118
  104.0 0.7 reduce_sum.391
  (290 shorter events, 11.7 us)
Async XLA Ops:
  0.6 2.3 %copy-start = (f32[27,4,16,128]{3,2,1,0:T(8,128)S(1)}, f32[27,4,16,128]{3,2,1,0:T(8,128)}, u32[]{:S(2)}) copy-start(f32[27,4,16,128]{3,2,1,0:T(8,128)} %param.19) | copy-start | bytes 2654212
  4.6 3.6 %copy-start.18 = (f32[4,16,128]{2,1,0:T(8,128)}, f32[4,16,128]{2,1,0:T(8,128)S(1)}, u32[]{:S(2)}) copy-start(f32[4,16,128]{2,1,0:T(8,128)S(1)} %reduce_sum.301) | copy-start | bytes 98308
  8.1 2.2 %copy-start.21 = (f32[4,16,128]{2,1,0:T(8,128)}, f32[4,16,128]{2,1,0:T(8,128)S(1)}, u32[]{:S(2)}) copy-start(f32[4,16,128]{2,1,0:T(8,128)S(1)} %get-tuple-element.49) | copy-start | bytes 98308
  8.1 2.2 %copy-start.24 = (f32[4,16,128]{2,1,0:T(8,128)}, f32[4,16,128]{2,1,0:T(8,128)S(1)}, u32[]{:S(2)}) copy-start(f32[4,16,128]{2,1,0:T(8,128)S(1)} %get-tuple-element.51) | copy-start | bytes 98308
  8.1 2.2 %copy-start.27 = (f32[4,16,128]{2,1,0:T(8,128)}, f32[4,16,128]{2,1,0:T(8,128)S(1)}, u32[]{:S(2)}) copy-start(f32[4,16,128]{2,1,0:T(8,128)S(1)} %get-tuple-element.53) | copy-start | bytes 98308
  8.1 2.2 %copy-start.42 = (f32[4,16,128]{2,1,0:T(8,128)}, f32[4,16,128]{2,1,0:T(8,128)S(1)}, u32[]{:S(2)}) copy-start(f32[4,16,128]{2,1,0:T(8,128)S(1)} %get-tuple-element.48) | copy-start | bytes 98308
  8.1 32.2 %copy-start.45 = (f32[4,16,128]{2,1,0:T(8,128)}, f32[4,16,128]{2,1,0:T(8,128)S(1)}, u32[]{:S(2)}) copy-start(f32[4,16,128]{2,1,0:T(8,128)S(1)} %get-tuple-element.125) | copy-start | bytes 98308
  8.1 33.9 %copy-start.15 = (f32[4,16,128]{2,1,0:T(8,128)}, f32[4,16,128]{2,1,0:T(8,128)S(1)}, u32[]{:S(2)}) copy-start(f32[4,16,128]{2,1,0:T(8,128)S(1)} %get-tuple-element.124) | copy-start | bytes 98308
  10.3 1.2 %copy-start.33 = (f32[27,4,16,128]{3,2,1,0:T(8,128)S(1)}, f32[27,4,16,128]{3,2,1,0:T(8,128)}, u32[]{:S(2)}) copy-start(f32[27,4,16,128]{3,2,1,0:T(8,128)} %param.20) | copy-start | bytes 2654212
  11.6 5.9 %collective-permute-start = (f32[2,3,3,1,16,128]{5,4,2,1,3,0:T(8,128)S(1)}, f32[2,3,3,1,16,128]{5,4,2,1,3,0:T(8,128)S(1)}, u32[]{:S(2)}, u32[]{:S(2)}) collective-permute-start(f32[2,3,3,1,16,128]{5,4,2,1,3,0:T(8,128)S(1)} %pad_maximum_fusion.11), channel_id=1, source_target_pairs={{0,120},{8,0},{16,8},{24,16},{32,24},{40,32},{48,40},{56,48},{64,5... | collective-permute-start | bytes 442376 | tf_op jit(solution)/shard_map/ppermute | solution.py:63
  13.2 5.4 %collective-permute-start.1 = (f32[2,3,3,1,16,128]{5,4,2,1,3,0:T(8,128)S(1)}, f32[2,3,3,1,16,128]{5,4,2,1,3,0:T(8,128)S(1)}, u32[]{:S(2)}, u32[]{:S(2)}) collective-permute-start(f32[2,3,3,1,16,128]{5,4,2,1,3,0:T(8,128)S(1)} %pad_maximum_fusion.12), channel_id=1, source_target_pairs={{0,8},{8,16},{16,24},{24,32},{32,40},{40,48},{48,56},{56,64},{64,7... | collective-permute-start | bytes 442376 | tf_op jit(solution)/shard_map/ppermute | solution.py:62
  19.2 5.1 %collective-permute-start.2 = (f32[2,2,3,3,4,1,128]{6,4,3,2,1,5,0:T(4,128)S(1)}, f32[2,2,3,3,4,1,128]{6,4,3,2,1,5,0:T(4,128)S(1)}, u32[]{:S(2)}, u32[]{:S(2)}) collective-permute-start(f32[2,2,3,3,4,1,128]{6,4,3,2,1,5,0:T(4,128)S(1)} %pad_maximum_fusion.13), channel_id=1, source_target_pairs={{0,4},{4,0},{1,5},{5,1},{2,6},{6,2},{3,7},{7,3},{8,12},{12,8},{9,1... | collective-permute-start | bytes 221192 | tf_op jit(solution)/shard_map/ppermute | solution.py:60
  25.6 4.4 %collective-permute-start.4 = (f32[2,3,3,4,16,1]{4,3,2,1,5,0:T(4,128)S(1)}, f32[2,3,3,4,16,1]{4,3,2,1,5,0:T(4,128)S(1)}, u32[]{:S(2)}, u32[]{:S(2)}) collective-permute-start(f32[2,3,3,4,16,1]{4,3,2,1,5,0:T(4,128)S(1)} %pad_maximum_fusion.15), channel_id=1, source_target_pairs={{0,3},{1,0},{2,1},{3,2},{4,7},{5,4},{6,5},{7,6},{8,11},{9,8},{10,9... | collective-permute-start | bytes 13832 | tf_op jit(solution)/shard_map/ppermute | solution.py:63
  30.0 4.0 %collective-permute-start.3 = (f32[2,3,3,4,16,1]{4,3,2,1,5,0:T(4,128)S(1)}, f32[2,3,3,4,16,1]{4,3,2,1,5,0:T(4,128)S(1)}, u32[]{:S(2)}, u32[]{:S(2)}) collective-permute-start(f32[2,3,3,4,16,1]{4,3,2,1,5,0:T(4,128)S(1)} %pad_maximum_fusion.14), channel_id=1, source_target_pairs={{0,1},{1,2},{2,3},{3,0},{4,5},{5,6},{6,7},{7,4},{8,9},{9,10},{10,1... | collective-permute-start | bytes 13832 | tf_op jit(solution)/shard_map/ppermute | solution.py:62
  37.1 1.0 copy-start.30
  38.8 1.7 %copy-start.47 = (f32[4,16,128]{2,1,0:T(8,128)}, f32[4,16,128]{2,1,0:T(8,128)S(1)}, u32[]{:S(2)}) copy-start(f32[4,16,128]{2,1,0:T(8,128)S(1)} %get-tuple-element.40) | copy-start | bytes 98308
  38.8 2.8 %copy-start.34 = (f32[4,16,128]{2,1,0:T(8,128)}, f32[4,16,128]{2,1,0:T(8,128)S(1)}, u32[]{:S(2)}) copy-start(f32[4,16,128]{2,1,0:T(8,128)S(1)} %get-tuple-element.41) | copy-start | bytes 98308
  38.9 2.8 %copy-start.36 = (f32[4,16,128]{2,1,0:T(8,128)}, f32[4,16,128]{2,1,0:T(8,128)S(1)}, u32[]{:S(2)}) copy-start(f32[4,16,128]{2,1,0:T(8,128)S(1)} %get-tuple-element.43) | copy-start | bytes 98308
  38.9 2.8 %copy-start.38 = (f32[4,16,128]{2,1,0:T(8,128)}, f32[4,16,128]{2,1,0:T(8,128)S(1)}, u32[]{:S(2)}) copy-start(f32[4,16,128]{2,1,0:T(8,128)S(1)} %get-tuple-element.45) | copy-start | bytes 98308
  38.9 2.8 %copy-start.40 = (f32[4,16,128]{2,1,0:T(8,128)}, f32[4,16,128]{2,1,0:T(8,128)S(1)}, u32[]{:S(2)}) copy-start(f32[4,16,128]{2,1,0:T(8,128)S(1)} %get-tuple-element.47) | copy-start | bytes 98308
  42.4 8.5 %collective-permute-start.5 = (f32[1,3,3,1,16,128]{5,4,2,1,3,0:T(8,128)S(1)}, f32[1,3,3,1,16,128]{5,4,2,1,3,0:T(8,128)S(1)}, u32[]{:S(2)}, u32[]{:S(2)}) collective-permute-start(f32[1,3,3,1,16,128]{5,4,2,1,3,0:T(8,128)S(1)} %slice_bitcast_fusion.13), channel_id=1, source_target_pairs={{0,8},{8,16},{16,24},{24,32},{32,40},{40,48},{48,56},{56,64},{64,7... | collective-permute-start | bytes 221192 | tf_op jit(solution)/shard_map/ppermute | solution.py:62
  47.6 3.8 %collective-permute-start.6 = (f32[1,3,3,1,16,128]{5,4,2,1,3,0:T(8,128)S(1)}, f32[1,3,3,1,16,128]{5,4,2,1,3,0:T(8,128)S(1)}, u32[]{:S(2)}, u32[]{:S(2)}) collective-permute-start(f32[1,3,3,1,16,128]{5,4,2,1,3,0:T(8,128)S(1)} %slice_bitcast_fusion.12), channel_id=1, source_target_pairs={{0,120},{8,0},{16,8},{24,16},{32,24},{40,32},{48,40},{56,48},{64,5... | collective-permute-start | bytes 221192 | tf_op jit(solution)/shard_map/ppermute | solution.py:63
  52.1 3.9 %copy-start.66 = (f32[16,2]{1,0:T(8,128)S(1)}, f32[16,2]{1,0:T(8,128)}, u32[]{:S(2)}) copy-start(f32[16,2]{1,0:T(8,128)} %copy-done.65) | copy-start | bytes 388
  52.8 7.9 %collective-permute-start.7 = (f32[2,1,3,3,4,1,128]{6,4,2,3,5,1,0:T(4,128)}, f32[2,1,3,3,4,1,128]{6,4,2,3,5,1,0:T(4,128)}, u32[]{:S(2)}, u32[]{:S(2)}) collective-permute-start(f32[2,1,3,3,4,1,128]{6,4,2,3,5,1,0:T(4,128)} %pad_maximum_fusion.16), channel_id=1, source_target_pairs={{0,4},{4,0},{1,5},{5,1},{2,6},{6,2},{3,7},{7,3},{8,12},{12,8},{9,1... | collective-permute-start | bytes 110600 | tf_op jit(solution)/shard_map/ppermute | solution.py:60
  62.5 1.0 copy-start.8
  62.5 1.0 copy-start.10
  63.4 6.3 %collective-permute-start.9 = (f32[1,3,3,4,16,1]{4,3,2,1,5,0:T(4,128)}, f32[1,3,3,4,16,1]{4,3,2,1,5,0:T(4,128)}, u32[]{:S(2)}, u32[]{:S(2)}) collective-permute-start(f32[1,3,3,4,16,1]{4,3,2,1,5,0:T(4,128)} %bitcast.83), channel_id=1, source_target_pairs={{0,3},{1,0},{2,1},{3,2},{4,7},{5,4},{6,5},{7,6},{8,11},{9,8},{10,9... | collective-permute-start | bytes 6920 | tf_op jit(solution)/shard_map/ppermute | solution.py:63
  64.4 7.0 %collective-permute-start.8 = (f32[1,3,3,4,16,1]{4,3,2,1,5,0:T(4,128)}, f32[1,3,3,4,16,1]{4,3,2,1,5,0:T(4,128)}, u32[]{:S(2)}, u32[]{:S(2)}) collective-permute-start(f32[1,3,3,4,16,1]{4,3,2,1,5,0:T(4,128)} %bitcast.242), channel_id=1, source_target_pairs={{0,1},{1,2},{2,3},{3,0},{4,5},{5,6},{6,7},{7,4},{8,9},{9,10},{10,1... | collective-permute-start | bytes 6920 | tf_op jit(solution)/shard_map/ppermute | solution.py:62
  67.8 1.0 copy-start.11
  69.6 2.8 %copy-start.9 = (f32[3,3,4,16,128]{4,3,1,2,0:T(8,128)S(1)}, f32[3,3,4,16,128]{4,3,1,2,0:T(8,128)}, u32[]{:S(2)}) copy-start(f32[3,3,4,16,128]{4,3,1,2,0:T(8,128)} %copy-done.8) | copy-start | bytes 884740
  72.4 1.0 copy-start.31
  72.4 1.0 %copy-start.32 = (f32[3,3,4,16,1]{4,3,1,2,0:T(8,128)S(1)}, f32[3,3,4,16,1]{4,3,1,2,0:T(8,128)}, u32[]{:S(2)}) copy-start(f32[3,3,4,16,1]{4,3,1,2,0:T(8,128)} %copy.611) | copy-start | bytes 6916
  73.5 1.1 %copy-start.2 = (f32[3,3,1,4,16,128]{5,4,1,3,0,2:T(8,128)S(1)}, f32[3,3,1,4,16,128]{5,4,1,3,0,2:T(8,128)}, u32[]{:S(2)}) copy-start(f32[3,3,1,4,16,128]{5,4,1,3,0,2:T(8,128)} %get-tuple-element.61) | copy-start | bytes 884740
  73.5 1.1 %copy-start.13 = (f32[4,16,128]{2,1,0:T(8,128)S(1)}, f32[4,16,128]{2,1,0:T(8,128)}, u32[]{:S(2)}) copy-start(f32[4,16,128]{2,1,0:T(8,128)} %param.21) | copy-start | bytes 98308
  73.5 1.1 %copy-start.16 = (f32[4,16,128]{2,1,0:T(8,128)S(1)}, f32[4,16,128]{2,1,0:T(8,128)}, u32[]{:S(2)}) copy-start(f32[4,16,128]{2,1,0:T(8,128)} %copy-done.15) | copy-start | bytes 98308
  73.5 1.1 %copy-start.19 = (f32[4,16,128]{2,1,0:T(8,128)S(1)}, f32[4,16,128]{2,1,0:T(8,128)}, u32[]{:S(2)}) copy-start(f32[4,16,128]{2,1,0:T(8,128)} %copy-done.18) | copy-start | bytes 98308
  73.5 1.1 %copy-start.22 = (f32[4,16,128]{2,1,0:T(8,128)S(1)}, f32[4,16,128]{2,1,0:T(8,128)}, u32[]{:S(2)}) copy-start(f32[4,16,128]{2,1,0:T(8,128)} %copy-done.21) | copy-start | bytes 98308
  73.5 1.1 %copy-start.25 = (f32[4,16,128]{2,1,0:T(8,128)S(1)}, f32[4,16,128]{2,1,0:T(8,128)}, u32[]{:S(2)}) copy-start(f32[4,16,128]{2,1,0:T(8,128)} %copy-done.24) | copy-start | bytes 98308
  73.5 1.1 %copy-start.28 = (f32[4,16,128]{2,1,0:T(8,128)S(1)}, f32[4,16,128]{2,1,0:T(8,128)}, u32[]{:S(2)}) copy-start(f32[4,16,128]{2,1,0:T(8,128)} %copy-done.27) | copy-start | bytes 98308
  73.5 1.1 %copy-start.58 = (f32[3,3,3]{1,0,2:T(4,128)S(1)}, f32[3,3,3]{1,0,2:T(4,128)}, u32[]{:S(2)}) copy-start(f32[3,3,3]{1,0,2:T(4,128)} %constant.58) | copy-start | bytes 328
  73.5 1.1 %copy-start.61 = (f32[3,3,3]{1,0,2:T(4,128)S(1)}, f32[3,3,3]{1,0,2:T(4,128)}, u32[]{:S(2)}) copy-start(f32[3,3,3]{1,0,2:T(4,128)} %constant.57) | copy-start | bytes 328
  73.7 2.4 %copy-start.6 = (f32[3,3,1,4,16,128]{5,4,1,3,0,2:T(8,128)}, f32[3,3,1,4,16,128]{5,4,1,3,0,2:T(8,128)S(1)}, u32[]{:S(2)}) copy-start(f32[3,3,1,4,16,128]{5,4,1,3,0,2:T(8,128)S(1)} %maximum_bitcast_fusion.15) | copy-start | bytes 884740
  76.1 0.8 copy-start.39
  76.1 0.8 copy-start.41
  76.2 0.8 copy-start.43
  76.2 0.8 copy-start.48
  76.2 0.8 copy-start.77
  77.0 1.7 %copy-start.53 = (s32[4,16,128]{2,1,0:T(8,128)S(1)}, s32[4,16,128]{2,1,0:T(8,128)}, u32[]{:S(2)}) copy-start(s32[4,16,128]{2,1,0:T(8,128)} %param.22) | copy-start | bytes 98308
  78.7 1.0 copy-start.44
  78.7 1.0 copy-start.59
  78.7 1.0 copy-start.62
  79.6 1.2 %copy-start.1 = (f32[3,3,3,4,16,128]{5,4,1,3,0,2:T(8,128)S(1)}, f32[3,3,3,4,16,128]{5,4,1,3,0,2:T(8,128)}, u32[]{:S(2)}) copy-start(f32[3,3,3,4,16,128]{5,4,1,3,0,2:T(8,128)} %get-tuple-element.58) | copy-start | bytes 2654212
  79.6 1.2 %copy-start.3 = (f32[3,3,1,4,16,128]{5,4,1,3,0,2:T(8,128)S(1)}, f32[3,3,1,4,16,128]{5,4,1,3,0,2:T(8,128)}, u32[]{:S(2)}) copy-start(f32[3,3,1,4,16,128]{5,4,1,3,0,2:T(8,128)} %get-tuple-element.61) | copy-start | bytes 884740
  79.6 1.3 %copy-start.5 = (f32[3,3,1,4,16,128]{5,4,1,3,0,2:T(8,128)S(1)}, f32[3,3,1,4,16,128]{5,4,1,3,0,2:T(8,128)}, u32[]{:S(2)}) copy-start(f32[3,3,1,4,16,128]{5,4,1,3,0,2:T(8,128)} %copy-done.4) | copy-start | bytes 884740
  79.6 1.4 %copy-start.7 = (f32[3,3,1,4,16,128]{5,4,1,3,0,2:T(8,128)S(1)}, f32[3,3,1,4,16,128]{5,4,1,3,0,2:T(8,128)}, u32[]{:S(2)}) copy-start(f32[3,3,1,4,16,128]{5,4,1,3,0,2:T(8,128)} %copy-done.6) | copy-start | bytes 884740
  79.6 1.4 %copy-start.14 = (f32[4,16,128]{2,1,0:T(8,128)S(1)}, f32[4,16,128]{2,1,0:T(8,128)}, u32[]{:S(2)}) copy-start(f32[4,16,128]{2,1,0:T(8,128)} %param.21) | copy-start | bytes 98308
  81.0 13.2 %copy-start.49 = (f32[4,16,128]{2,1,0:T(8,128)S(1)}, f32[4,16,128]{2,1,0:T(8,128)}, u32[]{:S(2)}) copy-start(f32[4,16,128]{2,1,0:T(8,128)} %get-tuple-element.50) | copy-start | bytes 98308
  81.0 13.2 %copy-start.50 = (f32[4,16,128]{2,1,0:T(8,128)S(1)}, f32[4,16,128]{2,1,0:T(8,128)}, u32[]{:S(2)}) copy-start(f32[4,16,128]{2,1,0:T(8,128)} %get-tuple-element.52) | copy-start | bytes 98308
  81.0 13.2 %copy-start.51 = (f32[4,16,128]{2,1,0:T(8,128)S(1)}, f32[4,16,128]{2,1,0:T(8,128)}, u32[]{:S(2)}) copy-start(f32[4,16,128]{2,1,0:T(8,128)} %get-tuple-element.54) | copy-start | bytes 98308
  84.4 9.8 %copy-start.20 = (f32[4,16,128]{2,1,0:T(8,128)S(1)}, f32[4,16,128]{2,1,0:T(8,128)}, u32[]{:S(2)}) copy-start(f32[4,16,128]{2,1,0:T(8,128)} %copy-done.18) | copy-start | bytes 98308
  84.4 9.8 %copy-start.23 = (f32[4,16,128]{2,1,0:T(8,128)S(1)}, f32[4,16,128]{2,1,0:T(8,128)}, u32[]{:S(2)}) copy-start(f32[4,16,128]{2,1,0:T(8,128)} %copy-done.21) | copy-start | bytes 98308
  84.4 9.8 %copy-start.26 = (f32[4,16,128]{2,1,0:T(8,128)S(1)}, f32[4,16,128]{2,1,0:T(8,128)}, u32[]{:S(2)}) copy-start(f32[4,16,128]{2,1,0:T(8,128)} %copy-done.24) | copy-start | bytes 98308
  84.4 9.8 %copy-start.29 = (f32[4,16,128]{2,1,0:T(8,128)S(1)}, f32[4,16,128]{2,1,0:T(8,128)}, u32[]{:S(2)}) copy-start(f32[4,16,128]{2,1,0:T(8,128)} %copy-done.27) | copy-start | bytes 98308
  84.4 19.6 %all-to-all-start = ((f32[128,1,8]{2,1,0:T(1,128)}), f32[128,1,8]{2,1,0:T(1,128)S(1)}, u32[]{:S(2)}, u32[]{:S(2)}) async-start(f32[128,1,8]{2,1,0:T(1,128)} %bitcast.93), calls=%async_computation | async-start | bytes 131072 | tf_op jit(solution)/shard_map/all_to_all | solution.py:118
  (26 other events, 18.6 us)

commit v3 on v2

--- a/solution.py
+++ b/solution.py
@@ -2,6 +2,8 @@
 import jax.numpy as jnp
 import numpy as np
 from jax import lax
+from jax.experimental import pallas as pl
+from jax.experimental.pallas import tpu as pltpu
 from jax.sharding import PartitionSpec as P
 
 
@@ -18,6 +20,9 @@
     moved = np.abs(steps).sum(axis=1)
     weights = np.array([8.0 / 27.0, 2.0 / 27.0, 1.0 / 54.0, 1.0 / 216.0])[moved]
     return (steps, weights)
+
+
+STEPS, WEIGHTS = lattice_table()
 
 
 def collide(pops, rate, gamma):
@@ -42,16 +47,6 @@
     return ((1.0 - gamma) * relaxed + gamma * flipped, flipped - relaxed)
 
 
-def adjoint_collide(pops, rate, gamma, adj_post):
-
-    def forward(values):
-        return collide(values, rate, gamma)
-
-    post, pullback, deriv = jax.vjp(forward, pops, has_aux=True)
-    (adj_pre,) = pullback(adj_post)
-    return (adj_pre, jnp.sum(adj_post * deriv, axis=0))
-
-
 def halo_exchange(up, down, axis):
     size = lax.axis_size(axis)
     if size == 1:
@@ -64,34 +59,191 @@
     return lo, hi
 
 
-def move_axis(cubes, signs, axis, d):
-    n = cubes[0].shape[3 + d]
-    ups, downs = [], []
-    for cube, sign in zip(cubes, signs):
-        plus = lax.index_in_dim(cube, 1 + sign, axis=d, keepdims=False)
-        minus = lax.index_in_dim(cube, 1 - sign, axis=d, keepdims=False)
-        ups.append(lax.slice_in_dim(plus, n - 1, n, axis=2 + d))
-        downs.append(lax.slice_in_dim(minus, 0, 1, axis=2 + d))
-    lo, hi = halo_exchange(jnp.stack(ups), jnp.stack(downs), axis)
+def shifted(cube, lo, hi, d, sign):
+    n = cube.shape[3 + d]
+    plus = lax.index_in_dim(cube, 1 + sign, axis=d, keepdims=False)
+    minus = lax.index_in_dim(cube, 1 - sign, axis=d, keepdims=False)
+    still = lax.index_in_dim(cube, 1, axis=d, keepdims=False)
+    plus = jnp.concatenate([lo, lax.slice_in_dim(plus, 0, n - 1, axis=2 + d)], axis=2 + d)
+    minus = jnp.concatenate([lax.slice_in_dim(minus, 1, n, axis=2 + d), hi], axis=2 + d)
+    groups = [None, still, None]
+    groups[1 + sign] = plus
+    groups[1 - sign] = minus
+    return jnp.stack(groups, axis=d)
+
+
+def faces(cube, sign, d):
+    n = cube.shape[3 + d]
+    plus = lax.index_in_dim(cube, 1 + sign, axis=d, keepdims=False)
+    minus = lax.index_in_dim(cube, 1 - sign, axis=d, keepdims=False)
+    return lax.slice_in_dim(plus, n - 1, n, axis=2 + d), lax.slice_in_dim(minus, 0, 1, axis=2 + d)
+
+
+def halos(fields, signs):
+    cubes = [f.reshape((3, 3, 3) + f.shape[1:]) for f in fields]
+    sx, sy, sz = cubes[0].shape[3:]
+    x_up, x_dn = zip(*[faces(c, s, 0) for c, s in zip(cubes, signs)])
+    xlo, xhi = halo_exchange(jnp.stack(x_up), jnp.stack(x_dn), "gx")
+    y_up, y_dn = [], []
+    for k, (c, s) in enumerate(zip(cubes, signs)):
+        top = shifted(c[:, :, :, :, sy - 1 : sy], xlo[k][:, :, :, sy - 1 : sy], xhi[k][:, :, :, sy - 1 : sy], 0, s)
+        bot = shifted(c[:, :, :, :, 0:1], xlo[k][:, :, :, 0:1], xhi[k][:, :, :, 0:1], 0, s)
+        y_up.append(lax.index_in_dim(top, 1 + s, axis=1, keepdims=False))
+        y_dn.append(lax.index_in_dim(bot, 1 - s, axis=1, keepdims=False))
+    ylo, yhi = halo_exchange(jnp.stack(y_up), jnp.stack(y_dn), "gy")
+    z_up, z_dn = [], []
+    for k, (c, s) in enumerate(zip(cubes, signs)):
+        cols = []
+        for z0 in (sz - 1, 0):
+            col = shifted(c[..., z0 : z0 + 1], xlo[k][..., z0 : z0 + 1], xhi[k][..., z0 : z0 + 1], 0, s)
+            col = shifted(col, ylo[k][..., z0 : z0 + 1], yhi[k][..., z0 : z0 + 1], 1, s)
+            cols.append(col)
+        z_up.append(lax.index_in_dim(cols[0], 1 + s, axis=2, keepdims=False))
+        z_dn.append(lax.index_in_dim(cols[1], 1 - s, axis=2, keepdims=False))
+    zlo, zhi = halo_exchange(jnp.stack(z_up), jnp.stack(z_dn), "gz")
     out = []
-    for k, (cube, sign) in enumerate(zip(cubes, signs)):
-        plus = lax.index_in_dim(cube, 1 + sign, axis=d, keepdims=False)
-        minus = lax.index_in_dim(cube, 1 - sign, axis=d, keepdims=False)
-        still = lax.index_in_dim(cube, 1, axis=d, keepdims=False)
-        plus = jnp.concatenate([lo[k], lax.slice_in_dim(plus, 0, n - 1, axis=2 + d)], axis=2 + d)
-        minus = jnp.concatenate([lax.slice_in_dim(minus, 1, n, axis=2 + d), hi[k]], axis=2 + d)
-        groups = [None, still, None]
-        groups[1 + sign] = plus
-        groups[1 - sign] = minus
-        out.append(jnp.stack(groups, axis=d))
+    for k in range(len(cubes)):
+        out.append(
+            (
+                xlo[k].reshape(9, sy, sz),
+                xhi[k].reshape(9, sy, sz),
+                ylo[k].reshape(9, sx, sz),
+                yhi[k].reshape(9, sx, sz),
+                zlo[k].reshape(9, sx, sy, 1),
+                zhi[k].reshape(9, sx, sy, 1),
+            )
+        )
     return out
 
 
-def propagate(fields, signs):
-    cubes = [field.reshape((3, 3, 3) + field.shape[1:]) for field in fields]
-    for d, axis in enumerate(("gx", "gy", "gz")):
-        cubes = move_axis(cubes, signs, axis, d)
-    return [cube.reshape(field.shape) for cube, field in zip(cubes, fields)]
+def move_into(dst, src, hal, sign):
+    xlo, xhi, ylo, yhi, zlo, zhi = hal
+    _, sx, sy, sz = src.shape
+    rows = lax.broadcasted_iota(jnp.int32, (sy, sz), 0)
+    lanes = lax.broadcasted_iota(jnp.int32, (sy, sz), 1)
+    for q in range(27):
+        cx, cy, cz = (int(v) for v in STEPS[q])
+        vx, vy, vz = sign * cx, sign * cy, sign * cz
+        for i in range(sx):
+            j = i - vx
+            if j < 0:
+                t = xlo[(cy + 1) * 3 + cz + 1]
+            elif j >= sx:
+                t = xhi[(cy + 1) * 3 + cz + 1]
+            else:
+                t = src[q, j]
+            if vy == 1:
+                t = jnp.where(rows == 0, ylo[(cx + 1) * 3 + cz + 1, pl.ds(i, 1), :], pltpu.roll(t, 1, 0))
+            elif vy == -1:
+                t = jnp.where(rows == sy - 1, yhi[(cx + 1) * 3 + cz + 1, pl.ds(i, 1), :], pltpu.roll(t, sy - 1, 0))
+            if vz == 1:
+                t = jnp.where(lanes == 0, zlo[(cx + 1) * 3 + cy + 1, i], pltpu.roll(t, 1, 1))
+            elif vz == -1:
+                t = jnp.where(lanes == sz - 1, zhi[(cx + 1) * 3 + cy + 1, i], pltpu.roll(t, sz - 1, 1))
+            dst[q, i] = t
+
+
+def adjoint_rows(F, A, om, ga):
+    rho = sum(F)
+    mom = []
+    for axis in range(3):
+        pos = [F[q] for q in range(27) if STEPS[q, axis] == 1]
+        neg = [F[q] for q in range(27) if STEPS[q, axis] == -1]
+        mom.append(sum(pos) - sum(neg))
+    vel = (mom[0] / rho, mom[1] / rho, mom[2] / rho)
+    uu = vel[0] * vel[0] + vel[1] * vel[1] + vel[2] * vel[2]
+    sens = 0.0
+    e_rho = 0.0
+    s0 = 0.0
+    sm = [0.0, 0.0, 0.0]
+    for q in range(27):
+        c = STEPS[q]
+        w = float(WEIGHTS[q])
+        cu = None
+        for axis in range(3):
+            if c[axis] == 1:
+                cu = vel[axis] if cu is None else cu + vel[axis]
+            elif c[axis] == -1:
+                cu = -vel[axis] if cu is None else cu - vel[axis]
+        if cu is None:
+            eq = w * rho * (1.0 - 1.5 * uu)
+        else:
+            eq = w * rho * (1.0 + 3.0 * cu + 4.5 * cu * cu - 1.5 * uu)
+        bgk = F[q] - om * (F[q] - eq)
+        sens = sens + A[q] * (F[26 - q] - bgk)
+        aw = A[q] * w
+        s0 = s0 + aw
+        if cu is None:
+            e_rho = e_rho + aw * (1.0 + 1.5 * uu)
+        else:
+            e_rho = e_rho + aw * (1.0 - 4.5 * cu * cu + 1.5 * uu)
+            t = aw * (1.0 + 3.0 * cu)
+            for axis in range(3):
+                if c[axis] == 1:
+                    sm[axis] = sm[axis] + t
+                elif c[axis] == -1:
+                    sm[axis] = sm[axis] - t
+    em = [3.0 * sm[axis] - 3.0 * vel[axis] * s0 for axis in range(3)]
+    keep = 1.0 - ga
+    out = []
+    for p in range(27):
+        c = STEPS[p]
+        g = e_rho
+        for axis in range(3):
+            if c[axis] == 1:
+                g = g + em[axis]
+            elif c[axis] == -1:
+                g = g - em[axis]
+        out.append(keep * ((1.0 - om) * A[p] + om * g) + ga * A[26 - p])
+    return out, sens
+
+
+def chunked_adjoint(f_ref, a_ref, rate_ref, gamma_ref, out_ref, sens_ref):
+    _, sx, sy, sz = out_ref.shape
+    halves = sy // 8
+
+    def body(step, carry):
+        i = step // halves
+        h = pl.multiple_of((step % halves) * 8, 8)
+        F = [f_ref[q, i, pl.ds(h, 8), :] for q in range(27)]
+        A = [a_ref[q, i, pl.ds(h, 8), :] for q in range(27)]
+        om = rate_ref[i, pl.ds(h, 8), :]
+        ga = gamma_ref[i, pl.ds(h, 8), :]
+        adj, sens = adjoint_rows(F, A, om, ga)
+        for q in range(27):
+            out_ref[q, i, pl.ds(h, 8), :] = adj[q]
+        sens_ref[i, pl.ds(h, 8), :] = sens
+        return carry
+
+    lax.fori_loop(0, sx * halves, body, 0)
+
+
+def next_kernel(cf_ref, ae_ref, *refs):
+    hal_f = refs[0:6]
+    hal_a = refs[6:12]
+    rate_ref, gamma_ref, out_ref, sens_ref, fs, as_ = refs[12:]
+    move_into(fs, cf_ref, hal_f, 1)
+    move_into(as_, ae_ref, hal_a, -1)
+    chunked_adjoint(fs, as_, rate_ref, gamma_ref, out_ref, sens_ref)
+
+
+def now_kernel(an_ref, f_ref, *refs):
+    hal = refs[0:6]
+    rate_ref, gamma_ref, out_ref, sens_ref, as_ = refs[6:]
+    move_into(as_, an_ref, hal, -1)
+    chunked_adjoint(f_ref, as_, rate_ref, gamma_ref, out_ref, sens_ref)
+
+
+def run_stage(kernel, args, shape, scratch):
+    _, sx, sy, sz = shape
+    return pl.pallas_call(
+        kernel,
+        out_shape=(
+            jax.ShapeDtypeStruct(shape, jnp.float32),
+            jax.ShapeDtypeStruct((sx, sy, sz), jnp.float32),
+        ),
+        scratch_shapes=[pltpu.VMEM(shape, jnp.float32) for _ in range(scratch)],
+    )(*args)
 
 
 def shards(check_pops, adjoint_end, relax_rate, wall_flag, patch_of_cell, porosity, patch_slot):
@@ -103,10 +255,13 @@
     walls = wall_flag.astype(jnp.float32)
     gamma = walls * solid
     post_now, _ = collide(check_pops, relax_rate, gamma)
-    pops_next, post_adj_next = propagate([post_now, adjoint_end], [1, -1])
-    adj_next, sens_next = adjoint_collide(pops_next, relax_rate, gamma, post_adj_next)
-    (post_adj,) = propagate([adj_next], [-1])
-    adjoint_start, sens_now = adjoint_collide(check_pops, relax_rate, gamma, post_adj)
+    hal_f, hal_a = halos([post_now, adjoint_end], [1, -1])
+    shape = check_pops.shape
+    adj_next, sens_next = run_stage(
+        next_kernel, (post_now, adjoint_end) + hal_f + hal_a + (relax_rate, gamma), shape, 2
+    )
+    (hal_n,) = halos([adj_next], [-1])
+    adjoint_start, sens_now = run_stage(now_kernel, (adj_next, check_pops) + hal_n + (relax_rate, gamma), shape, 1)
     density = walls * (sens_next + sens_now)
     boxes = density.reshape(sx, 2, sy // 2, 2, sz // 2).sum(axis=(2, 4))
     parts = jnp.stack([boxes[0], boxes[1 : sx - 1].sum(axis=0), boxes[sx - 1]])

time: 106 us -> 100 us (0.943)
  blocking collectives: 0 us -> 22.7 us
  waiting for transfers between devices: 16.3 us -> 4.61 us
  other arithmetic: 18.6 us -> 7.16 us
  starting transfers between devices: 31.6 us -> 20.5 us
  Pallas kernels: 0 us -> 9.04 us
  local copies, waits for them, and re-layouts: 36 us -> 33.8 us
    all_to_all x0 -> x1, blocking collectives: none -> 22.7 us  [shards(): lax.all_to_all(placed.reshape(devices, count // devices), ('gx', 'gy', 'g...]
    all_to_all x1 -> x0, starting transfers between devices: 9.75 us -> none  [shards(): lax.all_to_all(placed.reshape(devices, count // devices), ('gx', 'gy', 'g...]
    pallas_call x0 -> x2, Pallas kernels: none -> 9.04 us  [run_stage(): pl.pallas_call(kernel, out_shape=(jax.ShapeDtypeStruct(shape, jnp.float32...]
    slice x46 -> x71, local copies, waits for them, and re-layouts: 6.21 us -> 14 us  [the longest x15 3.71 us: halos(): col = shifted(col, ylo[k][..., z0:z0 + 1], yhi[k][..., z0:z0 + 1], 1, s)]
    unnamed x165 -> x59, local copies, waits for them, and re-layouts: 18.3 us -> 10.6 us
    all_to_all x1 -> x0, waiting for transfers between devices: 7.59 us -> none  [shards(): lax.all_to_all(placed.reshape(devices, count // devices), ('gx', 'gy', 'g...]
    squeeze x18 -> x6, local copies, waits for them, and re-layouts: 6.18 us -> 0.05 us  [the longest x4 0.03 us: shifted(): plus = lax.index_in_dim(cube, 1 + sign, axis=d, keepdims=False)]
    another operation x12 -> x13, local copies, waits for them, and re-layouts: 1.08 us -> 6.66 us  [the longest x3 3.01 us: halos(): zlo[k].reshape(9, sx, sy, 1)]
  transfers between devices with their start and end apart: 11 -> 10, of which waited for: 7 -> 5; matrix products, arithmetic and copies ran while one was open for 14% -> 14% of each run, Pallas kernels for 0% -> 0%
where the time goes in v3:
time: 100 us; the launch traced here: 99.3 us
  local copies, waits for them, and re-layouts  33.8 us (34%)
  blocking collectives  22.7 us (23%)
  starting transfers between devices  20.5 us (20%)
  Pallas kernels  9.04 us (9%)
  other arithmetic  7.16 us (7%)
  waiting for transfers between devices  4.61 us (5%)
  between operations  1.51 us (2%)
    all_to_all x1, blocking collectives, shards(): lax.all_to_all(placed.reshape(devices, count // devices), ('gx', 'gy', 'g...  22.7 us
    unnamed x59, local copies, waits for them, and re-layouts  10.6 us
    ppermute x4, starting transfers between devices, halo_exchange(): hi = lax.ppermute(down, axis, [(i, (i - 1) % size) for i in range(size)])  10.3 us
    pallas_call x2, Pallas kernels, run_stage(): pl.pallas_call(kernel, out_shape=(jax.ShapeDtypeStruct(shape, jnp.float32...  9.04 us
    ppermute x2, starting transfers between devices, halo_exchange(): both = lax.ppermute(jnp.stack([up, down]), axis, [(0, 1), (1, 0)])  6.89 us
    slice x15, local copies, waits for them, and re-layouts, halos(): col = shifted(col, ylo[k][..., z0:z0 + 1], yhi[k][..., z0:z0 + 1], 1, s)  3.71 us
    slice x18, local copies, waits for them, and re-layouts, shifted(): lax.slice_in_dim(minus, 1, n, axis=2 + d)  3.62 us
    ppermute x4, starting transfers between devices, halo_exchange(): lo = lax.ppermute(up, axis, [(i, (i + 1) % size) for i in range(size)])  3.31 us
  transfers between devices with their start and end apart: 10, of which 5 were waited for; matrix products, arithmetic and copies ran while one was open for 14% of the time, Pallas kernels for 0%

profile of v3, /device:TPU:1, one launch (start us, length us, event | category | flops | bytes accessed | tf_op | source)
XLA Modules:
  0.0 99.3 jit_solution(15122648037940486962)
XLA Ops:
  0.6 1.2 %slice_reduce_fusion.6 = (f32[4,16,128]{2,1,0:T(8,128)S(1)}, f32[4,16,128]{2,1,0:T(8,128)S(1)}) fusion(f32[3,3,3,4,16,128]{5,4,3,2,1,0:T(8,128)} %bitcast.348), kind=kLoop, calls=%fused_computation.16 | loop fusion | flops 131072 | bytes 655360 | tf_op jit(solution)/shard_map/reduce_sum | solution.py:33
  1.8 1.1 %slice_reduce_fusion.4 = (f32[4,16,128]{2,1,0:T(8,128)S(1)}, f32[4,16,128]{2,1,0:T(8,128)S(1)}) fusion(f32[3,3,3,4,16,128]{5,4,3,2,1,0:T(8,128)} %bitcast.349), kind=kLoop, calls=%fused_computation.14 | loop fusion | flops 131072 | bytes 655360 | tf_op jit(solution)/shard_map/reduce_sum | solution.py:34
  3.0 0.9 slice.624
  4.1 0.6 copy-done.16
  5.0 0.6 gather_fusion
  6.0 0.7 copy-done.8
  6.8 0.7 copy-done.7
  7.5 1.4 %fusion.7.cf_ref = f32[27,4,16,128]{3,2,1,0:T(8,128)S(1)} fusion(f32[27,4,16,128]{3,2,1,0:T(8,128)S(1)} %copy-done, f32[4,16,128]{2,1,0:T(8,128)S(1)} %get-tuple-element.152.refs_13_.refs_7_, f32[4,16,128]{2,1,0:T(8,128)S(1)} %get-tuple-element.22, f32[4,16,128]{2,1,0:T(8,128)S(1)} %get-tuple-element.25, f32[27]{0:T(128)S(1)} %copy-done.18, ...), kind=kLoop, calls=%fused_computation.9 | loop fusion | flops 4202496 | bytes 2032048 | tf_op jit(solution)/shard_map/add | solution.py:47
  9.0 3.1 %collective-permute-start = (f32[2,3,3,1,16,128]{5,4,2,1,3,0:T(8,128)S(1)}, f32[2,3,3,1,16,128]{5,4,2,1,3,0:T(8,128)S(1)}, u32[]{:S(2)}, u32[]{:S(2)}) collective-permute-start(f32[2,3,3,1,16,128]{5,4,2,1,3,0:T(8,128)S(1)} %pad_maximum_fusion), channel_id=1, source_target_pairs={{0,8},{8,16},{16,24},{24,32},{32,40},{40,48},{48,56},{56,64},{64,7... | collective-permute-start | bytes 442376 | tf_op jit(solution)/shard_map/ppermute | solution.py:57
  12.3 0.7 fusion.24
  13.0 0.6 slice.830
  14.2 0.3 copy.760
  14.5 0.6 slice.900
  15.1 0.6 slice.870
  15.8 0.6 slice.818
  16.4 0.6 slice.834
  17.0 0.3 fusion.23
  17.9 0.3 copy.838
  18.5 0.3 copy.844
  18.8 0.3 copy.840
  19.1 0.7 fusion.30
  20.0 0.7 fusion.29
  21.5 0.7 copy-done.13
  22.4 0.7 copy-done.12
  23.5 0.7 copy-done.11
  24.2 0.7 copy-done.10
  24.9 0.7 copy-done.9
  25.8 3.4 %collective-permute-start.2 = (f32[2,2,3,3,4,1,128]{6,4,3,2,1,5,0:T(4,128)S(1)}, f32[2,2,3,3,4,1,128]{6,4,3,2,1,5,0:T(4,128)S(1)}, u32[]{:S(2)}, u32[]{:S(2)}) collective-permute-start(f32[2,2,3,3,4,1,128]{6,4,3,2,1,5,0:T(4,128)S(1)} %pad_maximum_fusion.2), channel_id=1, source_target_pairs={{0,4},{4,0},{1,5},{5,1},{2,6},{6,2},{3,7},{7,3},{8,12},{12,8},{9,1... | collective-permute-start | bytes 221192 | tf_op jit(solution)/shard_map/ppermute | solution.py:55
  29.7 1.3 %collective-permute-done.2 = f32[2,2,3,3,4,1,128]{6,4,3,2,1,5,0:T(4,128)S(1)} collective-permute-done((f32[2,2,3,3,4,1,128]{6,4,3,2,1,5,0:T(4,128)S(1)}, f32[2,2,3,3,4,1,128]{6,4,3,2,1,5,0:T(4,128)S(1)}, u32[]{:S(2)}, u32[]{:S(2)}) %collective-permute-start.2) | collective-permute-done | bytes 73760 | tf_op jit(solution)/shard_map/ppermute | solution.py:55
  30.9 0.7 fusion.33
  31.6 0.3 copy.772
  32.0 0.3 copy.754
  32.4 0.3 copy.771
  32.7 0.3 copy.753
  33.6 2.5 %collective-permute-start.4 = (f32[2,3,3,4,16,1]{4,3,2,1,5,0:T(4,128)S(1)}, f32[2,3,3,4,16,1]{4,3,2,1,5,0:T(4,128)S(1)}, u32[]{:S(2)}, u32[]{:S(2)}) collective-permute-start(f32[2,3,3,4,16,1]{4,3,2,1,5,0:T(4,128)S(1)} %pad_maximum_fusion.10), channel_id=1, source_target_pairs={{0,3},{1,0},{2,1},{3,2},{4,7},{5,4},{6,5},{7,6},{8,11},{9,8},{10,9... | collective-permute-start | bytes 13832 | tf_op jit(solution)/shard_map/ppermute | solution.py:58
  36.6 0.6 collective-permute-done.4
  37.2 1.0 %copy.785.refs_5_ = f32[9,4,16,1]{3,2,1,0:T(8,128)} copy(f32[9,4,16,1]{2,1,0,3:T(4,128)S(1)} %bitcast.417) | data formatting | bytes 4608 | tf_op jit(solution)/shard_map/reshape;squeeze | solution.py:113
  38.2 1.0 %copy.787.refs_11_ = f32[9,4,16,1]{3,2,1,0:T(8,128)} copy(f32[9,4,16,1]{2,1,0,3:T(4,128)S(1)} %bitcast.415) | data formatting | bytes 4608 | tf_op jit(solution)/shard_map/reshape;squeeze | solution.py:113
  39.2 1.4 %collective-permute-done.3 = f32[2,3,3,4,16,1]{4,3,2,1,5,0:T(4,128)S(1)} collective-permute-done((f32[2,3,3,4,16,1]{4,3,2,1,5,0:T(4,128)S(1)}, f32[2,3,3,4,16,1]{4,3,2,1,5,0:T(4,128)S(1)}, u32[]{:S(2)}, u32[]{:S(2)}) %collective-permute-start.3) | collective-permute-done | bytes 4640 | tf_op jit(solution)/shard_map/ppermute | solution.py:57
  40.6 1.0 %copy.784.refs_4_ = f32[9,4,16,1]{3,2,1,0:T(8,128)} copy(f32[9,4,16,1]{2,1,0,3:T(4,128)S(1)} %bitcast.418) | data formatting | bytes 4608 | tf_op jit(solution)/shard_map/reshape;squeeze | solution.py:112
  41.6 1.0 %copy.786.refs_10_ = f32[9,4,16,1]{3,2,1,0:T(8,128)} copy(f32[9,4,16,1]{2,1,0,3:T(4,128)S(1)} %bitcast.416) | data formatting | bytes 4608 | tf_op jit(solution)/shard_map/reshape;squeeze | solution.py:112
  42.6 4.8 %shard_map.122 = (f32[27,4,16,128]{3,2,1,0:T(8,128)}, f32[4,16,128]{2,1,0:T(8,128)}) custom-call(f32[27,4,16,128]{3,2,1,0:T(8,128)} %copy-done.1, f32[27,4,16,128]{3,2,1,0:T(8,128)} %ae_ref.1, f32[9,16,128]{2,1,0:T(8,128)} %bitcast.369, f32[9,16,128]{2,1,0:T(8,128)} %bitcast.371, f32[9,4,128]{2,1,0:T(4,128)} %bitcast.376, f32[9,4,128]{2,1,0:T(4,128)} %bitcast.375, ...), custom_call_target="tpu_custom_call" | custom-call | tf_op jit(solution)/shard_map/pallas_call | solution.py:239
  47.4 1.2 %fusion.22 = (f32[9,4,16,128]{3,2,1,0:T(8,128)S(1)}, f32[9,4,16,128]{3,2,1,0:T(8,128)S(1)}) fusion(f32[27,4,16,128]{3,2,1,0:T(8,128)} %get-tuple-element.6.an_ref), kind=kLoop, calls=%fused_computation.171 | loop fusion | bytes 1179648 | tf_op jit(solution)/shard_map/slice | solution.py:78
  48.9 0.3 fusion.20
  49.2 5.0 %collective-permute-start.6 = (f32[1,3,3,1,16,128]{5,4,2,1,3,0:T(8,128)S(1)}, f32[1,3,3,1,16,128]{5,4,2,1,3,0:T(8,128)S(1)}, u32[]{:S(2)}, u32[]{:S(2)}) collective-permute-start(f32[1,3,3,1,16,128]{5,4,2,1,3,0:T(8,128)S(1)} %slice_bitcast_fusion), channel_id=1, source_target_pairs={{0,120},{8,0},{16,8},{24,16},{32,24},{40,32},{48,40},{56,48},{64,5... | collective-permute-start | bytes 221192 | tf_op jit(solution)/shard_map/ppermute | solution.py:58
  54.6 0.3 copy.854
  55.1 0.3 copy.857
  56.1 0.5 copy-done.4
  56.8 0.5 copy-done.5
  57.4 3.5 %collective-permute-start.7 = (f32[2,1,3,3,4,1,128]{6,4,3,2,5,1,0:T(4,128)S(1)}, f32[2,1,3,3,4,1,128]{6,4,3,2,5,1,0:T(4,128)S(1)}, u32[]{:S(2)}, u32[]{:S(2)}) collective-permute-start(f32[2,1,3,3,4,1,128]{6,4,3,2,5,1,0:T(4,128)S(1)} %pad_maximum_fusion.11), channel_id=1, source_target_pairs={{0,4},{4,0},{1,5},{5,1},{2,6},{6,2},{3,7},{7,3},{8,12},{12,8},{9,1... | collective-permute-start | bytes 110600 | tf_op jit(solution)/shard_map/ppermute | solution.py:55
  61.8 0.5 collective-permute-done.7
  62.3 0.6 slice_bitcast_fusion.39
  63.0 0.3 copy.816
  63.3 0.3 copy.807
  63.7 0.3 copy.817
  64.0 0.3 copy.808
  64.8 2.7 %collective-permute-start.9 = (f32[1,3,3,4,16,1]{4,3,2,1,5,0:T(4,128)S(1)}, f32[1,3,3,4,16,1]{4,3,2,1,5,0:T(4,128)S(1)}, u32[]{:S(2)}, u32[]{:S(2)}) collective-permute-start(f32[1,3,3,4,16,1]{4,3,2,1,5,0:T(4,128)S(1)} %fusion.8), channel_id=1, source_target_pairs={{0,3},{1,0},{2,1},{3,2},{4,7},{5,4},{6,5},{7,6},{8,11},{9,8},{10,9... | collective-permute-start | bytes 6920 | tf_op jit(solution)/shard_map/ppermute | solution.py:58
  67.6 0.8 collective-permute-done.9
  68.4 1.0 %copy.821.refs_5_ = f32[9,4,16,1]{3,2,1,0:T(8,128)} copy(f32[9,4,16,1]{2,1,0,3:T(4,128)S(1)} %bitcast.422) | data formatting | bytes 4608 | tf_op jit(solution)/shard_map/reshape;squeeze | solution.py:113
  69.4 1.0 %copy.820.refs_4_ = f32[9,4,16,1]{3,2,1,0:T(8,128)} copy(f32[9,4,16,1]{2,1,0,3:T(4,128)S(1)} %bitcast.421) | data formatting | bytes 4608 | tf_op jit(solution)/shard_map/reshape;squeeze | solution.py:112
  70.4 4.2 %shard_map.123 = (f32[27,4,16,128]{3,2,1,0:T(8,128)}, f32[4,16,128]{2,1,0:T(8,128)}) custom-call(f32[27,4,16,128]{3,2,1,0:T(8,128)} %get-tuple-element.6.an_ref, f32[27,4,16,128]{3,2,1,0:T(8,128)} %f_ref.1, f32[9,16,128]{2,1,0:T(8,128)} %bitcast.361, f32[9,16,128]{2,1,0:T(8,128)} %bitcast.358, f32[9,4,128]{2,1,0:T(4,128)} %bitcast.378, ...), custom_call_target="tpu_custom_call" | custom-call | tf_op jit(solution)/shard_map/pallas_call | solution.py:239
  74.7 0.8 add_multiply_fusion
  75.9 22.7 %all_to_all.9 = f32[128,1,8]{2,1,0:T(1,128)S(1)} all-to-all(f32[128,1,8]{2,1,0:T(1,128)S(1)} %bitcast.372), channel_id=1, replica_groups=mesh['gx'=16,'gy'=2,'gz'=4] {'gx','gy','gz'}, dimensions={0} | all-to-all | bytes 8192 | tf_op jit(solution)/shard_map/all_to_all | solution.py:273
  98.6 0.7 reduce_sum.109
  (199 shorter events, 9.6 us)
Async XLA Ops:
  0.6 2.3 %copy-start = (f32[27,4,16,128]{3,2,1,0:T(8,128)S(1)}, f32[27,4,16,128]{3,2,1,0:T(8,128)}, u32[]{:S(2)}) copy-start(f32[27,4,16,128]{3,2,1,0:T(8,128)} %f_ref.1) | copy-start | bytes 2654212
  2.9 1.1 %copy-start.15 = (s32[1024]{0:T(1024)S(1)}, s32[1024]{0:T(1024)}, u32[]{:S(2)}) copy-start(s32[1024]{0:T(1024)} %param.17) | copy-start | bytes 12292
  3.0 2.9 %copy-start.2 = (f32[27,4,16,128]{3,2,1,0:T(8,128)S(1)}, f32[27,4,16,128]{3,2,1,0:T(8,128)}, u32[]{:S(2)}) copy-start(f32[27,4,16,128]{3,2,1,0:T(8,128)} %ae_ref.1) | copy-start | bytes 2654212
  4.0 0.7 copy-start.16
  5.9 0.8 copy-start.8
  6.7 0.8 copy-start.7
  6.7 0.8 copy-start.20
  6.7 2.1 %copy-start.6 = (f32[4,16,128]{2,1,0:T(8,128)}, f32[4,16,128]{2,1,0:T(8,128)S(1)}, u32[]{:S(2)}) copy-start(f32[4,16,128]{2,1,0:T(8,128)S(1)} %get-tuple-element.152.refs_13_.refs_7_) | copy-start | bytes 98308
  6.7 0.7 copy-start.17
  6.8 0.7 copy-start.18
  6.8 0.7 copy-start.19
  8.9 8.1 %copy-start.1 = (f32[27,4,16,128]{3,2,1,0:T(8,128)}, f32[27,4,16,128]{3,2,1,0:T(8,128)S(1)}, u32[]{:S(2)}) copy-start(f32[27,4,16,128]{3,2,1,0:T(8,128)S(1)} %fusion.7.cf_ref) | copy-start | bytes 2654212
  9.0 10.1 %collective-permute-start = (f32[2,3,3,1,16,128]{5,4,2,1,3,0:T(8,128)S(1)}, f32[2,3,3,1,16,128]{5,4,2,1,3,0:T(8,128)S(1)}, u32[]{:S(2)}, u32[]{:S(2)}) collective-permute-start(f32[2,3,3,1,16,128]{5,4,2,1,3,0:T(8,128)S(1)} %pad_maximum_fusion), channel_id=1, source_target_pairs={{0,8},{8,16},{16,24},{24,32},{32,40},{40,48},{48,56},{56,64},{64,7... | collective-permute-start | bytes 442376 | tf_op jit(solution)/shard_map/ppermute | solution.py:57
  12.1 7.9 %collective-permute-start.1 = (f32[2,3,3,1,16,128]{5,4,2,1,3,0:T(8,128)S(1)}, f32[2,3,3,1,16,128]{5,4,2,1,3,0:T(8,128)S(1)}, u32[]{:S(2)}, u32[]{:S(2)}) collective-permute-start(f32[2,3,3,1,16,128]{5,4,2,1,3,0:T(8,128)S(1)} %pad_maximum_fusion.1), channel_id=1, source_target_pairs={{0,120},{8,0},{16,8},{24,16},{32,24},{40,32},{48,40},{56,48},{64,5... | collective-permute-start | bytes 442376 | tf_op jit(solution)/shard_map/ppermute | solution.py:58
  21.4 0.7 copy-start.13
  22.4 0.7 copy-start.12
  23.5 0.7 copy-start.11
  24.2 0.7 copy-start.10
  24.9 0.7 copy-start.9
  25.8 5.1 %collective-permute-start.2 = (f32[2,2,3,3,4,1,128]{6,4,3,2,1,5,0:T(4,128)S(1)}, f32[2,2,3,3,4,1,128]{6,4,3,2,1,5,0:T(4,128)S(1)}, u32[]{:S(2)}, u32[]{:S(2)}) collective-permute-start(f32[2,2,3,3,4,1,128]{6,4,3,2,1,5,0:T(4,128)S(1)} %pad_maximum_fusion.2), channel_id=1, source_target_pairs={{0,4},{4,0},{1,5},{5,1},{2,6},{6,2},{3,7},{7,3},{8,12},{12,8},{9,1... | collective-permute-start | bytes 221192 | tf_op jit(solution)/shard_map/ppermute | solution.py:55
  33.6 3.6 %collective-permute-start.4 = (f32[2,3,3,4,16,1]{4,3,2,1,5,0:T(4,128)S(1)}, f32[2,3,3,4,16,1]{4,3,2,1,5,0:T(4,128)S(1)}, u32[]{:S(2)}, u32[]{:S(2)}) collective-permute-start(f32[2,3,3,4,16,1]{4,3,2,1,5,0:T(4,128)S(1)} %pad_maximum_fusion.10), channel_id=1, source_target_pairs={{0,3},{1,0},{2,1},{3,2},{4,7},{5,4},{6,5},{7,6},{8,11},{9,8},{10,9... | collective-permute-start | bytes 13832 | tf_op jit(solution)/shard_map/ppermute | solution.py:58
  36.5 4.1 %collective-permute-start.3 = (f32[2,3,3,4,16,1]{4,3,2,1,5,0:T(4,128)S(1)}, f32[2,3,3,4,16,1]{4,3,2,1,5,0:T(4,128)S(1)}, u32[]{:S(2)}, u32[]{:S(2)}) collective-permute-start(f32[2,3,3,4,16,1]{4,3,2,1,5,0:T(4,128)S(1)} %pad_maximum_fusion.9), channel_id=1, source_target_pairs={{0,1},{1,2},{2,3},{3,0},{4,5},{5,6},{6,7},{7,4},{8,9},{9,10},{10,1... | collective-permute-start | bytes 13832 | tf_op jit(solution)/shard_map/ppermute | solution.py:57
  47.4 1.3 %copy-start.3 = (f32[27,4,16,128]{3,2,1,0:T(8,128)S(1)}, f32[27,4,16,128]{3,2,1,0:T(8,128)}, u32[]{:S(2)}) copy-start(f32[27,4,16,128]{3,2,1,0:T(8,128)} %get-tuple-element.6.an_ref) | copy-start | bytes 2654212
  49.2 6.8 %collective-permute-start.6 = (f32[1,3,3,1,16,128]{5,4,2,1,3,0:T(8,128)S(1)}, f32[1,3,3,1,16,128]{5,4,2,1,3,0:T(8,128)S(1)}, u32[]{:S(2)}, u32[]{:S(2)}) collective-permute-start(f32[1,3,3,1,16,128]{5,4,2,1,3,0:T(8,128)S(1)} %slice_bitcast_fusion), channel_id=1, source_target_pairs={{0,120},{8,0},{16,8},{24,16},{32,24},{40,32},{48,40},{56,48},{64,5... | collective-permute-start | bytes 221192 | tf_op jit(solution)/shard_map/ppermute | solution.py:58
  54.2 2.5 %collective-permute-start.5 = (f32[1,3,3,1,16,128]{5,4,2,1,3,0:T(8,128)S(1)}, f32[1,3,3,1,16,128]{5,4,2,1,3,0:T(8,128)S(1)}, u32[]{:S(2)}, u32[]{:S(2)}) collective-permute-start(f32[1,3,3,1,16,128]{5,4,2,1,3,0:T(8,128)S(1)} %slice_bitcast_fusion.1), channel_id=1, source_target_pairs={{0,8},{8,16},{16,24},{24,32},{32,40},{40,48},{48,56},{56,64},{64,7... | collective-permute-start | bytes 221192 | tf_op jit(solution)/shard_map/ppermute | solution.py:57
  56.0 0.6 copy-start.4
  56.7 0.6 copy-start.5
  57.4 4.9 %collective-permute-start.7 = (f32[2,1,3,3,4,1,128]{6,4,3,2,5,1,0:T(4,128)S(1)}, f32[2,1,3,3,4,1,128]{6,4,3,2,5,1,0:T(4,128)S(1)}, u32[]{:S(2)}, u32[]{:S(2)}) collective-permute-start(f32[2,1,3,3,4,1,128]{6,4,3,2,5,1,0:T(4,128)S(1)} %pad_maximum_fusion.11), channel_id=1, source_target_pairs={{0,4},{4,0},{1,5},{5,1},{2,6},{6,2},{3,7},{7,3},{8,12},{12,8},{9,1... | collective-permute-start | bytes 110600 | tf_op jit(solution)/shard_map/ppermute | solution.py:55
  64.6 4.9 %collective-permute-start.8 = (f32[1,3,3,4,16,1]{4,3,2,1,5,0:T(4,128)S(1)}, f32[1,3,3,4,16,1]{4,3,2,1,5,0:T(4,128)S(1)}, u32[]{:S(2)}, u32[]{:S(2)}) collective-permute-start(f32[1,3,3,4,16,1]{4,3,2,1,5,0:T(4,128)S(1)} %fusion.9), channel_id=1, source_target_pairs={{0,1},{1,2},{2,3},{3,0},{4,5},{5,6},{6,7},{7,4},{8,9},{9,10},{10,1... | collective-permute-start | bytes 6920 | tf_op jit(solution)/shard_map/ppermute | solution.py:57
  64.8 3.6 %collective-permute-start.9 = (f32[1,3,3,4,16,1]{4,3,2,1,5,0:T(4,128)S(1)}, f32[1,3,3,4,16,1]{4,3,2,1,5,0:T(4,128)S(1)}, u32[]{:S(2)}, u32[]{:S(2)}) collective-permute-start(f32[1,3,3,4,16,1]{4,3,2,1,5,0:T(4,128)S(1)} %fusion.8), channel_id=1, source_target_pairs={{0,3},{1,0},{2,1},{3,2},{4,7},{5,4},{6,5},{7,6},{8,11},{9,8},{10,9... | collective-permute-start | bytes 6920 | tf_op jit(solution)/shard_map/ppermute | solution.py:58
  70.4 4.2 %copy-start.14 = (f32[4,16,128]{2,1,0:T(8,128)S(1)}, f32[4,16,128]{2,1,0:T(8,128)}, u32[]{:S(2)}) copy-start(f32[4,16,128]{2,1,0:T(8,128)} %get-tuple-element.8) | copy-start | bytes 98308

commit v4 on v3

--- a/solution.py
+++ b/solution.py
@@ -98,8 +98,8 @@
             col = shifted(c[..., z0 : z0 + 1], xlo[k][..., z0 : z0 + 1], xhi[k][..., z0 : z0 + 1], 0, s)
             col = shifted(col, ylo[k][..., z0 : z0 + 1], yhi[k][..., z0 : z0 + 1], 1, s)
             cols.append(col)
-        z_up.append(lax.index_in_dim(cols[0], 1 + s, axis=2, keepdims=False))
-        z_dn.append(lax.index_in_dim(cols[1], 1 - s, axis=2, keepdims=False))
+        z_up.append(jnp.swapaxes(lax.index_in_dim(cols[0], 1 + s, axis=2, keepdims=False)[..., 0], -1, -2))
+        z_dn.append(jnp.swapaxes(lax.index_in_dim(cols[1], 1 - s, axis=2, keepdims=False)[..., 0], -1, -2))
     zlo, zhi = halo_exchange(jnp.stack(z_up), jnp.stack(z_dn), "gz")
     out = []
     for k in range(len(cubes)):
@@ -109,8 +109,8 @@
                 xhi[k].reshape(9, sy, sz),
                 ylo[k].reshape(9, sx, sz),
                 yhi[k].reshape(9, sx, sz),
-                zlo[k].reshape(9, sx, sy, 1),
-                zhi[k].reshape(9, sx, sy, 1),
+                zlo[k].reshape(9, sy, sx),
+                zhi[k].reshape(9, sy, sx),
             )
         )
     return out
@@ -124,6 +124,10 @@
     for q in range(27):
         cx, cy, cz = (int(v) for v in STEPS[q])
         vx, vy, vz = sign * cx, sign * cy, sign * cz
+        if vz == 1:
+            zcol = zlo[(cx + 1) * 3 + cy + 1]
+        elif vz == -1:
+            zcol = zhi[(cx + 1) * 3 + cy + 1]
         for i in range(sx):
             j = i - vx
             if j < 0:
@@ -137,9 +141,9 @@
             elif vy == -1:
                 t = jnp.where(rows == sy - 1, yhi[(cx + 1) * 3 + cz + 1, pl.ds(i, 1), :], pltpu.roll(t, sy - 1, 0))
             if vz == 1:
-                t = jnp.where(lanes == 0, zlo[(cx + 1) * 3 + cy + 1, i], pltpu.roll(t, 1, 1))
+                t = jnp.where(lanes == 0, zcol[:, i : i + 1], pltpu.roll(t, 1, 1))
             elif vz == -1:
-                t = jnp.where(lanes == sz - 1, zhi[(cx + 1) * 3 + cy + 1, i], pltpu.roll(t, sz - 1, 1))
+                t = jnp.where(lanes == sz - 1, zcol[:, i : i + 1], pltpu.roll(t, sz - 1, 1))
             dst[q, i] = t
 
 

time: 100 us -> 98.5 us (0.985)
  local copies, waits for them, and re-layouts: 33.8 us -> 31 us
  waiting for transfers between devices: 4.61 us -> 5.81 us
    another operation x6 -> x0, local copies, waits for them, and re-layouts: 6 us -> none  [the longest x3 3.01 us: halos(): zlo[k].reshape(9, sx, sy, 1)]
    slice x2 -> x8, local copies, waits for them, and re-layouts: 0.01 us -> 3.05 us  [the longest x3 1.53 us: halos(): zlo[k].reshape(9, sy, sx)]
    ppermute x0 -> x2, local copies, waits for them, and re-layouts: none -> 1.5 us  [the longest x1 0.75 us: halo_exchange(): lo = lax.ppermute(up, axis, [(i, (i + 1) % size) for i in range(size)])]
    slice x15 -> x11, local copies, waits for them, and re-layouts: 3.71 us -> 2.42 us  [halos(): col = shifted(col, ylo[k][..., z0:z0 + 1], yhi[k][..., z0:z0 + 1], 1, s)]
    ppermute x4, waiting for transfers between devices: 1.41 us -> 2.64 us  [halo_exchange(): lo = lax.ppermute(up, axis, [(i, (i + 1) % size) for i in range(size)])]
  transfers between devices with their start and end apart: 10 -> 10, of which waited for: 5 -> 5; matrix products, arithmetic and copies ran while one was open for 14% -> 13% of each run, Pallas kernels for 0% -> 0%
where the time goes in v4:
time: 98.5 us; the launch traced here: 97.7 us
  local copies, waits for them, and re-layouts  31 us (31%)
  blocking collectives  22.7 us (23%)
  starting transfers between devices  20.3 us (21%)
  Pallas kernels  9.1 us (9%)
  other arithmetic  7.16 us (7%)
  waiting for transfers between devices  5.81 us (6%)
  between operations  1.53 us (2%)
    all_to_all x1, blocking collectives, shards(): lax.all_to_all(placed.reshape(devices, count // devices), ('gx', 'gy', 'g...  22.7 us
    unnamed x59, local copies, waits for them, and re-layouts  10.6 us
    ppermute x4, starting transfers between devices, halo_exchange(): hi = lax.ppermute(down, axis, [(i, (i - 1) % size) for i in range(size)])  10.3 us
    pallas_call x2, Pallas kernels, run_stage(): pl.pallas_call(kernel, out_shape=(jax.ShapeDtypeStruct(shape, jnp.float32...  9.1 us
    ppermute x2, starting transfers between devices, halo_exchange(): both = lax.ppermute(jnp.stack([up, down]), axis, [(0, 1), (1, 0)])  6.71 us
    slice x18, local copies, waits for them, and re-layouts, shifted(): lax.slice_in_dim(minus, 1, n, axis=2 + d)  3.62 us
    ppermute x4, starting transfers between devices, halo_exchange(): lo = lax.ppermute(up, axis, [(i, (i + 1) % size) for i in range(size)])  3.31 us
    ppermute x4, waiting for transfers between devices, halo_exchange(): lo = lax.ppermute(up, axis, [(i, (i + 1) % size) for i in range(size)])  2.64 us
  transfers between devices with their start and end apart: 10, of which 5 were waited for; matrix products, arithmetic and copies ran while one was open for 13% of the time, Pallas kernels for 0%

profile of v4, /device:TPU:1, one launch (start us, length us, event | category | flops | bytes accessed | tf_op | source)
XLA Modules:
  0.0 97.7 jit_solution(742975666617832807)
XLA Ops:
  0.6 1.2 %slice_reduce_fusion.6 = (f32[4,16,128]{2,1,0:T(8,128)S(1)}, f32[4,16,128]{2,1,0:T(8,128)S(1)}) fusion(f32[3,3,3,4,16,128]{5,4,3,2,1,0:T(8,128)} %bitcast.394), kind=kLoop, calls=%fused_computation.16 | loop fusion | flops 131072 | bytes 655360 | tf_op jit(solution)/shard_map/reduce_sum | solution.py:33
  1.8 1.1 %slice_reduce_fusion.4 = (f32[4,16,128]{2,1,0:T(8,128)S(1)}, f32[4,16,128]{2,1,0:T(8,128)S(1)}) fusion(f32[3,3,3,4,16,128]{5,4,3,2,1,0:T(8,128)} %bitcast.395), kind=kLoop, calls=%fused_computation.14 | loop fusion | flops 131072 | bytes 655360 | tf_op jit(solution)/shard_map/reduce_sum | solution.py:34
  3.0 0.9 slice.624
  4.1 0.6 copy-done.16
  5.0 0.6 gather_fusion
  6.0 0.7 copy-done.8
  6.8 0.7 copy-done.7
  7.5 1.4 %fusion.7.cf_ref = f32[27,4,16,128]{3,2,1,0:T(8,128)S(1)} fusion(f32[27,4,16,128]{3,2,1,0:T(8,128)S(1)} %copy-done, f32[4,16,128]{2,1,0:T(8,128)S(1)} %get-tuple-element.152.refs_13_.refs_7_, f32[4,16,128]{2,1,0:T(8,128)S(1)} %get-tuple-element.22, f32[4,16,128]{2,1,0:T(8,128)S(1)} %get-tuple-element.25, f32[27]{0:T(128)S(1)} %copy-done.18, ...), kind=kLoop, calls=%fused_computation.9 | loop fusion | flops 4202496 | bytes 2032048 | tf_op jit(solution)/shard_map/add | solution.py:47
  9.0 3.1 %collective-permute-start = (f32[2,3,3,1,16,128]{5,4,2,1,3,0:T(8,128)S(1)}, f32[2,3,3,1,16,128]{5,4,2,1,3,0:T(8,128)S(1)}, u32[]{:S(2)}, u32[]{:S(2)}) collective-permute-start(f32[2,3,3,1,16,128]{5,4,2,1,3,0:T(8,128)S(1)} %pad_maximum_fusion), channel_id=1, source_target_pairs={{0,8},{8,16},{16,24},{24,32},{32,40},{40,48},{48,56},{56,64},{64,7... | collective-permute-start | bytes 442376 | tf_op jit(solution)/shard_map/ppermute | solution.py:57
  12.3 0.7 fusion.24
  13.0 0.6 slice.830
  14.2 0.3 copy.750
  14.5 0.6 slice.900
  15.1 0.6 slice.870
  15.8 0.6 slice.818
  16.4 0.6 slice.834
  17.0 0.3 fusion.23
  17.3 0.3 copy.840
  17.6 0.3 copy.837
  17.9 0.3 copy.836
  18.5 0.3 copy.842
  18.8 0.3 copy.838
  19.1 0.7 fusion.30
  20.0 0.7 fusion.29
  21.5 0.7 copy-done.13
  22.4 0.7 copy-done.12
  23.5 0.7 copy-done.11
  24.2 0.7 copy-done.10
  24.9 0.7 copy-done.9
  25.8 3.4 %collective-permute-start.2 = (f32[2,2,3,3,4,1,128]{6,4,3,2,1,5,0:T(4,128)S(1)}, f32[2,2,3,3,4,1,128]{6,4,3,2,1,5,0:T(4,128)S(1)}, u32[]{:S(2)}, u32[]{:S(2)}) collective-permute-start(f32[2,2,3,3,4,1,128]{6,4,3,2,1,5,0:T(4,128)S(1)} %pad_maximum_fusion.2), channel_id=1, source_target_pairs={{0,4},{4,0},{1,5},{5,1},{2,6},{6,2},{3,7},{7,3},{8,12},{12,8},{9,1... | collective-permute-start | bytes 221192 | tf_op jit(solution)/shard_map/ppermute | solution.py:55
  29.7 1.3 %collective-permute-done.2 = f32[2,2,3,3,4,1,128]{6,4,3,2,1,5,0:T(4,128)S(1)} collective-permute-done((f32[2,2,3,3,4,1,128]{6,4,3,2,1,5,0:T(4,128)S(1)}, f32[2,2,3,3,4,1,128]{6,4,3,2,1,5,0:T(4,128)S(1)}, u32[]{:S(2)}, u32[]{:S(2)}) %collective-permute-start.2) | collective-permute-done | bytes 73760 | tf_op jit(solution)/shard_map/ppermute | solution.py:55
  30.9 0.7 fusion.33
  31.7 0.3 copy.763
  32.0 0.3 copy.744
  32.4 0.3 copy.762
  32.7 0.3 copy.743
  33.6 2.5 %collective-permute-start.4 = (f32[2,3,3,16,4]{3,4,2,1,0:T(4,128)S(1)}, f32[2,3,3,16,4]{3,4,2,1,0:T(4,128)S(1)}, u32[]{:S(2)}, u32[]{:S(2)}) collective-permute-start(f32[2,3,3,16,4]{3,4,2,1,0:T(4,128)S(1)} %pad_maximum_fusion.10), channel_id=1, source_target_pairs={{0,3},{1,0},{2,1},{3,2},{4,7},{5,4},{6,5},{7,6},{8,11},{9,8},{10,9... | collective-permute-start | bytes 13832 | tf_op jit(solution)/shard_map/ppermute | solution.py:58
  36.6 0.6 collective-permute-done.4
  37.2 0.8 copy.777
  38.0 2.6 %collective-permute-done.3 = f32[2,3,3,16,4]{3,4,2,1,0:T(4,128)S(1)} collective-permute-done((f32[2,3,3,16,4]{3,4,2,1,0:T(4,128)S(1)}, f32[2,3,3,16,4]{3,4,2,1,0:T(4,128)S(1)}, u32[]{:S(2)}, u32[]{:S(2)}) %collective-permute-start.3) | collective-permute-done | bytes 4640 | tf_op jit(solution)/shard_map/ppermute | solution.py:57
  40.6 0.8 copy.776
  41.4 0.7 copy.775
  42.1 0.8 copy.756
  42.9 4.9 %shard_map.122 = (f32[27,4,16,128]{3,2,1,0:T(8,128)}, f32[4,16,128]{2,1,0:T(8,128)}) custom-call(f32[27,4,16,128]{3,2,1,0:T(8,128)} %copy-done.1, f32[27,4,16,128]{3,2,1,0:T(8,128)} %ae_ref.1, f32[9,16,128]{2,1,0:T(8,128)} %bitcast.415, f32[9,16,128]{2,1,0:T(8,128)} %bitcast.417, f32[9,4,128]{2,1,0:T(4,128)} %bitcast.428, f32[9,4,128]{2,1,0:T(4,128)} %bitcast.427, ...), custom_call_target="tpu_custom_call" | custom-call | tf_op jit(solution)/shard_map/pallas_call | solution.py:243
  47.8 1.2 %fusion.22 = (f32[9,4,16,128]{3,2,1,0:T(8,128)S(1)}, f32[9,4,16,128]{3,2,1,0:T(8,128)S(1)}) fusion(f32[27,4,16,128]{3,2,1,0:T(8,128)} %get-tuple-element.6.an_ref), kind=kLoop, calls=%fused_computation.177 | loop fusion | bytes 1179648 | tf_op jit(solution)/shard_map/slice | solution.py:78
  49.2 0.3 fusion.20
  49.5 5.0 %collective-permute-start.6 = (f32[1,3,3,1,16,128]{5,4,2,1,3,0:T(8,128)S(1)}, f32[1,3,3,1,16,128]{5,4,2,1,3,0:T(8,128)S(1)}, u32[]{:S(2)}, u32[]{:S(2)}) collective-permute-start(f32[1,3,3,1,16,128]{5,4,2,1,3,0:T(8,128)S(1)} %slice_bitcast_fusion), channel_id=1, source_target_pairs={{0,120},{8,0},{16,8},{24,16},{32,24},{40,32},{48,40},{56,48},{64,5... | collective-permute-start | bytes 221192 | tf_op jit(solution)/shard_map/ppermute | solution.py:58
  54.9 0.3 copy.852
  55.2 0.3 copy.851
  55.5 0.3 copy.855
  55.7 0.3 copy.856
  56.5 0.5 copy-done.4
  57.1 0.5 copy-done.5
  57.8 3.3 %collective-permute-start.7 = (f32[2,1,3,3,4,1,128]{6,4,3,2,5,1,0:T(4,128)S(1)}, f32[2,1,3,3,4,1,128]{6,4,3,2,5,1,0:T(4,128)S(1)}, u32[]{:S(2)}, u32[]{:S(2)}) collective-permute-start(f32[2,1,3,3,4,1,128]{6,4,3,2,5,1,0:T(4,128)S(1)} %pad_maximum_fusion.11), channel_id=1, source_target_pairs={{0,4},{4,0},{1,5},{5,1},{2,6},{6,2},{3,7},{7,3},{8,12},{12,8},{9,1... | collective-permute-start | bytes 110600 | tf_op jit(solution)/shard_map/ppermute | solution.py:55
  62.0 0.5 collective-permute-done.7
  62.5 0.6 slice_bitcast_fusion.45
  63.7 2.7 %collective-permute-start.9 = (f32[1,3,3,16,4]{3,4,2,1,0:T(4,128)S(1)}, f32[1,3,3,16,4]{3,4,2,1,0:T(4,128)S(1)}, u32[]{:S(2)}, u32[]{:S(2)}) collective-permute-start(f32[1,3,3,16,4]{3,4,2,1,0:T(4,128)S(1)} %fusion.8), channel_id=1, source_target_pairs={{0,3},{1,0},{2,1},{3,2},{4,7},{5,4},{6,5},{7,6},{8,11},{9,8},{10,9... | collective-permute-start | bytes 6920 | tf_op jit(solution)/shard_map/ppermute | solution.py:58
  66.5 0.8 collective-permute-done.9
  67.3 0.7 copy.819
  68.0 0.8 copy.805
  68.8 4.2 %shard_map.123 = (f32[27,4,16,128]{3,2,1,0:T(8,128)}, f32[4,16,128]{2,1,0:T(8,128)}) custom-call(f32[27,4,16,128]{3,2,1,0:T(8,128)} %get-tuple-element.6.an_ref, f32[27,4,16,128]{3,2,1,0:T(8,128)} %f_ref.1, f32[9,16,128]{2,1,0:T(8,128)} %bitcast.407, f32[9,16,128]{2,1,0:T(8,128)} %bitcast.404, f32[9,4,128]{2,1,0:T(4,128)} %bitcast.464, ...), custom_call_target="tpu_custom_call" | custom-call | tf_op jit(solution)/shard_map/pallas_call | solution.py:243
  73.0 0.8 add_multiply_fusion
  74.3 22.7 %all_to_all.9 = f32[128,1,8]{2,1,0:T(1,128)S(1)} all-to-all(f32[128,1,8]{2,1,0:T(1,128)S(1)} %bitcast.424), channel_id=1, replica_groups=mesh['gx'=16,'gy'=2,'gz'=4] {'gx','gy','gz'}, dimensions={0} | all-to-all | bytes 8192 | tf_op jit(solution)/shard_map/all_to_all | solution.py:277
  97.0 0.7 reduce_sum.109
  (197 shorter events, 8.5 us)
Async XLA Ops:
  0.6 2.3 %copy-start = (f32[27,4,16,128]{3,2,1,0:T(8,128)S(1)}, f32[27,4,16,128]{3,2,1,0:T(8,128)}, u32[]{:S(2)}) copy-start(f32[27,4,16,128]{3,2,1,0:T(8,128)} %f_ref.1) | copy-start | bytes 2654212
  2.9 1.1 %copy-start.15 = (s32[1024]{0:T(1024)S(1)}, s32[1024]{0:T(1024)}, u32[]{:S(2)}) copy-start(s32[1024]{0:T(1024)} %param.17) | copy-start | bytes 12292
  3.0 2.9 %copy-start.2 = (f32[27,4,16,128]{3,2,1,0:T(8,128)S(1)}, f32[27,4,16,128]{3,2,1,0:T(8,128)}, u32[]{:S(2)}) copy-start(f32[27,4,16,128]{3,2,1,0:T(8,128)} %ae_ref.1) | copy-start | bytes 2654212
  4.0 0.7 copy-start.16
  5.9 0.8 copy-start.8
  6.7 0.8 copy-start.7
  6.7 0.8 copy-start.20
  6.7 2.1 %copy-start.6 = (f32[4,16,128]{2,1,0:T(8,128)}, f32[4,16,128]{2,1,0:T(8,128)S(1)}, u32[]{:S(2)}) copy-start(f32[4,16,128]{2,1,0:T(8,128)S(1)} %get-tuple-element.152.refs_13_.refs_7_) | copy-start | bytes 98308
  6.7 0.7 copy-start.17
  6.8 0.7 copy-start.18
  6.8 0.7 copy-start.19
  8.9 8.1 %copy-start.1 = (f32[27,4,16,128]{3,2,1,0:T(8,128)}, f32[27,4,16,128]{3,2,1,0:T(8,128)S(1)}, u32[]{:S(2)}) copy-start(f32[27,4,16,128]{3,2,1,0:T(8,128)S(1)} %fusion.7.cf_ref) | copy-start | bytes 2654212
  9.0 10.1 %collective-permute-start = (f32[2,3,3,1,16,128]{5,4,2,1,3,0:T(8,128)S(1)}, f32[2,3,3,1,16,128]{5,4,2,1,3,0:T(8,128)S(1)}, u32[]{:S(2)}, u32[]{:S(2)}) collective-permute-start(f32[2,3,3,1,16,128]{5,4,2,1,3,0:T(8,128)S(1)} %pad_maximum_fusion), channel_id=1, source_target_pairs={{0,8},{8,16},{16,24},{24,32},{32,40},{40,48},{48,56},{56,64},{64,7... | collective-permute-start | bytes 442376 | tf_op jit(solution)/shard_map/ppermute | solution.py:57
  12.1 7.9 %collective-permute-start.1 = (f32[2,3,3,1,16,128]{5,4,2,1,3,0:T(8,128)S(1)}, f32[2,3,3,1,16,128]{5,4,2,1,3,0:T(8,128)S(1)}, u32[]{:S(2)}, u32[]{:S(2)}) collective-permute-start(f32[2,3,3,1,16,128]{5,4,2,1,3,0:T(8,128)S(1)} %pad_maximum_fusion.1), channel_id=1, source_target_pairs={{0,120},{8,0},{16,8},{24,16},{32,24},{40,32},{48,40},{56,48},{64,5... | collective-permute-start | bytes 442376 | tf_op jit(solution)/shard_map/ppermute | solution.py:58
  21.5 0.7 copy-start.13
  22.4 0.7 copy-start.12
  23.5 0.7 copy-start.11
  24.2 0.7 copy-start.10
  24.9 0.7 copy-start.9
  25.8 5.1 %collective-permute-start.2 = (f32[2,2,3,3,4,1,128]{6,4,3,2,1,5,0:T(4,128)S(1)}, f32[2,2,3,3,4,1,128]{6,4,3,2,1,5,0:T(4,128)S(1)}, u32[]{:S(2)}, u32[]{:S(2)}) collective-permute-start(f32[2,2,3,3,4,1,128]{6,4,3,2,1,5,0:T(4,128)S(1)} %pad_maximum_fusion.2), channel_id=1, source_target_pairs={{0,4},{4,0},{1,5},{5,1},{2,6},{6,2},{3,7},{7,3},{8,12},{12,8},{9,1... | collective-permute-start | bytes 221192 | tf_op jit(solution)/shard_map/ppermute | solution.py:55
  33.6 3.6 %collective-permute-start.4 = (f32[2,3,3,16,4]{3,4,2,1,0:T(4,128)S(1)}, f32[2,3,3,16,4]{3,4,2,1,0:T(4,128)S(1)}, u32[]{:S(2)}, u32[]{:S(2)}) collective-permute-start(f32[2,3,3,16,4]{3,4,2,1,0:T(4,128)S(1)} %pad_maximum_fusion.10), channel_id=1, source_target_pairs={{0,3},{1,0},{2,1},{3,2},{4,7},{5,4},{6,5},{7,6},{8,11},{9,8},{10,9... | collective-permute-start | bytes 13832 | tf_op jit(solution)/shard_map/ppermute | solution.py:58
  36.5 4.1 %collective-permute-start.3 = (f32[2,3,3,16,4]{3,4,2,1,0:T(4,128)S(1)}, f32[2,3,3,16,4]{3,4,2,1,0:T(4,128)S(1)}, u32[]{:S(2)}, u32[]{:S(2)}) collective-permute-start(f32[2,3,3,16,4]{3,4,2,1,0:T(4,128)S(1)} %pad_maximum_fusion.9), channel_id=1, source_target_pairs={{0,1},{1,2},{2,3},{3,0},{4,5},{5,6},{6,7},{7,4},{8,9},{9,10},{10,1... | collective-permute-start | bytes 13832 | tf_op jit(solution)/shard_map/ppermute | solution.py:57
  47.8 1.3 %copy-start.3 = (f32[27,4,16,128]{3,2,1,0:T(8,128)S(1)}, f32[27,4,16,128]{3,2,1,0:T(8,128)}, u32[]{:S(2)}) copy-start(f32[27,4,16,128]{3,2,1,0:T(8,128)} %get-tuple-element.6.an_ref) | copy-start | bytes 2654212
  49.5 6.8 %collective-permute-start.6 = (f32[1,3,3,1,16,128]{5,4,2,1,3,0:T(8,128)S(1)}, f32[1,3,3,1,16,128]{5,4,2,1,3,0:T(8,128)S(1)}, u32[]{:S(2)}, u32[]{:S(2)}) collective-permute-start(f32[1,3,3,1,16,128]{5,4,2,1,3,0:T(8,128)S(1)} %slice_bitcast_fusion), channel_id=1, source_target_pairs={{0,120},{8,0},{16,8},{24,16},{32,24},{40,32},{48,40},{56,48},{64,5... | collective-permute-start | bytes 221192 | tf_op jit(solution)/shard_map/ppermute | solution.py:58
  54.5 2.5 %collective-permute-start.5 = (f32[1,3,3,1,16,128]{5,4,2,1,3,0:T(8,128)S(1)}, f32[1,3,3,1,16,128]{5,4,2,1,3,0:T(8,128)S(1)}, u32[]{:S(2)}, u32[]{:S(2)}) collective-permute-start(f32[1,3,3,1,16,128]{5,4,2,1,3,0:T(8,128)S(1)} %slice_bitcast_fusion.1), channel_id=1, source_target_pairs={{0,8},{8,16},{16,24},{24,32},{32,40},{40,48},{48,56},{56,64},{64,7... | collective-permute-start | bytes 221192 | tf_op jit(solution)/shard_map/ppermute | solution.py:57
  56.4 0.6 copy-start.4
  57.0 0.6 copy-start.5
  57.8 4.7 %collective-permute-start.7 = (f32[2,1,3,3,4,1,128]{6,4,3,2,5,1,0:T(4,128)S(1)}, f32[2,1,3,3,4,1,128]{6,4,3,2,5,1,0:T(4,128)S(1)}, u32[]{:S(2)}, u32[]{:S(2)}) collective-permute-start(f32[2,1,3,3,4,1,128]{6,4,3,2,5,1,0:T(4,128)S(1)} %pad_maximum_fusion.11), channel_id=1, source_target_pairs={{0,4},{4,0},{1,5},{5,1},{2,6},{6,2},{3,7},{7,3},{8,12},{12,8},{9,1... | collective-permute-start | bytes 110600 | tf_op jit(solution)/shard_map/ppermute | solution.py:55
  63.4 4.6 %collective-permute-start.8 = (f32[1,3,3,16,4]{3,4,2,1,0:T(4,128)S(1)}, f32[1,3,3,16,4]{3,4,2,1,0:T(4,128)S(1)}, u32[]{:S(2)}, u32[]{:S(2)}) collective-permute-start(f32[1,3,3,16,4]{3,4,2,1,0:T(4,128)S(1)} %fusion.9), channel_id=1, source_target_pairs={{0,1},{1,2},{2,3},{3,0},{4,5},{5,6},{6,7},{7,4},{8,9},{9,10},{10,1... | collective-permute-start | bytes 6920 | tf_op jit(solution)/shard_map/ppermute | solution.py:57
  63.7 3.6 %collective-permute-start.9 = (f32[1,3,3,16,4]{3,4,2,1,0:T(4,128)S(1)}, f32[1,3,3,16,4]{3,4,2,1,0:T(4,128)S(1)}, u32[]{:S(2)}, u32[]{:S(2)}) collective-permute-start(f32[1,3,3,16,4]{3,4,2,1,0:T(4,128)S(1)} %fusion.8), channel_id=1, source_target_pairs={{0,3},{1,0},{2,1},{3,2},{4,7},{5,4},{6,5},{7,6},{8,11},{9,8},{10,9... | collective-permute-start | bytes 6920 | tf_op jit(solution)/shard_map/ppermute | solution.py:58
  68.8 4.2 %copy-start.14 = (f32[4,16,128]{2,1,0:T(8,128)S(1)}, f32[4,16,128]{2,1,0:T(8,128)}, u32[]{:S(2)}) copy-start(f32[4,16,128]{2,1,0:T(8,128)} %get-tuple-element.8) | copy-start | bytes 98308

commit v5 on v4

--- a/solution.py
+++ b/solution.py
@@ -84,22 +84,26 @@
     sx, sy, sz = cubes[0].shape[3:]
     x_up, x_dn = zip(*[faces(c, s, 0) for c, s in zip(cubes, signs)])
     xlo, xhi = halo_exchange(jnp.stack(x_up), jnp.stack(x_dn), "gx")
+    both = jnp.stack(cubes)
+    rows = jnp.concatenate([both[..., sy - 1 : sy, :], both[..., 0:1, :]], axis=5)
+    cols = jnp.concatenate([both[..., sz - 1 : sz], both[..., 0:1]], axis=6)
     y_up, y_dn = [], []
-    for k, (c, s) in enumerate(zip(cubes, signs)):
-        top = shifted(c[:, :, :, :, sy - 1 : sy], xlo[k][:, :, :, sy - 1 : sy], xhi[k][:, :, :, sy - 1 : sy], 0, s)
-        bot = shifted(c[:, :, :, :, 0:1], xlo[k][:, :, :, 0:1], xhi[k][:, :, :, 0:1], 0, s)
+    for k, s in enumerate(signs):
+        top = shifted(rows[k][..., 0:1, :], xlo[k][:, :, :, sy - 1 : sy], xhi[k][:, :, :, sy - 1 : sy], 0, s)
+        bot = shifted(rows[k][..., 1:2, :], xlo[k][:, :, :, 0:1], xhi[k][:, :, :, 0:1], 0, s)
         y_up.append(lax.index_in_dim(top, 1 + s, axis=1, keepdims=False))
         y_dn.append(lax.index_in_dim(bot, 1 - s, axis=1, keepdims=False))
     ylo, yhi = halo_exchange(jnp.stack(y_up), jnp.stack(y_dn), "gy")
     z_up, z_dn = [], []
-    for k, (c, s) in enumerate(zip(cubes, signs)):
-        cols = []
-        for z0 in (sz - 1, 0):
-            col = shifted(c[..., z0 : z0 + 1], xlo[k][..., z0 : z0 + 1], xhi[k][..., z0 : z0 + 1], 0, s)
+    for k, s in enumerate(signs):
+        picked = []
+        for at, z0 in ((0, sz - 1), (1, 0)):
+            col = cols[k][..., at : at + 1]
+            col = shifted(col, xlo[k][..., z0 : z0 + 1], xhi[k][..., z0 : z0 + 1], 0, s)
             col = shifted(col, ylo[k][..., z0 : z0 + 1], yhi[k][..., z0 : z0 + 1], 1, s)
-            cols.append(col)
-        z_up.append(jnp.swapaxes(lax.index_in_dim(cols[0], 1 + s, axis=2, keepdims=False)[..., 0], -1, -2))
-        z_dn.append(jnp.swapaxes(lax.index_in_dim(cols[1], 1 - s, axis=2, keepdims=False)[..., 0], -1, -2))
+            picked.append(col)
+        z_up.append(jnp.swapaxes(lax.index_in_dim(picked[0], 1 + s, axis=2, keepdims=False)[..., 0], -1, -2))
+        z_dn.append(jnp.swapaxes(lax.index_in_dim(picked[1], 1 - s, axis=2, keepdims=False)[..., 0], -1, -2))
     zlo, zhi = halo_exchange(jnp.stack(z_up), jnp.stack(z_dn), "gz")
     out = []
     for k in range(len(cubes)):

time: 98.5 us -> 92.4 us (0.938)
  local copies, waits for them, and re-layouts: 31 us -> 21.7 us
  other arithmetic: 7.16 us -> 12.5 us
  blocking collectives: 22.7 us -> 20.1 us
  waiting for transfers between devices: 5.81 us -> 8.01 us
  starting transfers between devices: 20.3 us -> 18.8 us
    unnamed x59 -> x51, local copies, waits for them, and re-layouts: 10.6 us -> 2.18 us
    ppermute x4, starting transfers between devices: 10.3 us -> 6.96 us  [halo_exchange(): hi = lax.ppermute(down, axis, [(i, (i - 1) % size) for i in range(size)])]
    slice x18, local copies, waits for them, and re-layouts: 3.62 us -> 0.55 us  [shifted(): lax.slice_in_dim(minus, 1, n, axis=2 + d)]
    all_to_all x1, blocking collectives: 22.7 us -> 20.1 us  [shards(): lax.all_to_all(placed.reshape(devices, count // devices), ('gx', 'gy', 'g...]
    slice x23, local copies, waits for them, and re-layouts: 3.57 us -> 5.61 us  [the longest x3 3.63 us: halos(): cols = jnp.concatenate([both[..., sz - 1:sz], both[..., 0:1]], axis=6)]
    another operation x0 -> x1, other arithmetic: none -> 1.83 us  [halos(): both = jnp.stack(cubes)]
    ppermute x4, starting transfers between devices: 3.31 us -> 5.03 us  [halo_exchange(): lo = lax.ppermute(up, axis, [(i, (i + 1) % size) for i in range(size)])]
    ppermute x4, waiting for transfers between devices: 1.41 us -> 2.87 us  [halo_exchange(): hi = lax.ppermute(down, axis, [(i, (i - 1) % size) for i in range(size)])]
  transfers between devices with their start and end apart: 10 -> 10, of which waited for: 5 -> 8; matrix products, arithmetic and copies ran while one was open for 13% -> 15% of each run, Pallas kernels for 0% -> 0%
where the time goes in v5:
time: 92.4 us; the launch traced here: 91.9 us
  local copies, waits for them, and re-layouts  21.7 us (23%)
  blocking collectives  20.1 us (22%)
  starting transfers between devices  18.8 us (20%)
  other arithmetic  12.5 us (14%)
  Pallas kernels  9.11 us (10%)
  waiting for transfers between devices  8.01 us (9%)
  between operations  1.7 us (2%)
    all_to_all x1, blocking collectives, shards(): lax.all_to_all(placed.reshape(devices, count // devices), ('gx', 'gy', 'g...  20.1 us
    pallas_call x2, Pallas kernels, run_stage(): pl.pallas_call(kernel, out_shape=(jax.ShapeDtypeStruct(shape, jnp.float32...  9.11 us
    ppermute x4, starting transfers between devices, halo_exchange(): hi = lax.ppermute(down, axis, [(i, (i - 1) % size) for i in range(size)])  6.96 us
    ppermute x2, starting transfers between devices, halo_exchange(): both = lax.ppermute(jnp.stack([up, down]), axis, [(0, 1), (1, 0)])  6.77 us
    ppermute x4, starting transfers between devices, halo_exchange(): lo = lax.ppermute(up, axis, [(i, (i + 1) % size) for i in range(size)])  5.03 us
    ppermute x4, waiting for transfers between devices, halo_exchange(): lo = lax.ppermute(up, axis, [(i, (i + 1) % size) for i in range(size)])  3.87 us
    slice x3, local copies, waits for them, and re-layouts, halos(): cols = jnp.concatenate([both[..., sz - 1:sz], both[..., 0:1]], axis=6)  3.63 us
    ppermute x4, waiting for transfers between devices, halo_exchange(): hi = lax.ppermute(down, axis, [(i, (i - 1) % size) for i in range(size)])  2.87 us
  transfers between devices with their start and end apart: 10, of which 8 were waited for; matrix products, arithmetic and copies ran while one was open for 15% of the time, Pallas kernels for 0%

profile of v5, /device:TPU:1, one launch (start us, length us, event | category | flops | bytes accessed | tf_op | source)
XLA Modules:
  0.0 91.9 jit_solution(10424371059383929221)
XLA Ops:
  0.7 1.2 %slice_reduce_fusion.2 = (f32[4,16,128]{2,1,0:T(8,128)S(1)}, f32[4,16,128]{2,1,0:T(8,128)S(1)}) fusion(f32[3,3,3,4,16,128]{5,4,3,2,1,0:T(8,128)} %bitcast.432), kind=kLoop, calls=%fused_computation.14 | loop fusion | flops 131072 | bytes 655360 | tf_op jit(solution)/shard_map/reduce_sum | solution.py:33
  1.9 1.1 %slice_reduce_fusion = (f32[4,16,128]{2,1,0:T(8,128)S(1)}, f32[4,16,128]{2,1,0:T(8,128)S(1)}) fusion(f32[3,3,3,4,16,128]{5,4,3,2,1,0:T(8,128)} %bitcast.433), kind=kLoop, calls=%fused_computation.12 | loop fusion | flops 131072 | bytes 655360 | tf_op jit(solution)/shard_map/reduce_sum | solution.py:34
  3.0 1.1 %slice_reduce_fusion.4 = (f32[4,16,128]{2,1,0:T(8,128)S(1)}, f32[4,16,128]{2,1,0:T(8,128)S(1)}) fusion(f32[27,4,16,128]{3,2,1,0:T(8,128)} %f_ref.1), kind=kLoop, calls=%fused_computation.16 | loop fusion | flops 131072 | bytes 655360 | tf_op jit(solution)/shard_map/reduce_sum | solution.py:32
  4.2 0.2 copy.1192
  4.4 0.8 slice.664
  5.3 0.6 gather_fusion
  5.9 0.1 copy.1295
  6.4 1.4 %fusion.7.cf_ref = f32[27,4,16,128]{3,2,1,0:T(8,128)S(1)} fusion(f32[27,4,16,128]{3,2,1,0:T(8,128)S(1)} %copy-done, f32[4,16,128]{2,1,0:T(8,128)S(1)} %get-tuple-element.158.refs_13_.refs_7_, f32[4,16,128]{2,1,0:T(8,128)S(1)} %get-tuple-element.18, f32[4,16,128]{2,1,0:T(8,128)S(1)} %get-tuple-element.21, f32[27]{0:T(128)S(1)} %copy-done.18, ...), kind=kLoop, calls=%fused_computation.11 | loop fusion | flops 4202496 | bytes 2032048 | tf_op jit(solution)/shard_map/add | solution.py:47
  8.0 0.8 pad_maximum_fusion.4
  8.7 1.4 %collective-permute-start.1 = (f32[2,3,3,1,16,128]{5,4,2,1,3,0:T(8,128)}, f32[2,3,3,1,16,128]{5,4,2,1,3,0:T(8,128)}, u32[]{:S(2)}, u32[]{:S(2)}) collective-permute-start(f32[2,3,3,1,16,128]{5,4,2,1,3,0:T(8,128)} %pad_maximum_fusion.4), channel_id=1, source_target_pairs={{0,120},{8,0},{16,8},{24,16},{32,24},{40,32},{48,40},{56,48},{64,5... | collective-permute-start | bytes 442376 | tf_op jit(solution)/shard_map/ppermute | solution.py:58
  10.1 0.7 pad_maximum_fusion.3
  10.8 1.6 %collective-permute-start = (f32[2,3,3,1,16,128]{5,4,2,1,3,0:T(8,128)}, f32[2,3,3,1,16,128]{5,4,2,1,3,0:T(8,128)}, u32[]{:S(2)}, u32[]{:S(2)}) collective-permute-start(f32[2,3,3,1,16,128]{5,4,2,1,3,0:T(8,128)} %pad_maximum_fusion.3), channel_id=1, source_target_pairs={{0,8},{8,16},{16,24},{24,32},{32,40},{40,48},{48,56},{56,64},{64,7... | collective-permute-start | bytes 442376 | tf_op jit(solution)/shard_map/ppermute | solution.py:57
  12.5 1.8 %slice_maximum_fusion = (f32[2,3,3,3,4,16,1]{6,5,4,3,2,1,0:T(8,128)S(1)}, f32[2,3,3,3,4,16,1]{6,5,4,3,2,1,0:T(8,128)}) fusion(f32[1,3,3,3,4,16,128]{6,5,4,3,2,1,0:T(8,128)S(1)} %bitcast.438, f32[1,3,3,3,4,16,128]{6,5,4,3,2,1,0:T(8,128)S(1)} %bitcast.434), kind=kLoop, calls=%fused_computation.2 | loop fusion | flops 6912 | bytes 1797120 | tf_op jit(solution)/shard_map/stack | solution.py:87
  14.3 0.8 fusion.8
  15.1 2.0 %copy.1216 = f32[2,3,3,3,4,16,1]{5,4,6,3,2,1,0:T(4,128)} copy(f32[2,3,3,3,4,16,1]{6,5,4,3,2,1,0:T(8,128)S(1)} %get-tuple-element.22) | data formatting | bytes 27648 | tf_op jit(solution)/shard_map/slice | solution.py:89
  17.1 1.3 %copy.1217 = f32[2,3,3,3,4,16,1]{5,4,6,3,2,1,0:T(4,128)S(1)} copy(f32[2,3,3,3,4,16,1]{6,5,4,3,2,1,0:T(8,128)S(1)} %copy-done.4) | data formatting | bytes 27648 | tf_op jit(solution)/shard_map/slice | solution.py:89
  19.3 1.6 %fusion.29 = (f32[1,3,3,1,16,128]{5,4,2,1,3,0:T(8,128)}, f32[3,3,1,16,128]{4,3,1,0,2:T(8,128)S(1)}, f32[3,3,1,16,128]{4,3,1,0,2:T(8,128)S(1)}, f32[1,3,3,1,16,128]{5,4,2,1,3,0:T(8,128)}) fusion(f32[2,3,3,1,16,128]{5,4,2,1,3,0:T(8,128)} %collective-permute-done.1), kind=kLoop, calls=%fused_computation.219 | loop fusion | bytes 442368 | tf_op jit(solution)/shard_map/slice | solution.py:92
  21.0 1.6 %fusion.30 = (f32[1,3,3,1,16,128]{5,4,2,1,3,0:T(8,128)}, f32[3,3,1,16,128]{4,3,1,0,2:T(8,128)S(1)}, f32[3,3,1,16,128]{4,3,1,0,2:T(8,128)S(1)}, f32[1,3,3,1,16,128]{5,4,2,1,3,0:T(8,128)}) fusion(f32[2,3,3,1,16,128]{5,4,2,1,3,0:T(8,128)} %collective-permute-done), kind=kLoop, calls=%fused_computation.220 | loop fusion | bytes 442368 | tf_op jit(solution)/shard_map/slice | solution.py:92
  22.9 0.1 copy.1235
  23.0 0.1 copy.1236
  23.6 3.4 %collective-permute-start.2 = (f32[2,2,3,3,4,1,128]{6,4,3,2,1,5,0:T(4,128)S(1)}, f32[2,2,3,3,4,1,128]{6,4,3,2,1,5,0:T(4,128)S(1)}, u32[]{:S(2)}, u32[]{:S(2)}) collective-permute-start(f32[2,2,3,3,4,1,128]{6,4,3,2,1,5,0:T(4,128)S(1)} %pad_maximum_fusion.6), channel_id=1, source_target_pairs={{0,4},{4,0},{1,5},{5,1},{2,6},{6,2},{3,7},{7,3},{8,12},{12,8},{9,1... | collective-permute-start | bytes 221192 | tf_op jit(solution)/shard_map/ppermute | solution.py:55
  26.9 0.1 copy.1243
  27.0 0.1 copy.1244
  27.3 0.1 copy.1218
  27.4 0.1 copy.1219
  27.6 0.1 copy.1226
  27.7 0.1 copy.1227
  28.3 0.4 collective-permute-done.2
  28.7 0.6 fusion.34
  30.0 2.5 %collective-permute-start.4 = (f32[2,3,3,16,4]{3,4,2,1,0:T(4,128)S(1)}, f32[2,3,3,16,4]{3,4,2,1,0:T(4,128)S(1)}, u32[]{:S(2)}, u32[]{:S(2)}) collective-permute-start(f32[2,3,3,16,4]{3,4,2,1,0:T(4,128)S(1)} %pad_maximum_fusion.14), channel_id=1, source_target_pairs={{0,3},{1,0},{2,1},{3,2},{4,7},{5,4},{6,5},{7,6},{8,11},{9,8},{10,9... | collective-permute-start | bytes 13832 | tf_op jit(solution)/shard_map/ppermute | solution.py:58
  33.0 0.6 collective-permute-done.4
  33.6 0.8 copy.1251
  34.4 0.8 copy.1253
  35.2 1.9 %collective-permute-done.3 = f32[2,3,3,16,4]{3,4,2,1,0:T(4,128)S(1)} collective-permute-done((f32[2,3,3,16,4]{3,4,2,1,0:T(4,128)S(1)}, f32[2,3,3,16,4]{3,4,2,1,0:T(4,128)S(1)}, u32[]{:S(2)}, u32[]{:S(2)}) %collective-permute-start.3) | collective-permute-done | bytes 4640 | tf_op jit(solution)/shard_map/ppermute | solution.py:57
  37.0 0.8 copy.1252
  37.8 0.8 copy.1234
  38.6 4.9 %shard_map.122 = (f32[27,4,16,128]{3,2,1,0:T(8,128)}, f32[4,16,128]{2,1,0:T(8,128)}) custom-call(f32[27,4,16,128]{3,2,1,0:T(8,128)} %copy-done.1, f32[27,4,16,128]{3,2,1,0:T(8,128)} %ae_ref.1, f32[9,16,128]{2,1,0:T(8,128)} %bitcast.456, f32[9,16,128]{2,1,0:T(8,128)} %bitcast.454, f32[9,4,128]{2,1,0:T(4,128)} %bitcast.469, f32[9,4,128]{2,1,0:T(4,128)} %bitcast.468, ...), custom_call_target="tpu_custom_call" | custom-call | tf_op jit(solution)/shard_map/pallas_call | solution.py:247
  43.4 1.2 %fusion.25 = (f32[9,4,16,128]{3,2,1,0:T(8,128)S(1)}, f32[9,4,16,128]{3,2,1,0:T(8,128)S(1)}) fusion(f32[27,4,16,128]{3,2,1,0:T(8,128)} %get-tuple-element.6.an_ref), kind=kLoop, calls=%fused_computation.215 | loop fusion | bytes 1179648 | tf_op jit(solution)/shard_map/slice | solution.py:78
  44.6 0.2 copy-done.2
  44.8 0.3 fusion.23
  45.2 0.7 copy.1314
  45.9 0.7 copy.1315
  46.7 2.8 %collective-permute-start.5 = (f32[1,3,3,1,16,128]{5,4,2,1,3,0:T(8,128)S(1)}, f32[1,3,3,1,16,128]{5,4,2,1,3,0:T(8,128)S(1)}, u32[]{:S(2)}, u32[]{:S(2)}) collective-permute-start(f32[1,3,3,1,16,128]{5,4,2,1,3,0:T(8,128)S(1)} %slice_bitcast_fusion.2), channel_id=1, source_target_pairs={{0,8},{8,16},{16,24},{24,32},{32,40},{40,48},{48,56},{56,64},{64,7... | collective-permute-start | bytes 221192 | tf_op jit(solution)/shard_map/ppermute | solution.py:57
  49.5 1.9 %collective-permute-start.6 = (f32[1,3,3,1,16,128]{5,4,2,1,3,0:T(8,128)S(1)}, f32[1,3,3,1,16,128]{5,4,2,1,3,0:T(8,128)S(1)}, u32[]{:S(2)}, u32[]{:S(2)}) collective-permute-start(f32[1,3,3,1,16,128]{5,4,2,1,3,0:T(8,128)S(1)} %slice_bitcast_fusion.1), channel_id=1, source_target_pairs={{0,120},{8,0},{16,8},{24,16},{32,24},{40,32},{48,40},{56,48},{64,5... | collective-permute-start | bytes 221192 | tf_op jit(solution)/shard_map/ppermute | solution.py:58
  51.6 0.5 collective-permute-done.5
  52.2 1.2 %collective-permute-done.6 = f32[1,3,3,1,16,128]{5,4,2,1,3,0:T(8,128)S(1)} collective-permute-done((f32[1,3,3,1,16,128]{5,4,2,1,3,0:T(8,128)S(1)}, f32[1,3,3,1,16,128]{5,4,2,1,3,0:T(8,128)S(1)}, u32[]{:S(2)}, u32[]{:S(2)}) %collective-permute-start.6) | collective-permute-done | bytes 73760 | tf_op jit(solution)/shard_map/ppermute | solution.py:58
  53.5 0.1 copy.1279
  53.6 0.1 copy.1282
  54.0 3.4 %collective-permute-start.7 = (f32[2,1,3,3,4,1,128]{6,4,3,2,5,1,0:T(4,128)S(1)}, f32[2,1,3,3,4,1,128]{6,4,3,2,5,1,0:T(4,128)S(1)}, u32[]{:S(2)}, u32[]{:S(2)}) collective-permute-start(f32[2,1,3,3,4,1,128]{6,4,3,2,5,1,0:T(4,128)S(1)} %pad_maximum_fusion.15), channel_id=1, source_target_pairs={{0,4},{4,0},{1,5},{5,1},{2,6},{6,2},{3,7},{7,3},{8,12},{12,8},{9,1... | collective-permute-start | bytes 110600 | tf_op jit(solution)/shard_map/ppermute | solution.py:55
  57.4 0.1 copy.1266
  57.5 0.1 copy.1269
  57.8 0.9 collective-permute-done.7
  58.7 0.6 slice_bitcast_fusion.74
  59.7 1.1 %collective-permute-start.9 = (f32[1,3,3,16,4]{3,4,2,1,0:T(4,128)S(1)}, f32[1,3,3,16,4]{3,4,2,1,0:T(4,128)S(1)}, u32[]{:S(2)}, u32[]{:S(2)}) collective-permute-start(f32[1,3,3,16,4]{3,4,2,1,0:T(4,128)S(1)} %fusion.12), channel_id=1, source_target_pairs={{0,3},{1,0},{2,1},{3,2},{4,7},{5,4},{6,5},{7,6},{8,11},{9,8},{10,9... | collective-permute-start | bytes 6920 | tf_op jit(solution)/shard_map/ppermute | solution.py:58
  60.9 0.5 collective-permute-start.8
  61.5 1.1 %collective-permute-done.9 = f32[1,3,3,16,4]{3,4,2,1,0:T(4,128)S(1)} collective-permute-done((f32[1,3,3,16,4]{3,4,2,1,0:T(4,128)S(1)}, f32[1,3,3,16,4]{3,4,2,1,0:T(4,128)S(1)}, u32[]{:S(2)}, u32[]{:S(2)}) %collective-permute-start.9) | collective-permute-done | bytes 2336 | tf_op jit(solution)/shard_map/ppermute | solution.py:58
  62.6 0.7 copy.1291
  63.4 1.4 %collective-permute-done.8 = f32[1,3,3,16,4]{3,4,2,1,0:T(4,128)S(1)} collective-permute-done((f32[1,3,3,16,4]{3,4,2,1,0:T(4,128)S(1)}, f32[1,3,3,16,4]{3,4,2,1,0:T(4,128)S(1)}, u32[]{:S(2)}, u32[]{:S(2)}) %collective-permute-start.8) | collective-permute-done | bytes 2336 | tf_op jit(solution)/shard_map/ppermute | solution.py:57
  64.8 0.8 copy.1278
  65.6 4.2 %shard_map.123 = (f32[27,4,16,128]{3,2,1,0:T(8,128)}, f32[4,16,128]{2,1,0:T(8,128)}) custom-call(f32[27,4,16,128]{3,2,1,0:T(8,128)} %get-tuple-element.6.an_ref, f32[27,4,16,128]{3,2,1,0:T(8,128)} %f_ref.1, f32[9,16,128]{2,1,0:T(8,128)} %bitcast.442, f32[9,16,128]{2,1,0:T(8,128)} %bitcast.445, f32[9,4,128]{2,1,0:T(4,128)} %bitcast.491, ...), custom_call_target="tpu_custom_call" | custom-call | tf_op jit(solution)/shard_map/pallas_call | solution.py:247
  69.8 0.8 add_multiply_fusion
  70.7 0.1 reduce_sum.106
  71.1 20.1 %all_to_all.9 = f32[128,1,8]{2,1,0:T(1,128)S(1)} all-to-all(f32[128,1,8]{2,1,0:T(1,128)S(1)} %bitcast.463), channel_id=1, replica_groups=mesh['gx'=16,'gy'=2,'gz'=4] {'gx','gy','gz'}, dimensions={0} | all-to-all | bytes 8192 | tf_op jit(solution)/shard_map/all_to_all | solution.py:281
  91.2 0.7 reduce_sum.109
  (192 shorter events, 5.3 us)
Async XLA Ops:
  0.6 5.6 %copy-start = (f32[27,4,16,128]{3,2,1,0:T(8,128)S(1)}, f32[27,4,16,128]{3,2,1,0:T(8,128)}, u32[]{:S(2)}) copy-start(f32[27,4,16,128]{3,2,1,0:T(8,128)} %f_ref.1) | copy-start | bytes 2654212
  0.6 3.5 %copy-start.14 = (s32[1024]{0:T(1024)S(1)}, s32[1024]{0:T(1024)}, u32[]{:S(2)}) copy-start(s32[1024]{0:T(1024)} %param.17) | copy-start | bytes 12292
  0.7 3.5 %copy-start.15 = (f32[1024]{0:T(1024)S(1)}, f32[1024]{0:T(1024)}, u32[]{:S(2)}) copy-start(f32[1024]{0:T(1024)} %param.16) | copy-start | bytes 12292
  0.7 5.6 %copy-start.11 = (s32[4,16,128]{2,1,0:T(8,128)S(1)}, s32[4,16,128]{2,1,0:T(8,128)}, u32[]{:S(2)}) copy-start(s32[4,16,128]{2,1,0:T(8,128)} %param.14) | copy-start | bytes 98308
  1.8 4.5 %copy-start.10 = (f32[4,16,128]{2,1,0:T(8,128)S(1)}, f32[4,16,128]{2,1,0:T(8,128)}, u32[]{:S(2)}) copy-start(f32[4,16,128]{2,1,0:T(8,128)} %refs_6_.1) | copy-start | bytes 98308
  1.9 4.5 %copy-start.16 = (f32[27]{0:T(128)S(1)}, f32[27]{0:T(128)}, u32[]{:S(2)}) copy-start(f32[27]{0:T(128)} %constant.24.clone) | copy-start | bytes 328
  1.9 4.5 %copy-start.17 = (f32[27]{0:T(128)S(1)}, f32[27]{0:T(128)}, u32[]{:S(2)}) copy-start(f32[27]{0:T(128)} %constant.25.clone) | copy-start | bytes 328
  1.9 4.5 %copy-start.18 = (f32[27]{0:T(128)S(1)}, f32[27]{0:T(128)}, u32[]{:S(2)}) copy-start(f32[27]{0:T(128)} %constant.26.clone) | copy-start | bytes 328
  1.9 4.5 %copy-start.19 = (f32[27]{0:T(128)S(1)}, f32[27]{0:T(128)}, u32[]{:S(2)}) copy-start(f32[27]{0:T(128)} %constant.27.clone) | copy-start | bytes 328
  6.3 1.6 %copy-start.8 = (f32[4,16,128]{2,1,0:T(8,128)}, f32[4,16,128]{2,1,0:T(8,128)S(1)}, u32[]{:S(2)}) copy-start(f32[4,16,128]{2,1,0:T(8,128)S(1)} %get-tuple-element.158.refs_13_.refs_7_) | copy-start | bytes 98308
  6.4 1.5 %copy-start.3 = (f32[27,4,16,128]{3,2,1,0:T(8,128)S(1)}, f32[27,4,16,128]{3,2,1,0:T(8,128)}, u32[]{:S(2)}) copy-start(f32[27,4,16,128]{3,2,1,0:T(8,128)} %ae_ref.1) | copy-start | bytes 2654212
  7.8 6.5 %copy-start.1 = (f32[27,4,16,128]{3,2,1,0:T(8,128)}, f32[27,4,16,128]{3,2,1,0:T(8,128)S(1)}, u32[]{:S(2)}) copy-start(f32[27,4,16,128]{3,2,1,0:T(8,128)S(1)} %fusion.7.cf_ref) | copy-start | bytes 2654212
  8.7 10.6 %collective-permute-start.1 = (f32[2,3,3,1,16,128]{5,4,2,1,3,0:T(8,128)}, f32[2,3,3,1,16,128]{5,4,2,1,3,0:T(8,128)}, u32[]{:S(2)}, u32[]{:S(2)}) collective-permute-start(f32[2,3,3,1,16,128]{5,4,2,1,3,0:T(8,128)} %pad_maximum_fusion.4), channel_id=1, source_target_pairs={{0,120},{8,0},{16,8},{24,16},{32,24},{40,32},{48,40},{56,48},{64,5... | collective-permute-start | bytes 442376 | tf_op jit(solution)/shard_map/ppermute | solution.py:58
  10.8 10.2 %collective-permute-start = (f32[2,3,3,1,16,128]{5,4,2,1,3,0:T(8,128)}, f32[2,3,3,1,16,128]{5,4,2,1,3,0:T(8,128)}, u32[]{:S(2)}, u32[]{:S(2)}) collective-permute-start(f32[2,3,3,1,16,128]{5,4,2,1,3,0:T(8,128)} %pad_maximum_fusion.3), channel_id=1, source_target_pairs={{0,8},{8,16},{16,24},{24,32},{32,40},{40,48},{48,56},{56,64},{64,7... | collective-permute-start | bytes 442376 | tf_op jit(solution)/shard_map/ppermute | solution.py:57
  15.1 2.0 %copy-start.4 = (f32[2,3,3,3,4,16,1]{6,5,4,3,2,1,0:T(8,128)S(1)}, f32[2,3,3,3,4,16,1]{6,5,4,3,2,1,0:T(8,128)}, u32[]{:S(2)}) copy-start(f32[2,3,3,3,4,16,1]{6,5,4,3,2,1,0:T(8,128)} %get-tuple-element.23) | copy-start | bytes 41476
  17.1 1.3 %copy-start.9 = (f32[2,3,3,3,4,16,1]{5,4,6,3,2,1,0:T(4,128)S(1)}, f32[2,3,3,3,4,16,1]{5,4,6,3,2,1,0:T(4,128)}, u32[]{:S(2)}) copy-start(f32[2,3,3,3,4,16,1]{5,4,6,3,2,1,0:T(4,128)} %copy.1216) | copy-start | bytes 41476
  17.1 1.5 %copy-start.5 = (f32[2,3,3,3,4,2,128]{6,5,4,3,2,1,0:T(2,128)S(1)}, f32[2,3,3,3,4,2,128]{6,5,4,3,2,1,0:T(2,128)}, u32[]{:S(2)}) copy-start(f32[2,3,3,3,4,2,128]{6,5,4,3,2,1,0:T(2,128)} %fusion.8) | copy-start | bytes 663556
  23.6 5.1 %collective-permute-start.2 = (f32[2,2,3,3,4,1,128]{6,4,3,2,1,5,0:T(4,128)S(1)}, f32[2,2,3,3,4,1,128]{6,4,3,2,1,5,0:T(4,128)S(1)}, u32[]{:S(2)}, u32[]{:S(2)}) collective-permute-start(f32[2,2,3,3,4,1,128]{6,4,3,2,1,5,0:T(4,128)S(1)} %pad_maximum_fusion.6), channel_id=1, source_target_pairs={{0,4},{4,0},{1,5},{5,1},{2,6},{6,2},{3,7},{7,3},{8,12},{12,8},{9,1... | collective-permute-start | bytes 221192 | tf_op jit(solution)/shard_map/ppermute | solution.py:55
  30.0 3.6 %collective-permute-start.4 = (f32[2,3,3,16,4]{3,4,2,1,0:T(4,128)S(1)}, f32[2,3,3,16,4]{3,4,2,1,0:T(4,128)S(1)}, u32[]{:S(2)}, u32[]{:S(2)}) collective-permute-start(f32[2,3,3,16,4]{3,4,2,1,0:T(4,128)S(1)} %pad_maximum_fusion.14), channel_id=1, source_target_pairs={{0,3},{1,0},{2,1},{3,2},{4,7},{5,4},{6,5},{7,6},{8,11},{9,8},{10,9... | collective-permute-start | bytes 13832 | tf_op jit(solution)/shard_map/ppermute | solution.py:58
  32.9 4.1 %collective-permute-start.3 = (f32[2,3,3,16,4]{3,4,2,1,0:T(4,128)S(1)}, f32[2,3,3,16,4]{3,4,2,1,0:T(4,128)S(1)}, u32[]{:S(2)}, u32[]{:S(2)}) collective-permute-start(f32[2,3,3,16,4]{3,4,2,1,0:T(4,128)S(1)} %pad_maximum_fusion.13), channel_id=1, source_target_pairs={{0,1},{1,2},{2,3},{3,0},{4,5},{5,6},{6,7},{7,4},{8,9},{9,10},{10,1... | collective-permute-start | bytes 13832 | tf_op jit(solution)/shard_map/ppermute | solution.py:57
  43.4 1.3 %copy-start.2 = (f32[27,4,16,128]{3,2,1,0:T(8,128)S(1)}, f32[27,4,16,128]{3,2,1,0:T(8,128)}, u32[]{:S(2)}) copy-start(f32[27,4,16,128]{3,2,1,0:T(8,128)} %get-tuple-element.6.an_ref) | copy-start | bytes 2654212
  46.7 5.4 %collective-permute-start.5 = (f32[1,3,3,1,16,128]{5,4,2,1,3,0:T(8,128)S(1)}, f32[1,3,3,1,16,128]{5,4,2,1,3,0:T(8,128)S(1)}, u32[]{:S(2)}, u32[]{:S(2)}) collective-permute-start(f32[1,3,3,1,16,128]{5,4,2,1,3,0:T(8,128)S(1)} %slice_bitcast_fusion.2), channel_id=1, source_target_pairs={{0,8},{8,16},{16,24},{24,32},{32,40},{40,48},{48,56},{56,64},{64,7... | collective-permute-start | bytes 221192 | tf_op jit(solution)/shard_map/ppermute | solution.py:57
  49.5 3.8 %collective-permute-start.6 = (f32[1,3,3,1,16,128]{5,4,2,1,3,0:T(8,128)S(1)}, f32[1,3,3,1,16,128]{5,4,2,1,3,0:T(8,128)S(1)}, u32[]{:S(2)}, u32[]{:S(2)}) collective-permute-start(f32[1,3,3,1,16,128]{5,4,2,1,3,0:T(8,128)S(1)} %slice_bitcast_fusion.1), channel_id=1, source_target_pairs={{0,120},{8,0},{16,8},{24,16},{32,24},{40,32},{48,40},{56,48},{64,5... | collective-permute-start | bytes 221192 | tf_op jit(solution)/shard_map/ppermute | solution.py:58
  52.1 13.5 %copy-start.6 = (f32[1,3,3,1,16,128]{5,4,2,1,3,0:T(8,128)}, f32[1,3,3,1,16,128]{5,4,2,1,3,0:T(8,128)S(1)}, u32[]{:S(2)}) copy-start(f32[1,3,3,1,16,128]{5,4,2,1,3,0:T(8,128)S(1)} %collective-permute-done.5) | copy-start | bytes 221188
  53.4 12.2 %copy-start.7 = (f32[1,3,3,1,16,128]{5,4,2,1,3,0:T(8,128)}, f32[1,3,3,1,16,128]{5,4,2,1,3,0:T(8,128)S(1)}, u32[]{:S(2)}) copy-start(f32[1,3,3,1,16,128]{5,4,2,1,3,0:T(8,128)S(1)} %collective-permute-done.6) | copy-start | bytes 221188
  54.0 4.7 %collective-permute-start.7 = (f32[2,1,3,3,4,1,128]{6,4,3,2,5,1,0:T(4,128)S(1)}, f32[2,1,3,3,4,1,128]{6,4,3,2,5,1,0:T(4,128)S(1)}, u32[]{:S(2)}, u32[]{:S(2)}) collective-permute-start(f32[2,1,3,3,4,1,128]{6,4,3,2,5,1,0:T(4,128)S(1)} %pad_maximum_fusion.15), channel_id=1, source_target_pairs={{0,4},{4,0},{1,5},{5,1},{2,6},{6,2},{3,7},{7,3},{8,12},{12,8},{9,1... | collective-permute-start | bytes 110600 | tf_op jit(solution)/shard_map/ppermute | solution.py:55
  57.4 12.4 %copy-start.12 = (s32[4,16,128]{2,1,0:T(8,128)S(1)}, s32[4,16,128]{2,1,0:T(8,128)}, u32[]{:S(2)}) copy-start(s32[4,16,128]{2,1,0:T(8,128)} %param.14) | copy-start | bytes 98308
  57.4 12.4 %copy-start.13 = (f32[4,16,128]{2,1,0:T(8,128)S(1)}, f32[4,16,128]{2,1,0:T(8,128)}, u32[]{:S(2)}) copy-start(f32[4,16,128]{2,1,0:T(8,128)} %get-tuple-element.8) | copy-start | bytes 98308
  59.7 3.0 %collective-permute-start.9 = (f32[1,3,3,16,4]{3,4,2,1,0:T(4,128)S(1)}, f32[1,3,3,16,4]{3,4,2,1,0:T(4,128)S(1)}, u32[]{:S(2)}, u32[]{:S(2)}) collective-permute-start(f32[1,3,3,16,4]{3,4,2,1,0:T(4,128)S(1)} %fusion.12), channel_id=1, source_target_pairs={{0,3},{1,0},{2,1},{3,2},{4,7},{5,4},{6,5},{7,6},{8,11},{9,8},{10,9... | collective-permute-start | bytes 6920 | tf_op jit(solution)/shard_map/ppermute | solution.py:58
  60.9 3.9 %collective-permute-start.8 = (f32[1,3,3,16,4]{3,4,2,1,0:T(4,128)S(1)}, f32[1,3,3,16,4]{3,4,2,1,0:T(4,128)S(1)}, u32[]{:S(2)}, u32[]{:S(2)}) collective-permute-start(f32[1,3,3,16,4]{3,4,2,1,0:T(4,128)S(1)} %fusion.13), channel_id=1, source_target_pairs={{0,1},{1,2},{2,3},{3,0},{4,5},{5,6},{6,7},{7,4},{8,9},{9,10},{10,1... | collective-permute-start | bytes 6920 | tf_op jit(solution)/shard_map/ppermute | solution.py:57

commit v6 on v5

--- a/solution.py
+++ b/solution.py
@@ -85,12 +85,12 @@
     x_up, x_dn = zip(*[faces(c, s, 0) for c, s in zip(cubes, signs)])
     xlo, xhi = halo_exchange(jnp.stack(x_up), jnp.stack(x_dn), "gx")
     both = jnp.stack(cubes)
-    rows = jnp.concatenate([both[..., sy - 1 : sy, :], both[..., 0:1, :]], axis=5)
-    cols = jnp.concatenate([both[..., sz - 1 : sz], both[..., 0:1]], axis=6)
+    rows = jnp.stack([both[..., sy - 1, :], both[..., 0, :]])
+    cols = jnp.stack([both[..., sz - 1], both[..., 0]])
     y_up, y_dn = [], []
     for k, s in enumerate(signs):
-        top = shifted(rows[k][..., 0:1, :], xlo[k][:, :, :, sy - 1 : sy], xhi[k][:, :, :, sy - 1 : sy], 0, s)
-        bot = shifted(rows[k][..., 1:2, :], xlo[k][:, :, :, 0:1], xhi[k][:, :, :, 0:1], 0, s)
+        top = shifted(rows[0, k], xlo[k][:, :, :, sy - 1, :], xhi[k][:, :, :, sy - 1, :], 0, s)
+        bot = shifted(rows[1, k], xlo[k][:, :, :, 0, :], xhi[k][:, :, :, 0, :], 0, s)
         y_up.append(lax.index_in_dim(top, 1 + s, axis=1, keepdims=False))
         y_dn.append(lax.index_in_dim(bot, 1 - s, axis=1, keepdims=False))
     ylo, yhi = halo_exchange(jnp.stack(y_up), jnp.stack(y_dn), "gy")
@@ -98,12 +98,11 @@
     for k, s in enumerate(signs):
         picked = []
         for at, z0 in ((0, sz - 1), (1, 0)):
-            col = cols[k][..., at : at + 1]
-            col = shifted(col, xlo[k][..., z0 : z0 + 1], xhi[k][..., z0 : z0 + 1], 0, s)
-            col = shifted(col, ylo[k][..., z0 : z0 + 1], yhi[k][..., z0 : z0 + 1], 1, s)
+            col = shifted(cols[at, k], xlo[k][..., z0], xhi[k][..., z0], 0, s)
+            col = shifted(col, ylo[k][..., z0][..., None], yhi[k][..., z0][..., None], 1, s)
             picked.append(col)
-        z_up.append(jnp.swapaxes(lax.index_in_dim(picked[0], 1 + s, axis=2, keepdims=False)[..., 0], -1, -2))
-        z_dn.append(jnp.swapaxes(lax.index_in_dim(picked[1], 1 - s, axis=2, keepdims=False)[..., 0], -1, -2))
+        z_up.append(jnp.swapaxes(lax.index_in_dim(picked[0], 1 + s, axis=2, keepdims=False), -1, -2))
+        z_dn.append(jnp.swapaxes(lax.index_in_dim(picked[1], 1 - s, axis=2, keepdims=False), -1, -2))
     zlo, zhi = halo_exchange(jnp.stack(z_up), jnp.stack(z_dn), "gz")
     out = []
     for k in range(len(cubes)):

time: 92.4 us -> 96 us (1.039)
  local copies, waits for them, and re-layouts: 21.7 us -> 27.4 us
  waiting for transfers between devices: 8.01 us -> 5.93 us
    squeeze x4 -> x6, local copies, waits for them, and re-layouts: 0.05 us -> 2.5 us  [shifted(): minus = lax.index_in_dim(cube, 1 - sign, axis=d, keepdims=False)]
    slice x38 -> x22, local copies, waits for them, and re-layouts: 9.96 us -> 12 us  [the longest x2 3.7 us: halos(): cols = jnp.stack([both[..., sz - 1], both[..., 0]])]
    ppermute x4, waiting for transfers between devices: 3.87 us -> 2.22 us  [halo_exchange(): lo = lax.ppermute(up, axis, [(i, (i + 1) % size) for i in range(size)])]
    ppermute x4, waiting for transfers between devices: 2.87 us -> 1.37 us  [halo_exchange(): hi = lax.ppermute(down, axis, [(i, (i - 1) % size) for i in range(size)])]
    ppermute x2, waiting for transfers between devices: 1.28 us -> 2.34 us  [halo_exchange(): both = lax.ppermute(jnp.stack([up, down]), axis, [(0, 1), (1, 0)])]
    unnamed x51 -> x49, local copies, waits for them, and re-layouts: 2.18 us -> 2.67 us
  transfers between devices with their start and end apart: 10 -> 10, of which waited for: 8 -> 6; matrix products, arithmetic and copies ran while one was open for 15% -> 21% of each run, Pallas kernels for 0% -> 0%
where the time goes in v6:
time: 96 us; the launch traced here: 95.3 us
  local copies, waits for them, and re-layouts  27.4 us (29%)
  blocking collectives  20.2 us (21%)
  starting transfers between devices  19.2 us (20%)
  other arithmetic  11.6 us (12%)
  Pallas kernels  9.12 us (9%)
  waiting for transfers between devices  5.93 us (6%)
  between operations  1.76 us (2%)
    all_to_all x1, blocking collectives, shards(): lax.all_to_all(placed.reshape(devices, count // devices), ('gx', 'gy', 'g...  20.2 us
    pallas_call x2, Pallas kernels, run_stage(): pl.pallas_call(kernel, out_shape=(jax.ShapeDtypeStruct(shape, jnp.float32...  9.12 us
    ppermute x4, starting transfers between devices, halo_exchange(): hi = lax.ppermute(down, axis, [(i, (i - 1) % size) for i in range(size)])  7.83 us
    ppermute x2, starting transfers between devices, halo_exchange(): both = lax.ppermute(jnp.stack([up, down]), axis, [(0, 1), (1, 0)])  6.77 us
    ppermute x4, starting transfers between devices, halo_exchange(): lo = lax.ppermute(up, axis, [(i, (i + 1) % size) for i in range(size)])  4.6 us
    slice x2, local copies, waits for them, and re-layouts, halos(): cols = jnp.stack([both[..., sz - 1], both[..., 0]])  3.7 us
    unnamed x49, local copies, waits for them, and re-layouts  2.67 us
    squeeze x6, local copies, waits for them, and re-layouts, shifted(): minus = lax.index_in_dim(cube, 1 - sign, axis=d, keepdims=False)  2.5 us
  transfers between devices with their start and end apart: 10, of which 6 were waited for; matrix products, arithmetic and copies ran while one was open for 21% of the time, Pallas kernels for 0%

profile of v6, /device:TPU:1, one launch (start us, length us, event | category | flops | bytes accessed | tf_op | source)
XLA Modules:
  0.0 95.3 jit_solution(2448105283904872248)
XLA Ops:
  0.7 1.2 %slice_reduce_fusion.2 = (f32[4,16,128]{2,1,0:T(8,128)S(1)}, f32[4,16,128]{2,1,0:T(8,128)S(1)}) fusion(f32[3,3,3,4,16,128]{5,4,3,2,1,0:T(8,128)} %bitcast.378), kind=kLoop, calls=%fused_computation.14 | loop fusion | flops 131072 | bytes 655360 | tf_op jit(solution)/shard_map/reduce_sum | solution.py:33
  1.9 1.1 %slice_reduce_fusion = (f32[4,16,128]{2,1,0:T(8,128)S(1)}, f32[4,16,128]{2,1,0:T(8,128)S(1)}) fusion(f32[3,3,3,4,16,128]{5,4,3,2,1,0:T(8,128)} %bitcast.379), kind=kLoop, calls=%fused_computation.12 | loop fusion | flops 131072 | bytes 655360 | tf_op jit(solution)/shard_map/reduce_sum | solution.py:34
  3.0 1.1 %slice_reduce_fusion.4 = (f32[4,16,128]{2,1,0:T(8,128)S(1)}, f32[4,16,128]{2,1,0:T(8,128)S(1)}) fusion(f32[27,4,16,128]{3,2,1,0:T(8,128)} %f_ref.1), kind=kLoop, calls=%fused_computation.16 | loop fusion | flops 131072 | bytes 655360 | tf_op jit(solution)/shard_map/reduce_sum | solution.py:32
  4.2 0.2 copy.293
  4.4 0.8 slice.696
  5.3 0.6 gather_fusion
  6.4 1.4 %fusion.7.cf_ref = f32[27,4,16,128]{3,2,1,0:T(8,128)S(1)} fusion(f32[27,4,16,128]{3,2,1,0:T(8,128)S(1)} %copy-done, f32[4,16,128]{2,1,0:T(8,128)S(1)} %get-tuple-element.150.refs_13_.refs_7_, f32[4,16,128]{2,1,0:T(8,128)S(1)} %get-tuple-element.30, f32[4,16,128]{2,1,0:T(8,128)S(1)} %get-tuple-element.33, f32[27]{0:T(128)S(1)} %copy-done.17, ...), kind=kLoop, calls=%fused_computation.11 | loop fusion | flops 4202496 | bytes 2032048 | tf_op jit(solution)/shard_map/add | solution.py:47
  8.0 0.8 pad_maximum_fusion.2
  8.7 1.4 %collective-permute-start.1 = (f32[2,3,3,1,16,128]{5,4,2,1,3,0:T(8,128)}, f32[2,3,3,1,16,128]{5,4,2,1,3,0:T(8,128)}, u32[]{:S(2)}, u32[]{:S(2)}) collective-permute-start(f32[2,3,3,1,16,128]{5,4,2,1,3,0:T(8,128)} %pad_maximum_fusion.2), channel_id=1, source_target_pairs={{0,120},{8,0},{16,8},{24,16},{32,24},{40,32},{48,40},{56,48},{64,5... | collective-permute-start | bytes 442376 | tf_op jit(solution)/shard_map/ppermute | solution.py:58
  10.2 0.7 pad_maximum_fusion.1
  10.9 1.6 %collective-permute-start = (f32[2,3,3,1,16,128]{5,4,2,1,3,0:T(8,128)}, f32[2,3,3,1,16,128]{5,4,2,1,3,0:T(8,128)}, u32[]{:S(2)}, u32[]{:S(2)}) collective-permute-start(f32[2,3,3,1,16,128]{5,4,2,1,3,0:T(8,128)} %pad_maximum_fusion.1), channel_id=1, source_target_pairs={{0,8},{8,16},{16,24},{24,32},{32,40},{40,48},{48,56},{56,64},{64,7... | collective-permute-start | bytes 442376 | tf_op jit(solution)/shard_map/ppermute | solution.py:57
  12.5 0.3 copy.301
  12.9 0.3 copy.302
  13.2 1.3 %pad_maximum_fusion = (f32[2,3,3,3,4,16,1]{6,4,3,2,1,0,5:T(4,128)S(1)}, f32[2,3,3,3,4,16,1]{6,4,3,2,1,0,5:T(4,128)S(1)}) fusion(f32[1,3,3,3,4,16,128]{6,4,3,2,1,0,5:T(4,128)S(1)} %bitcast.383, f32[1,3,3,3,4,16,128]{6,4,3,2,1,0,5:T(4,128)S(1)} %copy.302), kind=kLoop, calls=%fused_computation.1 | loop fusion | flops 6912 | bytes 1797120 | tf_op jit(solution)/shard_map/stack | solution.py:87
  14.5 0.7 maximum_bitcast_fusion.1
  15.3 2.1 %copy.317 = f32[2,3,3,3,4,16,1]{5,4,3,2,1,0,6:T(4,128)} copy(f32[2,3,3,3,4,16,1]{6,4,3,2,1,0,5:T(4,128)S(1)} %get-tuple-element.34) | data formatting | bytes 27648 | tf_op jit(solution)/shard_map/slice | solution.py:89
  17.4 0.8 slice_bitcast_fusion.21
  18.3 0.8 slice_bitcast_fusion.45
  19.1 0.8 slice_bitcast_fusion.39
  20.0 1.6 %copy.309 = f32[2,3,3,3,4,16,1]{5,4,3,2,1,0,6:T(4,128)S(1)} copy(f32[2,3,3,3,4,16,1]{6,4,3,2,1,0,5:T(4,128)S(1)} %get-tuple-element.35) | data formatting | bytes 27648 | tf_op jit(solution)/shard_map/slice | solution.py:89
  22.0 1.6 %fusion.25 = (f32[1,3,3,1,16,128]{5,4,2,1,3,0:T(8,128)}, f32[3,3,1,16,128]{4,3,1,0,2:T(8,128)S(1)}, f32[1,3,3,1,16,128]{5,4,2,1,3,0:T(8,128)S(1)}) fusion(f32[2,3,3,1,16,128]{5,4,2,1,3,0:T(8,128)} %collective-permute-done.1), kind=kLoop, calls=%fused_computation.204 | loop fusion | bytes 368640 | tf_op jit(solution)/shard_map/slice | solution.py:92
  23.6 0.8 slice_reduce_fusion.13
  24.4 1.6 %fusion.26 = (f32[1,3,3,1,16,128]{5,4,2,1,3,0:T(8,128)}, f32[3,3,1,16,128]{4,3,1,0,2:T(8,128)S(1)}, f32[1,3,3,1,16,128]{5,4,2,1,3,0:T(8,128)S(1)}) fusion(f32[2,3,3,1,16,128]{5,4,2,1,3,0:T(8,128)} %collective-permute-done), kind=kLoop, calls=%fused_computation.205 | loop fusion | bytes 368640 | tf_op jit(solution)/shard_map/slice | solution.py:92
  25.9 0.8 slice_reduce_fusion.12
  26.7 0.2 slice_reduce_fusion.10
  26.9 0.2 slice_reduce_fusion.11
  27.5 3.4 %collective-permute-start.2 = (f32[2,2,3,3,4,128]{5,4,2,3,1,0:T(4,128)S(1)}, f32[2,2,3,3,4,128]{5,4,2,3,1,0:T(4,128)S(1)}, u32[]{:S(2)}, u32[]{:S(2)}) collective-permute-start(f32[2,2,3,3,4,128]{5,4,2,3,1,0:T(4,128)S(1)} %pad_maximum_fusion.3), channel_id=1, source_target_pairs={{0,4},{4,0},{1,5},{5,1},{2,6},{6,2},{3,7},{7,3},{8,12},{12,8},{9,1... | collective-permute-start | bytes 221192 | tf_op jit(solution)/shard_map/ppermute | solution.py:55
  31.5 1.1 %collective-permute-done.2 = f32[2,2,3,3,4,128]{5,4,2,3,1,0:T(4,128)S(1)} collective-permute-done((f32[2,2,3,3,4,128]{5,4,2,3,1,0:T(4,128)S(1)}, f32[2,2,3,3,4,128]{5,4,2,3,1,0:T(4,128)S(1)}, u32[]{:S(2)}, u32[]{:S(2)}) %collective-permute-start.2) | collective-permute-done | bytes 73760 | tf_op jit(solution)/shard_map/ppermute | solution.py:55
  33.3 2.5 %collective-permute-start.4 = (f32[2,3,3,16,4]{3,4,1,2,0:T(4,128)S(1)}, f32[2,3,3,16,4]{3,4,1,2,0:T(4,128)S(1)}, u32[]{:S(2)}, u32[]{:S(2)}) collective-permute-start(f32[2,3,3,16,4]{3,4,1,2,0:T(4,128)S(1)} %pad_maximum_fusion.11), channel_id=1, source_target_pairs={{0,3},{1,0},{2,1},{3,2},{4,7},{5,4},{6,5},{7,6},{8,11},{9,8},{10,9... | collective-permute-start | bytes 13832 | tf_op jit(solution)/shard_map/ppermute | solution.py:58
  36.3 0.6 copy.325
  36.9 0.6 copy.326
  37.5 0.6 copy.307
  38.1 0.6 copy.308
  38.8 0.8 copy.324
  39.5 0.8 copy.328
  40.4 0.8 copy.327
  41.1 0.7 copy.316
  41.9 4.9 %shard_map.122 = (f32[27,4,16,128]{3,2,1,0:T(8,128)}, f32[4,16,128]{2,1,0:T(8,128)}) custom-call(f32[27,4,16,128]{3,2,1,0:T(8,128)} %copy-done.2, f32[27,4,16,128]{3,2,1,0:T(8,128)} %ae_ref.1, f32[9,16,128]{2,1,0:T(8,128)} %bitcast.390, f32[9,16,128]{2,1,0:T(8,128)} %bitcast.387, f32[9,4,128]{2,1,0:T(4,128)} %bitcast.416, f32[9,4,128]{2,1,0:T(4,128)} %bitcast.417, ...), custom_call_target="tpu_custom_call" | custom-call | tf_op jit(solution)/shard_map/pallas_call | solution.py:246
  46.8 1.2 %fusion.22 = (f32[9,4,16,128]{3,2,1,0:T(8,128)S(1)}, f32[9,4,16,128]{3,2,1,0:T(8,128)S(1)}) fusion(f32[27,4,16,128]{3,2,1,0:T(8,128)} %get-tuple-element.6.an_ref), kind=kLoop, calls=%fused_computation.201 | loop fusion | bytes 1179648 | tf_op jit(solution)/shard_map/slice | solution.py:78
  47.9 0.2 copy-done.1
  48.1 0.3 fusion.20
  48.5 2.8 %collective-permute-start.5 = (f32[1,3,3,1,16,128]{5,4,2,1,3,0:T(8,128)S(1)}, f32[1,3,3,1,16,128]{5,4,2,1,3,0:T(8,128)S(1)}, u32[]{:S(2)}, u32[]{:S(2)}) collective-permute-start(f32[1,3,3,1,16,128]{5,4,2,1,3,0:T(8,128)S(1)} %slice_bitcast_fusion.1), channel_id=1, source_target_pairs={{0,8},{8,16},{16,24},{24,32},{32,40},{40,48},{48,56},{56,64},{64,7... | collective-permute-start | bytes 221192 | tf_op jit(solution)/shard_map/ppermute | solution.py:57
  51.3 0.3 copy.370
  51.6 0.3 copy.372
  51.9 2.1 %collective-permute-start.6 = (f32[1,3,3,1,16,128]{5,4,2,1,3,0:T(8,128)S(1)}, f32[1,3,3,1,16,128]{5,4,2,1,3,0:T(8,128)S(1)}, u32[]{:S(2)}, u32[]{:S(2)}) collective-permute-start(f32[1,3,3,1,16,128]{5,4,2,1,3,0:T(8,128)S(1)} %slice_bitcast_fusion), channel_id=1, source_target_pairs={{0,120},{8,0},{16,8},{24,16},{32,24},{40,32},{48,40},{56,48},{64,5... | collective-permute-start | bytes 221192 | tf_op jit(solution)/shard_map/ppermute | solution.py:58
  54.0 0.3 copy.371
  54.3 0.3 copy.367
  54.6 0.3 copy.369
  54.9 0.3 copy.368
  55.2 0.2 slice_reduce_fusion.7
  55.4 0.5 collective-permute-done.6
  55.9 0.2 slice_reduce_fusion.6
  56.4 3.4 %collective-permute-start.7 = (f32[2,1,3,3,4,128]{5,4,3,2,1,0:T(4,128)S(1)}, f32[2,1,3,3,4,128]{5,4,3,2,1,0:T(4,128)S(1)}, u32[]{:S(2)}, u32[]{:S(2)}) collective-permute-start(f32[2,1,3,3,4,128]{5,4,3,2,1,0:T(4,128)S(1)} %pad_maximum_fusion.12), channel_id=1, source_target_pairs={{0,4},{4,0},{1,5},{5,1},{2,6},{6,2},{3,7},{7,3},{8,12},{12,8},{9,1... | collective-permute-start | bytes 110600 | tf_op jit(solution)/shard_map/ppermute | solution.py:55
  60.0 1.2 %collective-permute-done.7 = f32[2,1,3,3,4,128]{5,4,3,2,1,0:T(4,128)S(1)} collective-permute-done((f32[2,1,3,3,4,128]{5,4,3,2,1,0:T(4,128)S(1)}, f32[2,1,3,3,4,128]{5,4,3,2,1,0:T(4,128)S(1)}, u32[]{:S(2)}, u32[]{:S(2)}) %collective-permute-start.7) | collective-permute-done | bytes 36896 | tf_op jit(solution)/shard_map/ppermute | solution.py:55
  61.3 0.6 slice_bitcast_fusion.59
  62.2 1.8 %collective-permute-start.9 = (f32[1,3,3,16,4]{3,4,2,1,0:T(4,128)S(1)}, f32[1,3,3,16,4]{3,4,2,1,0:T(4,128)S(1)}, u32[]{:S(2)}, u32[]{:S(2)}) collective-permute-start(f32[1,3,3,16,4]{3,4,2,1,0:T(4,128)S(1)} %fusion.8), channel_id=1, source_target_pairs={{0,3},{1,0},{2,1},{3,2},{4,7},{5,4},{6,5},{7,6},{8,11},{9,8},{10,9... | collective-permute-start | bytes 6920 | tf_op jit(solution)/shard_map/ppermute | solution.py:58
  64.4 0.8 collective-permute-done.9
  65.2 0.7 copy.348
  66.0 2.1 %collective-permute-done.8 = f32[1,3,3,16,4]{3,4,2,1,0:T(4,128)S(1)} collective-permute-done((f32[1,3,3,16,4]{3,4,2,1,0:T(4,128)S(1)}, f32[1,3,3,16,4]{3,4,2,1,0:T(4,128)S(1)}, u32[]{:S(2)}, u32[]{:S(2)}) %collective-permute-start.8) | collective-permute-done | bytes 2336 | tf_op jit(solution)/shard_map/ppermute | solution.py:57
  68.1 0.8 copy.342
  68.9 4.2 %shard_map.123 = (f32[27,4,16,128]{3,2,1,0:T(8,128)}, f32[4,16,128]{2,1,0:T(8,128)}) custom-call(f32[27,4,16,128]{3,2,1,0:T(8,128)} %get-tuple-element.6.an_ref, f32[27,4,16,128]{3,2,1,0:T(8,128)} %f_ref.1, f32[9,16,128]{2,1,0:T(8,128)} %bitcast.393, f32[9,16,128]{2,1,0:T(8,128)} %bitcast.396, f32[9,4,128]{2,1,0:T(4,128)} %bitcast.445, ...), custom_call_target="tpu_custom_call" | custom-call | tf_op jit(solution)/shard_map/pallas_call | solution.py:246
  73.1 0.8 add_multiply_fusion
  74.4 20.2 %all_to_all.9 = f32[128,1,8]{2,1,0:T(1,128)S(1)} all-to-all(f32[128,1,8]{2,1,0:T(1,128)S(1)} %bitcast.413), channel_id=1, replica_groups=mesh['gx'=16,'gy'=2,'gz'=4] {'gx','gy','gz'}, dimensions={0} | all-to-all | bytes 8192 | tf_op jit(solution)/shard_map/all_to_all | solution.py:280
  94.6 0.7 reduce_sum.109
  (189 shorter events, 4.9 us)
Async XLA Ops:
  0.6 5.6 %copy-start = (f32[27,4,16,128]{3,2,1,0:T(8,128)S(1)}, f32[27,4,16,128]{3,2,1,0:T(8,128)}, u32[]{:S(2)}) copy-start(f32[27,4,16,128]{3,2,1,0:T(8,128)} %f_ref.1) | copy-start | bytes 2654212
  0.6 3.5 %copy-start.13 = (s32[1024]{0:T(1024)S(1)}, s32[1024]{0:T(1024)}, u32[]{:S(2)}) copy-start(s32[1024]{0:T(1024)} %param.17) | copy-start | bytes 12292
  0.7 3.5 %copy-start.14 = (f32[1024]{0:T(1024)S(1)}, f32[1024]{0:T(1024)}, u32[]{:S(2)}) copy-start(f32[1024]{0:T(1024)} %param.16) | copy-start | bytes 12292
  0.7 5.6 %copy-start.10 = (s32[4,16,128]{2,1,0:T(8,128)S(1)}, s32[4,16,128]{2,1,0:T(8,128)}, u32[]{:S(2)}) copy-start(s32[4,16,128]{2,1,0:T(8,128)} %param.14) | copy-start | bytes 98308
  1.8 4.5 %copy-start.9 = (f32[4,16,128]{2,1,0:T(8,128)S(1)}, f32[4,16,128]{2,1,0:T(8,128)}, u32[]{:S(2)}) copy-start(f32[4,16,128]{2,1,0:T(8,128)} %refs_6_.1) | copy-start | bytes 98308
  1.9 4.5 %copy-start.15 = (f32[27]{0:T(128)S(1)}, f32[27]{0:T(128)}, u32[]{:S(2)}) copy-start(f32[27]{0:T(128)} %constant.24.clone) | copy-start | bytes 328
  1.9 4.5 %copy-start.16 = (f32[27]{0:T(128)S(1)}, f32[27]{0:T(128)}, u32[]{:S(2)}) copy-start(f32[27]{0:T(128)} %constant.25.clone) | copy-start | bytes 328
  1.9 4.5 %copy-start.17 = (f32[27]{0:T(128)S(1)}, f32[27]{0:T(128)}, u32[]{:S(2)}) copy-start(f32[27]{0:T(128)} %constant.26.clone) | copy-start | bytes 328
  1.9 4.5 %copy-start.18 = (f32[27]{0:T(128)S(1)}, f32[27]{0:T(128)}, u32[]{:S(2)}) copy-start(f32[27]{0:T(128)} %constant.27.clone) | copy-start | bytes 328
  6.3 1.6 %copy-start.8 = (f32[4,16,128]{2,1,0:T(8,128)}, f32[4,16,128]{2,1,0:T(8,128)S(1)}, u32[]{:S(2)}) copy-start(f32[4,16,128]{2,1,0:T(8,128)S(1)} %get-tuple-element.150.refs_13_.refs_7_) | copy-start | bytes 98308
  6.4 1.5 %copy-start.3 = (f32[27,4,16,128]{3,2,1,0:T(8,128)S(1)}, f32[27,4,16,128]{3,2,1,0:T(8,128)}, u32[]{:S(2)}) copy-start(f32[27,4,16,128]{3,2,1,0:T(8,128)} %ae_ref.1) | copy-start | bytes 2654212
  7.8 5.0 %copy-start.2 = (f32[27,4,16,128]{3,2,1,0:T(8,128)}, f32[27,4,16,128]{3,2,1,0:T(8,128)S(1)}, u32[]{:S(2)}) copy-start(f32[27,4,16,128]{3,2,1,0:T(8,128)S(1)} %fusion.7.cf_ref) | copy-start | bytes 2654212
  8.7 13.2 %collective-permute-start.1 = (f32[2,3,3,1,16,128]{5,4,2,1,3,0:T(8,128)}, f32[2,3,3,1,16,128]{5,4,2,1,3,0:T(8,128)}, u32[]{:S(2)}, u32[]{:S(2)}) collective-permute-start(f32[2,3,3,1,16,128]{5,4,2,1,3,0:T(8,128)} %pad_maximum_fusion.2), channel_id=1, source_target_pairs={{0,120},{8,0},{16,8},{24,16},{32,24},{40,32},{48,40},{56,48},{64,5... | collective-permute-start | bytes 442376 | tf_op jit(solution)/shard_map/ppermute | solution.py:58
  10.9 13.5 %collective-permute-start = (f32[2,3,3,1,16,128]{5,4,2,1,3,0:T(8,128)}, f32[2,3,3,1,16,128]{5,4,2,1,3,0:T(8,128)}, u32[]{:S(2)}, u32[]{:S(2)}) collective-permute-start(f32[2,3,3,1,16,128]{5,4,2,1,3,0:T(8,128)} %pad_maximum_fusion.1), channel_id=1, source_target_pairs={{0,8},{8,16},{16,24},{24,32},{32,40},{40,48},{48,56},{56,64},{64,7... | collective-permute-start | bytes 442376 | tf_op jit(solution)/shard_map/ppermute | solution.py:57
  23.6 9.0 %copy-start.4 = (f32[1,3,3,1,16,128]{5,4,2,1,3,0:T(8,128)}, f32[1,3,3,1,16,128]{5,4,2,1,3,0:T(8,128)S(1)}, u32[]{:S(2)}) copy-start(f32[1,3,3,1,16,128]{5,4,2,1,3,0:T(8,128)S(1)} %get-tuple-element.58) | copy-start | bytes 221188
  25.9 7.3 %copy-start.5 = (f32[1,3,3,1,16,128]{5,4,2,1,3,0:T(8,128)}, f32[1,3,3,1,16,128]{5,4,2,1,3,0:T(8,128)S(1)}, u32[]{:S(2)}) copy-start(f32[1,3,3,1,16,128]{5,4,2,1,3,0:T(8,128)S(1)} %get-tuple-element.61) | copy-start | bytes 221188
  27.5 5.1 %collective-permute-start.2 = (f32[2,2,3,3,4,128]{5,4,2,3,1,0:T(4,128)S(1)}, f32[2,2,3,3,4,128]{5,4,2,3,1,0:T(4,128)S(1)}, u32[]{:S(2)}, u32[]{:S(2)}) collective-permute-start(f32[2,2,3,3,4,128]{5,4,2,3,1,0:T(4,128)S(1)} %pad_maximum_fusion.3), channel_id=1, source_target_pairs={{0,4},{4,0},{1,5},{5,1},{2,6},{6,2},{3,7},{7,3},{8,12},{12,8},{9,1... | collective-permute-start | bytes 221192 | tf_op jit(solution)/shard_map/ppermute | solution.py:55
  33.3 5.4 %collective-permute-start.4 = (f32[2,3,3,16,4]{3,4,1,2,0:T(4,128)S(1)}, f32[2,3,3,16,4]{3,4,1,2,0:T(4,128)S(1)}, u32[]{:S(2)}, u32[]{:S(2)}) collective-permute-start(f32[2,3,3,16,4]{3,4,1,2,0:T(4,128)S(1)} %pad_maximum_fusion.11), channel_id=1, source_target_pairs={{0,3},{1,0},{2,1},{3,2},{4,7},{5,4},{6,5},{7,6},{8,11},{9,8},{10,9... | collective-permute-start | bytes 13832 | tf_op jit(solution)/shard_map/ppermute | solution.py:58
  36.3 4.1 %collective-permute-start.3 = (f32[2,3,3,16,4]{3,4,1,2,0:T(4,128)S(1)}, f32[2,3,3,16,4]{3,4,1,2,0:T(4,128)S(1)}, u32[]{:S(2)}, u32[]{:S(2)}) collective-permute-start(f32[2,3,3,16,4]{3,4,1,2,0:T(4,128)S(1)} %pad_maximum_fusion.10), channel_id=1, source_target_pairs={{0,1},{1,2},{2,3},{3,0},{4,5},{5,6},{6,7},{7,4},{8,9},{9,10},{10,1... | collective-permute-start | bytes 13832 | tf_op jit(solution)/shard_map/ppermute | solution.py:57
  46.7 1.3 %copy-start.1 = (f32[27,4,16,128]{3,2,1,0:T(8,128)S(1)}, f32[27,4,16,128]{3,2,1,0:T(8,128)}, u32[]{:S(2)}) copy-start(f32[27,4,16,128]{3,2,1,0:T(8,128)} %get-tuple-element.6.an_ref) | copy-start | bytes 2654212
  48.5 6.7 %collective-permute-start.5 = (f32[1,3,3,1,16,128]{5,4,2,1,3,0:T(8,128)S(1)}, f32[1,3,3,1,16,128]{5,4,2,1,3,0:T(8,128)S(1)}, u32[]{:S(2)}, u32[]{:S(2)}) collective-permute-start(f32[1,3,3,1,16,128]{5,4,2,1,3,0:T(8,128)S(1)} %slice_bitcast_fusion.1), channel_id=1, source_target_pairs={{0,8},{8,16},{16,24},{24,32},{32,40},{40,48},{48,56},{56,64},{64,7... | collective-permute-start | bytes 221192 | tf_op jit(solution)/shard_map/ppermute | solution.py:57
  51.9 4.0 %collective-permute-start.6 = (f32[1,3,3,1,16,128]{5,4,2,1,3,0:T(8,128)S(1)}, f32[1,3,3,1,16,128]{5,4,2,1,3,0:T(8,128)S(1)}, u32[]{:S(2)}, u32[]{:S(2)}) collective-permute-start(f32[1,3,3,1,16,128]{5,4,2,1,3,0:T(8,128)S(1)} %slice_bitcast_fusion), channel_id=1, source_target_pairs={{0,120},{8,0},{16,8},{24,16},{32,24},{40,32},{48,40},{56,48},{64,5... | collective-permute-start | bytes 221192 | tf_op jit(solution)/shard_map/ppermute | solution.py:58
  55.2 13.7 %copy-start.6 = (f32[1,3,3,1,16,128]{5,4,2,1,3,0:T(8,128)}, f32[1,3,3,1,16,128]{5,4,2,1,3,0:T(8,128)S(1)}, u32[]{:S(2)}) copy-start(f32[1,3,3,1,16,128]{5,4,2,1,3,0:T(8,128)S(1)} %collective-permute-done.5) | copy-start | bytes 221188
  55.9 12.9 %copy-start.7 = (f32[1,3,3,1,16,128]{5,4,2,1,3,0:T(8,128)}, f32[1,3,3,1,16,128]{5,4,2,1,3,0:T(8,128)S(1)}, u32[]{:S(2)}) copy-start(f32[1,3,3,1,16,128]{5,4,2,1,3,0:T(8,128)S(1)} %collective-permute-done.6) | copy-start | bytes 221188
  56.4 16.7 %copy-start.11 = (s32[4,16,128]{2,1,0:T(8,128)S(1)}, s32[4,16,128]{2,1,0:T(8,128)}, u32[]{:S(2)}) copy-start(s32[4,16,128]{2,1,0:T(8,128)} %param.14) | copy-start | bytes 98308
  56.4 16.7 %copy-start.12 = (f32[4,16,128]{2,1,0:T(8,128)S(1)}, f32[4,16,128]{2,1,0:T(8,128)}, u32[]{:S(2)}) copy-start(f32[4,16,128]{2,1,0:T(8,128)} %get-tuple-element.8) | copy-start | bytes 98308
  56.4 4.9 %collective-permute-start.7 = (f32[2,1,3,3,4,128]{5,4,3,2,1,0:T(4,128)S(1)}, f32[2,1,3,3,4,128]{5,4,3,2,1,0:T(4,128)S(1)}, u32[]{:S(2)}, u32[]{:S(2)}) collective-permute-start(f32[2,1,3,3,4,128]{5,4,3,2,1,0:T(4,128)S(1)} %pad_maximum_fusion.12), channel_id=1, source_target_pairs={{0,4},{4,0},{1,5},{5,1},{2,6},{6,2},{3,7},{7,3},{8,12},{12,8},{9,1... | collective-permute-start | bytes 110600 | tf_op jit(solution)/shard_map/ppermute | solution.py:55
  62.2 3.0 %collective-permute-start.9 = (f32[1,3,3,16,4]{3,4,2,1,0:T(4,128)S(1)}, f32[1,3,3,16,4]{3,4,2,1,0:T(4,128)S(1)}, u32[]{:S(2)}, u32[]{:S(2)}) collective-permute-start(f32[1,3,3,16,4]{3,4,2,1,0:T(4,128)S(1)} %fusion.8), channel_id=1, source_target_pairs={{0,3},{1,0},{2,1},{3,2},{4,7},{5,4},{6,5},{7,6},{8,11},{9,8},{10,9... | collective-permute-start | bytes 6920 | tf_op jit(solution)/shard_map/ppermute | solution.py:58
  64.2 3.9 %collective-permute-start.8 = (f32[1,3,3,16,4]{3,4,2,1,0:T(4,128)S(1)}, f32[1,3,3,16,4]{3,4,2,1,0:T(4,128)S(1)}, u32[]{:S(2)}, u32[]{:S(2)}) collective-permute-start(f32[1,3,3,16,4]{3,4,2,1,0:T(4,128)S(1)} %fusion.9), channel_id=1, source_target_pairs={{0,1},{1,2},{2,3},{3,0},{4,5},{5,6},{6,7},{7,4},{8,9},{9,10},{10,1... | collective-permute-start | bytes 6920 | tf_op jit(solution)/shard_map/ppermute | solution.py:57

commit v7 on v5

--- a/solution.py
+++ b/solution.py
@@ -226,6 +226,50 @@
     lax.fori_loop(0, sx * halves, body, 0)
 
 
+def collide_rows(F, om, ga):
+    rho = sum(F)
+    mom = []
+    for axis in range(3):
+        pos = [F[q] for q in range(27) if STEPS[q, axis] == 1]
+        neg = [F[q] for q in range(27) if STEPS[q, axis] == -1]
+        mom.append(sum(pos) - sum(neg))
+    vel = (mom[0] / rho, mom[1] / rho, mom[2] / rho)
+    uu = vel[0] * vel[0] + vel[1] * vel[1] + vel[2] * vel[2]
+    out = []
+    for q in range(27):
+        c = STEPS[q]
+        w = float(WEIGHTS[q])
+        cu = None
+        for axis in range(3):
+            if c[axis] == 1:
+                cu = vel[axis] if cu is None else cu + vel[axis]
+            elif c[axis] == -1:
+                cu = -vel[axis] if cu is None else cu - vel[axis]
+        if cu is None:
+            eq = w * rho * (1.0 - 1.5 * uu)
+        else:
+            eq = w * rho * (1.0 + 3.0 * cu + 4.5 * cu * cu - 1.5 * uu)
+        bgk = F[q] - om * (F[q] - eq)
+        out.append((1.0 - ga) * bgk + ga * F[26 - q])
+    return out
+
+
+def collide_kernel(f_ref, rate_ref, gamma_ref, out_ref):
+    _, sx, sy, sz = out_ref.shape
+    halves = sy // 8
+
+    def body(step, carry):
+        i = step // halves
+        h = pl.multiple_of((step % halves) * 8, 8)
+        F = [f_ref[q, i, pl.ds(h, 8), :] for q in range(27)]
+        post = collide_rows(F, rate_ref[i, pl.ds(h, 8), :], gamma_ref[i, pl.ds(h, 8), :])
+        for q in range(27):
+            out_ref[q, i, pl.ds(h, 8), :] = post[q]
+        return carry
+
+    lax.fori_loop(0, sx * halves, body, 0)
+
+
 def next_kernel(cf_ref, ae_ref, *refs):
     hal_f = refs[0:6]
     hal_a = refs[6:12]
@@ -262,7 +306,9 @@
     solid = jnp.broadcast_to(looked[:, :, None, :, None, 0], (sx, 2, sy // 2, 2, sz // 2)).reshape(sx, sy, sz)
     walls = wall_flag.astype(jnp.float32)
     gamma = walls * solid
-    post_now, _ = collide(check_pops, relax_rate, gamma)
+    post_now = pl.pallas_call(collide_kernel, out_shape=jax.ShapeDtypeStruct(check_pops.shape, jnp.float32))(
+        check_pops, relax_rate, gamma
+    )
     hal_f, hal_a = halos([post_now, adjoint_end], [1, -1])
     shape = check_pops.shape
     adj_next, sens_next = run_stage(

time: 92.4 us -> 92.5 us (level)
  other arithmetic: 12.5 us -> 7.59 us
  waiting for transfers between devices: 8.01 us -> 4.77 us
  Pallas kernels: 9.11 us -> 12 us
  local copies, waits for them, and re-layouts: 21.7 us -> 23.8 us
  blocking collectives: 20.1 us -> 21.9 us
  starting transfers between devices: 18.8 us -> 20.3 us
    ppermute x4, starting transfers between devices: 5.03 us -> 9.36 us  [halo_exchange(): lo = lax.ppermute(up, axis, [(i, (i + 1) % size) for i in range(size)])]
    reduce_sum x4 -> x0, other arithmetic: 3.42 us -> none  [the longest x1 1.17 us: collide(): mom_y = jnp.sum(cube[:, 2], axis=(0, 1)) - jnp.sum(cube[:, 0], axis=(0, 1))]
    ppermute x4, waiting for transfers between devices: 3.87 us -> 0.9 us  [halo_exchange(): lo = lax.ppermute(up, axis, [(i, (i + 1) % size) for i in range(size)])]
    pallas_call x0 -> x1, Pallas kernels: none -> 2.93 us  [shards(): pl.pallas_call(collide_kernel, out_shape=jax.ShapeDtypeStruct(check_pops....]
    ppermute x4, starting transfers between devices: 6.96 us -> 4.21 us  [halo_exchange(): hi = lax.ppermute(down, axis, [(i, (i - 1) % size) for i in range(size)])]
    slice x3, local copies, waits for them, and re-layouts: 1.26 us -> 3.43 us  [faces(): minus = lax.index_in_dim(cube, 1 - sign, axis=d, keepdims=False)]
    all_to_all x1, blocking collectives: 20.1 us -> 21.9 us  [shards(): lax.all_to_all(placed.reshape(devices, count // devices), ('gx', 'gy', 'g...]
    another operation x2, other arithmetic: 1.45 us -> 0.03 us  [halos(): xlo, xhi = halo_exchange(jnp.stack(x_up), jnp.stack(x_dn), 'gx')]
  transfers between devices with their start and end apart: 10 -> 10, of which waited for: 8 -> 5; matrix products, arithmetic and copies ran while one was open for 15% -> 14% of each run, Pallas kernels for 0% -> 0%
where the time goes in v7:
time: 92.5 us; the launch traced here: 92 us
  local copies, waits for them, and re-layouts  23.8 us (26%)
  blocking collectives  21.9 us (24%)
  starting transfers between devices  20.3 us (22%)
  Pallas kernels  12 us (13%)
  other arithmetic  7.59 us (8%)
  waiting for transfers between devices  4.77 us (5%)
  between operations  1.52 us (2%)
    all_to_all x1, blocking collectives, shards(): lax.all_to_all(placed.reshape(devices, count // devices), ('gx', 'gy', 'g...  21.9 us
    ppermute x4, starting transfers between devices, halo_exchange(): lo = lax.ppermute(up, axis, [(i, (i + 1) % size) for i in range(size)])  9.36 us
    pallas_call x2, Pallas kernels, run_stage(): pl.pallas_call(kernel, out_shape=(jax.ShapeDtypeStruct(shape, jnp.float32...  9.1 us
    ppermute x2, starting transfers between devices, halo_exchange(): both = lax.ppermute(jnp.stack([up, down]), axis, [(0, 1), (1, 0)])  6.77 us
    slice x3, local copies, waits for them, and re-layouts, halos(): cols = jnp.concatenate([both[..., sz - 1:sz], both[..., 0:1]], axis=6)  4.47 us
    ppermute x4, starting transfers between devices, halo_exchange(): hi = lax.ppermute(down, axis, [(i, (i - 1) % size) for i in range(size)])  4.21 us
    slice x3, local copies, waits for them, and re-layouts, faces(): minus = lax.index_in_dim(cube, 1 - sign, axis=d, keepdims=False)  3.43 us
    pallas_call x1, Pallas kernels, shards(): pl.pallas_call(collide_kernel, out_shape=jax.ShapeDtypeStruct(check_pops....  2.93 us
  transfers between devices with their start and end apart: 10, of which 5 were waited for; matrix products, arithmetic and copies ran while one was open for 14% of the time, Pallas kernels for 0%

profile of v7, /device:TPU:1, one launch (start us, length us, event | category | flops | bytes accessed | tf_op | source)
XLA Modules:
  0.0 92.0 jit_solution(1941885157152774347)
XLA Ops:
  0.6 0.8 slice.644
  1.6 0.7 convert_element_type.8
  2.3 0.7 pad_maximum_fusion.42
  3.0 0.2 copy.1188
  3.2 0.6 gather_fusion
  3.8 0.1 copy.1291
  4.0 0.1 reshape.44
  4.1 1.1 %fusion.19 = (f32[9,4,16,128]{3,2,1,0:T(8,128)S(1)}, f32[9,4,16,128]{3,2,1,0:T(8,128)S(1)}) fusion(f32[27,4,16,128]{3,2,1,0:T(8,128)} %ae_ref.1), kind=kLoop, calls=%fused_computation.197 | loop fusion | bytes 1179648 | tf_op jit(solution)/shard_map/slice | solution.py:78
  5.2 0.6 convert_multiply_fusion.gamma_ref.refs_13_.refs_7_
  5.8 2.9 %shard_map.86.cf_ref = f32[27,4,16,128]{3,2,1,0:T(8,128)} custom-call(f32[27,4,16,128]{3,2,1,0:T(8,128)} %f_ref.3, f32[4,16,128]{2,1,0:T(8,128)} %refs_6_.1, f32[4,16,128]{2,1,0:T(8,128)} %convert_multiply_fusion.gamma_ref.refs_13_.refs_7_), custom_call_target="tpu_custom_call" | custom-call | tf_op jit(solution)/shard_map/pallas_call | solution.py:309
  8.8 1.2 %fusion.18 = (f32[9,4,16,128]{3,2,1,0:T(8,128)S(1)}, f32[9,4,16,128]{3,2,1,0:T(8,128)S(1)}) fusion(f32[27,4,16,128]{3,2,1,0:T(8,128)} %shard_map.86.cf_ref), kind=kLoop, calls=%fused_computation.196 | loop fusion | bytes 1179648 | tf_op jit(solution)/shard_map/slice | solution.py:78
  10.0 3.1 %collective-permute-start = (f32[2,3,3,1,16,128]{5,4,2,1,3,0:T(8,128)S(1)}, f32[2,3,3,1,16,128]{5,4,2,1,3,0:T(8,128)S(1)}, u32[]{:S(2)}, u32[]{:S(2)}) collective-permute-start(f32[2,3,3,1,16,128]{5,4,2,1,3,0:T(8,128)S(1)} %pad_maximum_fusion.3), channel_id=1, source_target_pairs={{0,8},{8,16},{16,24},{24,32},{32,40},{40,48},{48,56},{56,64},{64,7... | collective-permute-start | bytes 442376 | tf_op jit(solution)/shard_map/ppermute | solution.py:57
  13.3 0.2 fusion
  13.4 1.9 %slice_maximum_fusion = (f32[2,3,3,3,4,16,1]{6,5,4,3,2,1,0:T(8,128)}, f32[2,3,3,3,4,16,1]{6,5,4,3,2,1,0:T(8,128)S(1)}) fusion(f32[1,3,3,3,4,16,128]{6,5,4,3,2,1,0:T(8,128)S(1)} %bitcast.436, f32[1,3,3,3,4,16,128]{6,5,4,3,2,1,0:T(8,128)S(1)} %bitcast.432), kind=kLoop, calls=%fused_computation.2 | loop fusion | flops 6912 | bytes 1797120 | tf_op jit(solution)/shard_map/stack | solution.py:87
  15.3 0.1 copy.1312
  15.4 0.1 copy.1313
  15.9 2.8 %copy.1212 = f32[2,3,3,3,4,16,1]{5,4,6,3,2,1,0:T(4,128)S(1)} copy(f32[2,3,3,3,4,16,1]{6,5,4,3,2,1,0:T(8,128)} %get-tuple-element.10) | data formatting | bytes 27648 | tf_op jit(solution)/shard_map/slice | solution.py:89
  18.7 1.4 %copy.1213 = f32[2,3,3,3,4,16,1]{5,4,6,3,2,1,0:T(4,128)S(1)} copy(f32[2,3,3,3,4,16,1]{6,5,4,3,2,1,0:T(8,128)S(1)} %get-tuple-element.11) | data formatting | bytes 27648 | tf_op jit(solution)/shard_map/slice | solution.py:89
  20.2 0.7 fusion.22
  21.1 0.7 fusion.21
  22.0 0.1 copy.1239
  22.1 0.1 copy.1222
  22.2 0.1 copy.1232
  22.4 0.1 copy.1215
  22.5 0.1 copy.1240
  22.6 0.1 copy.1223
  22.7 0.1 copy.1231
  22.9 0.1 copy.1214
  23.3 3.4 %collective-permute-start.2 = (f32[2,2,3,3,4,1,128]{6,4,3,2,1,5,0:T(4,128)S(1)}, f32[2,2,3,3,4,1,128]{6,4,3,2,1,5,0:T(4,128)S(1)}, u32[]{:S(2)}, u32[]{:S(2)}) collective-permute-start(f32[2,2,3,3,4,1,128]{6,4,3,2,1,5,0:T(4,128)S(1)} %pad_maximum_fusion.6), channel_id=1, source_target_pairs={{0,4},{4,0},{1,5},{5,1},{2,6},{6,2},{3,7},{7,3},{8,12},{12,8},{9,1... | collective-permute-start | bytes 221192 | tf_op jit(solution)/shard_map/ppermute | solution.py:55
  27.3 1.1 %collective-permute-done.2 = f32[2,2,3,3,4,1,128]{6,4,3,2,1,5,0:T(4,128)S(1)} collective-permute-done((f32[2,2,3,3,4,1,128]{6,4,3,2,1,5,0:T(4,128)S(1)}, f32[2,2,3,3,4,1,128]{6,4,3,2,1,5,0:T(4,128)S(1)}, u32[]{:S(2)}, u32[]{:S(2)}) %collective-permute-start.2) | collective-permute-done | bytes 73760 | tf_op jit(solution)/shard_map/ppermute | solution.py:55
  28.4 0.6 fusion.26
  29.8 1.3 %collective-permute-start.3 = (f32[2,3,3,16,4]{3,4,2,1,0:T(4,128)S(1)}, f32[2,3,3,16,4]{3,4,2,1,0:T(4,128)S(1)}, u32[]{:S(2)}, u32[]{:S(2)}) collective-permute-start(f32[2,3,3,16,4]{3,4,2,1,0:T(4,128)S(1)} %pad_maximum_fusion.13), channel_id=1, source_target_pairs={{0,1},{1,2},{2,3},{3,0},{4,5},{5,6},{6,7},{7,4},{8,9},{9,10},{10,1... | collective-permute-start | bytes 13832 | tf_op jit(solution)/shard_map/ppermute | solution.py:57
  31.4 1.5 %collective-permute-start.4 = (f32[2,3,3,16,4]{3,4,2,1,0:T(4,128)S(1)}, f32[2,3,3,16,4]{3,4,2,1,0:T(4,128)S(1)}, u32[]{:S(2)}, u32[]{:S(2)}) collective-permute-start(f32[2,3,3,16,4]{3,4,2,1,0:T(4,128)S(1)} %pad_maximum_fusion.14), channel_id=1, source_target_pairs={{0,3},{1,0},{2,1},{3,2},{4,7},{5,4},{6,5},{7,6},{8,11},{9,8},{10,9... | collective-permute-start | bytes 13832 | tf_op jit(solution)/shard_map/ppermute | solution.py:58
  33.0 0.9 collective-permute-done.3
  33.9 0.8 copy.1248
  34.6 0.7 copy.1249
  35.4 0.8 copy.1230
  36.2 0.7 copy.1247
  36.9 4.9 %shard_map.87 = (f32[27,4,16,128]{3,2,1,0:T(8,128)}, f32[4,16,128]{2,1,0:T(8,128)}) custom-call(f32[27,4,16,128]{3,2,1,0:T(8,128)} %shard_map.86.cf_ref, f32[27,4,16,128]{3,2,1,0:T(8,128)} %ae_ref.1, f32[9,16,128]{2,1,0:T(8,128)} %bitcast.451, f32[9,16,128]{2,1,0:T(8,128)} %bitcast.453, f32[9,4,128]{2,1,0:T(4,128)} %bitcast.466, f32[9,4,128]{2,1,0:T(4,128)} %bitcast.465, ...), custom_call_target="tpu_custom_call" | custom-call | tf_op jit(solution)/shard_map/pallas_call | solution.py:291
  41.8 1.2 %fusion.17 = (f32[9,4,16,128]{3,2,1,0:T(8,128)S(1)}, f32[9,4,16,128]{3,2,1,0:T(8,128)S(1)}) fusion(f32[27,4,16,128]{3,2,1,0:T(8,128)} %get-tuple-element.6.an_ref), kind=kLoop, calls=%fused_computation.195 | loop fusion | bytes 1179648 | tf_op jit(solution)/shard_map/slice | solution.py:78
  43.0 1.2 %fusion.16 = (f32[1,3,3,3,4,1,128]{6,5,4,3,2,1,0:T(1,128)S(1)}, f32[1,3,3,3,4,1,128]{6,5,4,3,2,1,0:T(1,128)S(1)}) fusion(f32[1,3,3,3,4,16,128]{6,5,4,3,2,1,0:T(8,128)} %bitcast.433), kind=kLoop, calls=%fused_computation.194 | loop fusion | bytes 221184 | tf_op jit(solution)/shard_map/slice | solution.py:88
  44.2 0.3 fusion.15
  44.6 3.8 %collective-permute-start.5 = (f32[1,3,3,1,16,128]{5,4,2,1,3,0:T(8,128)S(1)}, f32[1,3,3,1,16,128]{5,4,2,1,3,0:T(8,128)S(1)}, u32[]{:S(2)}, u32[]{:S(2)}) collective-permute-start(f32[1,3,3,1,16,128]{5,4,2,1,3,0:T(8,128)S(1)} %slice_bitcast_fusion.2), channel_id=1, source_target_pairs={{0,8},{8,16},{16,24},{24,32},{32,40},{40,48},{48,56},{56,64},{64,7... | collective-permute-start | bytes 221192 | tf_op jit(solution)/shard_map/ppermute | solution.py:57
  48.4 1.0 %collective-permute-start.6 = (f32[1,3,3,1,16,128]{5,4,2,1,3,0:T(8,128)S(1)}, f32[1,3,3,1,16,128]{5,4,2,1,3,0:T(8,128)S(1)}, u32[]{:S(2)}, u32[]{:S(2)}) collective-permute-start(f32[1,3,3,1,16,128]{5,4,2,1,3,0:T(8,128)S(1)} %slice_bitcast_fusion.1), channel_id=1, source_target_pairs={{0,120},{8,0},{16,8},{24,16},{32,24},{40,32},{48,40},{56,48},{64,5... | collective-permute-start | bytes 221192 | tf_op jit(solution)/shard_map/ppermute | solution.py:58
  49.4 0.7 copy.1310
  50.1 0.7 copy.1311
  51.0 1.2 %collective-permute-done.6 = f32[1,3,3,1,16,128]{5,4,2,1,3,0:T(8,128)S(1)} collective-permute-done((f32[1,3,3,1,16,128]{5,4,2,1,3,0:T(8,128)S(1)}, f32[1,3,3,1,16,128]{5,4,2,1,3,0:T(8,128)S(1)}, u32[]{:S(2)}, u32[]{:S(2)}) %collective-permute-start.6) | collective-permute-done | bytes 73760 | tf_op jit(solution)/shard_map/ppermute | solution.py:58
  52.5 3.4 %collective-permute-start.7 = (f32[2,1,3,3,4,1,128]{6,4,3,2,5,1,0:T(4,128)S(1)}, f32[2,1,3,3,4,1,128]{6,4,3,2,5,1,0:T(4,128)S(1)}, u32[]{:S(2)}, u32[]{:S(2)}) collective-permute-start(f32[2,1,3,3,4,1,128]{6,4,3,2,5,1,0:T(4,128)S(1)} %pad_maximum_fusion.15), channel_id=1, source_target_pairs={{0,4},{4,0},{1,5},{5,1},{2,6},{6,2},{3,7},{7,3},{8,12},{12,8},{9,1... | collective-permute-start | bytes 110600 | tf_op jit(solution)/shard_map/ppermute | solution.py:55
  55.9 0.1 copy.1278
  56.0 0.1 copy.1265
  56.1 0.1 copy.1275
  56.3 0.1 copy.1262
  56.8 0.6 collective-permute-done.7
  57.3 0.6 slice_bitcast_fusion.74
  58.3 1.2 %collective-permute-start.8 = (f32[1,3,3,16,4]{3,4,2,1,0:T(4,128)S(1)}, f32[1,3,3,16,4]{3,4,2,1,0:T(4,128)S(1)}, u32[]{:S(2)}, u32[]{:S(2)}) collective-permute-start(f32[1,3,3,16,4]{3,4,2,1,0:T(4,128)S(1)} %fusion.5), channel_id=1, source_target_pairs={{0,1},{1,2},{2,3},{3,0},{4,5},{5,6},{6,7},{7,4},{8,9},{9,10},{10,1... | collective-permute-start | bytes 6920 | tf_op jit(solution)/shard_map/ppermute | solution.py:57
  59.7 1.6 %collective-permute-start.9 = (f32[1,3,3,16,4]{3,4,2,1,0:T(4,128)S(1)}, f32[1,3,3,16,4]{3,4,2,1,0:T(4,128)S(1)}, u32[]{:S(2)}, u32[]{:S(2)}) collective-permute-start(f32[1,3,3,16,4]{3,4,2,1,0:T(4,128)S(1)} %fusion.4), channel_id=1, source_target_pairs={{0,3},{1,0},{2,1},{3,2},{4,7},{5,4},{6,5},{7,6},{8,11},{9,8},{10,9... | collective-permute-start | bytes 6920 | tf_op jit(solution)/shard_map/ppermute | solution.py:58
  61.4 1.0 %collective-permute-done.9 = f32[1,3,3,16,4]{3,4,2,1,0:T(4,128)S(1)} collective-permute-done((f32[1,3,3,16,4]{3,4,2,1,0:T(4,128)S(1)}, f32[1,3,3,16,4]{3,4,2,1,0:T(4,128)S(1)}, u32[]{:S(2)}, u32[]{:S(2)}) %collective-permute-start.9) | collective-permute-done | bytes 2336 | tf_op jit(solution)/shard_map/ppermute | solution.py:58
  62.4 0.7 copy.1287
  63.1 0.8 copy.1274
  63.9 4.2 %shard_map.88 = (f32[27,4,16,128]{3,2,1,0:T(8,128)}, f32[4,16,128]{2,1,0:T(8,128)}) custom-call(f32[27,4,16,128]{3,2,1,0:T(8,128)} %get-tuple-element.6.an_ref, f32[27,4,16,128]{3,2,1,0:T(8,128)} %f_ref.3, f32[9,16,128]{2,1,0:T(8,128)} %bitcast.439, f32[9,16,128]{2,1,0:T(8,128)} %bitcast.442, f32[9,4,128]{2,1,0:T(4,128)} %bitcast.488, ...), custom_call_target="tpu_custom_call" | custom-call | tf_op jit(solution)/shard_map/pallas_call | solution.py:291
  68.1 0.8 add_multiply_fusion
  69.0 0.1 reduce_sum.36
  69.4 21.9 %all_to_all.9 = f32[128,1,8]{2,1,0:T(1,128)S(1)} all-to-all(f32[128,1,8]{2,1,0:T(1,128)S(1)} %bitcast.460), channel_id=1, replica_groups=mesh['gx'=16,'gy'=2,'gz'=4] {'gx','gy','gz'}, dimensions={0} | all-to-all | bytes 8192 | tf_op jit(solution)/shard_map/all_to_all | solution.py:327
  91.3 0.7 reduce_sum.39
  (159 shorter events, 4.7 us)
Async XLA Ops:
  0.6 4.6 %copy-start.5 = (s32[4,16,128]{2,1,0:T(8,128)S(1)}, s32[4,16,128]{2,1,0:T(8,128)}, u32[]{:S(2)}) copy-start(s32[4,16,128]{2,1,0:T(8,128)} %param.10) | copy-start | bytes 98308
  5.8 7.4 %copy-start.2 = (f32[27,4,16,128]{3,2,1,0:T(8,128)S(1)}, f32[27,4,16,128]{3,2,1,0:T(8,128)}, u32[]{:S(2)}) copy-start(f32[27,4,16,128]{3,2,1,0:T(8,128)} %ae_ref.1) | copy-start | bytes 2654212
  8.8 4.5 %copy-start = (f32[27,4,16,128]{3,2,1,0:T(8,128)S(1)}, f32[27,4,16,128]{3,2,1,0:T(8,128)}, u32[]{:S(2)}) copy-start(f32[27,4,16,128]{3,2,1,0:T(8,128)} %shard_map.86.cf_ref) | copy-start | bytes 2654212
  10.0 10.2 %collective-permute-start = (f32[2,3,3,1,16,128]{5,4,2,1,3,0:T(8,128)S(1)}, f32[2,3,3,1,16,128]{5,4,2,1,3,0:T(8,128)S(1)}, u32[]{:S(2)}, u32[]{:S(2)}) collective-permute-start(f32[2,3,3,1,16,128]{5,4,2,1,3,0:T(8,128)S(1)} %pad_maximum_fusion.3), channel_id=1, source_target_pairs={{0,8},{8,16},{16,24},{24,32},{32,40},{40,48},{48,56},{56,64},{64,7... | collective-permute-start | bytes 442376 | tf_op jit(solution)/shard_map/ppermute | solution.py:57
  13.1 8.0 %collective-permute-start.1 = (f32[2,3,3,1,16,128]{5,4,2,1,3,0:T(8,128)S(1)}, f32[2,3,3,1,16,128]{5,4,2,1,3,0:T(8,128)S(1)}, u32[]{:S(2)}, u32[]{:S(2)}) collective-permute-start(f32[2,3,3,1,16,128]{5,4,2,1,3,0:T(8,128)S(1)} %pad_maximum_fusion.4), channel_id=1, source_target_pairs={{0,120},{8,0},{16,8},{24,16},{32,24},{40,32},{48,40},{56,48},{64,5... | collective-permute-start | bytes 442376 | tf_op jit(solution)/shard_map/ppermute | solution.py:58
  23.3 5.1 %collective-permute-start.2 = (f32[2,2,3,3,4,1,128]{6,4,3,2,1,5,0:T(4,128)S(1)}, f32[2,2,3,3,4,1,128]{6,4,3,2,1,5,0:T(4,128)S(1)}, u32[]{:S(2)}, u32[]{:S(2)}) collective-permute-start(f32[2,2,3,3,4,1,128]{6,4,3,2,1,5,0:T(4,128)S(1)} %pad_maximum_fusion.6), channel_id=1, source_target_pairs={{0,4},{4,0},{1,5},{5,1},{2,6},{6,2},{3,7},{7,3},{8,12},{12,8},{9,1... | collective-permute-start | bytes 221192 | tf_op jit(solution)/shard_map/ppermute | solution.py:55
  29.8 4.1 %collective-permute-start.3 = (f32[2,3,3,16,4]{3,4,2,1,0:T(4,128)S(1)}, f32[2,3,3,16,4]{3,4,2,1,0:T(4,128)S(1)}, u32[]{:S(2)}, u32[]{:S(2)}) collective-permute-start(f32[2,3,3,16,4]{3,4,2,1,0:T(4,128)S(1)} %pad_maximum_fusion.13), channel_id=1, source_target_pairs={{0,1},{1,2},{2,3},{3,0},{4,5},{5,6},{6,7},{7,4},{8,9},{9,10},{10,1... | collective-permute-start | bytes 13832 | tf_op jit(solution)/shard_map/ppermute | solution.py:57
  31.4 3.2 %collective-permute-start.4 = (f32[2,3,3,16,4]{3,4,2,1,0:T(4,128)S(1)}, f32[2,3,3,16,4]{3,4,2,1,0:T(4,128)S(1)}, u32[]{:S(2)}, u32[]{:S(2)}) collective-permute-start(f32[2,3,3,16,4]{3,4,2,1,0:T(4,128)S(1)} %pad_maximum_fusion.14), channel_id=1, source_target_pairs={{0,3},{1,0},{2,1},{3,2},{4,7},{5,4},{6,5},{7,6},{8,11},{9,8},{10,9... | collective-permute-start | bytes 13832 | tf_op jit(solution)/shard_map/ppermute | solution.py:58
  41.8 2.4 %copy-start.1 = (f32[27,4,16,128]{3,2,1,0:T(8,128)S(1)}, f32[27,4,16,128]{3,2,1,0:T(8,128)}, u32[]{:S(2)}) copy-start(f32[27,4,16,128]{3,2,1,0:T(8,128)} %get-tuple-element.6.an_ref) | copy-start | bytes 2654212
  44.6 7.6 %collective-permute-start.5 = (f32[1,3,3,1,16,128]{5,4,2,1,3,0:T(8,128)S(1)}, f32[1,3,3,1,16,128]{5,4,2,1,3,0:T(8,128)S(1)}, u32[]{:S(2)}, u32[]{:S(2)}) collective-permute-start(f32[1,3,3,1,16,128]{5,4,2,1,3,0:T(8,128)S(1)} %slice_bitcast_fusion.2), channel_id=1, source_target_pairs={{0,8},{8,16},{16,24},{24,32},{32,40},{40,48},{48,56},{56,64},{64,7... | collective-permute-start | bytes 221192 | tf_op jit(solution)/shard_map/ppermute | solution.py:57
  48.4 3.8 %collective-permute-start.6 = (f32[1,3,3,1,16,128]{5,4,2,1,3,0:T(8,128)S(1)}, f32[1,3,3,1,16,128]{5,4,2,1,3,0:T(8,128)S(1)}, u32[]{:S(2)}, u32[]{:S(2)}) collective-permute-start(f32[1,3,3,1,16,128]{5,4,2,1,3,0:T(8,128)S(1)} %slice_bitcast_fusion.1), channel_id=1, source_target_pairs={{0,120},{8,0},{16,8},{24,16},{32,24},{40,32},{48,40},{56,48},{64,5... | collective-permute-start | bytes 221192 | tf_op jit(solution)/shard_map/ppermute | solution.py:58
  52.2 11.7 %copy-start.4 = (f32[1,3,3,1,16,128]{5,4,2,1,3,0:T(8,128)}, f32[1,3,3,1,16,128]{5,4,2,1,3,0:T(8,128)S(1)}, u32[]{:S(2)}) copy-start(f32[1,3,3,1,16,128]{5,4,2,1,3,0:T(8,128)S(1)} %collective-permute-done.6) | copy-start | bytes 221188
  52.3 11.6 %copy-start.3 = (f32[1,3,3,1,16,128]{5,4,2,1,3,0:T(8,128)}, f32[1,3,3,1,16,128]{5,4,2,1,3,0:T(8,128)S(1)}, u32[]{:S(2)}) copy-start(f32[1,3,3,1,16,128]{5,4,2,1,3,0:T(8,128)S(1)} %collective-permute-done.5) | copy-start | bytes 221188
  52.5 4.8 %collective-permute-start.7 = (f32[2,1,3,3,4,1,128]{6,4,3,2,5,1,0:T(4,128)S(1)}, f32[2,1,3,3,4,1,128]{6,4,3,2,5,1,0:T(4,128)S(1)}, u32[]{:S(2)}, u32[]{:S(2)}) collective-permute-start(f32[2,1,3,3,4,1,128]{6,4,3,2,5,1,0:T(4,128)S(1)} %pad_maximum_fusion.15), channel_id=1, source_target_pairs={{0,4},{4,0},{1,5},{5,1},{2,6},{6,2},{3,7},{7,3},{8,12},{12,8},{9,1... | collective-permute-start | bytes 110600 | tf_op jit(solution)/shard_map/ppermute | solution.py:55
  56.5 11.6 %copy-start.6 = (f32[4,16,128]{2,1,0:T(8,128)S(1)}, f32[4,16,128]{2,1,0:T(8,128)}, u32[]{:S(2)}) copy-start(f32[4,16,128]{2,1,0:T(8,128)} %get-tuple-element.8) | copy-start | bytes 98308
  58.3 4.8 %collective-permute-start.8 = (f32[1,3,3,16,4]{3,4,2,1,0:T(4,128)S(1)}, f32[1,3,3,16,4]{3,4,2,1,0:T(4,128)S(1)}, u32[]{:S(2)}, u32[]{:S(2)}) collective-permute-start(f32[1,3,3,16,4]{3,4,2,1,0:T(4,128)S(1)} %fusion.5), channel_id=1, source_target_pairs={{0,1},{1,2},{2,3},{3,0},{4,5},{5,6},{6,7},{7,4},{8,9},{9,10},{10,1... | collective-permute-start | bytes 6920 | tf_op jit(solution)/shard_map/ppermute | solution.py:57
  59.7 2.7 %collective-permute-start.9 = (f32[1,3,3,16,4]{3,4,2,1,0:T(4,128)S(1)}, f32[1,3,3,16,4]{3,4,2,1,0:T(4,128)S(1)}, u32[]{:S(2)}, u32[]{:S(2)}) collective-permute-start(f32[1,3,3,16,4]{3,4,2,1,0:T(4,128)S(1)} %fusion.4), channel_id=1, source_target_pairs={{0,3},{1,0},{2,1},{3,2},{4,7},{5,4},{6,5},{7,6},{8,11},{9,8},{10,9... | collective-permute-start | bytes 6920 | tf_op jit(solution)/shard_map/ppermute | solution.py:58

commit v8 on v5

--- a/solution.py
+++ b/solution.py
@@ -105,22 +105,18 @@
         z_up.append(jnp.swapaxes(lax.index_in_dim(picked[0], 1 + s, axis=2, keepdims=False)[..., 0], -1, -2))
         z_dn.append(jnp.swapaxes(lax.index_in_dim(picked[1], 1 - s, axis=2, keepdims=False)[..., 0], -1, -2))
     zlo, zhi = halo_exchange(jnp.stack(z_up), jnp.stack(z_dn), "gz")
-    out = []
-    for k in range(len(cubes)):
-        out.append(
-            (
-                xlo[k].reshape(9, sy, sz),
-                xhi[k].reshape(9, sy, sz),
-                ylo[k].reshape(9, sx, sz),
-                yhi[k].reshape(9, sx, sz),
-                zlo[k].reshape(9, sy, sx),
-                zhi[k].reshape(9, sy, sx),
-            )
-        )
-    return out
-
-
-def move_into(dst, src, hal, sign):
+    nf = len(cubes)
+    return (
+        xlo.reshape(nf * 9, sy, sz),
+        xhi.reshape(nf * 9, sy, sz),
+        ylo.reshape(nf * 9, sx, sz),
+        yhi.reshape(nf * 9, sx, sz),
+        zlo.reshape(nf * 9, sy, sx),
+        zhi.reshape(nf * 9, sy, sx),
+    )
+
+
+def move_into(dst, src, hal, sign, base):
     xlo, xhi, ylo, yhi, zlo, zhi = hal
     _, sx, sy, sz = src.shape
     rows = lax.broadcasted_iota(jnp.int32, (sy, sz), 0)
@@ -129,21 +125,21 @@
         cx, cy, cz = (int(v) for v in STEPS[q])
         vx, vy, vz = sign * cx, sign * cy, sign * cz
         if vz == 1:
-            zcol = zlo[(cx + 1) * 3 + cy + 1]
+            zcol = zlo[base + (cx + 1) * 3 + cy + 1]
         elif vz == -1:
-            zcol = zhi[(cx + 1) * 3 + cy + 1]
+            zcol = zhi[base + (cx + 1) * 3 + cy + 1]
         for i in range(sx):
             j = i - vx
             if j < 0:
-                t = xlo[(cy + 1) * 3 + cz + 1]
+                t = xlo[base + (cy + 1) * 3 + cz + 1]
             elif j >= sx:
-                t = xhi[(cy + 1) * 3 + cz + 1]
+                t = xhi[base + (cy + 1) * 3 + cz + 1]
             else:
                 t = src[q, j]
             if vy == 1:
-                t = jnp.where(rows == 0, ylo[(cx + 1) * 3 + cz + 1, pl.ds(i, 1), :], pltpu.roll(t, 1, 0))
+                t = jnp.where(rows == 0, ylo[base + (cx + 1) * 3 + cz + 1, pl.ds(i, 1), :], pltpu.roll(t, 1, 0))
             elif vy == -1:
-                t = jnp.where(rows == sy - 1, yhi[(cx + 1) * 3 + cz + 1, pl.ds(i, 1), :], pltpu.roll(t, sy - 1, 0))
+                t = jnp.where(rows == sy - 1, yhi[base + (cx + 1) * 3 + cz + 1, pl.ds(i, 1), :], pltpu.roll(t, sy - 1, 0))
             if vz == 1:
                 t = jnp.where(lanes == 0, zcol[:, i : i + 1], pltpu.roll(t, 1, 1))
             elif vz == -1:
@@ -227,18 +223,17 @@
 
 
 def next_kernel(cf_ref, ae_ref, *refs):
-    hal_f = refs[0:6]
-    hal_a = refs[6:12]
-    rate_ref, gamma_ref, out_ref, sens_ref, fs, as_ = refs[12:]
-    move_into(fs, cf_ref, hal_f, 1)
-    move_into(as_, ae_ref, hal_a, -1)
+    hal = refs[0:6]
+    rate_ref, gamma_ref, out_ref, sens_ref, fs, as_ = refs[6:]
+    move_into(fs, cf_ref, hal, 1, 0)
+    move_into(as_, ae_ref, hal, -1, 9)
     chunked_adjoint(fs, as_, rate_ref, gamma_ref, out_ref, sens_ref)
 
 
 def now_kernel(an_ref, f_ref, *refs):
     hal = refs[0:6]
     rate_ref, gamma_ref, out_ref, sens_ref, as_ = refs[6:]
-    move_into(as_, an_ref, hal, -1)
+    move_into(as_, an_ref, hal, -1, 0)
     chunked_adjoint(f_ref, as_, rate_ref, gamma_ref, out_ref, sens_ref)
 
 
@@ -263,12 +258,12 @@
     walls = wall_flag.astype(jnp.float32)
     gamma = walls * solid
     post_now, _ = collide(check_pops, relax_rate, gamma)
-    hal_f, hal_a = halos([post_now, adjoint_end], [1, -1])
+    hal = halos([post_now, adjoint_end], [1, -1])
     shape = check_pops.shape
     adj_next, sens_next = run_stage(
-        next_kernel, (post_now, adjoint_end) + hal_f + hal_a + (relax_rate, gamma), shape, 2
-    )
-    (hal_n,) = halos([adj_next], [-1])
+        next_kernel, (post_now, adjoint_end) + hal + (relax_rate, gamma), shape, 2
+    )
+    hal_n = halos([adj_next], [-1])
     adjoint_start, sens_now = run_stage(now_kernel, (adj_next, check_pops) + hal_n + (relax_rate, gamma), shape, 1)
     density = walls * (sens_next + sens_now)
     boxes = density.reshape(sx, 2, sy // 2, 2, sz // 2).sum(axis=(2, 4))

time: 92.4 us -> 89.1 us (0.964)
  local copies, waits for them, and re-layouts: 21.7 us -> 19 us
    slice x6 -> x1, local copies, waits for them, and re-layouts: 3.04 us -> 0.64 us  [halo_exchange(): return (both[0], both[1])]
    squeeze x0 -> x3, local copies, waits for them, and re-layouts: none -> 1.88 us  [the longest x1 0.93 us: halos(): xhi[k][:, :, :, sy - 1:sy]]
    slice x2 -> x1, local copies, waits for them, and re-layouts: 1.62 us -> 0.01 us  [halos(): xlo[k][:, :, :, sy - 1:sy]]
    slice x2 -> x1, local copies, waits for them, and re-layouts: 1.61 us -> 0.01 us  [halos(): xhi[k][:, :, :, sy - 1:sy]]
  transfers between devices with their start and end apart: 10 -> 10, of which waited for: 8 -> 7; matrix products, arithmetic and copies ran while one was open for 15% -> 15% of each run, Pallas kernels for 0% -> 0%
where the time goes in v8:
time: 89.1 us; the launch traced here: 88.6 us
  blocking collectives  20.1 us (23%)
  local copies, waits for them, and re-layouts  19 us (21%)
  starting transfers between devices  18.8 us (21%)
  other arithmetic  12.5 us (14%)
  Pallas kernels  9.08 us (10%)
  waiting for transfers between devices  7.36 us (8%)
  between operations  1.7 us (2%)
    all_to_all x1, blocking collectives, shards(): lax.all_to_all(placed.reshape(devices, count // devices), ('gx', 'gy', 'g...  20.1 us
    pallas_call x2, Pallas kernels, run_stage(): pl.pallas_call(kernel, out_shape=(jax.ShapeDtypeStruct(shape, jnp.float32...  9.08 us
    ppermute x2, starting transfers between devices, halo_exchange(): both = lax.ppermute(jnp.stack([up, down]), axis, [(0, 1), (1, 0)])  6.77 us
    ppermute x4, starting transfers between devices, halo_exchange(): hi = lax.ppermute(down, axis, [(i, (i - 1) % size) for i in range(size)])  6.28 us
    ppermute x4, starting transfers between devices, halo_exchange(): lo = lax.ppermute(up, axis, [(i, (i + 1) % size) for i in range(size)])  5.71 us
    ppermute x4, waiting for transfers between devices, halo_exchange(): lo = lax.ppermute(up, axis, [(i, (i + 1) % size) for i in range(size)])  3.81 us
    slice x3, local copies, waits for them, and re-layouts, halos(): cols = jnp.concatenate([both[..., sz - 1:sz], both[..., 0:1]], axis=6)  3.61 us
    ppermute x4, waiting for transfers between devices, halo_exchange(): hi = lax.ppermute(down, axis, [(i, (i - 1) % size) for i in range(size)])  2.27 us
  transfers between devices with their start and end apart: 10, of which 7 were waited for; matrix products, arithmetic and copies ran while one was open for 15% of the time, Pallas kernels for 0%

profile of v8, /device:TPU:1, one launch (start us, length us, event | category | flops | bytes accessed | tf_op | source)
XLA Modules:
  0.0 88.6 jit_solution(11653943712861495842)
XLA Ops:
  0.7 1.2 %slice_reduce_fusion.2 = (f32[4,16,128]{2,1,0:T(8,128)S(1)}, f32[4,16,128]{2,1,0:T(8,128)S(1)}) fusion(f32[3,3,3,4,16,128]{5,4,3,2,1,0:T(8,128)} %bitcast.426), kind=kLoop, calls=%fused_computation.14 | loop fusion | flops 131072 | bytes 655360 | tf_op jit(solution)/shard_map/reduce_sum | solution.py:33
  1.9 1.1 %slice_reduce_fusion = (f32[4,16,128]{2,1,0:T(8,128)S(1)}, f32[4,16,128]{2,1,0:T(8,128)S(1)}) fusion(f32[3,3,3,4,16,128]{5,4,3,2,1,0:T(8,128)} %bitcast.427), kind=kLoop, calls=%fused_computation.12 | loop fusion | flops 131072 | bytes 655360 | tf_op jit(solution)/shard_map/reduce_sum | solution.py:34
  3.0 1.1 %slice_reduce_fusion.4 = (f32[4,16,128]{2,1,0:T(8,128)S(1)}, f32[4,16,128]{2,1,0:T(8,128)S(1)}) fusion(f32[27,4,16,128]{3,2,1,0:T(8,128)} %f_ref.1), kind=kLoop, calls=%fused_computation.16 | loop fusion | flops 131072 | bytes 655360 | tf_op jit(solution)/shard_map/reduce_sum | solution.py:32
  4.2 0.2 copy.1155
  4.4 0.8 slice.648
  5.3 0.6 gather_fusion
  5.9 0.1 copy.1256
  6.1 0.1 reshape.123
  6.4 1.4 %fusion.7.cf_ref = f32[27,4,16,128]{3,2,1,0:T(8,128)S(1)} fusion(f32[27,4,16,128]{3,2,1,0:T(8,128)S(1)} %copy-done, f32[4,16,128]{2,1,0:T(8,128)S(1)} %get-tuple-element.148.refs_7_, f32[4,16,128]{2,1,0:T(8,128)S(1)} %get-tuple-element.18, f32[4,16,128]{2,1,0:T(8,128)S(1)} %get-tuple-element.21, f32[27]{0:T(128)S(1)} %copy-done.18, ...), kind=kLoop, calls=%fused_computation.11 | loop fusion | flops 4202496 | bytes 2032048 | tf_op jit(solution)/shard_map/add | solution.py:47
  8.0 0.8 pad_maximum_fusion.4
  8.8 1.4 %collective-permute-start.1 = (f32[2,3,3,1,16,128]{5,4,2,1,3,0:T(8,128)}, f32[2,3,3,1,16,128]{5,4,2,1,3,0:T(8,128)}, u32[]{:S(2)}, u32[]{:S(2)}) collective-permute-start(f32[2,3,3,1,16,128]{5,4,2,1,3,0:T(8,128)} %pad_maximum_fusion.4), channel_id=1, source_target_pairs={{0,120},{8,0},{16,8},{24,16},{32,24},{40,32},{48,40},{56,48},{64,5... | collective-permute-start | bytes 442376 | tf_op jit(solution)/shard_map/ppermute | solution.py:58
  10.1 0.7 pad_maximum_fusion.3
  10.8 1.6 %collective-permute-start = (f32[2,3,3,1,16,128]{5,4,2,1,3,0:T(8,128)}, f32[2,3,3,1,16,128]{5,4,2,1,3,0:T(8,128)}, u32[]{:S(2)}, u32[]{:S(2)}) collective-permute-start(f32[2,3,3,1,16,128]{5,4,2,1,3,0:T(8,128)} %pad_maximum_fusion.3), channel_id=1, source_target_pairs={{0,8},{8,16},{16,24},{24,32},{32,40},{40,48},{48,56},{56,64},{64,7... | collective-permute-start | bytes 442376 | tf_op jit(solution)/shard_map/ppermute | solution.py:57
  12.5 1.9 %slice_maximum_fusion = (f32[2,3,3,3,4,16,1]{6,5,4,3,2,1,0:T(8,128)S(1)}, f32[2,3,3,3,4,16,1]{6,5,4,3,2,1,0:T(8,128)}) fusion(f32[1,3,3,3,4,16,128]{6,5,4,3,2,1,0:T(8,128)S(1)} %bitcast.432, f32[1,3,3,3,4,16,128]{6,5,4,3,2,1,0:T(8,128)S(1)} %bitcast.428), kind=kLoop, calls=%fused_computation.2 | loop fusion | flops 6912 | bytes 1797120 | tf_op jit(solution)/shard_map/stack | solution.py:87
  14.3 0.8 fusion.8
  15.2 2.0 %copy.1179 = f32[2,3,3,3,4,16,1]{5,4,6,3,2,1,0:T(4,128)} copy(f32[2,3,3,3,4,16,1]{6,5,4,3,2,1,0:T(8,128)S(1)} %get-tuple-element.22) | data formatting | bytes 27648 | tf_op jit(solution)/shard_map/slice | solution.py:89
  17.1 1.3 %copy.1180 = f32[2,3,3,3,4,16,1]{5,4,6,3,2,1,0:T(4,128)S(1)} copy(f32[2,3,3,3,4,16,1]{6,5,4,3,2,1,0:T(8,128)S(1)} %copy-done.4) | data formatting | bytes 27648 | tf_op jit(solution)/shard_map/slice | solution.py:89
  19.0 0.1 copy.1277
  19.1 0.1 copy.1278
  19.3 0.9 %slice_bitcast_fusion.6 = (f32[3,3,1,16,128]{4,3,1,0,2:T(8,128)S(1)}, f32[3,3,1,16,128]{4,3,1,0,2:T(8,128)S(1)}) fusion(f32[2,3,3,1,16,128]{5,4,2,1,3,0:T(8,128)} %collective-permute-done.1), kind=kLoop, calls=%fused_computation.38 | loop fusion | bytes 294912 | tf_op jit(solution)/shard_map/squeeze | solution.py:92
  20.4 0.9 %slice_bitcast_fusion.5 = (f32[3,3,1,16,128]{4,3,1,0,2:T(8,128)S(1)}, f32[3,3,1,16,128]{4,3,1,0,2:T(8,128)S(1)}) fusion(f32[2,3,3,1,16,128]{5,4,2,1,3,0:T(8,128)} %collective-permute-done), kind=kLoop, calls=%fused_computation.37 | loop fusion | bytes 294912 | tf_op jit(solution)/shard_map/squeeze | solution.py:92
  21.6 0.1 copy.1198
  21.7 0.1 copy.1199
  22.2 3.4 %collective-permute-start.2 = (f32[2,2,3,3,4,1,128]{6,4,3,2,1,5,0:T(4,128)S(1)}, f32[2,2,3,3,4,1,128]{6,4,3,2,1,5,0:T(4,128)S(1)}, u32[]{:S(2)}, u32[]{:S(2)}) collective-permute-start(f32[2,2,3,3,4,1,128]{6,4,3,2,1,5,0:T(4,128)S(1)} %pad_maximum_fusion.6), channel_id=1, source_target_pairs={{0,4},{4,0},{1,5},{5,1},{2,6},{6,2},{3,7},{7,3},{8,12},{12,8},{9,1... | collective-permute-start | bytes 221192 | tf_op jit(solution)/shard_map/ppermute | solution.py:55
  25.6 0.1 copy.1206
  25.7 0.1 copy.1207
  26.0 0.1 copy.1181
  26.1 0.1 copy.1182
  26.3 0.1 copy.1189
  26.4 0.1 copy.1190
  26.9 0.4 collective-permute-done.2
  28.1 2.5 %collective-permute-start.4 = (f32[2,3,3,16,4]{3,4,2,1,0:T(4,128)S(1)}, f32[2,3,3,16,4]{3,4,2,1,0:T(4,128)S(1)}, u32[]{:S(2)}, u32[]{:S(2)}) collective-permute-start(f32[2,3,3,16,4]{3,4,2,1,0:T(4,128)S(1)} %pad_maximum_fusion.14), channel_id=1, source_target_pairs={{0,3},{1,0},{2,1},{3,2},{4,7},{5,4},{6,5},{7,6},{8,11},{9,8},{10,9... | collective-permute-start | bytes 13832 | tf_op jit(solution)/shard_map/ppermute | solution.py:58
  31.1 0.6 fusion.36
  31.7 0.8 copy.1214
  32.6 2.5 %collective-permute-done.3 = f32[2,3,3,16,4]{3,4,2,1,0:T(4,128)S(1)} collective-permute-done((f32[2,3,3,16,4]{3,4,2,1,0:T(4,128)S(1)}, f32[2,3,3,16,4]{3,4,2,1,0:T(4,128)S(1)}, u32[]{:S(2)}, u32[]{:S(2)}) %collective-permute-start.3) | collective-permute-done | bytes 4640 | tf_op jit(solution)/shard_map/ppermute | solution.py:57
  35.1 0.8 copy.1197
  35.9 4.8 %shard_map.122 = (f32[27,4,16,128]{3,2,1,0:T(8,128)}, f32[4,16,128]{2,1,0:T(8,128)}) custom-call(f32[27,4,16,128]{3,2,1,0:T(8,128)} %copy-done.1, f32[27,4,16,128]{3,2,1,0:T(8,128)} %ae_ref.1, f32[18,16,128]{2,1,0:T(8,128)} %bitcast.9.refs_0_, f32[18,16,128]{2,1,0:T(8,128)} %bitcast.14.refs_1_, f32[18,4,128]{2,1,0:T(4,128)} %bitcast.455, ...), custom_call_target="tpu_custom_call" | custom-call | tf_op jit(solution)/shard_map/pallas_call | solution.py:242
  40.8 1.2 %fusion.25 = (f32[9,4,16,128]{3,2,1,0:T(8,128)S(1)}, f32[9,4,16,128]{3,2,1,0:T(8,128)S(1)}) fusion(f32[27,4,16,128]{3,2,1,0:T(8,128)} %get-tuple-element.6.an_ref), kind=kLoop, calls=%fused_computation.215 | loop fusion | bytes 1179648 | tf_op jit(solution)/shard_map/slice | solution.py:78
  42.0 0.2 copy-done.2
  42.1 0.3 fusion.23
  42.5 0.7 copy.1275
  43.2 0.7 copy.1276
  44.0 2.8 %collective-permute-start.5 = (f32[1,3,3,1,16,128]{5,4,2,1,3,0:T(8,128)S(1)}, f32[1,3,3,1,16,128]{5,4,2,1,3,0:T(8,128)S(1)}, u32[]{:S(2)}, u32[]{:S(2)}) collective-permute-start(f32[1,3,3,1,16,128]{5,4,2,1,3,0:T(8,128)S(1)} %slice_bitcast_fusion.2), channel_id=1, source_target_pairs={{0,8},{8,16},{16,24},{24,32},{32,40},{40,48},{48,56},{56,64},{64,7... | collective-permute-start | bytes 221192 | tf_op jit(solution)/shard_map/ppermute | solution.py:57
  46.9 1.9 %collective-permute-start.6 = (f32[1,3,3,1,16,128]{5,4,2,1,3,0:T(8,128)S(1)}, f32[1,3,3,1,16,128]{5,4,2,1,3,0:T(8,128)S(1)}, u32[]{:S(2)}, u32[]{:S(2)}) collective-permute-start(f32[1,3,3,1,16,128]{5,4,2,1,3,0:T(8,128)S(1)} %slice_bitcast_fusion.1), channel_id=1, source_target_pairs={{0,120},{8,0},{16,8},{24,16},{32,24},{40,32},{48,40},{56,48},{64,5... | collective-permute-start | bytes 221192 | tf_op jit(solution)/shard_map/ppermute | solution.py:58
  48.9 0.5 collective-permute-done.5
  49.5 1.2 %collective-permute-done.6 = f32[1,3,3,1,16,128]{5,4,2,1,3,0:T(8,128)S(1)} collective-permute-done((f32[1,3,3,1,16,128]{5,4,2,1,3,0:T(8,128)S(1)}, f32[1,3,3,1,16,128]{5,4,2,1,3,0:T(8,128)S(1)}, u32[]{:S(2)}, u32[]{:S(2)}) %collective-permute-start.6) | collective-permute-done | bytes 73760 | tf_op jit(solution)/shard_map/ppermute | solution.py:58
  50.8 0.1 copy.1240
  50.9 0.1 copy.1243
  51.3 3.4 %collective-permute-start.7 = (f32[2,1,3,3,4,1,128]{6,4,3,2,5,1,0:T(4,128)S(1)}, f32[2,1,3,3,4,1,128]{6,4,3,2,5,1,0:T(4,128)S(1)}, u32[]{:S(2)}, u32[]{:S(2)}) collective-permute-start(f32[2,1,3,3,4,1,128]{6,4,3,2,5,1,0:T(4,128)S(1)} %pad_maximum_fusion.15), channel_id=1, source_target_pairs={{0,4},{4,0},{1,5},{5,1},{2,6},{6,2},{3,7},{7,3},{8,12},{12,8},{9,1... | collective-permute-start | bytes 110600 | tf_op jit(solution)/shard_map/ppermute | solution.py:55
  54.8 0.1 copy.1227
  54.9 0.1 copy.1230
  55.2 0.9 collective-permute-done.7
  56.0 0.6 slice_bitcast_fusion.82
  57.0 0.4 collective-permute-start.9
  57.6 1.2 %collective-permute-start.8 = (f32[1,3,3,16,4]{3,4,2,1,0:T(4,128)S(1)}, f32[1,3,3,16,4]{3,4,2,1,0:T(4,128)S(1)}, u32[]{:S(2)}, u32[]{:S(2)}) collective-permute-start(f32[1,3,3,16,4]{3,4,2,1,0:T(4,128)S(1)} %fusion.13), channel_id=1, source_target_pairs={{0,1},{1,2},{2,3},{3,0},{4,5},{5,6},{6,7},{7,4},{8,9},{9,10},{10,1... | collective-permute-start | bytes 6920 | tf_op jit(solution)/shard_map/ppermute | solution.py:57
  58.9 1.1 %collective-permute-done.9 = f32[1,3,3,16,4]{3,4,2,1,0:T(4,128)S(1)} collective-permute-done((f32[1,3,3,16,4]{3,4,2,1,0:T(4,128)S(1)}, f32[1,3,3,16,4]{3,4,2,1,0:T(4,128)S(1)}, u32[]{:S(2)}, u32[]{:S(2)}) %collective-permute-start.9) | collective-permute-done | bytes 2336 | tf_op jit(solution)/shard_map/ppermute | solution.py:58
  60.0 0.8 copy.1252
  60.7 0.7 collective-permute-done.8
  61.5 0.7 copy.1239
  62.2 4.2 %shard_map.123 = (f32[27,4,16,128]{3,2,1,0:T(8,128)}, f32[4,16,128]{2,1,0:T(8,128)}) custom-call(f32[27,4,16,128]{3,2,1,0:T(8,128)} %get-tuple-element.6.an_ref, f32[27,4,16,128]{3,2,1,0:T(8,128)} %f_ref.1, f32[9,16,128]{2,1,0:T(8,128)} %bitcast.436, f32[9,16,128]{2,1,0:T(8,128)} %bitcast.439, f32[9,4,128]{2,1,0:T(4,128)} %bitcast.477, ...), custom_call_target="tpu_custom_call" | custom-call | tf_op jit(solution)/shard_map/pallas_call | solution.py:242
  66.5 0.8 add_multiply_fusion
  67.4 0.1 reduce_sum.106
  67.8 20.1 %all_to_all.9 = f32[128,1,8]{2,1,0:T(1,128)S(1)} all-to-all(f32[128,1,8]{2,1,0:T(1,128)S(1)} %bitcast.451), channel_id=1, replica_groups=mesh['gx'=16,'gy'=2,'gz'=4] {'gx','gy','gz'}, dimensions={0} | all-to-all | bytes 8192 | tf_op jit(solution)/shard_map/all_to_all | solution.py:276
  87.9 0.7 reduce_sum.109
  (189 shorter events, 5.0 us)
Async XLA Ops:
  0.6 5.6 %copy-start = (f32[27,4,16,128]{3,2,1,0:T(8,128)S(1)}, f32[27,4,16,128]{3,2,1,0:T(8,128)}, u32[]{:S(2)}) copy-start(f32[27,4,16,128]{3,2,1,0:T(8,128)} %f_ref.1) | copy-start | bytes 2654212
  0.6 3.5 %copy-start.14 = (s32[1024]{0:T(1024)S(1)}, s32[1024]{0:T(1024)}, u32[]{:S(2)}) copy-start(s32[1024]{0:T(1024)} %param.17) | copy-start | bytes 12292
  0.7 3.5 %copy-start.15 = (f32[1024]{0:T(1024)S(1)}, f32[1024]{0:T(1024)}, u32[]{:S(2)}) copy-start(f32[1024]{0:T(1024)} %param.16) | copy-start | bytes 12292
  0.7 5.6 %copy-start.11 = (s32[4,16,128]{2,1,0:T(8,128)S(1)}, s32[4,16,128]{2,1,0:T(8,128)}, u32[]{:S(2)}) copy-start(s32[4,16,128]{2,1,0:T(8,128)} %param.14) | copy-start | bytes 98308
  1.8 4.5 %copy-start.10 = (f32[4,16,128]{2,1,0:T(8,128)S(1)}, f32[4,16,128]{2,1,0:T(8,128)}, u32[]{:S(2)}) copy-start(f32[4,16,128]{2,1,0:T(8,128)} %refs_6_.3) | copy-start | bytes 98308
  1.9 4.5 %copy-start.16 = (f32[27]{0:T(128)S(1)}, f32[27]{0:T(128)}, u32[]{:S(2)}) copy-start(f32[27]{0:T(128)} %constant.24.clone) | copy-start | bytes 328
  1.9 4.5 %copy-start.17 = (f32[27]{0:T(128)S(1)}, f32[27]{0:T(128)}, u32[]{:S(2)}) copy-start(f32[27]{0:T(128)} %constant.25.clone) | copy-start | bytes 328
  1.9 4.5 %copy-start.18 = (f32[27]{0:T(128)S(1)}, f32[27]{0:T(128)}, u32[]{:S(2)}) copy-start(f32[27]{0:T(128)} %constant.26.clone) | copy-start | bytes 328
  1.9 4.5 %copy-start.19 = (f32[27]{0:T(128)S(1)}, f32[27]{0:T(128)}, u32[]{:S(2)}) copy-start(f32[27]{0:T(128)} %constant.27.clone) | copy-start | bytes 328
  6.3 1.6 %copy-start.8 = (f32[4,16,128]{2,1,0:T(8,128)}, f32[4,16,128]{2,1,0:T(8,128)S(1)}, u32[]{:S(2)}) copy-start(f32[4,16,128]{2,1,0:T(8,128)S(1)} %get-tuple-element.148.refs_7_) | copy-start | bytes 98308
  6.4 1.5 %copy-start.3 = (f32[27,4,16,128]{3,2,1,0:T(8,128)S(1)}, f32[27,4,16,128]{3,2,1,0:T(8,128)}, u32[]{:S(2)}) copy-start(f32[27,4,16,128]{3,2,1,0:T(8,128)} %ae_ref.1) | copy-start | bytes 2654212
  7.8 6.5 %copy-start.1 = (f32[27,4,16,128]{3,2,1,0:T(8,128)}, f32[27,4,16,128]{3,2,1,0:T(8,128)S(1)}, u32[]{:S(2)}) copy-start(f32[27,4,16,128]{3,2,1,0:T(8,128)S(1)} %fusion.7.cf_ref) | copy-start | bytes 2654212
  8.8 10.6 %collective-permute-start.1 = (f32[2,3,3,1,16,128]{5,4,2,1,3,0:T(8,128)}, f32[2,3,3,1,16,128]{5,4,2,1,3,0:T(8,128)}, u32[]{:S(2)}, u32[]{:S(2)}) collective-permute-start(f32[2,3,3,1,16,128]{5,4,2,1,3,0:T(8,128)} %pad_maximum_fusion.4), channel_id=1, source_target_pairs={{0,120},{8,0},{16,8},{24,16},{32,24},{40,32},{48,40},{56,48},{64,5... | collective-permute-start | bytes 442376 | tf_op jit(solution)/shard_map/ppermute | solution.py:58
  10.8 9.5 %collective-permute-start = (f32[2,3,3,1,16,128]{5,4,2,1,3,0:T(8,128)}, f32[2,3,3,1,16,128]{5,4,2,1,3,0:T(8,128)}, u32[]{:S(2)}, u32[]{:S(2)}) collective-permute-start(f32[2,3,3,1,16,128]{5,4,2,1,3,0:T(8,128)} %pad_maximum_fusion.3), channel_id=1, source_target_pairs={{0,8},{8,16},{16,24},{24,32},{32,40},{40,48},{48,56},{56,64},{64,7... | collective-permute-start | bytes 442376 | tf_op jit(solution)/shard_map/ppermute | solution.py:57
  15.2 2.0 %copy-start.4 = (f32[2,3,3,3,4,16,1]{6,5,4,3,2,1,0:T(8,128)S(1)}, f32[2,3,3,3,4,16,1]{6,5,4,3,2,1,0:T(8,128)}, u32[]{:S(2)}) copy-start(f32[2,3,3,3,4,16,1]{6,5,4,3,2,1,0:T(8,128)} %get-tuple-element.23) | copy-start | bytes 41476
  17.1 1.3 %copy-start.9 = (f32[2,3,3,3,4,16,1]{5,4,6,3,2,1,0:T(4,128)S(1)}, f32[2,3,3,3,4,16,1]{5,4,6,3,2,1,0:T(4,128)}, u32[]{:S(2)}) copy-start(f32[2,3,3,3,4,16,1]{5,4,6,3,2,1,0:T(4,128)} %copy.1179) | copy-start | bytes 41476
  17.1 1.5 %copy-start.5 = (f32[2,3,3,3,4,2,128]{6,5,4,3,2,1,0:T(2,128)S(1)}, f32[2,3,3,3,4,2,128]{6,5,4,3,2,1,0:T(2,128)}, u32[]{:S(2)}) copy-start(f32[2,3,3,3,4,2,128]{6,5,4,3,2,1,0:T(2,128)} %fusion.8) | copy-start | bytes 663556
  22.2 5.1 %collective-permute-start.2 = (f32[2,2,3,3,4,1,128]{6,4,3,2,1,5,0:T(4,128)S(1)}, f32[2,2,3,3,4,1,128]{6,4,3,2,1,5,0:T(4,128)S(1)}, u32[]{:S(2)}, u32[]{:S(2)}) collective-permute-start(f32[2,2,3,3,4,1,128]{6,4,3,2,1,5,0:T(4,128)S(1)} %pad_maximum_fusion.6), channel_id=1, source_target_pairs={{0,4},{4,0},{1,5},{5,1},{2,6},{6,2},{3,7},{7,3},{8,12},{12,8},{9,1... | collective-permute-start | bytes 221192 | tf_op jit(solution)/shard_map/ppermute | solution.py:55
  28.1 3.7 %collective-permute-start.4 = (f32[2,3,3,16,4]{3,4,2,1,0:T(4,128)S(1)}, f32[2,3,3,16,4]{3,4,2,1,0:T(4,128)S(1)}, u32[]{:S(2)}, u32[]{:S(2)}) collective-permute-start(f32[2,3,3,16,4]{3,4,2,1,0:T(4,128)S(1)} %pad_maximum_fusion.14), channel_id=1, source_target_pairs={{0,3},{1,0},{2,1},{3,2},{4,7},{5,4},{6,5},{7,6},{8,11},{9,8},{10,9... | collective-permute-start | bytes 13832 | tf_op jit(solution)/shard_map/ppermute | solution.py:58
  31.0 4.1 %collective-permute-start.3 = (f32[2,3,3,16,4]{3,4,2,1,0:T(4,128)S(1)}, f32[2,3,3,16,4]{3,4,2,1,0:T(4,128)S(1)}, u32[]{:S(2)}, u32[]{:S(2)}) collective-permute-start(f32[2,3,3,16,4]{3,4,2,1,0:T(4,128)S(1)} %pad_maximum_fusion.13), channel_id=1, source_target_pairs={{0,1},{1,2},{2,3},{3,0},{4,5},{5,6},{6,7},{7,4},{8,9},{9,10},{10,1... | collective-permute-start | bytes 13832 | tf_op jit(solution)/shard_map/ppermute | solution.py:57
  40.8 1.3 %copy-start.2 = (f32[27,4,16,128]{3,2,1,0:T(8,128)S(1)}, f32[27,4,16,128]{3,2,1,0:T(8,128)}, u32[]{:S(2)}) copy-start(f32[27,4,16,128]{3,2,1,0:T(8,128)} %get-tuple-element.6.an_ref) | copy-start | bytes 2654212
  44.0 5.4 %collective-permute-start.5 = (f32[1,3,3,1,16,128]{5,4,2,1,3,0:T(8,128)S(1)}, f32[1,3,3,1,16,128]{5,4,2,1,3,0:T(8,128)S(1)}, u32[]{:S(2)}, u32[]{:S(2)}) collective-permute-start(f32[1,3,3,1,16,128]{5,4,2,1,3,0:T(8,128)S(1)} %slice_bitcast_fusion.2), channel_id=1, source_target_pairs={{0,8},{8,16},{16,24},{24,32},{32,40},{40,48},{48,56},{56,64},{64,7... | collective-permute-start | bytes 221192 | tf_op jit(solution)/shard_map/ppermute | solution.py:57
  46.9 3.8 %collective-permute-start.6 = (f32[1,3,3,1,16,128]{5,4,2,1,3,0:T(8,128)S(1)}, f32[1,3,3,1,16,128]{5,4,2,1,3,0:T(8,128)S(1)}, u32[]{:S(2)}, u32[]{:S(2)}) collective-permute-start(f32[1,3,3,1,16,128]{5,4,2,1,3,0:T(8,128)S(1)} %slice_bitcast_fusion.1), channel_id=1, source_target_pairs={{0,120},{8,0},{16,8},{24,16},{32,24},{40,32},{48,40},{56,48},{64,5... | collective-permute-start | bytes 221192 | tf_op jit(solution)/shard_map/ppermute | solution.py:58
  49.4 12.8 %copy-start.6 = (f32[1,3,3,1,16,128]{5,4,2,1,3,0:T(8,128)}, f32[1,3,3,1,16,128]{5,4,2,1,3,0:T(8,128)S(1)}, u32[]{:S(2)}) copy-start(f32[1,3,3,1,16,128]{5,4,2,1,3,0:T(8,128)S(1)} %collective-permute-done.5) | copy-start | bytes 221188
  50.7 11.5 %copy-start.7 = (f32[1,3,3,1,16,128]{5,4,2,1,3,0:T(8,128)}, f32[1,3,3,1,16,128]{5,4,2,1,3,0:T(8,128)S(1)}, u32[]{:S(2)}) copy-start(f32[1,3,3,1,16,128]{5,4,2,1,3,0:T(8,128)S(1)} %collective-permute-done.6) | copy-start | bytes 221188
  51.3 4.7 %collective-permute-start.7 = (f32[2,1,3,3,4,1,128]{6,4,3,2,5,1,0:T(4,128)S(1)}, f32[2,1,3,3,4,1,128]{6,4,3,2,5,1,0:T(4,128)S(1)}, u32[]{:S(2)}, u32[]{:S(2)}) collective-permute-start(f32[2,1,3,3,4,1,128]{6,4,3,2,5,1,0:T(4,128)S(1)} %pad_maximum_fusion.15), channel_id=1, source_target_pairs={{0,4},{4,0},{1,5},{5,1},{2,6},{6,2},{3,7},{7,3},{8,12},{12,8},{9,1... | collective-permute-start | bytes 110600 | tf_op jit(solution)/shard_map/ppermute | solution.py:55
  54.8 11.7 %copy-start.12 = (s32[4,16,128]{2,1,0:T(8,128)S(1)}, s32[4,16,128]{2,1,0:T(8,128)}, u32[]{:S(2)}) copy-start(s32[4,16,128]{2,1,0:T(8,128)} %param.14) | copy-start | bytes 98308
  54.8 11.7 %copy-start.13 = (f32[4,16,128]{2,1,0:T(8,128)S(1)}, f32[4,16,128]{2,1,0:T(8,128)}, u32[]{:S(2)}) copy-start(f32[4,16,128]{2,1,0:T(8,128)} %get-tuple-element.8) | copy-start | bytes 98308
  57.0 3.0 %collective-permute-start.9 = (f32[1,3,3,16,4]{3,4,2,1,0:T(4,128)S(1)}, f32[1,3,3,16,4]{3,4,2,1,0:T(4,128)S(1)}, u32[]{:S(2)}, u32[]{:S(2)}) collective-permute-start(f32[1,3,3,16,4]{3,4,2,1,0:T(4,128)S(1)} %fusion.12), channel_id=1, source_target_pairs={{0,3},{1,0},{2,1},{3,2},{4,7},{5,4},{6,5},{7,6},{8,11},{9,8},{10,9... | collective-permute-start | bytes 6920 | tf_op jit(solution)/shard_map/ppermute | solution.py:58
  57.6 3.9 %collective-permute-start.8 = (f32[1,3,3,16,4]{3,4,2,1,0:T(4,128)S(1)}, f32[1,3,3,16,4]{3,4,2,1,0:T(4,128)S(1)}, u32[]{:S(2)}, u32[]{:S(2)}) collective-permute-start(f32[1,3,3,16,4]{3,4,2,1,0:T(4,128)S(1)} %fusion.13), channel_id=1, source_target_pairs={{0,1},{1,2},{2,3},{3,0},{4,5},{5,6},{6,7},{7,4},{8,9},{9,10},{10,1... | collective-permute-start | bytes 6920 | tf_op jit(solution)/shard_map/ppermute | solution.py:57

commit v9 on v8

--- a/solution.py
+++ b/solution.py
@@ -86,7 +86,8 @@
     xlo, xhi = halo_exchange(jnp.stack(x_up), jnp.stack(x_dn), "gx")
     both = jnp.stack(cubes)
     rows = jnp.concatenate([both[..., sy - 1 : sy, :], both[..., 0:1, :]], axis=5)
-    cols = jnp.concatenate([both[..., sz - 1 : sz], both[..., 0:1]], axis=6)
+    lane = lax.broadcasted_iota(jnp.int32, both.shape, both.ndim - 1)
+    cols = [jnp.sum(jnp.where(lane == z0, both, 0.0), axis=-1) for z0 in (sz - 1, 0)]
     y_up, y_dn = [], []
     for k, s in enumerate(signs):
         top = shifted(rows[k][..., 0:1, :], xlo[k][:, :, :, sy - 1 : sy], xhi[k][:, :, :, sy - 1 : sy], 0, s)
@@ -98,12 +99,11 @@
     for k, s in enumerate(signs):
         picked = []
         for at, z0 in ((0, sz - 1), (1, 0)):
-            col = cols[k][..., at : at + 1]
-            col = shifted(col, xlo[k][..., z0 : z0 + 1], xhi[k][..., z0 : z0 + 1], 0, s)
-            col = shifted(col, ylo[k][..., z0 : z0 + 1], yhi[k][..., z0 : z0 + 1], 1, s)
+            col = shifted(cols[at][k], xlo[k][..., z0], xhi[k][..., z0], 0, s)
+            col = shifted(col, ylo[k][..., z0], yhi[k][..., z0], 1, s)
             picked.append(col)
-        z_up.append(jnp.swapaxes(lax.index_in_dim(picked[0], 1 + s, axis=2, keepdims=False)[..., 0], -1, -2))
-        z_dn.append(jnp.swapaxes(lax.index_in_dim(picked[1], 1 - s, axis=2, keepdims=False)[..., 0], -1, -2))
+        z_up.append(jnp.swapaxes(lax.index_in_dim(picked[0], 1 + s, axis=2, keepdims=False), -1, -2))
+        z_dn.append(jnp.swapaxes(lax.index_in_dim(picked[1], 1 - s, axis=2, keepdims=False), -1, -2))
     zlo, zhi = halo_exchange(jnp.stack(z_up), jnp.stack(z_dn), "gz")
     nf = len(cubes)
     return (

time: 89.1 us -> 90.1 us (1.011)
  local copies, waits for them, and re-layouts: 19 us -> 15.1 us
  blocking collectives: 20.1 us -> 22.1 us
  starting transfers between devices: 18.8 us -> 20.6 us
  waiting for transfers between devices: 7.36 us -> 8.33 us
    slice x29 -> x11, local copies, waits for them, and re-layouts: 6.06 us -> 1.64 us  [the longest x6 1.07 us: halos(): col = shifted(cols[at][k], xlo[k][..., z0], xhi[k][..., z0], 0, s)]
    reduce_sum x0 -> x2, other arithmetic: none -> 4.21 us  [halos(): jnp.sum(jnp.where(lane == z0, both, 0.0), axis=-1)]
    all_to_all x1, blocking collectives: 20.1 us -> 22.1 us  [shards(): lax.all_to_all(placed.reshape(devices, count // devices), ('gx', 'gy', 'g...]
    another operation x1 -> x0, other arithmetic: 1.88 us -> none  [halos(): both = jnp.stack(cubes)]
    ppermute x4, starting transfers between devices: 5.71 us -> 7.27 us  [halo_exchange(): lo = lax.ppermute(up, axis, [(i, (i + 1) % size) for i in range(size)])]
    another operation x2, other arithmetic: 1.45 us -> 0.03 us  [halos(): xlo, xhi = halo_exchange(jnp.stack(x_up), jnp.stack(x_dn), 'gx')]
    unnamed x51 -> x39, local copies, waits for them, and re-layouts: 2.18 us -> 0.87 us
    slice x1 -> x2, local copies, waits for them, and re-layouts: 0.08 us -> 1.26 us  [halos(): rows = jnp.concatenate([both[..., sy - 1:sy, :], both[..., 0:1, :]], axis=5)]
  transfers between devices with their start and end apart: 10 -> 10, of which waited for: 7 -> 6; matrix products, arithmetic and copies ran while one was open for 15% -> 11% of each run, Pallas kernels for 0% -> 0%
where the time goes in v9:
time: 90.1 us; the launch traced here: 89.6 us
  blocking collectives  22.1 us (25%)
  starting transfers between devices  20.6 us (23%)
  local copies, waits for them, and re-layouts  15.1 us (17%)
  other arithmetic  12.5 us (14%)
  Pallas kernels  9.08 us (10%)
  waiting for transfers between devices  8.33 us (9%)
  between operations  1.85 us (2%)
    all_to_all x1, blocking collectives, shards(): lax.all_to_all(placed.reshape(devices, count // devices), ('gx', 'gy', 'g...  22.1 us
    pallas_call x2, Pallas kernels, run_stage(): pl.pallas_call(kernel, out_shape=(jax.ShapeDtypeStruct(shape, jnp.float32...  9.08 us
    ppermute x4, starting transfers between devices, halo_exchange(): lo = lax.ppermute(up, axis, [(i, (i + 1) % size) for i in range(size)])  7.27 us
    ppermute x2, starting transfers between devices, halo_exchange(): both = lax.ppermute(jnp.stack([up, down]), axis, [(0, 1), (1, 0)])  6.77 us
    ppermute x4, starting transfers between devices, halo_exchange(): hi = lax.ppermute(down, axis, [(i, (i - 1) % size) for i in range(size)])  6.57 us
    reduce_sum x2, other arithmetic, halos(): jnp.sum(jnp.where(lane == z0, both, 0.0), axis=-1)  4.21 us
    ppermute x4, waiting for transfers between devices, halo_exchange(): hi = lax.ppermute(down, axis, [(i, (i - 1) % size) for i in range(size)])  3 us
    ppermute x4, waiting for transfers between devices, halo_exchange(): lo = lax.ppermute(up, axis, [(i, (i + 1) % size) for i in range(size)])  2.95 us
  transfers between devices with their start and end apart: 10, of which 6 were waited for; matrix products, arithmetic and copies ran while one was open for 11% of the time, Pallas kernels for 0%

profile of v9, /device:TPU:1, one launch (start us, length us, event | category | flops | bytes accessed | tf_op | source)
XLA Modules:
  0.0 89.6 jit_solution(3408883786840723128)
XLA Ops:
  0.7 1.2 %slice_reduce_fusion.2 = (f32[4,16,128]{2,1,0:T(8,128)S(1)}, f32[4,16,128]{2,1,0:T(8,128)S(1)}) fusion(f32[3,3,3,4,16,128]{5,4,3,2,1,0:T(8,128)} %bitcast.398), kind=kLoop, calls=%fused_computation.18 | loop fusion | flops 131072 | bytes 655360 | tf_op jit(solution)/shard_map/reduce_sum | solution.py:33
  1.9 1.1 %slice_reduce_fusion = (f32[4,16,128]{2,1,0:T(8,128)S(1)}, f32[4,16,128]{2,1,0:T(8,128)S(1)}) fusion(f32[3,3,3,4,16,128]{5,4,3,2,1,0:T(8,128)} %bitcast.399), kind=kLoop, calls=%fused_computation.16 | loop fusion | flops 131072 | bytes 655360 | tf_op jit(solution)/shard_map/reduce_sum | solution.py:34
  3.0 1.1 %slice_reduce_fusion.4 = (f32[4,16,128]{2,1,0:T(8,128)S(1)}, f32[4,16,128]{2,1,0:T(8,128)S(1)}) fusion(f32[27,4,16,128]{3,2,1,0:T(8,128)} %f_ref.1), kind=kLoop, calls=%fused_computation.20 | loop fusion | flops 131072 | bytes 655360 | tf_op jit(solution)/shard_map/reduce_sum | solution.py:32
  4.1 0.8 slice.650
  5.2 0.2 copy.488
  5.5 0.6 gather_fusion
  6.0 0.1 copy.565
  6.3 0.1 reshape.161
  6.6 1.4 %fusion.7.cf_ref = f32[27,4,16,128]{3,2,1,0:T(8,128)S(1)} fusion(f32[27,4,16,128]{3,2,1,0:T(8,128)S(1)} %copy-done, f32[4,16,128]{2,1,0:T(8,128)S(1)} %get-tuple-element.148.refs_7_, f32[4,16,128]{2,1,0:T(8,128)S(1)} %get-tuple-element.34, f32[4,16,128]{2,1,0:T(8,128)S(1)} %get-tuple-element.37, f32[27]{0:T(128)S(1)} %copy-done.14, ...), kind=kLoop, calls=%fused_computation.11 | loop fusion | flops 4202496 | bytes 2032048 | tf_op jit(solution)/shard_map/add | solution.py:47
  8.1 3.1 %collective-permute-start = (f32[2,3,3,1,16,128]{5,4,2,1,3,0:T(8,128)S(1)}, f32[2,3,3,1,16,128]{5,4,2,1,3,0:T(8,128)S(1)}, u32[]{:S(2)}, u32[]{:S(2)}) collective-permute-start(f32[2,3,3,1,16,128]{5,4,2,1,3,0:T(8,128)S(1)} %pad_maximum_fusion), channel_id=1, source_target_pairs={{0,8},{8,16},{16,24},{24,32},{32,40},{40,48},{48,56},{56,64},{64,7... | collective-permute-start | bytes 442376 | tf_op jit(solution)/shard_map/ppermute | solution.py:57
  11.7 0.3 copy_dynamic-update-slice_fusion.1
  12.1 0.4 copy_dynamic-update-slice_fusion
  12.5 2.5 %select_reduce_fusion = (f32[2,3,3,3,4,16]{4,3,2,5,1,0:T(4,128)S(1)}, f32[2,3,3,3,4,16]{4,3,2,5,1,0:T(4,128)S(1)}) fusion(f32[2,3,3,3,4,16,128]{6,4,3,2,5,1,0:T(4,128)S(1)} %copy_dynamic-update-slice_fusion, pred[128]{0:T(512)(128)(4,1)S(1)} %get-tuple-element.149, pred[128]{0:T(512)(128)(4,1)S(1)} %get-tuple-element.150), kind=kLoop, calls=%fused_computation.1 | loop fusion | flops 1762560 | bytes 1797376 | tf_op jit(solution)/shard_map/reduce_sum | solution.py:90
  15.0 0.1 slice_bitcast_fusion.5
  15.1 0.1 slice.922
  15.2 0.1 copy.527
  15.5 0.1 copy.536
  15.6 0.1 copy.534
  15.7 0.1 copy.528
  15.9 0.1 copy.529
  16.0 0.1 slice.941
  16.1 0.1 copy.535
  16.3 0.1 slice_bitcast_fusion.11
  16.4 0.1 slice.890
  16.6 0.1 copy.512
  16.7 0.1 copy.521
  16.8 0.1 copy.519
  17.0 0.1 copy.513
  17.1 0.1 copy.514
  17.2 0.1 slice.912
  17.4 0.1 copy.520
  17.6 0.2 slice_reduce_fusion.12
  17.7 0.2 slice_reduce_fusion.11
  18.0 0.2 slice_reduce_fusion.13
  18.2 0.2 slice_reduce_fusion.10
  18.9 3.4 %collective-permute-start.2 = (f32[2,2,3,3,4,1,128]{6,4,3,2,5,1,0:T(4,128)S(1)}, f32[2,2,3,3,4,1,128]{6,4,3,2,5,1,0:T(4,128)S(1)}, u32[]{:S(2)}, u32[]{:S(2)}) collective-permute-start(f32[2,2,3,3,4,1,128]{6,4,3,2,5,1,0:T(4,128)S(1)} %pad_maximum_fusion.3), channel_id=1, source_target_pairs={{0,4},{4,0},{1,5},{5,1},{2,6},{6,2},{3,7},{7,3},{8,12},{12,8},{9,1... | collective-permute-start | bytes 221192 | tf_op jit(solution)/shard_map/ppermute | solution.py:55
  22.8 1.3 %collective-permute-done.2 = f32[2,2,3,3,4,1,128]{6,4,3,2,5,1,0:T(4,128)S(1)} collective-permute-done((f32[2,2,3,3,4,1,128]{6,4,3,2,5,1,0:T(4,128)S(1)}, f32[2,2,3,3,4,1,128]{6,4,3,2,5,1,0:T(4,128)S(1)}, u32[]{:S(2)}, u32[]{:S(2)}) %collective-permute-start.2) | collective-permute-done | bytes 73760 | tf_op jit(solution)/shard_map/ppermute | solution.py:55
  24.8 2.5 %collective-permute-start.4 = (f32[2,3,3,16,4]{3,4,2,1,0:T(4,128)S(1)}, f32[2,3,3,16,4]{3,4,2,1,0:T(4,128)S(1)}, u32[]{:S(2)}, u32[]{:S(2)}) collective-permute-start(f32[2,3,3,16,4]{3,4,2,1,0:T(4,128)S(1)} %pad_maximum_fusion.11), channel_id=1, source_target_pairs={{0,3},{1,0},{2,1},{3,2},{4,7},{5,4},{6,5},{7,6},{8,11},{9,8},{10,9... | collective-permute-start | bytes 13832 | tf_op jit(solution)/shard_map/ppermute | solution.py:58
  27.8 0.6 fusion.28
  28.4 0.8 copy.541
  29.3 2.5 %collective-permute-done.3 = f32[2,3,3,16,4]{3,4,2,1,0:T(4,128)S(1)} collective-permute-done((f32[2,3,3,16,4]{3,4,2,1,0:T(4,128)S(1)}, f32[2,3,3,16,4]{3,4,2,1,0:T(4,128)S(1)}, u32[]{:S(2)}, u32[]{:S(2)}) %collective-permute-start.3) | collective-permute-done | bytes 4640 | tf_op jit(solution)/shard_map/ppermute | solution.py:57
  31.8 0.8 copy.526
  32.6 4.8 %shard_map.122 = (f32[27,4,16,128]{3,2,1,0:T(8,128)}, f32[4,16,128]{2,1,0:T(8,128)}) custom-call(f32[27,4,16,128]{3,2,1,0:T(8,128)} %copy-done.1, f32[27,4,16,128]{3,2,1,0:T(8,128)} %ae_ref.1, f32[18,16,128]{2,1,0:T(8,128)} %bitcast.409, f32[18,16,128]{2,1,0:T(8,128)} %bitcast.410, f32[18,4,128]{2,1,0:T(4,128)} %bitcast.431, f32[18,4,128]{2,1,0:T(4,128)} %bitcast.430, ...), custom_call_target="tpu_custom_call" | custom-call | tf_op jit(solution)/shard_map/pallas_call | solution.py:242
  37.5 1.7 %select_reduce_fusion.2 = (f32[27,4,16]{2,1,0:T(4,128)S(1)}, f32[27,4,16]{2,1,0:T(4,128)S(1)}) fusion(f32[27,4,16,128]{3,2,1,0:T(8,128)} %get-tuple-element.6.an_ref, pred[128]{0:T(512)(128)(4,1)S(1)} %get-tuple-element.149, pred[128]{0:T(512)(128)(4,1)S(1)} %get-tuple-element.150), kind=kLoop, calls=%fused_computation.14 | loop fusion | flops 881280 | bytes 898816 | tf_op jit(solution)/shard_map/reduce_sum | solution.py:90
  39.2 1.1 %fusion.25 = (f32[9,4,16,128]{3,2,1,0:T(8,128)S(1)}, f32[9,4,16,128]{3,2,1,0:T(8,128)S(1)}) fusion(f32[27,4,16,128]{3,2,1,0:T(8,128)} %get-tuple-element.6.an_ref), kind=kLoop, calls=%fused_computation.231 | loop fusion | bytes 1179648 | tf_op jit(solution)/shard_map/slice | solution.py:78
  40.3 1.2 %fusion.24 = (f32[1,3,3,3,4,1,128]{6,5,4,3,2,1,0:T(1,128)S(1)}, f32[1,3,3,3,4,1,128]{6,5,4,3,2,1,0:T(1,128)S(1)}) fusion(f32[1,3,3,3,4,16,128]{6,5,4,3,2,1,0:T(8,128)} %bitcast.401), kind=kLoop, calls=%fused_computation.230 | loop fusion | bytes 221184 | tf_op jit(solution)/shard_map/slice | solution.py:88
  41.7 4.0 %collective-permute-start.5 = (f32[1,3,3,1,16,128]{5,4,2,1,3,0:T(8,128)S(1)}, f32[1,3,3,1,16,128]{5,4,2,1,3,0:T(8,128)S(1)}, u32[]{:S(2)}, u32[]{:S(2)}) collective-permute-start(f32[1,3,3,1,16,128]{5,4,2,1,3,0:T(8,128)S(1)} %slice_bitcast_fusion.13), channel_id=1, source_target_pairs={{0,8},{8,16},{16,24},{24,32},{32,40},{40,48},{48,56},{56,64},{64,7... | collective-permute-start | bytes 221192 | tf_op jit(solution)/shard_map/ppermute | solution.py:57
  45.7 1.2 %collective-permute-start.6 = (f32[1,3,3,1,16,128]{5,4,2,1,3,0:T(8,128)S(1)}, f32[1,3,3,1,16,128]{5,4,2,1,3,0:T(8,128)S(1)}, u32[]{:S(2)}, u32[]{:S(2)}) collective-permute-start(f32[1,3,3,1,16,128]{5,4,2,1,3,0:T(8,128)S(1)} %slice_bitcast_fusion.12), channel_id=1, source_target_pairs={{0,120},{8,0},{16,8},{24,16},{32,24},{40,32},{48,40},{56,48},{64,5... | collective-permute-start | bytes 221192 | tf_op jit(solution)/shard_map/ppermute | solution.py:58
  47.0 0.4 collective-permute-done.5
  47.4 0.2 slice_reduce_fusion.7
  47.6 2.2 %collective-permute-done.6 = f32[1,3,3,1,16,128]{5,4,2,1,3,0:T(8,128)S(1)} collective-permute-done((f32[1,3,3,1,16,128]{5,4,2,1,3,0:T(8,128)S(1)}, f32[1,3,3,1,16,128]{5,4,2,1,3,0:T(8,128)S(1)}, u32[]{:S(2)}, u32[]{:S(2)}) %collective-permute-start.6) | collective-permute-done | bytes 73760 | tf_op jit(solution)/shard_map/ppermute | solution.py:58
  49.8 0.2 slice_reduce_fusion.6
  50.3 3.4 %collective-permute-start.7 = (f32[2,1,3,3,4,1,128]{6,4,3,2,5,1,0:T(4,128)S(1)}, f32[2,1,3,3,4,1,128]{6,4,3,2,5,1,0:T(4,128)S(1)}, u32[]{:S(2)}, u32[]{:S(2)}) collective-permute-start(f32[2,1,3,3,4,1,128]{6,4,3,2,5,1,0:T(4,128)S(1)} %pad_maximum_fusion.12), channel_id=1, source_target_pairs={{0,4},{4,0},{1,5},{5,1},{2,6},{6,2},{3,7},{7,3},{8,12},{12,8},{9,1... | collective-permute-start | bytes 110600 | tf_op jit(solution)/shard_map/ppermute | solution.py:55
  53.9 1.1 %collective-permute-done.7 = f32[2,1,3,3,4,1,128]{6,4,3,2,5,1,0:T(4,128)S(1)} collective-permute-done((f32[2,1,3,3,4,1,128]{6,4,3,2,5,1,0:T(4,128)S(1)}, f32[2,1,3,3,4,1,128]{6,4,3,2,5,1,0:T(4,128)S(1)}, u32[]{:S(2)}, u32[]{:S(2)}) %collective-permute-start.7) | collective-permute-done | bytes 36896 | tf_op jit(solution)/shard_map/ppermute | solution.py:55
  55.0 0.6 slice_bitcast_fusion.84
  56.2 2.7 %collective-permute-start.9 = (f32[1,3,3,16,4]{3,4,2,1,0:T(4,128)S(1)}, f32[1,3,3,16,4]{3,4,2,1,0:T(4,128)S(1)}, u32[]{:S(2)}, u32[]{:S(2)}) collective-permute-start(f32[1,3,3,16,4]{3,4,2,1,0:T(4,128)S(1)} %fusion.11), channel_id=1, source_target_pairs={{0,3},{1,0},{2,1},{3,2},{4,7},{5,4},{6,5},{7,6},{8,11},{9,8},{10,9... | collective-permute-start | bytes 6920 | tf_op jit(solution)/shard_map/ppermute | solution.py:58
  59.0 0.8 collective-permute-done.9
  59.8 0.8 copy.561
  60.6 0.8 copy.556
  61.3 4.2 %shard_map.123 = (f32[27,4,16,128]{3,2,1,0:T(8,128)}, f32[4,16,128]{2,1,0:T(8,128)}) custom-call(f32[27,4,16,128]{3,2,1,0:T(8,128)} %get-tuple-element.6.an_ref, f32[27,4,16,128]{3,2,1,0:T(8,128)} %f_ref.1, f32[9,16,128]{2,1,0:T(8,128)} %bitcast.405, f32[9,16,128]{2,1,0:T(8,128)} %bitcast.408, f32[9,4,128]{2,1,0:T(4,128)} %bitcast.447, ...), custom_call_target="tpu_custom_call" | custom-call | tf_op jit(solution)/shard_map/pallas_call | solution.py:242
  65.6 0.8 add_multiply_fusion
  66.4 0.1 reduce_sum.152
  66.9 22.1 %all_to_all.9 = f32[128,1,8]{2,1,0:T(1,128)S(1)} all-to-all(f32[128,1,8]{2,1,0:T(1,128)S(1)} %bitcast.425), channel_id=1, replica_groups=mesh['gx'=16,'gy'=2,'gz'=4] {'gx','gy','gz'}, dimensions={0} | all-to-all | bytes 8192 | tf_op jit(solution)/shard_map/all_to_all | solution.py:276
  89.0 0.7 reduce_sum.155
  (190 shorter events, 4.6 us)
Async XLA Ops:
  0.6 4.4 %copy-start = (f32[27,4,16,128]{3,2,1,0:T(8,128)S(1)}, f32[27,4,16,128]{3,2,1,0:T(8,128)}, u32[]{:S(2)}) copy-start(f32[27,4,16,128]{3,2,1,0:T(8,128)} %f_ref.1) | copy-start | bytes 2654212
  0.6 4.4 %copy-start.11 = (s32[1024]{0:T(1024)S(1)}, s32[1024]{0:T(1024)}, u32[]{:S(2)}) copy-start(s32[1024]{0:T(1024)} %param.17) | copy-start | bytes 12292
  0.7 4.6 %copy-start.12 = (f32[1024]{0:T(1024)S(1)}, f32[1024]{0:T(1024)}, u32[]{:S(2)}) copy-start(f32[1024]{0:T(1024)} %param.16) | copy-start | bytes 12292
  0.7 5.7 %copy-start.2 = (f32[27,4,16,128]{3,2,1,0:T(8,128)S(1)}, f32[27,4,16,128]{3,2,1,0:T(8,128)}, u32[]{:S(2)}) copy-start(f32[27,4,16,128]{3,2,1,0:T(8,128)} %ae_ref.1) | copy-start | bytes 2654212
  5.1 1.4 %copy-start.9 = (s32[4,16,128]{2,1,0:T(8,128)S(1)}, s32[4,16,128]{2,1,0:T(8,128)}, u32[]{:S(2)}) copy-start(s32[4,16,128]{2,1,0:T(8,128)} %param.14) | copy-start | bytes 98308
  5.1 1.4 %copy-start.8 = (f32[4,16,128]{2,1,0:T(8,128)S(1)}, f32[4,16,128]{2,1,0:T(8,128)}, u32[]{:S(2)}) copy-start(f32[4,16,128]{2,1,0:T(8,128)} %refs_6_.3) | copy-start | bytes 98308
  5.2 1.4 %copy-start.13 = (f32[27]{0:T(128)S(1)}, f32[27]{0:T(128)}, u32[]{:S(2)}) copy-start(f32[27]{0:T(128)} %constant.32.clone) | copy-start | bytes 328
  5.2 1.4 %copy-start.14 = (f32[27]{0:T(128)S(1)}, f32[27]{0:T(128)}, u32[]{:S(2)}) copy-start(f32[27]{0:T(128)} %constant.11.clone) | copy-start | bytes 328
  5.2 1.4 %copy-start.15 = (f32[27]{0:T(128)S(1)}, f32[27]{0:T(128)}, u32[]{:S(2)}) copy-start(f32[27]{0:T(128)} %constant.10.clone) | copy-start | bytes 328
  5.2 1.4 %copy-start.16 = (f32[27]{0:T(128)S(1)}, f32[27]{0:T(128)}, u32[]{:S(2)}) copy-start(f32[27]{0:T(128)} %constant.9.clone) | copy-start | bytes 328
  6.5 1.5 %copy-start.7 = (f32[4,16,128]{2,1,0:T(8,128)}, f32[4,16,128]{2,1,0:T(8,128)S(1)}, u32[]{:S(2)}) copy-start(f32[4,16,128]{2,1,0:T(8,128)S(1)} %get-tuple-element.148.refs_7_) | copy-start | bytes 98308
  8.0 4.1 %copy-start.1 = (f32[27,4,16,128]{3,2,1,0:T(8,128)}, f32[27,4,16,128]{3,2,1,0:T(8,128)S(1)}, u32[]{:S(2)}) copy-start(f32[27,4,16,128]{3,2,1,0:T(8,128)S(1)} %fusion.7.cf_ref) | copy-start | bytes 2654212
  8.1 9.4 %collective-permute-start = (f32[2,3,3,1,16,128]{5,4,2,1,3,0:T(8,128)S(1)}, f32[2,3,3,1,16,128]{5,4,2,1,3,0:T(8,128)S(1)}, u32[]{:S(2)}, u32[]{:S(2)}) collective-permute-start(f32[2,3,3,1,16,128]{5,4,2,1,3,0:T(8,128)S(1)} %pad_maximum_fusion), channel_id=1, source_target_pairs={{0,8},{8,16},{16,24},{24,32},{32,40},{40,48},{48,56},{56,64},{64,7... | collective-permute-start | bytes 442376 | tf_op jit(solution)/shard_map/ppermute | solution.py:57
  11.2 6.7 %collective-permute-start.1 = (f32[2,3,3,1,16,128]{5,4,2,1,3,0:T(8,128)S(1)}, f32[2,3,3,1,16,128]{5,4,2,1,3,0:T(8,128)S(1)}, u32[]{:S(2)}, u32[]{:S(2)}) collective-permute-start(f32[2,3,3,1,16,128]{5,4,2,1,3,0:T(8,128)S(1)} %pad_maximum_fusion.1), channel_id=1, source_target_pairs={{0,120},{8,0},{16,8},{24,16},{32,24},{40,32},{48,40},{56,48},{64,5... | collective-permute-start | bytes 442376 | tf_op jit(solution)/shard_map/ppermute | solution.py:58
  17.5 5.0 %copy-start.5 = (f32[2,3,3,1,16,128]{5,4,2,1,3,0:T(8,128)}, f32[2,3,3,1,16,128]{5,4,2,1,3,0:T(8,128)S(1)}, u32[]{:S(2)}) copy-start(f32[2,3,3,1,16,128]{5,4,2,1,3,0:T(8,128)S(1)} %collective-permute-done) | copy-start | bytes 442372
  17.9 6.4 %copy-start.6 = (f32[2,3,3,1,16,128]{5,4,2,1,3,0:T(8,128)}, f32[2,3,3,1,16,128]{5,4,2,1,3,0:T(8,128)S(1)}, u32[]{:S(2)}) copy-start(f32[2,3,3,1,16,128]{5,4,2,1,3,0:T(8,128)S(1)} %collective-permute-done.1) | copy-start | bytes 442372
  18.9 5.1 %collective-permute-start.2 = (f32[2,2,3,3,4,1,128]{6,4,3,2,5,1,0:T(4,128)S(1)}, f32[2,2,3,3,4,1,128]{6,4,3,2,5,1,0:T(4,128)S(1)}, u32[]{:S(2)}, u32[]{:S(2)}) collective-permute-start(f32[2,2,3,3,4,1,128]{6,4,3,2,5,1,0:T(4,128)S(1)} %pad_maximum_fusion.3), channel_id=1, source_target_pairs={{0,4},{4,0},{1,5},{5,1},{2,6},{6,2},{3,7},{7,3},{8,12},{12,8},{9,1... | collective-permute-start | bytes 221192 | tf_op jit(solution)/shard_map/ppermute | solution.py:55
  24.8 3.6 %collective-permute-start.4 = (f32[2,3,3,16,4]{3,4,2,1,0:T(4,128)S(1)}, f32[2,3,3,16,4]{3,4,2,1,0:T(4,128)S(1)}, u32[]{:S(2)}, u32[]{:S(2)}) collective-permute-start(f32[2,3,3,16,4]{3,4,2,1,0:T(4,128)S(1)} %pad_maximum_fusion.11), channel_id=1, source_target_pairs={{0,3},{1,0},{2,1},{3,2},{4,7},{5,4},{6,5},{7,6},{8,11},{9,8},{10,9... | collective-permute-start | bytes 13832 | tf_op jit(solution)/shard_map/ppermute | solution.py:58
  27.7 4.1 %collective-permute-start.3 = (f32[2,3,3,16,4]{3,4,2,1,0:T(4,128)S(1)}, f32[2,3,3,16,4]{3,4,2,1,0:T(4,128)S(1)}, u32[]{:S(2)}, u32[]{:S(2)}) collective-permute-start(f32[2,3,3,16,4]{3,4,2,1,0:T(4,128)S(1)} %pad_maximum_fusion.10), channel_id=1, source_target_pairs={{0,1},{1,2},{2,3},{3,0},{4,5},{5,6},{6,7},{7,4},{8,9},{9,10},{10,1... | collective-permute-start | bytes 13832 | tf_op jit(solution)/shard_map/ppermute | solution.py:57
  41.7 5.7 %collective-permute-start.5 = (f32[1,3,3,1,16,128]{5,4,2,1,3,0:T(8,128)S(1)}, f32[1,3,3,1,16,128]{5,4,2,1,3,0:T(8,128)S(1)}, u32[]{:S(2)}, u32[]{:S(2)}) collective-permute-start(f32[1,3,3,1,16,128]{5,4,2,1,3,0:T(8,128)S(1)} %slice_bitcast_fusion.13), channel_id=1, source_target_pairs={{0,8},{8,16},{16,24},{24,32},{32,40},{40,48},{48,56},{56,64},{64,7... | collective-permute-start | bytes 221192 | tf_op jit(solution)/shard_map/ppermute | solution.py:57
  45.7 4.0 %collective-permute-start.6 = (f32[1,3,3,1,16,128]{5,4,2,1,3,0:T(8,128)S(1)}, f32[1,3,3,1,16,128]{5,4,2,1,3,0:T(8,128)S(1)}, u32[]{:S(2)}, u32[]{:S(2)}) collective-permute-start(f32[1,3,3,1,16,128]{5,4,2,1,3,0:T(8,128)S(1)} %slice_bitcast_fusion.12), channel_id=1, source_target_pairs={{0,120},{8,0},{16,8},{24,16},{32,24},{40,32},{48,40},{56,48},{64,5... | collective-permute-start | bytes 221192 | tf_op jit(solution)/shard_map/ppermute | solution.py:58
  47.4 14.0 %copy-start.3 = (f32[1,3,3,1,16,128]{5,4,2,1,3,0:T(8,128)}, f32[1,3,3,1,16,128]{5,4,2,1,3,0:T(8,128)S(1)}, u32[]{:S(2)}) copy-start(f32[1,3,3,1,16,128]{5,4,2,1,3,0:T(8,128)S(1)} %collective-permute-done.5) | copy-start | bytes 221188
  49.8 11.6 %copy-start.4 = (f32[1,3,3,1,16,128]{5,4,2,1,3,0:T(8,128)}, f32[1,3,3,1,16,128]{5,4,2,1,3,0:T(8,128)S(1)}, u32[]{:S(2)}) copy-start(f32[1,3,3,1,16,128]{5,4,2,1,3,0:T(8,128)S(1)} %collective-permute-done.6) | copy-start | bytes 221188
  50.2 15.4 %copy-start.10 = (f32[4,16,128]{2,1,0:T(8,128)S(1)}, f32[4,16,128]{2,1,0:T(8,128)}, u32[]{:S(2)}) copy-start(f32[4,16,128]{2,1,0:T(8,128)} %get-tuple-element.8) | copy-start | bytes 98308
  50.3 4.7 %collective-permute-start.7 = (f32[2,1,3,3,4,1,128]{6,4,3,2,5,1,0:T(4,128)S(1)}, f32[2,1,3,3,4,1,128]{6,4,3,2,5,1,0:T(4,128)S(1)}, u32[]{:S(2)}, u32[]{:S(2)}) collective-permute-start(f32[2,1,3,3,4,1,128]{6,4,3,2,5,1,0:T(4,128)S(1)} %pad_maximum_fusion.12), channel_id=1, source_target_pairs={{0,4},{4,0},{1,5},{5,1},{2,6},{6,2},{3,7},{7,3},{8,12},{12,8},{9,1... | collective-permute-start | bytes 110600 | tf_op jit(solution)/shard_map/ppermute | solution.py:55
  55.9 4.6 %collective-permute-start.8 = (f32[1,3,3,16,4]{3,4,2,1,0:T(4,128)S(1)}, f32[1,3,3,16,4]{3,4,2,1,0:T(4,128)S(1)}, u32[]{:S(2)}, u32[]{:S(2)}) collective-permute-start(f32[1,3,3,16,4]{3,4,2,1,0:T(4,128)S(1)} %fusion.12), channel_id=1, source_target_pairs={{0,1},{1,2},{2,3},{3,0},{4,5},{5,6},{6,7},{7,4},{8,9},{9,10},{10,1... | collective-permute-start | bytes 6920 | tf_op jit(solution)/shard_map/ppermute | solution.py:57
  56.2 3.6 %collective-permute-start.9 = (f32[1,3,3,16,4]{3,4,2,1,0:T(4,128)S(1)}, f32[1,3,3,16,4]{3,4,2,1,0:T(4,128)S(1)}, u32[]{:S(2)}, u32[]{:S(2)}) collective-permute-start(f32[1,3,3,16,4]{3,4,2,1,0:T(4,128)S(1)} %fusion.11), channel_id=1, source_target_pairs={{0,3},{1,0},{2,1},{3,2},{4,7},{5,4},{6,5},{7,6},{8,11},{9,8},{10,9... | collective-permute-start | bytes 6920 | tf_op jit(solution)/shard_map/ppermute | solution.py:58

commit v10 on v8

--- a/solution.py
+++ b/solution.py
@@ -232,9 +232,25 @@
 
 def now_kernel(an_ref, f_ref, *refs):
     hal = refs[0:6]
-    rate_ref, gamma_ref, out_ref, sens_ref, as_ = refs[6:]
-    move_into(as_, an_ref, hal, -1, 0)
-    chunked_adjoint(f_ref, as_, rate_ref, gamma_ref, out_ref, sens_ref)
+    rate_ref, gamma_ref, moved_ref, sens_ref = refs[6:]
+    move_into(moved_ref, an_ref, hal, -1, 0)
+    _, sx, sy, sz = f_ref.shape
+    halves = sy // 8
+
+    def body(step, carry):
+        i = step // halves
+        h = pl.multiple_of((step % halves) * 8, 8)
+        F = [f_ref[q, i, pl.ds(h, 8), :] for q in range(27)]
+        A = [moved_ref[q, i, pl.ds(h, 8), :] for q in range(27)]
+        _, sens = adjoint_rows(F, A, rate_ref[i, pl.ds(h, 8), :], gamma_ref[i, pl.ds(h, 8), :])
+        sens_ref[i, pl.ds(h, 8), :] = sens
+        return carry
+
+    lax.fori_loop(0, sx * halves, body, 0)
+
+
+def start_kernel(f_ref, moved_ref, rate_ref, gamma_ref, out_ref, sens_ref):
+    chunked_adjoint(f_ref, moved_ref, rate_ref, gamma_ref, out_ref, sens_ref)
 
 
 def run_stage(kernel, args, shape, scratch):
@@ -264,7 +280,8 @@
         next_kernel, (post_now, adjoint_end) + hal + (relax_rate, gamma), shape, 2
     )
     hal_n = halos([adj_next], [-1])
-    adjoint_start, sens_now = run_stage(now_kernel, (adj_next, check_pops) + hal_n + (relax_rate, gamma), shape, 1)
+    post_adj, sens_now = run_stage(now_kernel, (adj_next, check_pops) + hal_n + (relax_rate, gamma), shape, 0)
+    adjoint_start, _ = run_stage(start_kernel, (check_pops, post_adj, relax_rate, gamma), shape, 0)
     density = walls * (sens_next + sens_now)
     boxes = density.reshape(sx, 2, sy // 2, 2, sz // 2).sum(axis=(2, 4))
     parts = jnp.stack([boxes[0], boxes[1 : sx - 1].sum(axis=0), boxes[sx - 1]])

time: 89.1 us -> 89.4 us (level)
  blocking collectives: 20.1 us -> 0 us
  starting transfers between devices: 18.8 us -> 29.2 us
  waiting for transfers between devices: 7.36 us -> 13.5 us
  Pallas kernels: 9.08 us -> 12.3 us
    all_to_all x1 -> x0, blocking collectives: 20.1 us -> none  [shards(): lax.all_to_all(placed.reshape(devices, count // devices), ('gx', 'gy', 'g...]
    all_to_all x0 -> x1, starting transfers between devices: none -> 10.5 us  [shards(): lax.all_to_all(placed.reshape(devices, count // devices), ('gx', 'gy', 'g...]
    all_to_all x0 -> x1, waiting for transfers between devices: none -> 6.12 us  [shards(): lax.all_to_all(placed.reshape(devices, count // devices), ('gx', 'gy', 'g...]
    pallas_call x2 -> x3, Pallas kernels: 9.08 us -> 12.3 us  [run_stage(): pl.pallas_call(kernel, out_shape=(jax.ShapeDtypeStruct(shape, jnp.float32...]
  transfers between devices with their start and end apart: 10 -> 11, of which waited for: 7 -> 8; matrix products, arithmetic and copies ran while one was open for 15% -> 15% of each run, Pallas kernels for 0% -> 4%
where the time goes in v10:
time: 89.4 us; the launch traced here: 88.8 us
  starting transfers between devices  29.2 us (33%)
  local copies, waits for them, and re-layouts  19.6 us (22%)
  waiting for transfers between devices  13.5 us (15%)
  other arithmetic  12.5 us (14%)
  Pallas kernels  12.3 us (14%)
  between operations  1.7 us (2%)
    pallas_call x3, Pallas kernels, run_stage(): pl.pallas_call(kernel, out_shape=(jax.ShapeDtypeStruct(shape, jnp.float32...  12.3 us
    all_to_all x1, starting transfers between devices, shards(): lax.all_to_all(placed.reshape(devices, count // devices), ('gx', 'gy', 'g...  10.5 us
    ppermute x2, starting transfers between devices, halo_exchange(): both = lax.ppermute(jnp.stack([up, down]), axis, [(0, 1), (1, 0)])  6.77 us
    ppermute x4, starting transfers between devices, halo_exchange(): hi = lax.ppermute(down, axis, [(i, (i - 1) % size) for i in range(size)])  6.27 us
    all_to_all x1, waiting for transfers between devices, shards(): lax.all_to_all(placed.reshape(devices, count // devices), ('gx', 'gy', 'g...  6.12 us
    ppermute x4, starting transfers between devices, halo_exchange(): lo = lax.ppermute(up, axis, [(i, (i + 1) % size) for i in range(size)])  5.72 us
    ppermute x4, waiting for transfers between devices, halo_exchange(): lo = lax.ppermute(up, axis, [(i, (i + 1) % size) for i in range(size)])  3.83 us
    slice x3, local copies, waits for them, and re-layouts, halos(): cols = jnp.concatenate([both[..., sz - 1:sz], both[..., 0:1]], axis=6)  3.63 us
  transfers between devices with their start and end apart: 11, of which 8 were waited for; matrix products, arithmetic and copies ran while one was open for 15% of the time, Pallas kernels for 4%

profile of v10, /device:TPU:1, one launch (start us, length us, event | category | flops | bytes accessed | tf_op | source)
XLA Modules:
  0.0 88.8 jit_solution(1155257068258774529)
XLA Ops:
  0.7 1.2 %slice_reduce_fusion.2 = (f32[4,16,128]{2,1,0:T(8,128)S(1)}, f32[4,16,128]{2,1,0:T(8,128)S(1)}) fusion(f32[3,3,3,4,16,128]{5,4,3,2,1,0:T(8,128)} %bitcast.426), kind=kLoop, calls=%fused_computation.14 | loop fusion | flops 131072 | bytes 655360 | tf_op jit(solution)/shard_map/reduce_sum | solution.py:33
  1.9 1.1 %slice_reduce_fusion = (f32[4,16,128]{2,1,0:T(8,128)S(1)}, f32[4,16,128]{2,1,0:T(8,128)S(1)}) fusion(f32[3,3,3,4,16,128]{5,4,3,2,1,0:T(8,128)} %bitcast.427), kind=kLoop, calls=%fused_computation.12 | loop fusion | flops 131072 | bytes 655360 | tf_op jit(solution)/shard_map/reduce_sum | solution.py:34
  3.0 1.1 %slice_reduce_fusion.4 = (f32[4,16,128]{2,1,0:T(8,128)S(1)}, f32[4,16,128]{2,1,0:T(8,128)S(1)}) fusion(f32[27,4,16,128]{3,2,1,0:T(8,128)} %f_ref.3), kind=kLoop, calls=%fused_computation.16 | loop fusion | flops 131072 | bytes 655360 | tf_op jit(solution)/shard_map/reduce_sum | solution.py:32
  4.2 0.2 copy.1155
  4.4 0.8 slice.648
  5.3 0.6 gather_fusion
  5.9 0.1 copy.1256
  6.4 1.4 %fusion.7.cf_ref = f32[27,4,16,128]{3,2,1,0:T(8,128)S(1)} fusion(f32[27,4,16,128]{3,2,1,0:T(8,128)S(1)} %copy-done, f32[4,16,128]{2,1,0:T(8,128)S(1)} %get-tuple-element.150.refs_7_.gamma_ref, f32[4,16,128]{2,1,0:T(8,128)S(1)} %get-tuple-element.20, f32[4,16,128]{2,1,0:T(8,128)S(1)} %get-tuple-element.23, f32[27]{0:T(128)S(1)} %copy-done.18, ...), kind=kLoop, calls=%fused_computation.11 | loop fusion | flops 4202496 | bytes 2032048 | tf_op jit(solution)/shard_map/add | solution.py:47
  8.0 0.8 pad_maximum_fusion.4
  8.7 1.4 %collective-permute-start.1 = (f32[2,3,3,1,16,128]{5,4,2,1,3,0:T(8,128)}, f32[2,3,3,1,16,128]{5,4,2,1,3,0:T(8,128)}, u32[]{:S(2)}, u32[]{:S(2)}) collective-permute-start(f32[2,3,3,1,16,128]{5,4,2,1,3,0:T(8,128)} %pad_maximum_fusion.4), channel_id=1, source_target_pairs={{0,120},{8,0},{16,8},{24,16},{32,24},{40,32},{48,40},{56,48},{64,5... | collective-permute-start | bytes 442376 | tf_op jit(solution)/shard_map/ppermute | solution.py:58
  10.1 0.7 pad_maximum_fusion.3
  10.8 1.6 %collective-permute-start = (f32[2,3,3,1,16,128]{5,4,2,1,3,0:T(8,128)}, f32[2,3,3,1,16,128]{5,4,2,1,3,0:T(8,128)}, u32[]{:S(2)}, u32[]{:S(2)}) collective-permute-start(f32[2,3,3,1,16,128]{5,4,2,1,3,0:T(8,128)} %pad_maximum_fusion.3), channel_id=1, source_target_pairs={{0,8},{8,16},{16,24},{24,32},{32,40},{40,48},{48,56},{56,64},{64,7... | collective-permute-start | bytes 442376 | tf_op jit(solution)/shard_map/ppermute | solution.py:57
  12.5 1.9 %slice_maximum_fusion = (f32[2,3,3,3,4,16,1]{6,5,4,3,2,1,0:T(8,128)S(1)}, f32[2,3,3,3,4,16,1]{6,5,4,3,2,1,0:T(8,128)}) fusion(f32[1,3,3,3,4,16,128]{6,5,4,3,2,1,0:T(8,128)S(1)} %bitcast.432, f32[1,3,3,3,4,16,128]{6,5,4,3,2,1,0:T(8,128)S(1)} %bitcast.428), kind=kLoop, calls=%fused_computation.2 | loop fusion | flops 6912 | bytes 1797120 | tf_op jit(solution)/shard_map/stack | solution.py:87
  14.3 0.8 fusion.8
  15.2 2.0 %copy.1179 = f32[2,3,3,3,4,16,1]{5,4,6,3,2,1,0:T(4,128)} copy(f32[2,3,3,3,4,16,1]{6,5,4,3,2,1,0:T(8,128)S(1)} %get-tuple-element.24) | data formatting | bytes 27648 | tf_op jit(solution)/shard_map/slice | solution.py:89
  17.2 1.3 %copy.1180 = f32[2,3,3,3,4,16,1]{5,4,6,3,2,1,0:T(4,128)S(1)} copy(f32[2,3,3,3,4,16,1]{6,5,4,3,2,1,0:T(8,128)S(1)} %copy-done.4) | data formatting | bytes 27648 | tf_op jit(solution)/shard_map/slice | solution.py:89
  19.3 0.9 %slice_bitcast_fusion.6 = (f32[3,3,1,16,128]{4,3,1,0,2:T(8,128)S(1)}, f32[3,3,1,16,128]{4,3,1,0,2:T(8,128)S(1)}) fusion(f32[2,3,3,1,16,128]{5,4,2,1,3,0:T(8,128)} %collective-permute-done.1), kind=kLoop, calls=%fused_computation.38 | loop fusion | bytes 294912 | tf_op jit(solution)/shard_map/squeeze | solution.py:92
  20.4 0.9 %slice_bitcast_fusion.5 = (f32[3,3,1,16,128]{4,3,1,0,2:T(8,128)S(1)}, f32[3,3,1,16,128]{4,3,1,0,2:T(8,128)S(1)}) fusion(f32[2,3,3,1,16,128]{5,4,2,1,3,0:T(8,128)} %collective-permute-done), kind=kLoop, calls=%fused_computation.37 | loop fusion | bytes 294912 | tf_op jit(solution)/shard_map/squeeze | solution.py:92
  21.6 0.1 copy.1198
  21.7 0.1 copy.1199
  22.3 3.4 %collective-permute-start.2 = (f32[2,2,3,3,4,1,128]{6,4,3,2,1,5,0:T(4,128)S(1)}, f32[2,2,3,3,4,1,128]{6,4,3,2,1,5,0:T(4,128)S(1)}, u32[]{:S(2)}, u32[]{:S(2)}) collective-permute-start(f32[2,2,3,3,4,1,128]{6,4,3,2,1,5,0:T(4,128)S(1)} %pad_maximum_fusion.6), channel_id=1, source_target_pairs={{0,4},{4,0},{1,5},{5,1},{2,6},{6,2},{3,7},{7,3},{8,12},{12,8},{9,1... | collective-permute-start | bytes 221192 | tf_op jit(solution)/shard_map/ppermute | solution.py:55
  25.7 0.1 copy.1206
  25.8 0.1 copy.1207
  26.0 0.1 copy.1181
  26.1 0.1 copy.1182
  26.3 0.1 copy.1189
  26.4 0.1 copy.1190
  27.0 0.4 collective-permute-done.2
  28.1 2.5 %collective-permute-start.4 = (f32[2,3,3,16,4]{3,4,2,1,0:T(4,128)S(1)}, f32[2,3,3,16,4]{3,4,2,1,0:T(4,128)S(1)}, u32[]{:S(2)}, u32[]{:S(2)}) collective-permute-start(f32[2,3,3,16,4]{3,4,2,1,0:T(4,128)S(1)} %pad_maximum_fusion.14), channel_id=1, source_target_pairs={{0,3},{1,0},{2,1},{3,2},{4,7},{5,4},{6,5},{7,6},{8,11},{9,8},{10,9... | collective-permute-start | bytes 13832 | tf_op jit(solution)/shard_map/ppermute | solution.py:58
  31.1 0.6 fusion.36
  31.7 0.8 copy.1214
  32.6 2.5 %collective-permute-done.3 = f32[2,3,3,16,4]{3,4,2,1,0:T(4,128)S(1)} collective-permute-done((f32[2,3,3,16,4]{3,4,2,1,0:T(4,128)S(1)}, f32[2,3,3,16,4]{3,4,2,1,0:T(4,128)S(1)}, u32[]{:S(2)}, u32[]{:S(2)}) %collective-permute-start.3) | collective-permute-done | bytes 4640 | tf_op jit(solution)/shard_map/ppermute | solution.py:57
  35.1 0.8 copy.1197
  36.0 4.9 %shard_map.122 = (f32[27,4,16,128]{3,2,1,0:T(8,128)}, f32[4,16,128]{2,1,0:T(8,128)}) custom-call(f32[27,4,16,128]{3,2,1,0:T(8,128)} %copy-done.1, f32[27,4,16,128]{3,2,1,0:T(8,128)} %ae_ref.1, f32[18,16,128]{2,1,0:T(8,128)} %bitcast.9.refs_0_, f32[18,16,128]{2,1,0:T(8,128)} %bitcast.14.refs_1_, f32[18,4,128]{2,1,0:T(4,128)} %bitcast.454, ...), custom_call_target="tpu_custom_call" | custom-call | tf_op jit(solution)/shard_map/pallas_call | solution.py:258
  40.8 1.2 %fusion.25 = (f32[9,4,16,128]{3,2,1,0:T(8,128)S(1)}, f32[9,4,16,128]{3,2,1,0:T(8,128)S(1)}) fusion(f32[27,4,16,128]{3,2,1,0:T(8,128)} %get-tuple-element.7.an_ref), kind=kLoop, calls=%fused_computation.215 | loop fusion | bytes 1179648 | tf_op jit(solution)/shard_map/slice | solution.py:78
  42.0 0.2 copy-done.2
  42.2 0.3 fusion.23
  42.6 0.7 copy.1275
  43.3 0.7 copy.1276
  44.1 2.8 %collective-permute-start.5 = (f32[1,3,3,1,16,128]{5,4,2,1,3,0:T(8,128)S(1)}, f32[1,3,3,1,16,128]{5,4,2,1,3,0:T(8,128)S(1)}, u32[]{:S(2)}, u32[]{:S(2)}) collective-permute-start(f32[1,3,3,1,16,128]{5,4,2,1,3,0:T(8,128)S(1)} %slice_bitcast_fusion.2), channel_id=1, source_target_pairs={{0,8},{8,16},{16,24},{24,32},{32,40},{40,48},{48,56},{56,64},{64,7... | collective-permute-start | bytes 221192 | tf_op jit(solution)/shard_map/ppermute | solution.py:57
  46.9 1.9 %collective-permute-start.6 = (f32[1,3,3,1,16,128]{5,4,2,1,3,0:T(8,128)S(1)}, f32[1,3,3,1,16,128]{5,4,2,1,3,0:T(8,128)S(1)}, u32[]{:S(2)}, u32[]{:S(2)}) collective-permute-start(f32[1,3,3,1,16,128]{5,4,2,1,3,0:T(8,128)S(1)} %slice_bitcast_fusion.1), channel_id=1, source_target_pairs={{0,120},{8,0},{16,8},{24,16},{32,24},{40,32},{48,40},{56,48},{64,5... | collective-permute-start | bytes 221192 | tf_op jit(solution)/shard_map/ppermute | solution.py:58
  49.0 0.5 collective-permute-done.5
  49.6 1.2 %collective-permute-done.6 = f32[1,3,3,1,16,128]{5,4,2,1,3,0:T(8,128)S(1)} collective-permute-done((f32[1,3,3,1,16,128]{5,4,2,1,3,0:T(8,128)S(1)}, f32[1,3,3,1,16,128]{5,4,2,1,3,0:T(8,128)S(1)}, u32[]{:S(2)}, u32[]{:S(2)}) %collective-permute-start.6) | collective-permute-done | bytes 73760 | tf_op jit(solution)/shard_map/ppermute | solution.py:58
  50.9 0.1 copy.1240
  51.0 0.1 copy.1243
  51.3 3.4 %collective-permute-start.7 = (f32[2,1,3,3,4,1,128]{6,4,3,2,5,1,0:T(4,128)S(1)}, f32[2,1,3,3,4,1,128]{6,4,3,2,5,1,0:T(4,128)S(1)}, u32[]{:S(2)}, u32[]{:S(2)}) collective-permute-start(f32[2,1,3,3,4,1,128]{6,4,3,2,5,1,0:T(4,128)S(1)} %pad_maximum_fusion.15), channel_id=1, source_target_pairs={{0,4},{4,0},{1,5},{5,1},{2,6},{6,2},{3,7},{7,3},{8,12},{12,8},{9,1... | collective-permute-start | bytes 110600 | tf_op jit(solution)/shard_map/ppermute | solution.py:55
  54.8 0.1 copy.1227
  54.9 0.1 copy.1230
  55.2 0.9 collective-permute-done.7
  56.1 0.6 slice_bitcast_fusion.82
  57.0 0.4 collective-permute-start.9
  57.6 1.2 %collective-permute-start.8 = (f32[1,3,3,16,4]{3,4,2,1,0:T(4,128)S(1)}, f32[1,3,3,16,4]{3,4,2,1,0:T(4,128)S(1)}, u32[]{:S(2)}, u32[]{:S(2)}) collective-permute-start(f32[1,3,3,16,4]{3,4,2,1,0:T(4,128)S(1)} %fusion.13), channel_id=1, source_target_pairs={{0,1},{1,2},{2,3},{3,0},{4,5},{5,6},{6,7},{7,4},{8,9},{9,10},{10,1... | collective-permute-start | bytes 6920 | tf_op jit(solution)/shard_map/ppermute | solution.py:57
  58.9 1.1 %collective-permute-done.9 = f32[1,3,3,16,4]{3,4,2,1,0:T(4,128)S(1)} collective-permute-done((f32[1,3,3,16,4]{3,4,2,1,0:T(4,128)S(1)}, f32[1,3,3,16,4]{3,4,2,1,0:T(4,128)S(1)}, u32[]{:S(2)}, u32[]{:S(2)}) %collective-permute-start.9) | collective-permute-done | bytes 2336 | tf_op jit(solution)/shard_map/ppermute | solution.py:58
  60.0 0.8 copy.1252
  60.8 0.7 collective-permute-done.8
  61.5 0.8 copy.1239
  62.3 3.7 %shard_map.123 = (f32[27,4,16,128]{3,2,1,0:T(8,128)}, f32[4,16,128]{2,1,0:T(8,128)}) custom-call(f32[27,4,16,128]{3,2,1,0:T(8,128)} %get-tuple-element.7.an_ref, f32[27,4,16,128]{3,2,1,0:T(8,128)} %f_ref.3, f32[9,16,128]{2,1,0:T(8,128)} %bitcast.436, f32[9,16,128]{2,1,0:T(8,128)} %bitcast.439, f32[9,4,128]{2,1,0:T(4,128)} %bitcast.476, ...), custom_call_target="tpu_custom_call" | custom-call | tf_op jit(solution)/shard_map/pallas_call | solution.py:258
  66.0 0.8 add_multiply_fusion
  66.9 0.1 reduce_sum.106
  67.2 0.7 all_to_all.6
  67.9 10.5 %all-to-all-start = ((f32[128,1,8]{2,1,0:T(1,128)}), f32[128,1,8]{2,1,0:T(1,128)S(1)}, u32[]{:S(2)}, u32[]{:S(2)}) async-start(f32[128,1,8]{2,1,0:T(1,128)} %bitcast.208), calls=%async_computation | async-start | bytes 131072 | tf_op jit(solution)/shard_map/all_to_all | solution.py:293
  78.4 3.7 %shard_map.124 = (f32[27,4,16,128]{3,2,1,0:T(8,128)}, f32[4,16,128]{2,1,0:T(8,128)}) custom-call(f32[27,4,16,128]{3,2,1,0:T(8,128)} %f_ref.3, f32[27,4,16,128]{3,2,1,0:T(8,128)} %get-tuple-element.8.moved_ref, f32[4,16,128]{2,1,0:T(8,128)} %rate_ref.1, f32[4,16,128]{2,1,0:T(8,128)} %copy-done.6), custom_call_target="tpu_custom_call" | custom-call | tf_op jit(solution)/shard_map/pallas_call | solution.py:258
  82.1 6.1 %all-to-all-done = f32[128,1,8]{2,1,0:T(1,128)S(1)} async-done(((f32[128,1,8]{2,1,0:T(1,128)}), f32[128,1,8]{2,1,0:T(1,128)S(1)}, u32[]{:S(2)}, u32[]{:S(2)}) %all-to-all-start) | async-done | bytes 4128 | tf_op jit(solution)/shard_map/all_to_all | solution.py:293
  88.2 0.7 reduce_sum.109
  (191 shorter events, 5.2 us)
Async XLA Ops:
  0.6 5.6 %copy-start = (f32[27,4,16,128]{3,2,1,0:T(8,128)S(1)}, f32[27,4,16,128]{3,2,1,0:T(8,128)}, u32[]{:S(2)}) copy-start(f32[27,4,16,128]{3,2,1,0:T(8,128)} %f_ref.3) | copy-start | bytes 2654212
  0.6 3.5 %copy-start.14 = (s32[1024]{0:T(1024)S(1)}, s32[1024]{0:T(1024)}, u32[]{:S(2)}) copy-start(s32[1024]{0:T(1024)} %param.17) | copy-start | bytes 12292
  0.7 3.5 %copy-start.15 = (f32[1024]{0:T(1024)S(1)}, f32[1024]{0:T(1024)}, u32[]{:S(2)}) copy-start(f32[1024]{0:T(1024)} %param.16) | copy-start | bytes 12292
  0.7 5.6 %copy-start.11 = (s32[4,16,128]{2,1,0:T(8,128)S(1)}, s32[4,16,128]{2,1,0:T(8,128)}, u32[]{:S(2)}) copy-start(s32[4,16,128]{2,1,0:T(8,128)} %param.14) | copy-start | bytes 98308
  1.8 4.5 %copy-start.9 = (f32[4,16,128]{2,1,0:T(8,128)S(1)}, f32[4,16,128]{2,1,0:T(8,128)}, u32[]{:S(2)}) copy-start(f32[4,16,128]{2,1,0:T(8,128)} %rate_ref.1) | copy-start | bytes 98308
  1.9 4.5 %copy-start.16 = (f32[27]{0:T(128)S(1)}, f32[27]{0:T(128)}, u32[]{:S(2)}) copy-start(f32[27]{0:T(128)} %constant.24.clone) | copy-start | bytes 328
  1.9 4.5 %copy-start.17 = (f32[27]{0:T(128)S(1)}, f32[27]{0:T(128)}, u32[]{:S(2)}) copy-start(f32[27]{0:T(128)} %constant.25.clone) | copy-start | bytes 328
  1.9 4.5 %copy-start.18 = (f32[27]{0:T(128)S(1)}, f32[27]{0:T(128)}, u32[]{:S(2)}) copy-start(f32[27]{0:T(128)} %constant.26.clone) | copy-start | bytes 328
  1.9 4.5 %copy-start.19 = (f32[27]{0:T(128)S(1)}, f32[27]{0:T(128)}, u32[]{:S(2)}) copy-start(f32[27]{0:T(128)} %constant.27.clone) | copy-start | bytes 328
  6.3 1.6 %copy-start.6 = (f32[4,16,128]{2,1,0:T(8,128)}, f32[4,16,128]{2,1,0:T(8,128)S(1)}, u32[]{:S(2)}) copy-start(f32[4,16,128]{2,1,0:T(8,128)S(1)} %get-tuple-element.150.refs_7_.gamma_ref) | copy-start | bytes 98308
  6.4 1.5 %copy-start.3 = (f32[27,4,16,128]{3,2,1,0:T(8,128)S(1)}, f32[27,4,16,128]{3,2,1,0:T(8,128)}, u32[]{:S(2)}) copy-start(f32[27,4,16,128]{3,2,1,0:T(8,128)} %ae_ref.1) | copy-start | bytes 2654212
  7.8 6.6 %copy-start.1 = (f32[27,4,16,128]{3,2,1,0:T(8,128)}, f32[27,4,16,128]{3,2,1,0:T(8,128)S(1)}, u32[]{:S(2)}) copy-start(f32[27,4,16,128]{3,2,1,0:T(8,128)S(1)} %fusion.7.cf_ref) | copy-start | bytes 2654212
  8.7 10.6 %collective-permute-start.1 = (f32[2,3,3,1,16,128]{5,4,2,1,3,0:T(8,128)}, f32[2,3,3,1,16,128]{5,4,2,1,3,0:T(8,128)}, u32[]{:S(2)}, u32[]{:S(2)}) collective-permute-start(f32[2,3,3,1,16,128]{5,4,2,1,3,0:T(8,128)} %pad_maximum_fusion.4), channel_id=1, source_target_pairs={{0,120},{8,0},{16,8},{24,16},{32,24},{40,32},{48,40},{56,48},{64,5... | collective-permute-start | bytes 442376 | tf_op jit(solution)/shard_map/ppermute | solution.py:58
  10.8 9.6 %collective-permute-start = (f32[2,3,3,1,16,128]{5,4,2,1,3,0:T(8,128)}, f32[2,3,3,1,16,128]{5,4,2,1,3,0:T(8,128)}, u32[]{:S(2)}, u32[]{:S(2)}) collective-permute-start(f32[2,3,3,1,16,128]{5,4,2,1,3,0:T(8,128)} %pad_maximum_fusion.3), channel_id=1, source_target_pairs={{0,8},{8,16},{16,24},{24,32},{32,40},{40,48},{48,56},{56,64},{64,7... | collective-permute-start | bytes 442376 | tf_op jit(solution)/shard_map/ppermute | solution.py:57
  15.2 2.0 %copy-start.4 = (f32[2,3,3,3,4,16,1]{6,5,4,3,2,1,0:T(8,128)S(1)}, f32[2,3,3,3,4,16,1]{6,5,4,3,2,1,0:T(8,128)}, u32[]{:S(2)}) copy-start(f32[2,3,3,3,4,16,1]{6,5,4,3,2,1,0:T(8,128)} %get-tuple-element.25) | copy-start | bytes 41476
  17.2 1.3 %copy-start.10 = (f32[2,3,3,3,4,16,1]{5,4,6,3,2,1,0:T(4,128)S(1)}, f32[2,3,3,3,4,16,1]{5,4,6,3,2,1,0:T(4,128)}, u32[]{:S(2)}) copy-start(f32[2,3,3,3,4,16,1]{5,4,6,3,2,1,0:T(4,128)} %copy.1179) | copy-start | bytes 41476
  17.2 1.5 %copy-start.5 = (f32[2,3,3,3,4,2,128]{6,5,4,3,2,1,0:T(2,128)S(1)}, f32[2,3,3,3,4,2,128]{6,5,4,3,2,1,0:T(2,128)}, u32[]{:S(2)}) copy-start(f32[2,3,3,3,4,2,128]{6,5,4,3,2,1,0:T(2,128)} %fusion.8) | copy-start | bytes 663556
  22.3 5.1 %collective-permute-start.2 = (f32[2,2,3,3,4,1,128]{6,4,3,2,1,5,0:T(4,128)S(1)}, f32[2,2,3,3,4,1,128]{6,4,3,2,1,5,0:T(4,128)S(1)}, u32[]{:S(2)}, u32[]{:S(2)}) collective-permute-start(f32[2,2,3,3,4,1,128]{6,4,3,2,1,5,0:T(4,128)S(1)} %pad_maximum_fusion.6), channel_id=1, source_target_pairs={{0,4},{4,0},{1,5},{5,1},{2,6},{6,2},{3,7},{7,3},{8,12},{12,8},{9,1... | collective-permute-start | bytes 221192 | tf_op jit(solution)/shard_map/ppermute | solution.py:55
  28.1 3.6 %collective-permute-start.4 = (f32[2,3,3,16,4]{3,4,2,1,0:T(4,128)S(1)}, f32[2,3,3,16,4]{3,4,2,1,0:T(4,128)S(1)}, u32[]{:S(2)}, u32[]{:S(2)}) collective-permute-start(f32[2,3,3,16,4]{3,4,2,1,0:T(4,128)S(1)} %pad_maximum_fusion.14), channel_id=1, source_target_pairs={{0,3},{1,0},{2,1},{3,2},{4,7},{5,4},{6,5},{7,6},{8,11},{9,8},{10,9... | collective-permute-start | bytes 13832 | tf_op jit(solution)/shard_map/ppermute | solution.py:58
  31.0 4.1 %collective-permute-start.3 = (f32[2,3,3,16,4]{3,4,2,1,0:T(4,128)S(1)}, f32[2,3,3,16,4]{3,4,2,1,0:T(4,128)S(1)}, u32[]{:S(2)}, u32[]{:S(2)}) collective-permute-start(f32[2,3,3,16,4]{3,4,2,1,0:T(4,128)S(1)} %pad_maximum_fusion.13), channel_id=1, source_target_pairs={{0,1},{1,2},{2,3},{3,0},{4,5},{5,6},{6,7},{7,4},{8,9},{9,10},{10,1... | collective-permute-start | bytes 13832 | tf_op jit(solution)/shard_map/ppermute | solution.py:57
  40.8 1.3 %copy-start.2 = (f32[27,4,16,128]{3,2,1,0:T(8,128)S(1)}, f32[27,4,16,128]{3,2,1,0:T(8,128)}, u32[]{:S(2)}) copy-start(f32[27,4,16,128]{3,2,1,0:T(8,128)} %get-tuple-element.7.an_ref) | copy-start | bytes 2654212
  44.1 5.4 %collective-permute-start.5 = (f32[1,3,3,1,16,128]{5,4,2,1,3,0:T(8,128)S(1)}, f32[1,3,3,1,16,128]{5,4,2,1,3,0:T(8,128)S(1)}, u32[]{:S(2)}, u32[]{:S(2)}) collective-permute-start(f32[1,3,3,1,16,128]{5,4,2,1,3,0:T(8,128)S(1)} %slice_bitcast_fusion.2), channel_id=1, source_target_pairs={{0,8},{8,16},{16,24},{24,32},{32,40},{40,48},{48,56},{56,64},{64,7... | collective-permute-start | bytes 221192 | tf_op jit(solution)/shard_map/ppermute | solution.py:57
  46.9 3.8 %collective-permute-start.6 = (f32[1,3,3,1,16,128]{5,4,2,1,3,0:T(8,128)S(1)}, f32[1,3,3,1,16,128]{5,4,2,1,3,0:T(8,128)S(1)}, u32[]{:S(2)}, u32[]{:S(2)}) collective-permute-start(f32[1,3,3,1,16,128]{5,4,2,1,3,0:T(8,128)S(1)} %slice_bitcast_fusion.1), channel_id=1, source_target_pairs={{0,120},{8,0},{16,8},{24,16},{32,24},{40,32},{48,40},{56,48},{64,5... | collective-permute-start | bytes 221192 | tf_op jit(solution)/shard_map/ppermute | solution.py:58
  49.5 12.8 %copy-start.7 = (f32[1,3,3,1,16,128]{5,4,2,1,3,0:T(8,128)}, f32[1,3,3,1,16,128]{5,4,2,1,3,0:T(8,128)S(1)}, u32[]{:S(2)}) copy-start(f32[1,3,3,1,16,128]{5,4,2,1,3,0:T(8,128)S(1)} %collective-permute-done.5) | copy-start | bytes 221188
  50.8 11.5 %copy-start.8 = (f32[1,3,3,1,16,128]{5,4,2,1,3,0:T(8,128)}, f32[1,3,3,1,16,128]{5,4,2,1,3,0:T(8,128)S(1)}, u32[]{:S(2)}) copy-start(f32[1,3,3,1,16,128]{5,4,2,1,3,0:T(8,128)S(1)} %collective-permute-done.6) | copy-start | bytes 221188
  51.3 4.7 %collective-permute-start.7 = (f32[2,1,3,3,4,1,128]{6,4,3,2,5,1,0:T(4,128)S(1)}, f32[2,1,3,3,4,1,128]{6,4,3,2,5,1,0:T(4,128)S(1)}, u32[]{:S(2)}, u32[]{:S(2)}) collective-permute-start(f32[2,1,3,3,4,1,128]{6,4,3,2,5,1,0:T(4,128)S(1)} %pad_maximum_fusion.15), channel_id=1, source_target_pairs={{0,4},{4,0},{1,5},{5,1},{2,6},{6,2},{3,7},{7,3},{8,12},{12,8},{9,1... | collective-permute-start | bytes 110600 | tf_op jit(solution)/shard_map/ppermute | solution.py:55
  54.8 11.2 %copy-start.12 = (s32[4,16,128]{2,1,0:T(8,128)S(1)}, s32[4,16,128]{2,1,0:T(8,128)}, u32[]{:S(2)}) copy-start(s32[4,16,128]{2,1,0:T(8,128)} %param.14) | copy-start | bytes 98308
  54.8 11.2 %copy-start.13 = (f32[4,16,128]{2,1,0:T(8,128)S(1)}, f32[4,16,128]{2,1,0:T(8,128)}, u32[]{:S(2)}) copy-start(f32[4,16,128]{2,1,0:T(8,128)} %get-tuple-element.10) | copy-start | bytes 98308
  57.0 3.0 %collective-permute-start.9 = (f32[1,3,3,16,4]{3,4,2,1,0:T(4,128)S(1)}, f32[1,3,3,16,4]{3,4,2,1,0:T(4,128)S(1)}, u32[]{:S(2)}, u32[]{:S(2)}) collective-permute-start(f32[1,3,3,16,4]{3,4,2,1,0:T(4,128)S(1)} %fusion.12), channel_id=1, source_target_pairs={{0,3},{1,0},{2,1},{3,2},{4,7},{5,4},{6,5},{7,6},{8,11},{9,8},{10,9... | collective-permute-start | bytes 6920 | tf_op jit(solution)/shard_map/ppermute | solution.py:58
  57.6 3.9 %collective-permute-start.8 = (f32[1,3,3,16,4]{3,4,2,1,0:T(4,128)S(1)}, f32[1,3,3,16,4]{3,4,2,1,0:T(4,128)S(1)}, u32[]{:S(2)}, u32[]{:S(2)}) collective-permute-start(f32[1,3,3,16,4]{3,4,2,1,0:T(4,128)S(1)} %fusion.13), channel_id=1, source_target_pairs={{0,1},{1,2},{2,3},{3,0},{4,5},{5,6},{6,7},{7,4},{8,9},{9,10},{10,1... | collective-permute-start | bytes 6920 | tf_op jit(solution)/shard_map/ppermute | solution.py:57
  67.9 20.3 %all-to-all-start = ((f32[128,1,8]{2,1,0:T(1,128)}), f32[128,1,8]{2,1,0:T(1,128)S(1)}, u32[]{:S(2)}, u32[]{:S(2)}) async-start(f32[128,1,8]{2,1,0:T(1,128)} %bitcast.208), calls=%async_computation | async-start | bytes 131072 | tf_op jit(solution)/shard_map/all_to_all | solution.py:293

commit v11 on v9

--- a/solution.py
+++ b/solution.py
@@ -86,8 +86,8 @@
     xlo, xhi = halo_exchange(jnp.stack(x_up), jnp.stack(x_dn), "gx")
     both = jnp.stack(cubes)
     rows = jnp.concatenate([both[..., sy - 1 : sy, :], both[..., 0:1, :]], axis=5)
-    lane = lax.broadcasted_iota(jnp.int32, both.shape, both.ndim - 1)
-    cols = [jnp.sum(jnp.where(lane == z0, both, 0.0), axis=-1) for z0 in (sz - 1, 0)]
+    pick = (jnp.arange(sz)[:, None] == jnp.array([sz - 1, 0])[None, :]).astype(jnp.float32)
+    cols = jnp.einsum("nabcxyz,zk->knabcxy", both, pick, precision=lax.Precision.HIGHEST)
     y_up, y_dn = [], []
     for k, s in enumerate(signs):
         top = shifted(rows[k][..., 0:1, :], xlo[k][:, :, :, sy - 1 : sy], xhi[k][:, :, :, sy - 1 : sy], 0, s)
@@ -99,7 +99,7 @@
     for k, s in enumerate(signs):
         picked = []
         for at, z0 in ((0, sz - 1), (1, 0)):
-            col = shifted(cols[at][k], xlo[k][..., z0], xhi[k][..., z0], 0, s)
+            col = shifted(cols[at, k], xlo[k][..., z0], xhi[k][..., z0], 0, s)
             col = shifted(col, ylo[k][..., z0], yhi[k][..., z0], 1, s)
             picked.append(col)
         z_up.append(jnp.swapaxes(lax.index_in_dim(picked[0], 1 + s, axis=2, keepdims=False), -1, -2))

time: 90.1 us -> 95.4 us (1.059)
  matrix products: 0 us -> 9.47 us
  other arithmetic: 12.5 us -> 7.32 us
  waiting for transfers between devices: 8.33 us -> 5.5 us
  local copies, waits for them, and re-layouts: 15.1 us -> 17.6 us
  blocking collectives: 22.1 us -> 23.4 us
    dot_general x0 -> x2, matrix products: none -> 9.47 us  [halos(): jnp.einsum('nabcxyz,zk->knabcxy', both, pick, precision=lax.Precision.HIG...]
    reduce_sum x2 -> x0, other arithmetic: 4.21 us -> none  [halos(): jnp.sum(jnp.where(lane == z0, both, 0.0), axis=-1)]
    ppermute x4, starting transfers between devices: 7.27 us -> 9.86 us  [halo_exchange(): lo = lax.ppermute(up, axis, [(i, (i + 1) % size) for i in range(size)])]
    ppermute x4, waiting for transfers between devices: 2.95 us -> 0.57 us  [halo_exchange(): lo = lax.ppermute(up, axis, [(i, (i + 1) % size) for i in range(size)])]
    ppermute x4, starting transfers between devices: 6.57 us -> 4.19 us  [halo_exchange(): hi = lax.ppermute(down, axis, [(i, (i - 1) % size) for i in range(size)])]
    slice x3 -> x2, local copies, waits for them, and re-layouts: 0.03 us -> 1.67 us  [halos(): xhi[k][:, :, :, sy - 1:sy]]
    slice x3 -> x2, local copies, waits for them, and re-layouts: 0.03 us -> 1.66 us  [halos(): xlo[k][:, :, :, sy - 1:sy]]
    all_to_all x1, blocking collectives: 22.1 us -> 23.4 us  [shards(): lax.all_to_all(placed.reshape(devices, count // devices), ('gx', 'gy', 'g...]
  transfers between devices with their start and end apart: 10 -> 10, of which waited for: 6 -> 6; matrix products, arithmetic and copies ran while one was open for 11% -> 13% of each run, Pallas kernels for 0% -> 0%
where the time goes in v11:
time: 95.4 us; the launch traced here: 94.9 us
  blocking collectives  23.4 us (25%)
  starting transfers between devices  20.8 us (22%)
  local copies, waits for them, and re-layouts  17.6 us (18%)
  matrix products  9.47 us (10%)
  Pallas kernels  9.1 us (10%)
  other arithmetic  7.32 us (8%)
  waiting for transfers between devices  5.5 us (6%)
  between operations  1.83 us (2%)
    all_to_all x1, blocking collectives, shards(): lax.all_to_all(placed.reshape(devices, count // devices), ('gx', 'gy', 'g...  23.4 us
    ppermute x4, starting transfers between devices, halo_exchange(): lo = lax.ppermute(up, axis, [(i, (i + 1) % size) for i in range(size)])  9.86 us
    dot_general x2, matrix products, halos(): jnp.einsum('nabcxyz,zk->knabcxy', both, pick, precision=lax.Precision.HIG...  9.47 us
    pallas_call x2, Pallas kernels, run_stage(): pl.pallas_call(kernel, out_shape=(jax.ShapeDtypeStruct(shape, jnp.float32...  9.1 us
    ppermute x2, starting transfers between devices, halo_exchange(): both = lax.ppermute(jnp.stack([up, down]), axis, [(0, 1), (1, 0)])  6.77 us
    ppermute x4, starting transfers between devices, halo_exchange(): hi = lax.ppermute(down, axis, [(i, (i - 1) % size) for i in range(size)])  4.19 us
    ppermute x2, waiting for transfers between devices, halo_exchange(): both = lax.ppermute(jnp.stack([up, down]), axis, [(0, 1), (1, 0)])  2.47 us
    ppermute x4, waiting for transfers between devices, halo_exchange(): hi = lax.ppermute(down, axis, [(i, (i - 1) % size) for i in range(size)])  2.46 us
  transfers between devices with their start and end apart: 10, of which 6 were waited for; matrix products, arithmetic and copies ran while one was open for 13% of the time, Pallas kernels for 0%

profile of v11, /device:TPU:1, one launch (start us, length us, event | category | flops | bytes accessed | tf_op | source)
XLA Modules:
  0.0 94.9 jit_solution(991527934207245538)
XLA Ops:
  0.7 1.2 %slice_reduce_fusion.2 = (f32[4,16,128]{2,1,0:T(8,128)S(1)}, f32[4,16,128]{2,1,0:T(8,128)S(1)}) fusion(f32[3,3,3,4,16,128]{5,4,3,2,1,0:T(8,128)} %bitcast.407), kind=kLoop, calls=%fused_computation.16 | loop fusion | flops 131072 | bytes 655360 | tf_op jit(solution)/shard_map/reduce_sum | solution.py:33
  1.8 1.1 %slice_reduce_fusion = (f32[4,16,128]{2,1,0:T(8,128)S(1)}, f32[4,16,128]{2,1,0:T(8,128)S(1)}) fusion(f32[3,3,3,4,16,128]{5,4,3,2,1,0:T(8,128)} %bitcast.408), kind=kLoop, calls=%fused_computation.14 | loop fusion | flops 131072 | bytes 655360 | tf_op jit(solution)/shard_map/reduce_sum | solution.py:34
  3.0 0.9 slice.660
  4.1 0.2 copy.342
  4.4 0.6 gather_fusion
  5.0 0.1 copy.423
  5.2 0.1 reshape.164
  5.5 0.6 copy-done.7
  6.1 1.4 %fusion.11.cf_ref = f32[27,4,16,128]{3,2,1,0:T(8,128)S(1)} fusion(f32[27,4,16,128]{3,2,1,0:T(8,128)S(1)} %copy-done, f32[4,16,128]{2,1,0:T(8,128)S(1)} %get-tuple-element.142.refs_7_, f32[4,16,128]{2,1,0:T(8,128)S(1)} %get-tuple-element.30, f32[4,16,128]{2,1,0:T(8,128)S(1)} %get-tuple-element.33, f32[27]{0:T(128)S(1)} %copy-done.16, ...), kind=kLoop, calls=%fused_computation.13 | loop fusion | flops 4202496 | bytes 2032048 | tf_op jit(solution)/shard_map/add | solution.py:47
  7.6 3.1 %collective-permute-start = (f32[2,3,3,1,16,128]{5,4,2,1,3,0:T(8,128)S(1)}, f32[2,3,3,1,16,128]{5,4,2,1,3,0:T(8,128)S(1)}, u32[]{:S(2)}, u32[]{:S(2)}) collective-permute-start(f32[2,3,3,1,16,128]{5,4,2,1,3,0:T(8,128)S(1)} %pad_maximum_fusion.2), channel_id=1, source_target_pairs={{0,8},{8,16},{16,24},{24,32},{32,40},{40,48},{48,56},{56,64},{64,7... | collective-permute-start | bytes 442376 | tf_op jit(solution)/shard_map/ppermute | solution.py:57
  10.8 0.1 copy.466
  10.9 0.1 copy.467
  11.0 0.1 copy.468
  11.1 0.2 fusion.12
  11.6 0.4 copy-done.14
  12.0 6.3 %fusion = f32[2,2,3,3,3,4,16]{6,0,5,4,3,2,1:T(2,128)S(1)} fusion(f32[1,3,3,3,4,16,128]{6,5,4,3,2,1,0:T(8,128)S(1)} %bitcast.412, f32[1,3,3,3,4,16,128]{6,5,4,3,2,1,0:T(8,128)S(1)} %bitcast.410, s32[2]{0:T(128)S(1)} %copy-done.14), kind=kOutput, calls=%fused_computation.1 | convolution fusion | flops 11059456 | bytes 1797128 | tf_op jit(solution)/shard_map/nabcxyz,zk->knabcxy/dot_general | solution.py:90
  18.2 0.2 fusion.37
  18.6 0.2 slice_reduce_fusion.8
  18.7 0.2 slice_reduce_fusion.7
  19.0 0.2 slice_reduce_fusion.9
  19.2 0.2 slice_reduce_fusion.6
  20.0 3.4 %collective-permute-start.2 = (f32[2,2,3,3,4,1,128]{6,4,3,2,1,5,0:T(4,128)S(1)}, f32[2,2,3,3,4,1,128]{6,4,3,2,1,5,0:T(4,128)S(1)}, u32[]{:S(2)}, u32[]{:S(2)}) collective-permute-start(f32[2,2,3,3,4,1,128]{6,4,3,2,1,5,0:T(4,128)S(1)} %pad_maximum_fusion.4), channel_id=1, source_target_pairs={{0,4},{4,0},{1,5},{5,1},{2,6},{6,2},{3,7},{7,3},{8,12},{12,8},{9,1... | collective-permute-start | bytes 221192 | tf_op jit(solution)/shard_map/ppermute | solution.py:55
  23.8 1.4 %collective-permute-done.2 = f32[2,2,3,3,4,1,128]{6,4,3,2,1,5,0:T(4,128)S(1)} collective-permute-done((f32[2,2,3,3,4,1,128]{6,4,3,2,1,5,0:T(4,128)S(1)}, f32[2,2,3,3,4,1,128]{6,4,3,2,1,5,0:T(4,128)S(1)}, u32[]{:S(2)}, u32[]{:S(2)}) %collective-permute-start.2) | collective-permute-done | bytes 73760 | tf_op jit(solution)/shard_map/ppermute | solution.py:55
  25.2 0.2 slice_reduce_fusion.15
  25.4 0.2 slice_reduce_fusion.14
  25.6 0.1 copy.368
  25.7 0.1 copy.382
  25.8 0.1 copy.367
  26.0 0.1 copy.381
  26.7 1.3 %collective-permute-start.3 = (f32[2,3,3,16,4]{3,4,1,2,0:T(4,128)S(1)}, f32[2,3,3,16,4]{3,4,1,2,0:T(4,128)S(1)}, u32[]{:S(2)}, u32[]{:S(2)}) collective-permute-start(f32[2,3,3,16,4]{3,4,1,2,0:T(4,128)S(1)} %pad_maximum_fusion.11), channel_id=1, source_target_pairs={{0,1},{1,2},{2,3},{3,0},{4,5},{5,6},{6,7},{7,4},{8,9},{9,10},{10,1... | collective-permute-start | bytes 13832 | tf_op jit(solution)/shard_map/ppermute | solution.py:57
  28.3 1.5 %collective-permute-start.4 = (f32[2,3,3,16,4]{3,4,1,2,0:T(4,128)S(1)}, f32[2,3,3,16,4]{3,4,1,2,0:T(4,128)S(1)}, u32[]{:S(2)}, u32[]{:S(2)}) collective-permute-start(f32[2,3,3,16,4]{3,4,1,2,0:T(4,128)S(1)} %pad_maximum_fusion.12), channel_id=1, source_target_pairs={{0,3},{1,0},{2,1},{3,2},{4,7},{5,4},{6,5},{7,6},{8,11},{9,8},{10,9... | collective-permute-start | bytes 13832 | tf_op jit(solution)/shard_map/ppermute | solution.py:58
  29.9 0.6 fusion.41
  30.5 0.7 collective-permute-done.4
  31.2 0.8 copy.391
  32.0 0.9 copy.377
  32.9 4.9 %shard_map.140 = (f32[27,4,16,128]{3,2,1,0:T(8,128)}, f32[4,16,128]{2,1,0:T(8,128)}) custom-call(f32[27,4,16,128]{3,2,1,0:T(8,128)} %copy-done.1, f32[27,4,16,128]{3,2,1,0:T(8,128)} %ae_ref.1, f32[18,16,128]{2,1,0:T(8,128)} %bitcast.419, f32[18,16,128]{2,1,0:T(8,128)} %bitcast.420, f32[18,4,128]{2,1,0:T(4,128)} %bitcast.438, f32[18,4,128]{2,1,0:T(4,128)} %bitcast.437, ...), custom_call_target="tpu_custom_call" | custom-call | tf_op jit(solution)/shard_map/pallas_call | solution.py:242
  37.7 1.2 %fusion.32 = (f32[9,4,16,128]{3,2,1,0:T(8,128)S(1)}, f32[9,4,16,128]{3,2,1,0:T(8,128)S(1)}) fusion(f32[27,4,16,128]{3,2,1,0:T(8,128)} %get-tuple-element.6.an_ref), kind=kLoop, calls=%fused_computation.211 | loop fusion | bytes 1179648 | tf_op jit(solution)/shard_map/slice | solution.py:78
  38.9 0.2 copy-done.3
  39.1 3.2 %fusion.25 = f32[2,3,3,3,4,16]{5,0,4,3,2,1:T(2,128)S(1)} fusion(f32[3,3,3,4,16,128]{5,4,3,2,1,0:T(8,128)S(1)} %bitcast.413, s32[2]{0:T(128)S(1)} %copy-done.14), kind=kOutput, calls=%fused_computation.201 | convolution fusion | flops 5308672 | bytes 898568 | tf_op jit(solution)/shard_map/nabcxyz,zk->knabcxy/dot_general | solution.py:90
  42.5 4.2 %collective-permute-start.5 = (f32[1,3,3,1,16,128]{5,4,3,2,1,0:T(8,128)S(1)}, f32[1,3,3,1,16,128]{5,4,3,2,1,0:T(8,128)S(1)}, u32[]{:S(2)}, u32[]{:S(2)}) collective-permute-start(f32[1,3,3,1,16,128]{5,4,3,2,1,0:T(8,128)S(1)} %slice_bitcast_fusion.2), channel_id=1, source_target_pairs={{0,8},{8,16},{16,24},{24,32},{32,40},{40,48},{48,56},{56,64},{64,7... | collective-permute-start | bytes 221192 | tf_op jit(solution)/shard_map/ppermute | solution.py:57
  46.8 1.0 %collective-permute-start.6 = (f32[1,3,3,1,16,128]{5,4,3,2,1,0:T(8,128)S(1)}, f32[1,3,3,1,16,128]{5,4,3,2,1,0:T(8,128)S(1)}, u32[]{:S(2)}, u32[]{:S(2)}) collective-permute-start(f32[1,3,3,1,16,128]{5,4,3,2,1,0:T(8,128)S(1)} %slice_bitcast_fusion.1), channel_id=1, source_target_pairs={{0,120},{8,0},{16,8},{24,16},{32,24},{40,32},{48,40},{56,48},{64,5... | collective-permute-start | bytes 221192 | tf_op jit(solution)/shard_map/ppermute | solution.py:58
  47.9 0.6 collective-permute-done.5
  48.4 0.2 copy.394
  48.7 1.3 %fusion.35 = (f32[3,3,1,1,128]{3,2,4,1,0:T(1,128)S(1)}, f32[3,3,1,1,128]{3,2,4,1,0:T(1,128)S(1)}) fusion(f32[3,3,1,16,128]{3,2,4,1,0:T(1,128)S(1)} %bitcast.415), kind=kLoop, calls=%fused_computation.214 | loop fusion | bytes 18432 | tf_op jit(solution)/shard_map/slice | solution.py:93
  50.0 0.7 collective-permute-done.6
  50.7 0.2 copy.398
  50.9 1.3 %fusion.36 = (f32[3,3,1,1,128]{3,2,4,1,0:T(1,128)S(1)}, f32[3,3,1,1,128]{3,2,4,1,0:T(1,128)S(1)}) fusion(f32[3,3,1,16,128]{3,2,4,1,0:T(1,128)S(1)} %bitcast.418), kind=kLoop, calls=%fused_computation.215 | loop fusion | bytes 18432 | tf_op jit(solution)/shard_map/slice | solution.py:93
  52.3 0.4 copy.397
  52.7 0.4 copy.400
  53.1 0.4 copy.399
  53.5 0.4 copy.401
  54.0 3.4 %collective-permute-start.7 = (f32[2,1,3,3,4,1,128]{6,4,3,2,5,1,0:T(4,128)S(1)}, f32[2,1,3,3,4,1,128]{6,4,3,2,5,1,0:T(4,128)S(1)}, u32[]{:S(2)}, u32[]{:S(2)}) collective-permute-start(f32[2,1,3,3,4,1,128]{6,4,3,2,5,1,0:T(4,128)S(1)} %pad_maximum_fusion.13), channel_id=1, source_target_pairs={{0,4},{4,0},{1,5},{5,1},{2,6},{6,2},{3,7},{7,3},{8,12},{12,8},{9,1... | collective-permute-start | bytes 110600 | tf_op jit(solution)/shard_map/ppermute | solution.py:55
  57.7 1.1 %collective-permute-done.7 = f32[2,1,3,3,4,1,128]{6,4,3,2,5,1,0:T(4,128)S(1)} collective-permute-done((f32[2,1,3,3,4,1,128]{6,4,3,2,5,1,0:T(4,128)S(1)}, f32[2,1,3,3,4,1,128]{6,4,3,2,5,1,0:T(4,128)S(1)}, u32[]{:S(2)}, u32[]{:S(2)}) %collective-permute-start.7) | collective-permute-done | bytes 36896 | tf_op jit(solution)/shard_map/ppermute | solution.py:55
  58.8 0.6 slice_bitcast_fusion.64
  59.7 1.3 %collective-permute-start.8 = (f32[1,3,3,16,4]{3,4,1,2,0:T(4,128)S(1)}, f32[1,3,3,16,4]{3,4,1,2,0:T(4,128)S(1)}, u32[]{:S(2)}, u32[]{:S(2)}) collective-permute-start(f32[1,3,3,16,4]{3,4,1,2,0:T(4,128)S(1)} %fusion.14), channel_id=1, source_target_pairs={{0,1},{1,2},{2,3},{3,0},{4,5},{5,6},{6,7},{7,4},{8,9},{9,10},{10,1... | collective-permute-start | bytes 6920 | tf_op jit(solution)/shard_map/ppermute | solution.py:57
  61.2 1.5 %collective-permute-start.9 = (f32[1,3,3,16,4]{3,4,1,2,0:T(4,128)S(1)}, f32[1,3,3,16,4]{3,4,1,2,0:T(4,128)S(1)}, u32[]{:S(2)}, u32[]{:S(2)}) collective-permute-start(f32[1,3,3,16,4]{3,4,1,2,0:T(4,128)S(1)} %fusion.13), channel_id=1, source_target_pairs={{0,3},{1,0},{2,1},{3,2},{4,7},{5,4},{6,5},{7,6},{8,11},{9,8},{10,9... | collective-permute-start | bytes 6920 | tf_op jit(solution)/shard_map/ppermute | solution.py:58
  62.8 1.0 %collective-permute-done.9 = f32[1,3,3,16,4]{3,4,1,2,0:T(4,128)S(1)} collective-permute-done((f32[1,3,3,16,4]{3,4,1,2,0:T(4,128)S(1)}, f32[1,3,3,16,4]{3,4,1,2,0:T(4,128)S(1)}, u32[]{:S(2)}, u32[]{:S(2)}) %collective-permute-start.9) | collective-permute-done | bytes 2336 | tf_op jit(solution)/shard_map/ppermute | solution.py:58
  63.9 0.8 copy.417
  64.6 0.8 copy.410
  65.4 4.2 %shard_map.141 = (f32[27,4,16,128]{3,2,1,0:T(8,128)}, f32[4,16,128]{2,1,0:T(8,128)}) custom-call(f32[27,4,16,128]{3,2,1,0:T(8,128)} %get-tuple-element.6.an_ref, f32[27,4,16,128]{3,2,1,0:T(8,128)} %f_ref.1, f32[9,16,128]{2,1,0:T(8,128)} %bitcast.432, f32[9,16,128]{2,1,0:T(8,128)} %bitcast.433, f32[9,4,128]{2,1,0:T(4,128)} %bitcast.474, ...), custom_call_target="tpu_custom_call" | custom-call | tf_op jit(solution)/shard_map/pallas_call | solution.py:242
  69.6 0.8 add_multiply_fusion
  70.5 0.1 reduce_sum.106
  70.9 23.4 %all_to_all.9 = f32[128,1,8]{2,1,0:T(1,128)S(1)} all-to-all(f32[128,1,8]{2,1,0:T(1,128)S(1)} %bitcast.434), channel_id=1, replica_groups=mesh['gx'=16,'gy'=2,'gz'=4] {'gx','gy','gz'}, dimensions={0} | all-to-all | bytes 8192 | tf_op jit(solution)/shard_map/all_to_all | solution.py:276
  94.3 0.7 reduce_sum.109
  (186 shorter events, 4.2 us)
Async XLA Ops:
  0.6 2.3 %copy-start = (f32[27,4,16,128]{3,2,1,0:T(8,128)S(1)}, f32[27,4,16,128]{3,2,1,0:T(8,128)}, u32[]{:S(2)}) copy-start(f32[27,4,16,128]{3,2,1,0:T(8,128)} %f_ref.1) | copy-start | bytes 2654212
  0.6 3.4 %copy-start.12 = (s32[1024]{0:T(1024)S(1)}, s32[1024]{0:T(1024)}, u32[]{:S(2)}) copy-start(s32[1024]{0:T(1024)} %param.19) | copy-start | bytes 12292
  2.9 1.2 %copy-start.13 = (f32[1024]{0:T(1024)S(1)}, f32[1024]{0:T(1024)}, u32[]{:S(2)}) copy-start(f32[1024]{0:T(1024)} %param.18) | copy-start | bytes 12292
  3.0 2.3 %copy-start.2 = (f32[27,4,16,128]{3,2,1,0:T(8,128)S(1)}, f32[27,4,16,128]{3,2,1,0:T(8,128)}, u32[]{:S(2)}) copy-start(f32[27,4,16,128]{3,2,1,0:T(8,128)} %ae_ref.1) | copy-start | bytes 2654212
  4.4 1.0 %copy-start.10 = (s32[4,16,128]{2,1,0:T(8,128)S(1)}, s32[4,16,128]{2,1,0:T(8,128)}, u32[]{:S(2)}) copy-start(s32[4,16,128]{2,1,0:T(8,128)} %param.16) | copy-start | bytes 98308
  5.3 0.8 copy-start.7
  5.3 0.8 copy-start.15
  5.3 0.7 copy-start.16
  5.3 0.7 copy-start.17
  5.3 0.7 copy-start.18
  5.5 2.0 %copy-start.6 = (f32[4,16,128]{2,1,0:T(8,128)}, f32[4,16,128]{2,1,0:T(8,128)S(1)}, u32[]{:S(2)}) copy-start(f32[4,16,128]{2,1,0:T(8,128)S(1)} %get-tuple-element.142.refs_7_) | copy-start | bytes 98308
  7.5 4.1 %copy-start.1 = (f32[27,4,16,128]{3,2,1,0:T(8,128)}, f32[27,4,16,128]{3,2,1,0:T(8,128)S(1)}, u32[]{:S(2)}) copy-start(f32[27,4,16,128]{3,2,1,0:T(8,128)S(1)} %fusion.11.cf_ref) | copy-start | bytes 2654212
  7.6 10.9 %collective-permute-start = (f32[2,3,3,1,16,128]{5,4,2,1,3,0:T(8,128)S(1)}, f32[2,3,3,1,16,128]{5,4,2,1,3,0:T(8,128)S(1)}, u32[]{:S(2)}, u32[]{:S(2)}) collective-permute-start(f32[2,3,3,1,16,128]{5,4,2,1,3,0:T(8,128)S(1)} %pad_maximum_fusion.2), channel_id=1, source_target_pairs={{0,8},{8,16},{16,24},{24,32},{32,40},{40,48},{48,56},{56,64},{64,7... | collective-permute-start | bytes 442376 | tf_op jit(solution)/shard_map/ppermute | solution.py:57
  10.7 8.2 %collective-permute-start.1 = (f32[2,3,3,1,16,128]{5,4,2,1,3,0:T(8,128)S(1)}, f32[2,3,3,1,16,128]{5,4,2,1,3,0:T(8,128)S(1)}, u32[]{:S(2)}, u32[]{:S(2)}) collective-permute-start(f32[2,3,3,1,16,128]{5,4,2,1,3,0:T(8,128)S(1)} %pad_maximum_fusion.3), channel_id=1, source_target_pairs={{0,120},{8,0},{16,8},{24,16},{32,24},{40,32},{48,40},{56,48},{64,5... | collective-permute-start | bytes 442376 | tf_op jit(solution)/shard_map/ppermute | solution.py:58
  11.3 0.7 copy-start.14
  18.5 1.1 %copy-start.4 = (f32[2,3,3,1,16,128]{5,4,2,1,3,0:T(8,128)}, f32[2,3,3,1,16,128]{5,4,2,1,3,0:T(8,128)S(1)}, u32[]{:S(2)}) copy-start(f32[2,3,3,1,16,128]{5,4,2,1,3,0:T(8,128)S(1)} %collective-permute-done) | copy-start | bytes 442372
  18.9 0.8 copy-start.5
  20.0 5.1 %collective-permute-start.2 = (f32[2,2,3,3,4,1,128]{6,4,3,2,1,5,0:T(4,128)S(1)}, f32[2,2,3,3,4,1,128]{6,4,3,2,1,5,0:T(4,128)S(1)}, u32[]{:S(2)}, u32[]{:S(2)}) collective-permute-start(f32[2,2,3,3,4,1,128]{6,4,3,2,1,5,0:T(4,128)S(1)} %pad_maximum_fusion.4), channel_id=1, source_target_pairs={{0,4},{4,0},{1,5},{5,1},{2,6},{6,2},{3,7},{7,3},{8,12},{12,8},{9,1... | collective-permute-start | bytes 221192 | tf_op jit(solution)/shard_map/ppermute | solution.py:55
  26.7 5.4 %collective-permute-start.3 = (f32[2,3,3,16,4]{3,4,1,2,0:T(4,128)S(1)}, f32[2,3,3,16,4]{3,4,1,2,0:T(4,128)S(1)}, u32[]{:S(2)}, u32[]{:S(2)}) collective-permute-start(f32[2,3,3,16,4]{3,4,1,2,0:T(4,128)S(1)} %pad_maximum_fusion.11), channel_id=1, source_target_pairs={{0,1},{1,2},{2,3},{3,0},{4,5},{5,6},{6,7},{7,4},{8,9},{9,10},{10,1... | collective-permute-start | bytes 13832 | tf_op jit(solution)/shard_map/ppermute | solution.py:57
  28.3 2.9 %collective-permute-start.4 = (f32[2,3,3,16,4]{3,4,1,2,0:T(4,128)S(1)}, f32[2,3,3,16,4]{3,4,1,2,0:T(4,128)S(1)}, u32[]{:S(2)}, u32[]{:S(2)}) collective-permute-start(f32[2,3,3,16,4]{3,4,1,2,0:T(4,128)S(1)} %pad_maximum_fusion.12), channel_id=1, source_target_pairs={{0,3},{1,0},{2,1},{3,2},{4,7},{5,4},{6,5},{7,6},{8,11},{9,8},{10,9... | collective-permute-start | bytes 13832 | tf_op jit(solution)/shard_map/ppermute | solution.py:58
  37.7 1.3 %copy-start.3 = (f32[27,4,16,128]{3,2,1,0:T(8,128)S(1)}, f32[27,4,16,128]{3,2,1,0:T(8,128)}, u32[]{:S(2)}) copy-start(f32[27,4,16,128]{3,2,1,0:T(8,128)} %get-tuple-element.6.an_ref) | copy-start | bytes 2654212
  42.5 5.9 %collective-permute-start.5 = (f32[1,3,3,1,16,128]{5,4,3,2,1,0:T(8,128)S(1)}, f32[1,3,3,1,16,128]{5,4,3,2,1,0:T(8,128)S(1)}, u32[]{:S(2)}, u32[]{:S(2)}) collective-permute-start(f32[1,3,3,1,16,128]{5,4,3,2,1,0:T(8,128)S(1)} %slice_bitcast_fusion.2), channel_id=1, source_target_pairs={{0,8},{8,16},{16,24},{24,32},{32,40},{40,48},{48,56},{56,64},{64,7... | collective-permute-start | bytes 221192 | tf_op jit(solution)/shard_map/ppermute | solution.py:57
  46.8 3.8 %collective-permute-start.6 = (f32[1,3,3,1,16,128]{5,4,3,2,1,0:T(8,128)S(1)}, f32[1,3,3,1,16,128]{5,4,3,2,1,0:T(8,128)S(1)}, u32[]{:S(2)}, u32[]{:S(2)}) collective-permute-start(f32[1,3,3,1,16,128]{5,4,3,2,1,0:T(8,128)S(1)} %slice_bitcast_fusion.1), channel_id=1, source_target_pairs={{0,120},{8,0},{16,8},{24,16},{32,24},{40,32},{48,40},{56,48},{64,5... | collective-permute-start | bytes 221192 | tf_op jit(solution)/shard_map/ppermute | solution.py:58
  48.4 1.5 %copy-start.8 = (f32[1,3,3,1,16,128]{5,4,3,2,1,0:T(8,128)}, f32[1,3,3,1,16,128]{5,4,3,2,1,0:T(8,128)S(1)}, u32[]{:S(2)}) copy-start(f32[1,3,3,1,16,128]{5,4,3,2,1,0:T(8,128)S(1)} %collective-permute-done.5) | copy-start | bytes 221188
  50.7 1.5 %copy-start.9 = (f32[1,3,3,1,16,128]{5,4,3,2,1,0:T(8,128)}, f32[1,3,3,1,16,128]{5,4,3,2,1,0:T(8,128)S(1)}, u32[]{:S(2)}) copy-start(f32[1,3,3,1,16,128]{5,4,3,2,1,0:T(8,128)S(1)} %collective-permute-done.6) | copy-start | bytes 221188
  54.0 4.7 %collective-permute-start.7 = (f32[2,1,3,3,4,1,128]{6,4,3,2,5,1,0:T(4,128)S(1)}, f32[2,1,3,3,4,1,128]{6,4,3,2,5,1,0:T(4,128)S(1)}, u32[]{:S(2)}, u32[]{:S(2)}) collective-permute-start(f32[2,1,3,3,4,1,128]{6,4,3,2,5,1,0:T(4,128)S(1)} %pad_maximum_fusion.13), channel_id=1, source_target_pairs={{0,4},{4,0},{1,5},{5,1},{2,6},{6,2},{3,7},{7,3},{8,12},{12,8},{9,1... | collective-permute-start | bytes 110600 | tf_op jit(solution)/shard_map/ppermute | solution.py:55
  59.7 4.9 %collective-permute-start.8 = (f32[1,3,3,16,4]{3,4,1,2,0:T(4,128)S(1)}, f32[1,3,3,16,4]{3,4,1,2,0:T(4,128)S(1)}, u32[]{:S(2)}, u32[]{:S(2)}) collective-permute-start(f32[1,3,3,16,4]{3,4,1,2,0:T(4,128)S(1)} %fusion.14), channel_id=1, source_target_pairs={{0,1},{1,2},{2,3},{3,0},{4,5},{5,6},{6,7},{7,4},{8,9},{9,10},{10,1... | collective-permute-start | bytes 6920 | tf_op jit(solution)/shard_map/ppermute | solution.py:57
  61.2 2.7 %collective-permute-start.9 = (f32[1,3,3,16,4]{3,4,1,2,0:T(4,128)S(1)}, f32[1,3,3,16,4]{3,4,1,2,0:T(4,128)S(1)}, u32[]{:S(2)}, u32[]{:S(2)}) collective-permute-start(f32[1,3,3,16,4]{3,4,1,2,0:T(4,128)S(1)} %fusion.13), channel_id=1, source_target_pairs={{0,3},{1,0},{2,1},{3,2},{4,7},{5,4},{6,5},{7,6},{8,11},{9,8},{10,9... | collective-permute-start | bytes 6920 | tf_op jit(solution)/shard_map/ppermute | solution.py:58
  65.4 4.2 %copy-start.11 = (f32[4,16,128]{2,1,0:T(8,128)S(1)}, f32[4,16,128]{2,1,0:T(8,128)}, u32[]{:S(2)}) copy-start(f32[4,16,128]{2,1,0:T(8,128)} %get-tuple-element.8) | copy-start | bytes 98308

commit v12 on v8

--- a/solution.py
+++ b/solution.py
@@ -79,11 +79,13 @@
     return lax.slice_in_dim(plus, n - 1, n, axis=2 + d), lax.slice_in_dim(minus, 0, 1, axis=2 + d)
 
 
-def halos(fields, signs):
+def halos(fields, signs, given=None):
     cubes = [f.reshape((3, 3, 3) + f.shape[1:]) for f in fields]
     sx, sy, sz = cubes[0].shape[3:]
-    x_up, x_dn = zip(*[faces(c, s, 0) for c, s in zip(cubes, signs)])
-    xlo, xhi = halo_exchange(jnp.stack(x_up), jnp.stack(x_dn), "gx")
+    if given is None:
+        x_up, x_dn = zip(*[faces(c, s, 0) for c, s in zip(cubes, signs)])
+        given = (jnp.stack(x_up), jnp.stack(x_dn))
+    xlo, xhi = halo_exchange(given[0], given[1], "gx")
     both = jnp.stack(cubes)
     rows = jnp.concatenate([both[..., sy - 1 : sy, :], both[..., 0:1, :]], axis=5)
     cols = jnp.concatenate([both[..., sz - 1 : sz], both[..., 0:1]], axis=6)
@@ -224,10 +226,14 @@
 
 def next_kernel(cf_ref, ae_ref, *refs):
     hal = refs[0:6]
-    rate_ref, gamma_ref, out_ref, sens_ref, fs, as_ = refs[6:]
+    rate_ref, gamma_ref, out_ref, sens_ref, up_ref, down_ref, fs, as_ = refs[6:]
     move_into(fs, cf_ref, hal, 1, 0)
     move_into(as_, ae_ref, hal, -1, 9)
     chunked_adjoint(fs, as_, rate_ref, gamma_ref, out_ref, sens_ref)
+    sx = out_ref.shape[1]
+    for q in range(9):
+        up_ref[q] = out_ref[q, sx - 1]
+        down_ref[q] = out_ref[18 + q, 0]
 
 
 def now_kernel(an_ref, f_ref, *refs):
@@ -260,10 +266,18 @@
     post_now, _ = collide(check_pops, relax_rate, gamma)
     hal = halos([post_now, adjoint_end], [1, -1])
     shape = check_pops.shape
-    adj_next, sens_next = run_stage(
-        next_kernel, (post_now, adjoint_end) + hal + (relax_rate, gamma), shape, 2
-    )
-    hal_n = halos([adj_next], [-1])
+    _, sx, sy, sz = shape
+    adj_next, sens_next, x_up, x_dn = pl.pallas_call(
+        next_kernel,
+        out_shape=(
+            jax.ShapeDtypeStruct(shape, jnp.float32),
+            jax.ShapeDtypeStruct((sx, sy, sz), jnp.float32),
+            jax.ShapeDtypeStruct((9, sy, sz), jnp.float32),
+            jax.ShapeDtypeStruct((9, sy, sz), jnp.float32),
+        ),
+        scratch_shapes=[pltpu.VMEM(shape, jnp.float32) for _ in range(2)],
+    )(post_now, adjoint_end, *hal, relax_rate, gamma)
+    hal_n = halos([adj_next], [-1], (x_up.reshape(1, 3, 3, 1, sy, sz), x_dn.reshape(1, 3, 3, 1, sy, sz)))
     adjoint_start, sens_now = run_stage(now_kernel, (adj_next, check_pops) + hal_n + (relax_rate, gamma), shape, 1)
     density = walls * (sens_next + sens_now)
     boxes = density.reshape(sx, 2, sy // 2, 2, sz // 2).sum(axis=(2, 4))

time: 89.1 us -> 90.5 us (1.016)
  local copies, waits for them, and re-layouts: 19 us -> 20.3 us
    pallas_call x0 -> x1, Pallas kernels: none -> 4.92 us  [shards(): pl.pallas_call(next_kernel, out_shape=(jax.ShapeDtypeStruct(shape, jnp.fl...]
    pallas_call x2 -> x1, Pallas kernels: 9.08 us -> 4.23 us  [run_stage(): pl.pallas_call(kernel, out_shape=(jax.ShapeDtypeStruct(shape, jnp.float32...]
    slice x3, local copies, waits for them, and re-layouts: 3.61 us -> 5.06 us  [halos(): cols = jnp.concatenate([both[..., sz - 1:sz], both[..., 0:1]], axis=6)]
    slice x1, local copies, waits for them, and re-layouts: 0.08 us -> 1.27 us  [halos(): rows = jnp.concatenate([both[..., sy - 1:sy, :], both[..., 0:1, :]], axis=5)]
    slice x3 -> x2, local copies, waits for them, and re-layouts: 1.26 us -> 0.09 us  [faces(): minus = lax.index_in_dim(cube, 1 - sign, axis=d, keepdims=False)]
    unnamed x51 -> x53, local copies, waits for them, and re-layouts: 2.18 us -> 2.02 us
where the time goes in v12:
time: 90.5 us; the launch traced here: 89.9 us
  local copies, waits for them, and re-layouts  20.3 us (22%)
  blocking collectives  20.1 us (22%)
  starting transfers between devices  18.8 us (21%)
  other arithmetic  12.5 us (14%)
  Pallas kernels  9.15 us (10%)
  waiting for transfers between devices  7.34 us (8%)
  between operations  1.7 us (2%)
    all_to_all x1, blocking collectives, shards(): lax.all_to_all(placed.reshape(devices, count // devices), ('gx', 'gy', 'g...  20.1 us
    ppermute x2, starting transfers between devices, halo_exchange(): both = lax.ppermute(jnp.stack([up, down]), axis, [(0, 1), (1, 0)])  6.77 us
    ppermute x4, starting transfers between devices, halo_exchange(): hi = lax.ppermute(down, axis, [(i, (i - 1) % size) for i in range(size)])  6.28 us
    ppermute x4, starting transfers between devices, halo_exchange(): lo = lax.ppermute(up, axis, [(i, (i + 1) % size) for i in range(size)])  5.71 us
    slice x3, local copies, waits for them, and re-layouts, halos(): cols = jnp.concatenate([both[..., sz - 1:sz], both[..., 0:1]], axis=6)  5.06 us
    pallas_call x1, Pallas kernels, shards(): pl.pallas_call(next_kernel, out_shape=(jax.ShapeDtypeStruct(shape, jnp.fl...  4.92 us
    pallas_call x1, Pallas kernels, run_stage(): pl.pallas_call(kernel, out_shape=(jax.ShapeDtypeStruct(shape, jnp.float32...  4.23 us
    ppermute x4, waiting for transfers between devices, halo_exchange(): lo = lax.ppermute(up, axis, [(i, (i + 1) % size) for i in range(size)])  3.8 us
  transfers between devices with their start and end apart: 10, of which 7 were waited for; matrix products, arithmetic and copies ran while one was open for 15% of the time, Pallas kernels for 0%

profile of v12, /device:TPU:1, one launch (start us, length us, event | category | flops | bytes accessed | tf_op | source)
XLA Modules:
  0.0 89.9 jit_solution(4354132328258091147)
XLA Ops:
  0.7 1.2 %slice_reduce_fusion.2 = (f32[4,16,128]{2,1,0:T(8,128)S(1)}, f32[4,16,128]{2,1,0:T(8,128)S(1)}) fusion(f32[3,3,3,4,16,128]{5,4,3,2,1,0:T(8,128)} %bitcast.418), kind=kLoop, calls=%fused_computation.14 | loop fusion | flops 131072 | bytes 655360 | tf_op jit(solution)/shard_map/reduce_sum | solution.py:33
  1.9 1.1 %slice_reduce_fusion = (f32[4,16,128]{2,1,0:T(8,128)S(1)}, f32[4,16,128]{2,1,0:T(8,128)S(1)}) fusion(f32[3,3,3,4,16,128]{5,4,3,2,1,0:T(8,128)} %bitcast.419), kind=kLoop, calls=%fused_computation.12 | loop fusion | flops 131072 | bytes 655360 | tf_op jit(solution)/shard_map/reduce_sum | solution.py:34
  3.0 1.1 %slice_reduce_fusion.4 = (f32[4,16,128]{2,1,0:T(8,128)S(1)}, f32[4,16,128]{2,1,0:T(8,128)S(1)}) fusion(f32[27,4,16,128]{3,2,1,0:T(8,128)} %f_ref.1), kind=kLoop, calls=%fused_computation.16 | loop fusion | flops 131072 | bytes 655360 | tf_op jit(solution)/shard_map/reduce_sum | solution.py:32
  4.2 0.2 copy.1131
  4.4 0.8 slice.634
  5.3 0.6 gather_fusion
  5.9 0.1 copy.1230
  6.1 0.1 reshape.124
  6.4 1.4 %fusion.7.cf_ref = f32[27,4,16,128]{3,2,1,0:T(8,128)S(1)} fusion(f32[27,4,16,128]{3,2,1,0:T(8,128)S(1)} %copy-done, f32[4,16,128]{2,1,0:T(8,128)S(1)} %get-tuple-element.150.refs_7_, f32[4,16,128]{2,1,0:T(8,128)S(1)} %get-tuple-element.22, f32[4,16,128]{2,1,0:T(8,128)S(1)} %get-tuple-element.25, f32[27]{0:T(128)S(1)} %copy-done.17, ...), kind=kLoop, calls=%fused_computation.11 | loop fusion | flops 4202496 | bytes 2032048 | tf_op jit(solution)/shard_map/add | solution.py:47
  8.0 0.8 pad_maximum_fusion.4
  8.8 1.4 %collective-permute-start.1 = (f32[2,3,3,1,16,128]{5,4,2,1,3,0:T(8,128)}, f32[2,3,3,1,16,128]{5,4,2,1,3,0:T(8,128)}, u32[]{:S(2)}, u32[]{:S(2)}) collective-permute-start(f32[2,3,3,1,16,128]{5,4,2,1,3,0:T(8,128)} %pad_maximum_fusion.4), channel_id=1, source_target_pairs={{0,120},{8,0},{16,8},{24,16},{32,24},{40,32},{48,40},{56,48},{64,5... | collective-permute-start | bytes 442376 | tf_op jit(solution)/shard_map/ppermute | solution.py:58
  10.1 0.7 pad_maximum_fusion.3
  10.8 1.6 %collective-permute-start = (f32[2,3,3,1,16,128]{5,4,2,1,3,0:T(8,128)}, f32[2,3,3,1,16,128]{5,4,2,1,3,0:T(8,128)}, u32[]{:S(2)}, u32[]{:S(2)}) collective-permute-start(f32[2,3,3,1,16,128]{5,4,2,1,3,0:T(8,128)} %pad_maximum_fusion.3), channel_id=1, source_target_pairs={{0,8},{8,16},{16,24},{24,32},{32,40},{40,48},{48,56},{56,64},{64,7... | collective-permute-start | bytes 442376 | tf_op jit(solution)/shard_map/ppermute | solution.py:57
  12.5 1.9 %slice_maximum_fusion = (f32[2,3,3,3,4,16,1]{6,5,4,3,2,1,0:T(8,128)S(1)}, f32[2,3,3,3,4,16,1]{6,5,4,3,2,1,0:T(8,128)}) fusion(f32[1,3,3,3,4,16,128]{6,5,4,3,2,1,0:T(8,128)S(1)} %bitcast.422, f32[1,3,3,3,4,16,128]{6,5,4,3,2,1,0:T(8,128)S(1)} %bitcast.420), kind=kLoop, calls=%fused_computation.2 | loop fusion | flops 6912 | bytes 1797120 | tf_op jit(solution)/shard_map/stack | solution.py:89
  14.3 0.8 fusion.8
  15.2 2.0 %copy.1155 = f32[2,3,3,3,4,16,1]{5,4,6,3,2,1,0:T(4,128)} copy(f32[2,3,3,3,4,16,1]{6,5,4,3,2,1,0:T(8,128)S(1)} %get-tuple-element.26) | data formatting | bytes 27648 | tf_op jit(solution)/shard_map/slice | solution.py:91
  17.1 1.3 %copy.1156 = f32[2,3,3,3,4,16,1]{5,4,6,3,2,1,0:T(4,128)S(1)} copy(f32[2,3,3,3,4,16,1]{6,5,4,3,2,1,0:T(8,128)S(1)} %copy-done.3) | data formatting | bytes 27648 | tf_op jit(solution)/shard_map/slice | solution.py:91
  19.0 0.1 copy.1249
  19.1 0.1 copy.1250
  19.2 0.1 copy.1251
  19.3 0.9 %slice_bitcast_fusion.4 = (f32[3,3,1,16,128]{4,3,1,0,2:T(8,128)S(1)}, f32[3,3,1,16,128]{4,3,1,0,2:T(8,128)S(1)}) fusion(f32[2,3,3,1,16,128]{5,4,2,1,3,0:T(8,128)} %collective-permute-done.1), kind=kLoop, calls=%fused_computation.36 | loop fusion | bytes 294912 | tf_op jit(solution)/shard_map/squeeze | solution.py:94
  20.4 0.9 %slice_bitcast_fusion.3 = (f32[3,3,1,16,128]{4,3,1,0,2:T(8,128)S(1)}, f32[3,3,1,16,128]{4,3,1,0,2:T(8,128)S(1)}) fusion(f32[2,3,3,1,16,128]{5,4,2,1,3,0:T(8,128)} %collective-permute-done), kind=kLoop, calls=%fused_computation.35 | loop fusion | bytes 294912 | tf_op jit(solution)/shard_map/squeeze | solution.py:94
  21.6 0.1 copy.1174
  21.7 0.1 copy.1175
  22.2 3.4 %collective-permute-start.2 = (f32[2,2,3,3,4,1,128]{6,4,3,2,1,5,0:T(4,128)S(1)}, f32[2,2,3,3,4,1,128]{6,4,3,2,1,5,0:T(4,128)S(1)}, u32[]{:S(2)}, u32[]{:S(2)}) collective-permute-start(f32[2,2,3,3,4,1,128]{6,4,3,2,1,5,0:T(4,128)S(1)} %pad_maximum_fusion.6), channel_id=1, source_target_pairs={{0,4},{4,0},{1,5},{5,1},{2,6},{6,2},{3,7},{7,3},{8,12},{12,8},{9,1... | collective-permute-start | bytes 221192 | tf_op jit(solution)/shard_map/ppermute | solution.py:55
  25.6 0.1 copy.1182
  25.7 0.1 copy.1183
  26.0 0.1 copy.1157
  26.1 0.1 copy.1158
  26.3 0.1 copy.1165
  26.4 0.1 copy.1166
  26.9 0.4 collective-permute-done.2
  28.1 2.5 %collective-permute-start.4 = (f32[2,3,3,16,4]{3,4,2,1,0:T(4,128)S(1)}, f32[2,3,3,16,4]{3,4,2,1,0:T(4,128)S(1)}, u32[]{:S(2)}, u32[]{:S(2)}) collective-permute-start(f32[2,3,3,16,4]{3,4,2,1,0:T(4,128)S(1)} %pad_maximum_fusion.14), channel_id=1, source_target_pairs={{0,3},{1,0},{2,1},{3,2},{4,7},{5,4},{6,5},{7,6},{8,11},{9,8},{10,9... | collective-permute-start | bytes 13832 | tf_op jit(solution)/shard_map/ppermute | solution.py:58
  31.1 0.7 fusion.35
  31.7 0.8 copy.1190
  32.6 2.5 %collective-permute-done.3 = f32[2,3,3,16,4]{3,4,2,1,0:T(4,128)S(1)} collective-permute-done((f32[2,3,3,16,4]{3,4,2,1,0:T(4,128)S(1)}, f32[2,3,3,16,4]{3,4,2,1,0:T(4,128)S(1)}, u32[]{:S(2)}, u32[]{:S(2)}) %collective-permute-start.3) | collective-permute-done | bytes 4640 | tf_op jit(solution)/shard_map/ppermute | solution.py:57
  35.1 0.8 copy.1173
  35.9 4.9 %shard_map.122 = (f32[27,4,16,128]{3,2,1,0:T(8,128)}, f32[4,16,128]{2,1,0:T(8,128)}, f32[9,16,128]{2,1,0:T(8,128)}, f32[9,16,128]{2,1,0:T(8,128)}) custom-call(f32[27,4,16,128]{3,2,1,0:T(8,128)} %copy-done.1, f32[27,4,16,128]{3,2,1,0:T(8,128)} %ae_ref.1, f32[18,16,128]{2,1,0:T(8,128)} %bitcast.9.refs_0_, f32[18,16,128]{2,1,0:T(8,128)} %bitcast.14.refs_1_, ...), custom_call_target="tpu_custom_call" | custom-call | tf_op jit(solution)/shard_map/pallas_call | solution.py:270
  40.8 1.8 %fusion.23 = (f32[1,3,3,3,4,16,1]{6,5,4,3,2,1,0:T(8,128)S(1)}, f32[1,3,3,3,4,16,1]{6,5,4,3,2,1,0:T(8,128)S(1)}) fusion(f32[1,3,3,3,4,16,128]{6,5,4,3,2,1,0:T(8,128)} %bitcast.424), kind=kLoop, calls=%fused_computation.211 | loop fusion | bytes 27648 | tf_op jit(solution)/shard_map/slice | solution.py:91
  42.6 1.3 %fusion.24 = (f32[1,3,3,3,4,1,128]{6,5,4,3,2,1,0:T(1,128)S(1)}, f32[1,3,3,3,4,1,128]{6,5,4,3,2,1,0:T(1,128)S(1)}) fusion(f32[1,3,3,3,4,16,128]{6,5,4,3,2,1,0:T(8,128)} %bitcast.425), kind=kLoop, calls=%fused_computation.212 | loop fusion | bytes 221184 | tf_op jit(solution)/shard_map/slice | solution.py:90
  43.9 0.7 copy.1247
  44.6 0.7 copy.1248
  45.4 2.8 %collective-permute-start.5 = (f32[1,3,3,1,16,128]{5,4,2,1,3,0:T(8,128)S(1)}, f32[1,3,3,1,16,128]{5,4,2,1,3,0:T(8,128)S(1)}, u32[]{:S(2)}, u32[]{:S(2)}) collective-permute-start(f32[1,3,3,1,16,128]{5,4,2,1,3,0:T(8,128)S(1)} %bitcast.478), channel_id=1, source_target_pairs={{0,8},{8,16},{16,24},{24,32},{32,40},{40,48},{48,56},{56,64},{64,7... | collective-permute-start | bytes 221192 | tf_op jit(solution)/shard_map/ppermute | solution.py:57
  48.2 1.9 %collective-permute-start.6 = (f32[1,3,3,1,16,128]{5,4,2,1,3,0:T(8,128)S(1)}, f32[1,3,3,1,16,128]{5,4,2,1,3,0:T(8,128)S(1)}, u32[]{:S(2)}, u32[]{:S(2)}) collective-permute-start(f32[1,3,3,1,16,128]{5,4,2,1,3,0:T(8,128)S(1)} %bitcast.477), channel_id=1, source_target_pairs={{0,120},{8,0},{16,8},{24,16},{32,24},{40,32},{48,40},{56,48},{64,5... | collective-permute-start | bytes 221192 | tf_op jit(solution)/shard_map/ppermute | solution.py:58
  50.3 0.5 collective-permute-done.5
  50.9 1.2 %collective-permute-done.6 = f32[1,3,3,1,16,128]{5,4,2,1,3,0:T(8,128)S(1)} collective-permute-done((f32[1,3,3,1,16,128]{5,4,2,1,3,0:T(8,128)S(1)}, f32[1,3,3,1,16,128]{5,4,2,1,3,0:T(8,128)S(1)}, u32[]{:S(2)}, u32[]{:S(2)}) %collective-permute-start.6) | collective-permute-done | bytes 73760 | tf_op jit(solution)/shard_map/ppermute | solution.py:58
  52.2 0.1 copy.1214
  52.3 0.1 copy.1217
  52.7 3.4 %collective-permute-start.7 = (f32[2,1,3,3,4,1,128]{6,4,3,2,5,1,0:T(4,128)S(1)}, f32[2,1,3,3,4,1,128]{6,4,3,2,5,1,0:T(4,128)S(1)}, u32[]{:S(2)}, u32[]{:S(2)}) collective-permute-start(f32[2,1,3,3,4,1,128]{6,4,3,2,5,1,0:T(4,128)S(1)} %pad_maximum_fusion.15), channel_id=1, source_target_pairs={{0,4},{4,0},{1,5},{5,1},{2,6},{6,2},{3,7},{7,3},{8,12},{12,8},{9,1... | collective-permute-start | bytes 110600 | tf_op jit(solution)/shard_map/ppermute | solution.py:55
  56.1 0.1 copy.1201
  56.2 0.1 copy.1204
  56.6 0.9 collective-permute-done.7
  57.4 0.6 slice_bitcast_fusion.80
  58.4 0.4 collective-permute-start.9
  59.0 1.2 %collective-permute-start.8 = (f32[1,3,3,16,4]{3,4,2,1,0:T(4,128)S(1)}, f32[1,3,3,16,4]{3,4,2,1,0:T(4,128)S(1)}, u32[]{:S(2)}, u32[]{:S(2)}) collective-permute-start(f32[1,3,3,16,4]{3,4,2,1,0:T(4,128)S(1)} %fusion.13), channel_id=1, source_target_pairs={{0,1},{1,2},{2,3},{3,0},{4,5},{5,6},{6,7},{7,4},{8,9},{9,10},{10,1... | collective-permute-start | bytes 6920 | tf_op jit(solution)/shard_map/ppermute | solution.py:57
  60.3 1.1 %collective-permute-done.9 = f32[1,3,3,16,4]{3,4,2,1,0:T(4,128)S(1)} collective-permute-done((f32[1,3,3,16,4]{3,4,2,1,0:T(4,128)S(1)}, f32[1,3,3,16,4]{3,4,2,1,0:T(4,128)S(1)}, u32[]{:S(2)}, u32[]{:S(2)}) %collective-permute-start.9) | collective-permute-done | bytes 2336 | tf_op jit(solution)/shard_map/ppermute | solution.py:58
  61.4 0.8 copy.1226
  62.1 0.7 collective-permute-done.8
  62.9 0.7 copy.1213
  63.6 4.2 %shard_map.123 = (f32[27,4,16,128]{3,2,1,0:T(8,128)}, f32[4,16,128]{2,1,0:T(8,128)}) custom-call(f32[27,4,16,128]{3,2,1,0:T(8,128)} %get-tuple-element.8.an_ref, f32[27,4,16,128]{3,2,1,0:T(8,128)} %f_ref.1, f32[9,16,128]{2,1,0:T(8,128)} %bitcast.428, f32[9,16,128]{2,1,0:T(8,128)} %bitcast.431, f32[9,4,128]{2,1,0:T(4,128)} %bitcast.467, ...), custom_call_target="tpu_custom_call" | custom-call | tf_op jit(solution)/shard_map/pallas_call | solution.py:248
  67.9 0.8 add_multiply_fusion
  68.7 0.1 reduce_sum.106
  69.1 20.1 %all_to_all.9 = f32[128,1,8]{2,1,0:T(1,128)S(1)} all-to-all(f32[128,1,8]{2,1,0:T(1,128)S(1)} %bitcast.441), channel_id=1, replica_groups=mesh['gx'=16,'gy'=2,'gz'=4] {'gx','gy','gz'}, dimensions={0} | all-to-all | bytes 8192 | tf_op jit(solution)/shard_map/all_to_all | solution.py:290
  89.3 0.7 reduce_sum.109
  (188 shorter events, 4.8 us)
Async XLA Ops:
  0.6 5.6 %copy-start = (f32[27,4,16,128]{3,2,1,0:T(8,128)S(1)}, f32[27,4,16,128]{3,2,1,0:T(8,128)}, u32[]{:S(2)}) copy-start(f32[27,4,16,128]{3,2,1,0:T(8,128)} %f_ref.1) | copy-start | bytes 2654212
  0.6 3.5 %copy-start.13 = (s32[1024]{0:T(1024)S(1)}, s32[1024]{0:T(1024)}, u32[]{:S(2)}) copy-start(s32[1024]{0:T(1024)} %param.17) | copy-start | bytes 12292
  0.7 3.5 %copy-start.14 = (f32[1024]{0:T(1024)S(1)}, f32[1024]{0:T(1024)}, u32[]{:S(2)}) copy-start(f32[1024]{0:T(1024)} %param.16) | copy-start | bytes 12292
  0.7 5.6 %copy-start.10 = (s32[4,16,128]{2,1,0:T(8,128)S(1)}, s32[4,16,128]{2,1,0:T(8,128)}, u32[]{:S(2)}) copy-start(s32[4,16,128]{2,1,0:T(8,128)} %param.14) | copy-start | bytes 98308
  1.8 4.5 %copy-start.9 = (f32[4,16,128]{2,1,0:T(8,128)S(1)}, f32[4,16,128]{2,1,0:T(8,128)}, u32[]{:S(2)}) copy-start(f32[4,16,128]{2,1,0:T(8,128)} %refs_6_.3) | copy-start | bytes 98308
  1.9 4.5 %copy-start.15 = (f32[27]{0:T(128)S(1)}, f32[27]{0:T(128)}, u32[]{:S(2)}) copy-start(f32[27]{0:T(128)} %constant.24.clone) | copy-start | bytes 328
  1.9 4.5 %copy-start.16 = (f32[27]{0:T(128)S(1)}, f32[27]{0:T(128)}, u32[]{:S(2)}) copy-start(f32[27]{0:T(128)} %constant.25.clone) | copy-start | bytes 328
  1.9 4.5 %copy-start.17 = (f32[27]{0:T(128)S(1)}, f32[27]{0:T(128)}, u32[]{:S(2)}) copy-start(f32[27]{0:T(128)} %constant.26.clone) | copy-start | bytes 328
  1.9 4.5 %copy-start.18 = (f32[27]{0:T(128)S(1)}, f32[27]{0:T(128)}, u32[]{:S(2)}) copy-start(f32[27]{0:T(128)} %constant.27.clone) | copy-start | bytes 328
  6.3 1.6 %copy-start.7 = (f32[4,16,128]{2,1,0:T(8,128)}, f32[4,16,128]{2,1,0:T(8,128)S(1)}, u32[]{:S(2)}) copy-start(f32[4,16,128]{2,1,0:T(8,128)S(1)} %get-tuple-element.150.refs_7_) | copy-start | bytes 98308
  6.4 1.5 %copy-start.2 = (f32[27,4,16,128]{3,2,1,0:T(8,128)S(1)}, f32[27,4,16,128]{3,2,1,0:T(8,128)}, u32[]{:S(2)}) copy-start(f32[27,4,16,128]{3,2,1,0:T(8,128)} %ae_ref.1) | copy-start | bytes 2654212
  7.8 6.5 %copy-start.1 = (f32[27,4,16,128]{3,2,1,0:T(8,128)}, f32[27,4,16,128]{3,2,1,0:T(8,128)S(1)}, u32[]{:S(2)}) copy-start(f32[27,4,16,128]{3,2,1,0:T(8,128)S(1)} %fusion.7.cf_ref) | copy-start | bytes 2654212
  8.8 10.6 %collective-permute-start.1 = (f32[2,3,3,1,16,128]{5,4,2,1,3,0:T(8,128)}, f32[2,3,3,1,16,128]{5,4,2,1,3,0:T(8,128)}, u32[]{:S(2)}, u32[]{:S(2)}) collective-permute-start(f32[2,3,3,1,16,128]{5,4,2,1,3,0:T(8,128)} %pad_maximum_fusion.4), channel_id=1, source_target_pairs={{0,120},{8,0},{16,8},{24,16},{32,24},{40,32},{48,40},{56,48},{64,5... | collective-permute-start | bytes 442376 | tf_op jit(solution)/shard_map/ppermute | solution.py:58
  10.8 9.5 %collective-permute-start = (f32[2,3,3,1,16,128]{5,4,2,1,3,0:T(8,128)}, f32[2,3,3,1,16,128]{5,4,2,1,3,0:T(8,128)}, u32[]{:S(2)}, u32[]{:S(2)}) collective-permute-start(f32[2,3,3,1,16,128]{5,4,2,1,3,0:T(8,128)} %pad_maximum_fusion.3), channel_id=1, source_target_pairs={{0,8},{8,16},{16,24},{24,32},{32,40},{40,48},{48,56},{56,64},{64,7... | collective-permute-start | bytes 442376 | tf_op jit(solution)/shard_map/ppermute | solution.py:57
  15.2 2.0 %copy-start.3 = (f32[2,3,3,3,4,16,1]{6,5,4,3,2,1,0:T(8,128)S(1)}, f32[2,3,3,3,4,16,1]{6,5,4,3,2,1,0:T(8,128)}, u32[]{:S(2)}) copy-start(f32[2,3,3,3,4,16,1]{6,5,4,3,2,1,0:T(8,128)} %get-tuple-element.27) | copy-start | bytes 41476
  17.1 1.3 %copy-start.8 = (f32[2,3,3,3,4,16,1]{5,4,6,3,2,1,0:T(4,128)S(1)}, f32[2,3,3,3,4,16,1]{5,4,6,3,2,1,0:T(4,128)}, u32[]{:S(2)}) copy-start(f32[2,3,3,3,4,16,1]{5,4,6,3,2,1,0:T(4,128)} %copy.1155) | copy-start | bytes 41476
  17.1 1.5 %copy-start.4 = (f32[2,3,3,3,4,2,128]{6,5,4,3,2,1,0:T(2,128)S(1)}, f32[2,3,3,3,4,2,128]{6,5,4,3,2,1,0:T(2,128)}, u32[]{:S(2)}) copy-start(f32[2,3,3,3,4,2,128]{6,5,4,3,2,1,0:T(2,128)} %fusion.8) | copy-start | bytes 663556
  22.2 5.1 %collective-permute-start.2 = (f32[2,2,3,3,4,1,128]{6,4,3,2,1,5,0:T(4,128)S(1)}, f32[2,2,3,3,4,1,128]{6,4,3,2,1,5,0:T(4,128)S(1)}, u32[]{:S(2)}, u32[]{:S(2)}) collective-permute-start(f32[2,2,3,3,4,1,128]{6,4,3,2,1,5,0:T(4,128)S(1)} %pad_maximum_fusion.6), channel_id=1, source_target_pairs={{0,4},{4,0},{1,5},{5,1},{2,6},{6,2},{3,7},{7,3},{8,12},{12,8},{9,1... | collective-permute-start | bytes 221192 | tf_op jit(solution)/shard_map/ppermute | solution.py:55
  28.1 3.7 %collective-permute-start.4 = (f32[2,3,3,16,4]{3,4,2,1,0:T(4,128)S(1)}, f32[2,3,3,16,4]{3,4,2,1,0:T(4,128)S(1)}, u32[]{:S(2)}, u32[]{:S(2)}) collective-permute-start(f32[2,3,3,16,4]{3,4,2,1,0:T(4,128)S(1)} %pad_maximum_fusion.14), channel_id=1, source_target_pairs={{0,3},{1,0},{2,1},{3,2},{4,7},{5,4},{6,5},{7,6},{8,11},{9,8},{10,9... | collective-permute-start | bytes 13832 | tf_op jit(solution)/shard_map/ppermute | solution.py:58
  31.0 4.1 %collective-permute-start.3 = (f32[2,3,3,16,4]{3,4,2,1,0:T(4,128)S(1)}, f32[2,3,3,16,4]{3,4,2,1,0:T(4,128)S(1)}, u32[]{:S(2)}, u32[]{:S(2)}) collective-permute-start(f32[2,3,3,16,4]{3,4,2,1,0:T(4,128)S(1)} %pad_maximum_fusion.13), channel_id=1, source_target_pairs={{0,1},{1,2},{2,3},{3,0},{4,5},{5,6},{6,7},{7,4},{8,9},{9,10},{10,1... | collective-permute-start | bytes 13832 | tf_op jit(solution)/shard_map/ppermute | solution.py:57
  42.6 2.8 %copy-start.20 = (f32[9,16,128]{2,1,0:T(8,128)S(1)}, f32[9,16,128]{2,1,0:T(8,128)}, u32[]{:S(2)}) copy-start(f32[9,16,128]{2,1,0:T(8,128)} %get-tuple-element.9) | copy-start | bytes 221188
  42.6 5.6 %copy-start.19 = (f32[9,16,128]{2,1,0:T(8,128)S(1)}, f32[9,16,128]{2,1,0:T(8,128)}, u32[]{:S(2)}) copy-start(f32[9,16,128]{2,1,0:T(8,128)} %get-tuple-element.10) | copy-start | bytes 221188
  45.4 5.4 %collective-permute-start.5 = (f32[1,3,3,1,16,128]{5,4,2,1,3,0:T(8,128)S(1)}, f32[1,3,3,1,16,128]{5,4,2,1,3,0:T(8,128)S(1)}, u32[]{:S(2)}, u32[]{:S(2)}) collective-permute-start(f32[1,3,3,1,16,128]{5,4,2,1,3,0:T(8,128)S(1)} %bitcast.478), channel_id=1, source_target_pairs={{0,8},{8,16},{16,24},{24,32},{32,40},{40,48},{48,56},{56,64},{64,7... | collective-permute-start | bytes 221192 | tf_op jit(solution)/shard_map/ppermute | solution.py:57
  48.2 3.8 %collective-permute-start.6 = (f32[1,3,3,1,16,128]{5,4,2,1,3,0:T(8,128)S(1)}, f32[1,3,3,1,16,128]{5,4,2,1,3,0:T(8,128)S(1)}, u32[]{:S(2)}, u32[]{:S(2)}) collective-permute-start(f32[1,3,3,1,16,128]{5,4,2,1,3,0:T(8,128)S(1)} %bitcast.477), channel_id=1, source_target_pairs={{0,120},{8,0},{16,8},{24,16},{32,24},{40,32},{48,40},{56,48},{64,5... | collective-permute-start | bytes 221192 | tf_op jit(solution)/shard_map/ppermute | solution.py:58
  50.8 12.8 %copy-start.5 = (f32[1,3,3,1,16,128]{5,4,2,1,3,0:T(8,128)}, f32[1,3,3,1,16,128]{5,4,2,1,3,0:T(8,128)S(1)}, u32[]{:S(2)}) copy-start(f32[1,3,3,1,16,128]{5,4,2,1,3,0:T(8,128)S(1)} %collective-permute-done.5) | copy-start | bytes 221188
  52.1 11.5 %copy-start.6 = (f32[1,3,3,1,16,128]{5,4,2,1,3,0:T(8,128)}, f32[1,3,3,1,16,128]{5,4,2,1,3,0:T(8,128)S(1)}, u32[]{:S(2)}) copy-start(f32[1,3,3,1,16,128]{5,4,2,1,3,0:T(8,128)S(1)} %collective-permute-done.6) | copy-start | bytes 221188
  52.7 4.7 %collective-permute-start.7 = (f32[2,1,3,3,4,1,128]{6,4,3,2,5,1,0:T(4,128)S(1)}, f32[2,1,3,3,4,1,128]{6,4,3,2,5,1,0:T(4,128)S(1)}, u32[]{:S(2)}, u32[]{:S(2)}) collective-permute-start(f32[2,1,3,3,4,1,128]{6,4,3,2,5,1,0:T(4,128)S(1)} %pad_maximum_fusion.15), channel_id=1, source_target_pairs={{0,4},{4,0},{1,5},{5,1},{2,6},{6,2},{3,7},{7,3},{8,12},{12,8},{9,1... | collective-permute-start | bytes 110600 | tf_op jit(solution)/shard_map/ppermute | solution.py:55
  56.1 11.7 %copy-start.11 = (s32[4,16,128]{2,1,0:T(8,128)S(1)}, s32[4,16,128]{2,1,0:T(8,128)}, u32[]{:S(2)}) copy-start(s32[4,16,128]{2,1,0:T(8,128)} %param.14) | copy-start | bytes 98308
  56.1 11.7 %copy-start.12 = (f32[4,16,128]{2,1,0:T(8,128)S(1)}, f32[4,16,128]{2,1,0:T(8,128)}, u32[]{:S(2)}) copy-start(f32[4,16,128]{2,1,0:T(8,128)} %get-tuple-element.12) | copy-start | bytes 98308
  58.4 3.0 %collective-permute-start.9 = (f32[1,3,3,16,4]{3,4,2,1,0:T(4,128)S(1)}, f32[1,3,3,16,4]{3,4,2,1,0:T(4,128)S(1)}, u32[]{:S(2)}, u32[]{:S(2)}) collective-permute-start(f32[1,3,3,16,4]{3,4,2,1,0:T(4,128)S(1)} %fusion.12), channel_id=1, source_target_pairs={{0,3},{1,0},{2,1},{3,2},{4,7},{5,4},{6,5},{7,6},{8,11},{9,8},{10,9... | collective-permute-start | bytes 6920 | tf_op jit(solution)/shard_map/ppermute | solution.py:58
  59.0 3.9 %collective-permute-start.8 = (f32[1,3,3,16,4]{3,4,2,1,0:T(4,128)S(1)}, f32[1,3,3,16,4]{3,4,2,1,0:T(4,128)S(1)}, u32[]{:S(2)}, u32[]{:S(2)}) collective-permute-start(f32[1,3,3,16,4]{3,4,2,1,0:T(4,128)S(1)} %fusion.13), channel_id=1, source_target_pairs={{0,1},{1,2},{2,3},{3,0},{4,5},{5,6},{6,7},{7,4},{8,9},{9,10},{10,1... | collective-permute-start | bytes 6920 | tf_op jit(solution)/shard_map/ppermute | solution.py:57

commit v13 on v11

--- a/solution.py
+++ b/solution.py
@@ -79,6 +79,17 @@
     return lax.slice_in_dim(plus, n - 1, n, axis=2 + d), lax.slice_in_dim(minus, 0, 1, axis=2 + d)
 
 
+def columns_kernel(a_ref, b_ref, out_ref):
+    _, sx, sy, sz = a_ref.shape
+    pairs = [(r, q, i) for r in (a_ref, b_ref) for q in range(27) for i in range(sx)]
+    per = 128 // sy
+    for g in range(len(pairs) // per):
+        block = jnp.concatenate([r[q, i] for r, q, i in pairs[g * per : (g + 1) * per]], axis=0)
+        flipped = block.T
+        out_ref[0, pl.ds(g, 1), :] = flipped[sz - 1 : sz, :]
+        out_ref[1, pl.ds(g, 1), :] = flipped[0:1, :]
+
+
 def halos(fields, signs):
     cubes = [f.reshape((3, 3, 3) + f.shape[1:]) for f in fields]
     sx, sy, sz = cubes[0].shape[3:]
@@ -86,8 +97,14 @@
     xlo, xhi = halo_exchange(jnp.stack(x_up), jnp.stack(x_dn), "gx")
     both = jnp.stack(cubes)
     rows = jnp.concatenate([both[..., sy - 1 : sy, :], both[..., 0:1, :]], axis=5)
-    pick = (jnp.arange(sz)[:, None] == jnp.array([sz - 1, 0])[None, :]).astype(jnp.float32)
-    cols = jnp.einsum("nabcxyz,zk->knabcxy", both, pick, precision=lax.Precision.HIGHEST)
+    if len(fields) == 2 and sy * 8 == 128 and sz == 128:
+        flat = pl.pallas_call(
+            columns_kernel, out_shape=jax.ShapeDtypeStruct((2, 2 * 27 * sx * sy // 128, 128), jnp.float32)
+        )(fields[0], fields[1])
+        cols = flat.reshape((2, 2, 3, 3, 3, sx, sy))
+    else:
+        cols = None
+        edges = jnp.concatenate([both[..., sz - 1 : sz], both[..., 0:1]], axis=6)
     y_up, y_dn = [], []
     for k, s in enumerate(signs):
         top = shifted(rows[k][..., 0:1, :], xlo[k][:, :, :, sy - 1 : sy], xhi[k][:, :, :, sy - 1 : sy], 0, s)
@@ -99,8 +116,13 @@
     for k, s in enumerate(signs):
         picked = []
         for at, z0 in ((0, sz - 1), (1, 0)):
-            col = shifted(cols[at, k], xlo[k][..., z0], xhi[k][..., z0], 0, s)
-            col = shifted(col, ylo[k][..., z0], yhi[k][..., z0], 1, s)
+            if cols is None:
+                col = edges[k][..., at : at + 1]
+                col = shifted(col, xlo[k][..., z0 : z0 + 1], xhi[k][..., z0 : z0 + 1], 0, s)
+                col = shifted(col, ylo[k][..., z0 : z0 + 1], yhi[k][..., z0 : z0 + 1], 1, s)[..., 0]
+            else:
+                col = shifted(cols[at, k], xlo[k][..., z0], xhi[k][..., z0], 0, s)
+                col = shifted(col, ylo[k][..., z0], yhi[k][..., z0], 1, s)
             picked.append(col)
         z_up.append(jnp.swapaxes(lax.index_in_dim(picked[0], 1 + s, axis=2, keepdims=False), -1, -2))
         z_dn.append(jnp.swapaxes(lax.index_in_dim(picked[1], 1 - s, axis=2, keepdims=False), -1, -2))

time: 95.4 us -> 85.1 us (0.89)
  matrix products: 9.47 us -> 0 us
  Pallas kernels: 9.1 us -> 11.7 us
  blocking collectives: 23.4 us -> 21.4 us
  waiting for transfers between devices: 5.5 us -> 3.73 us
  other arithmetic: 7.32 us -> 8.4 us
    dot_general x2 -> x0, matrix products: 9.47 us -> none  [halos(): jnp.einsum('nabcxyz,zk->knabcxy', both, pick, precision=lax.Precision.HIG...]
    pallas_call x0 -> x1, Pallas kernels: none -> 2.65 us  [halos(): pl.pallas_call(columns_kernel, out_shape=jax.ShapeDtypeStruct((2, 2 * 27...]
    all_to_all x1, blocking collectives: 23.4 us -> 21.4 us  [shards(): lax.all_to_all(placed.reshape(devices, count // devices), ('gx', 'gy', 'g...]
    unnamed x47, local copies, waits for them, and re-layouts: 1.74 us -> 3.59 us
    slice x2 -> x3, local copies, waits for them, and re-layouts: 1.67 us -> 0.03 us  [halos(): xhi[k][:, :, :, sy - 1:sy]]
    slice x2 -> x3, local copies, waits for them, and re-layouts: 1.66 us -> 0.03 us  [halos(): xlo[k][:, :, :, sy - 1:sy]]
    slice x1 -> x2, local copies, waits for them, and re-layouts: 0.08 us -> 1.26 us  [halos(): rows = jnp.concatenate([both[..., sy - 1:sy, :], both[..., 0:1, :]], axis=5)]
    reduce_sum x1, other arithmetic: 0.04 us -> 1.21 us  [collide(): mom_x = jnp.sum(cube[2], axis=(0, 1)) - jnp.sum(cube[0], axis=(0, 1))]
  transfers between devices with their start and end apart: 10 -> 10, of which waited for: 6 -> 5; matrix products, arithmetic and copies ran while one was open for 13% -> 11% of each run, Pallas kernels for 0% -> 3%
where the time goes in v13:
time: 85.1 us; the launch traced here: 84.6 us
  blocking collectives  21.4 us (25%)
  starting transfers between devices  20.2 us (24%)
  local copies, waits for them, and re-layouts  17.3 us (20%)
  Pallas kernels  11.7 us (14%)
  other arithmetic  8.4 us (10%)
  waiting for transfers between devices  3.73 us (4%)
  between operations  1.85 us (2%)
    all_to_all x1, blocking collectives, shards(): lax.all_to_all(placed.reshape(devices, count // devices), ('gx', 'gy', 'g...  21.4 us
    pallas_call x2, Pallas kernels, run_stage(): pl.pallas_call(kernel, out_shape=(jax.ShapeDtypeStruct(shape, jnp.float32...  9.08 us
    ppermute x4, starting transfers between devices, halo_exchange(): lo = lax.ppermute(up, axis, [(i, (i + 1) % size) for i in range(size)])  8.92 us
    ppermute x2, starting transfers between devices, halo_exchange(): both = lax.ppermute(jnp.stack([up, down]), axis, [(0, 1), (1, 0)])  7.07 us
    ppermute x4, starting transfers between devices, halo_exchange(): hi = lax.ppermute(down, axis, [(i, (i - 1) % size) for i in range(size)])  4.19 us
    unnamed x47, local copies, waits for them, and re-layouts  3.59 us
    pallas_call x1, Pallas kernels, halos(): pl.pallas_call(columns_kernel, out_shape=jax.ShapeDtypeStruct((2, 2 * 27...  2.65 us
  transfers between devices with their start and end apart: 10, of which 5 were waited for; matrix products, arithmetic and copies ran while one was open for 11% of the time, Pallas kernels for 3%

profile of v13, /device:TPU:1, one launch (start us, length us, event | category | flops | bytes accessed | tf_op | source)
XLA Modules:
  0.0 84.6 jit_solution(14537454680743991562)
XLA Ops:
  0.7 1.2 %slice_reduce_fusion.4 = (f32[4,16,128]{2,1,0:T(8,128)S(1)}, f32[4,16,128]{2,1,0:T(8,128)S(1)}) fusion(f32[27,4,16,128]{3,2,1,0:T(8,128)} %f_ref.1), kind=kLoop, calls=%fused_computation.16 | loop fusion | flops 131072 | bytes 655360 | tf_op jit(solution)/shard_map/reduce_sum | solution.py:32
  1.9 1.1 %slice_reduce_fusion.2 = (f32[4,16,128]{2,1,0:T(8,128)S(1)}, f32[4,16,128]{2,1,0:T(8,128)S(1)}) fusion(f32[3,3,3,4,16,128]{5,4,3,2,1,0:T(8,128)} %bitcast.410), kind=kLoop, calls=%fused_computation.14 | loop fusion | flops 131072 | bytes 655360 | tf_op jit(solution)/shard_map/reduce_sum | solution.py:33
  3.0 1.1 %slice_reduce_fusion = (f32[4,16,128]{2,1,0:T(8,128)S(1)}, f32[4,16,128]{2,1,0:T(8,128)S(1)}) fusion(f32[3,3,3,4,16,128]{5,4,3,2,1,0:T(8,128)} %bitcast.411), kind=kLoop, calls=%fused_computation.12 | loop fusion | flops 131072 | bytes 655360 | tf_op jit(solution)/shard_map/reduce_sum | solution.py:34
  4.3 0.2 copy.472
  4.5 0.8 %slice.654 = s32[4,2,2]{2,1,0:T(2,128)S(1)} slice(s32[4,16,128]{2,1,0:T(8,128)} %param.15), slice={[0:4:1], [0:16:8], [0:128:64]} | slice | bytes 128 | tf_op jit(solution)/shard_map/slice | solution.py:276
  5.5 0.6 gather_fusion
  6.0 0.1 copy.555
  6.3 0.1 reshape.146
  6.6 1.4 %fusion.7.a_ref.cf_ref = f32[27,4,16,128]{3,2,1,0:T(8,128)S(1)} fusion(f32[27,4,16,128]{3,2,1,0:T(8,128)S(1)} %copy-done, f32[4,16,128]{2,1,0:T(8,128)S(1)} %get-tuple-element.146.refs_7_, f32[4,16,128]{2,1,0:T(8,128)S(1)} %get-tuple-element.30, f32[4,16,128]{2,1,0:T(8,128)S(1)} %get-tuple-element.33, f32[27]{0:T(128)S(1)} %copy-done.16, ...), kind=kLoop, calls=%fused_computation.9 | loop fusion | flops 4202496 | bytes 2032048 | tf_op jit(solution)/shard_map/add | solution.py:47
  8.1 3.1 %collective-permute-start = (f32[2,3,3,1,16,128]{5,4,2,1,3,0:T(8,128)S(1)}, f32[2,3,3,1,16,128]{5,4,2,1,3,0:T(8,128)S(1)}, u32[]{:S(2)}, u32[]{:S(2)}) collective-permute-start(f32[2,3,3,1,16,128]{5,4,2,1,3,0:T(8,128)S(1)} %pad_maximum_fusion), channel_id=1, source_target_pairs={{0,8},{8,16},{16,24},{24,32},{32,40},{40,48},{48,56},{56,64},{64,7... | collective-permute-start | bytes 442376 | tf_op jit(solution)/shard_map/ppermute | solution.py:57
  11.3 2.6 %shard_map.122 = f32[2,27,128]{2,1,0:T(8,128)} custom-call(f32[27,4,16,128]{3,2,1,0:T(8,128)} %copy-done.1, f32[27,4,16,128]{3,2,1,0:T(8,128)} %ae_ref.1), custom_call_target="tpu_custom_call" | custom-call | tf_op jit(solution)/shard_map/pallas_call | solution.py:101
  14.0 1.5 %copy_dynamic-update-slice_fusion.1 = f32[2,3,3,3,4,16,128]{6,4,3,2,5,1,0:T(4,128)S(1)} fusion(f32[1,3,3,3,4,16,128]{6,5,4,3,2,1,0:T(8,128)} %bitcast.412), kind=kLoop, calls=%fused_computation.11 | loop fusion | bytes 1769472
  15.5 0.4 copy_dynamic-update-slice_fusion
  16.1 0.1 copy-done.11
  16.3 0.2 reshape.150
  16.6 0.1 copy.570
  16.7 0.1 copy.569
  16.8 0.1 copy.568
  16.9 0.2 collective-permute-done.1
  17.2 0.2 slice_reduce_fusion.6
  17.4 0.2 slice_reduce_fusion.7
  17.6 0.2 slice_reduce_fusion.8
  17.8 0.2 slice_reduce_fusion.9
  18.3 3.7 %collective-permute-start.2 = (f32[2,2,3,3,4,1,128]{6,4,3,2,5,1,0:T(4,128)S(1)}, f32[2,2,3,3,4,1,128]{6,4,3,2,5,1,0:T(4,128)S(1)}, u32[]{:S(2)}, u32[]{:S(2)}) collective-permute-start(f32[2,2,3,3,4,1,128]{6,4,3,2,5,1,0:T(4,128)S(1)} %pad_maximum_fusion.3), channel_id=1, source_target_pairs={{0,4},{4,0},{1,5},{5,1},{2,6},{6,2},{3,7},{7,3},{8,12},{12,8},{9,1... | collective-permute-start | bytes 221192 | tf_op jit(solution)/shard_map/ppermute | solution.py:55
  22.7 1.0 %collective-permute-done.2 = f32[2,2,3,3,4,1,128]{6,4,3,2,5,1,0:T(4,128)S(1)} collective-permute-done((f32[2,2,3,3,4,1,128]{6,4,3,2,5,1,0:T(4,128)S(1)}, f32[2,2,3,3,4,1,128]{6,4,3,2,5,1,0:T(4,128)S(1)}, u32[]{:S(2)}, u32[]{:S(2)}) %collective-permute-start.2) | collective-permute-done | bytes 73760 | tf_op jit(solution)/shard_map/ppermute | solution.py:55
  23.9 0.2 slice_reduce_fusion.14
  24.1 0.1 copy.497
  24.2 0.2 slice_reduce_fusion.15
  24.4 0.1 copy.496
  24.9 1.3 %collective-permute-start.3 = (f32[2,3,3,16,4]{3,4,1,2,0:T(4,128)S(1)}, f32[2,3,3,16,4]{3,4,1,2,0:T(4,128)S(1)}, u32[]{:S(2)}, u32[]{:S(2)}) collective-permute-start(f32[2,3,3,16,4]{3,4,1,2,0:T(4,128)S(1)} %pad_maximum_fusion.10), channel_id=1, source_target_pairs={{0,1},{1,2},{2,3},{3,0},{4,5},{5,6},{6,7},{7,4},{8,9},{9,10},{10,1... | collective-permute-start | bytes 13832 | tf_op jit(solution)/shard_map/ppermute | solution.py:57
  26.2 0.1 copy.506
  26.4 0.1 copy.505
  26.9 1.5 %collective-permute-start.4 = (f32[2,3,3,16,4]{3,4,1,2,0:T(4,128)S(1)}, f32[2,3,3,16,4]{3,4,1,2,0:T(4,128)S(1)}, u32[]{:S(2)}, u32[]{:S(2)}) collective-permute-start(f32[2,3,3,16,4]{3,4,1,2,0:T(4,128)S(1)} %pad_maximum_fusion.11), channel_id=1, source_target_pairs={{0,3},{1,0},{2,1},{3,2},{4,7},{5,4},{6,5},{7,6},{8,11},{9,8},{10,9... | collective-permute-start | bytes 13832 | tf_op jit(solution)/shard_map/ppermute | solution.py:58
  28.4 0.7 fusion.29
  29.1 0.8 copy.504
  29.9 0.8 copy.513
  30.8 4.8 %shard_map.123 = (f32[27,4,16,128]{3,2,1,0:T(8,128)}, f32[4,16,128]{2,1,0:T(8,128)}) custom-call(f32[27,4,16,128]{3,2,1,0:T(8,128)} %copy-done.1, f32[27,4,16,128]{3,2,1,0:T(8,128)} %ae_ref.1, f32[18,16,128]{2,1,0:T(8,128)} %bitcast.422, f32[18,16,128]{2,1,0:T(8,128)} %bitcast.423, f32[18,4,128]{2,1,0:T(4,128)} %bitcast.438, f32[18,4,128]{2,1,0:T(4,128)} %bitcast.437, ...), custom_call_target="tpu_custom_call" | custom-call | tf_op jit(solution)/shard_map/pallas_call | solution.py:264
  35.6 1.2 %fusion.24 = (f32[9,4,16,128]{3,2,1,0:T(8,128)S(1)}, f32[9,4,16,128]{3,2,1,0:T(8,128)S(1)}) fusion(f32[27,4,16,128]{3,2,1,0:T(8,128)} %get-tuple-element.6.an_ref), kind=kLoop, calls=%fused_computation.231 | loop fusion | bytes 1179648 | tf_op jit(solution)/shard_map/slice | solution.py:78
  36.8 1.2 %fusion.23 = (f32[1,3,3,3,4,1,128]{6,5,4,3,2,1,0:T(1,128)S(1)}, f32[1,3,3,3,4,1,128]{6,5,4,3,2,1,0:T(1,128)S(1)}) fusion(f32[1,3,3,3,4,16,128]{6,5,4,3,2,1,0:T(8,128)} %bitcast.413), kind=kLoop, calls=%fused_computation.230 | loop fusion | bytes 221184 | tf_op jit(solution)/shard_map/slice | solution.py:99
  38.0 0.3 fusion.22
  38.4 3.3 %collective-permute-start.5 = (f32[1,3,3,1,16,128]{5,4,2,1,3,0:T(8,128)S(1)}, f32[1,3,3,1,16,128]{5,4,2,1,3,0:T(8,128)S(1)}, u32[]{:S(2)}, u32[]{:S(2)}) collective-permute-start(f32[1,3,3,1,16,128]{5,4,2,1,3,0:T(8,128)S(1)} %slice_bitcast_fusion.1), channel_id=1, source_target_pairs={{0,8},{8,16},{16,24},{24,32},{32,40},{40,48},{48,56},{56,64},{64,7... | collective-permute-start | bytes 221192 | tf_op jit(solution)/shard_map/ppermute | solution.py:57
  41.7 1.0 %collective-permute-start.6 = (f32[1,3,3,1,16,128]{5,4,2,1,3,0:T(8,128)S(1)}, f32[1,3,3,1,16,128]{5,4,2,1,3,0:T(8,128)S(1)}, u32[]{:S(2)}, u32[]{:S(2)}) collective-permute-start(f32[1,3,3,1,16,128]{5,4,2,1,3,0:T(8,128)S(1)} %slice_bitcast_fusion), channel_id=1, source_target_pairs={{0,120},{8,0},{16,8},{24,16},{32,24},{40,32},{48,40},{56,48},{64,5... | collective-permute-start | bytes 221192 | tf_op jit(solution)/shard_map/ppermute | solution.py:58
  42.7 0.7 copy.567
  43.4 0.7 copy.566
  44.3 1.1 %collective-permute-done.6 = f32[1,3,3,1,16,128]{5,4,2,1,3,0:T(8,128)S(1)} collective-permute-done((f32[1,3,3,1,16,128]{5,4,2,1,3,0:T(8,128)S(1)}, f32[1,3,3,1,16,128]{5,4,2,1,3,0:T(8,128)S(1)}, u32[]{:S(2)}, u32[]{:S(2)}) %collective-permute-start.6) | collective-permute-done | bytes 73760 | tf_op jit(solution)/shard_map/ppermute | solution.py:58
  45.8 3.4 %collective-permute-start.7 = (f32[2,1,3,3,4,1,128]{6,4,3,2,5,1,0:T(4,128)S(1)}, f32[2,1,3,3,4,1,128]{6,4,3,2,5,1,0:T(4,128)S(1)}, u32[]{:S(2)}, u32[]{:S(2)}) collective-permute-start(f32[2,1,3,3,4,1,128]{6,4,3,2,5,1,0:T(4,128)S(1)} %pad_maximum_fusion.12), channel_id=1, source_target_pairs={{0,4},{4,0},{1,5},{5,1},{2,6},{6,2},{3,7},{7,3},{8,12},{12,8},{9,1... | collective-permute-start | bytes 110600 | tf_op jit(solution)/shard_map/ppermute | solution.py:55
  49.2 0.1 copy.529
  49.3 0.1 copy.526
  49.6 0.1 copy.542
  49.7 0.1 copy.539
  50.0 0.6 collective-permute-done.7
  50.6 0.6 slice_bitcast_fusion.92
  51.6 1.3 %collective-permute-start.8 = (f32[1,3,3,16,4]{3,4,2,1,0:T(4,128)S(1)}, f32[1,3,3,16,4]{3,4,2,1,0:T(4,128)S(1)}, u32[]{:S(2)}, u32[]{:S(2)}) collective-permute-start(f32[1,3,3,16,4]{3,4,2,1,0:T(4,128)S(1)} %slice_bitcast_fusion.21), channel_id=1, source_target_pairs={{0,1},{1,2},{2,3},{3,0},{4,5},{5,6},{6,7},{7,4},{8,9},{9,10},{10,1... | collective-permute-start | bytes 6920 | tf_op jit(solution)/shard_map/ppermute | solution.py:57
  53.1 1.5 %collective-permute-start.9 = (f32[1,3,3,16,4]{3,4,2,1,0:T(4,128)S(1)}, f32[1,3,3,16,4]{3,4,2,1,0:T(4,128)S(1)}, u32[]{:S(2)}, u32[]{:S(2)}) collective-permute-start(f32[1,3,3,16,4]{3,4,2,1,0:T(4,128)S(1)} %slice_bitcast_fusion.10), channel_id=1, source_target_pairs={{0,3},{1,0},{2,1},{3,2},{4,7},{5,4},{6,5},{7,6},{8,11},{9,8},{10,9... | collective-permute-start | bytes 6920 | tf_op jit(solution)/shard_map/ppermute | solution.py:58
  54.7 0.8 collective-permute-done.8
  55.5 0.8 copy.538
  56.2 0.8 copy.551
  57.0 4.2 %shard_map.124 = (f32[27,4,16,128]{3,2,1,0:T(8,128)}, f32[4,16,128]{2,1,0:T(8,128)}) custom-call(f32[27,4,16,128]{3,2,1,0:T(8,128)} %get-tuple-element.6.an_ref, f32[27,4,16,128]{3,2,1,0:T(8,128)} %f_ref.1, f32[9,16,128]{2,1,0:T(8,128)} %bitcast.418, f32[9,16,128]{2,1,0:T(8,128)} %bitcast.421, f32[9,4,128]{2,1,0:T(4,128)} %bitcast.454, ...), custom_call_target="tpu_custom_call" | custom-call | tf_op jit(solution)/shard_map/pallas_call | solution.py:264
  61.2 0.8 add_multiply_fusion
  62.0 0.1 reshape.157
  62.1 0.1 reduce_sum.106
  62.3 0.1 select_reduce_fusion
  62.5 21.4 %all_to_all.9 = f32[128,1,8]{2,1,0:T(1,128)S(1)} all-to-all(f32[128,1,8]{2,1,0:T(1,128)S(1)} %bitcast.434), channel_id=1, replica_groups=mesh['gx'=16,'gy'=2,'gz'=4] {'gx','gy','gz'}, dimensions={0} | all-to-all | bytes 8192 | tf_op jit(solution)/shard_map/all_to_all | solution.py:298
  83.9 0.7 reduce_sum.109
  (199 shorter events, 4.2 us)
Async XLA Ops:
  0.6 3.5 %copy-start = (f32[27,4,16,128]{3,2,1,0:T(8,128)S(1)}, f32[27,4,16,128]{3,2,1,0:T(8,128)}, u32[]{:S(2)}) copy-start(f32[27,4,16,128]{3,2,1,0:T(8,128)} %f_ref.1) | copy-start | bytes 2654212
  0.6 3.5 %copy-start.14 = (s32[1024]{0:T(1024)S(1)}, s32[1024]{0:T(1024)}, u32[]{:S(2)}) copy-start(s32[1024]{0:T(1024)} %param.17) | copy-start | bytes 12292
  0.7 3.6 %copy-start.15 = (f32[1024]{0:T(1024)S(1)}, f32[1024]{0:T(1024)}, u32[]{:S(2)}) copy-start(f32[1024]{0:T(1024)} %param.16) | copy-start | bytes 12292
  0.7 5.7 %copy-start.3 = (f32[27,4,16,128]{3,2,1,0:T(8,128)S(1)}, f32[27,4,16,128]{3,2,1,0:T(8,128)}, u32[]{:S(2)}) copy-start(f32[27,4,16,128]{3,2,1,0:T(8,128)} %ae_ref.1) | copy-start | bytes 2654212
  4.1 2.4 %copy-start.12 = (s32[4,16,128]{2,1,0:T(8,128)S(1)}, s32[4,16,128]{2,1,0:T(8,128)}, u32[]{:S(2)}) copy-start(s32[4,16,128]{2,1,0:T(8,128)} %param.14) | copy-start | bytes 98308
  4.2 2.3 %copy-start.10 = (f32[4,16,128]{2,1,0:T(8,128)S(1)}, f32[4,16,128]{2,1,0:T(8,128)}, u32[]{:S(2)}) copy-start(f32[4,16,128]{2,1,0:T(8,128)} %refs_6_.3) | copy-start | bytes 98308
  4.2 2.3 %copy-start.16 = (f32[27]{0:T(128)S(1)}, f32[27]{0:T(128)}, u32[]{:S(2)}) copy-start(f32[27]{0:T(128)} %constant.26.clone) | copy-start | bytes 328
  4.2 2.3 %copy-start.17 = (f32[27]{0:T(128)S(1)}, f32[27]{0:T(128)}, u32[]{:S(2)}) copy-start(f32[27]{0:T(128)} %constant.25.clone) | copy-start | bytes 328
  4.2 2.3 %copy-start.18 = (f32[27]{0:T(128)S(1)}, f32[27]{0:T(128)}, u32[]{:S(2)}) copy-start(f32[27]{0:T(128)} %constant.24.clone) | copy-start | bytes 328
  4.2 2.3 %copy-start.19 = (f32[27]{0:T(128)S(1)}, f32[27]{0:T(128)}, u32[]{:S(2)}) copy-start(f32[27]{0:T(128)} %constant.27.clone) | copy-start | bytes 328
  6.5 1.5 %copy-start.9 = (f32[4,16,128]{2,1,0:T(8,128)}, f32[4,16,128]{2,1,0:T(8,128)S(1)}, u32[]{:S(2)}) copy-start(f32[4,16,128]{2,1,0:T(8,128)S(1)} %get-tuple-element.146.refs_7_) | copy-start | bytes 98308
  8.0 3.4 %copy-start.1 = (f32[27,4,16,128]{3,2,1,0:T(8,128)}, f32[27,4,16,128]{3,2,1,0:T(8,128)S(1)}, u32[]{:S(2)}) copy-start(f32[27,4,16,128]{3,2,1,0:T(8,128)S(1)} %fusion.7.a_ref.cf_ref) | copy-start | bytes 2654212
  8.1 9.3 %collective-permute-start = (f32[2,3,3,1,16,128]{5,4,2,1,3,0:T(8,128)S(1)}, f32[2,3,3,1,16,128]{5,4,2,1,3,0:T(8,128)S(1)}, u32[]{:S(2)}, u32[]{:S(2)}) collective-permute-start(f32[2,3,3,1,16,128]{5,4,2,1,3,0:T(8,128)S(1)} %pad_maximum_fusion), channel_id=1, source_target_pairs={{0,8},{8,16},{16,24},{24,32},{32,40},{40,48},{48,56},{56,64},{64,7... | collective-permute-start | bytes 442376 | tf_op jit(solution)/shard_map/ppermute | solution.py:57
  11.2 4.3 %copy-start.4 = (f32[27,4,16,128]{3,2,1,0:T(8,128)S(1)}, f32[27,4,16,128]{3,2,1,0:T(8,128)}, u32[]{:S(2)}) copy-start(f32[27,4,16,128]{3,2,1,0:T(8,128)} %ae_ref.1) | copy-start | bytes 2654212
  11.2 5.9 %collective-permute-start.1 = (f32[2,3,3,1,16,128]{5,4,2,1,3,0:T(8,128)S(1)}, f32[2,3,3,1,16,128]{5,4,2,1,3,0:T(8,128)S(1)}, u32[]{:S(2)}, u32[]{:S(2)}) collective-permute-start(f32[2,3,3,1,16,128]{5,4,2,1,3,0:T(8,128)S(1)} %pad_maximum_fusion.1), channel_id=1, source_target_pairs={{0,120},{8,0},{16,8},{24,16},{32,24},{40,32},{48,40},{56,48},{64,5... | collective-permute-start | bytes 442376 | tf_op jit(solution)/shard_map/ppermute | solution.py:58
  15.5 0.8 copy-start.11
  17.2 5.3 %copy-start.8 = (f32[2,3,3,1,16,128]{5,4,2,1,3,0:T(8,128)}, f32[2,3,3,1,16,128]{5,4,2,1,3,0:T(8,128)S(1)}, u32[]{:S(2)}) copy-start(f32[2,3,3,1,16,128]{5,4,2,1,3,0:T(8,128)S(1)} %collective-permute-done.1) | copy-start | bytes 442372
  17.4 6.5 %copy-start.7 = (f32[2,3,3,1,16,128]{5,4,2,1,3,0:T(8,128)}, f32[2,3,3,1,16,128]{5,4,2,1,3,0:T(8,128)S(1)}, u32[]{:S(2)}) copy-start(f32[2,3,3,1,16,128]{5,4,2,1,3,0:T(8,128)S(1)} %collective-permute-done) | copy-start | bytes 442372
  18.3 5.4 %collective-permute-start.2 = (f32[2,2,3,3,4,1,128]{6,4,3,2,5,1,0:T(4,128)S(1)}, f32[2,2,3,3,4,1,128]{6,4,3,2,5,1,0:T(4,128)S(1)}, u32[]{:S(2)}, u32[]{:S(2)}) collective-permute-start(f32[2,2,3,3,4,1,128]{6,4,3,2,5,1,0:T(4,128)S(1)} %pad_maximum_fusion.3), channel_id=1, source_target_pairs={{0,4},{4,0},{1,5},{5,1},{2,6},{6,2},{3,7},{7,3},{8,12},{12,8},{9,1... | collective-permute-start | bytes 221192 | tf_op jit(solution)/shard_map/ppermute | solution.py:55
  24.9 4.2 %collective-permute-start.3 = (f32[2,3,3,16,4]{3,4,1,2,0:T(4,128)S(1)}, f32[2,3,3,16,4]{3,4,1,2,0:T(4,128)S(1)}, u32[]{:S(2)}, u32[]{:S(2)}) collective-permute-start(f32[2,3,3,16,4]{3,4,1,2,0:T(4,128)S(1)} %pad_maximum_fusion.10), channel_id=1, source_target_pairs={{0,1},{1,2},{2,3},{3,0},{4,5},{5,6},{6,7},{7,4},{8,9},{9,10},{10,1... | collective-permute-start | bytes 13832 | tf_op jit(solution)/shard_map/ppermute | solution.py:57
  26.9 3.0 %collective-permute-start.4 = (f32[2,3,3,16,4]{3,4,1,2,0:T(4,128)S(1)}, f32[2,3,3,16,4]{3,4,1,2,0:T(4,128)S(1)}, u32[]{:S(2)}, u32[]{:S(2)}) collective-permute-start(f32[2,3,3,16,4]{3,4,1,2,0:T(4,128)S(1)} %pad_maximum_fusion.11), channel_id=1, source_target_pairs={{0,3},{1,0},{2,1},{3,2},{4,7},{5,4},{6,5},{7,6},{8,11},{9,8},{10,9... | collective-permute-start | bytes 13832 | tf_op jit(solution)/shard_map/ppermute | solution.py:58
  35.6 2.4 %copy-start.2 = (f32[27,4,16,128]{3,2,1,0:T(8,128)S(1)}, f32[27,4,16,128]{3,2,1,0:T(8,128)}, u32[]{:S(2)}) copy-start(f32[27,4,16,128]{3,2,1,0:T(8,128)} %get-tuple-element.6.an_ref) | copy-start | bytes 2654212
  38.4 7.2 %collective-permute-start.5 = (f32[1,3,3,1,16,128]{5,4,2,1,3,0:T(8,128)S(1)}, f32[1,3,3,1,16,128]{5,4,2,1,3,0:T(8,128)S(1)}, u32[]{:S(2)}, u32[]{:S(2)}) collective-permute-start(f32[1,3,3,1,16,128]{5,4,2,1,3,0:T(8,128)S(1)} %slice_bitcast_fusion.1), channel_id=1, source_target_pairs={{0,8},{8,16},{16,24},{24,32},{32,40},{40,48},{48,56},{56,64},{64,7... | collective-permute-start | bytes 221192 | tf_op jit(solution)/shard_map/ppermute | solution.py:57
  41.7 3.8 %collective-permute-start.6 = (f32[1,3,3,1,16,128]{5,4,2,1,3,0:T(8,128)S(1)}, f32[1,3,3,1,16,128]{5,4,2,1,3,0:T(8,128)S(1)}, u32[]{:S(2)}, u32[]{:S(2)}) collective-permute-start(f32[1,3,3,1,16,128]{5,4,2,1,3,0:T(8,128)S(1)} %slice_bitcast_fusion), channel_id=1, source_target_pairs={{0,120},{8,0},{16,8},{24,16},{32,24},{40,32},{48,40},{56,48},{64,5... | collective-permute-start | bytes 221192 | tf_op jit(solution)/shard_map/ppermute | solution.py:58
  45.4 11.6 %copy-start.6 = (f32[1,3,3,1,16,128]{5,4,2,1,3,0:T(8,128)}, f32[1,3,3,1,16,128]{5,4,2,1,3,0:T(8,128)S(1)}, u32[]{:S(2)}) copy-start(f32[1,3,3,1,16,128]{5,4,2,1,3,0:T(8,128)S(1)} %collective-permute-done.6) | copy-start | bytes 221188
  45.5 11.5 %copy-start.5 = (f32[1,3,3,1,16,128]{5,4,2,1,3,0:T(8,128)}, f32[1,3,3,1,16,128]{5,4,2,1,3,0:T(8,128)S(1)}, u32[]{:S(2)}) copy-start(f32[1,3,3,1,16,128]{5,4,2,1,3,0:T(8,128)S(1)} %collective-permute-done.5) | copy-start | bytes 221188
  45.8 4.8 %collective-permute-start.7 = (f32[2,1,3,3,4,1,128]{6,4,3,2,5,1,0:T(4,128)S(1)}, f32[2,1,3,3,4,1,128]{6,4,3,2,5,1,0:T(4,128)S(1)}, u32[]{:S(2)}, u32[]{:S(2)}) collective-permute-start(f32[2,1,3,3,4,1,128]{6,4,3,2,5,1,0:T(4,128)S(1)} %pad_maximum_fusion.12), channel_id=1, source_target_pairs={{0,4},{4,0},{1,5},{5,1},{2,6},{6,2},{3,7},{7,3},{8,12},{12,8},{9,1... | collective-permute-start | bytes 110600 | tf_op jit(solution)/shard_map/ppermute | solution.py:55
  49.8 11.4 %copy-start.13 = (f32[4,16,128]{2,1,0:T(8,128)S(1)}, f32[4,16,128]{2,1,0:T(8,128)}, u32[]{:S(2)}) copy-start(f32[4,16,128]{2,1,0:T(8,128)} %get-tuple-element.8) | copy-start | bytes 98308
  51.6 3.9 %collective-permute-start.8 = (f32[1,3,3,16,4]{3,4,2,1,0:T(4,128)S(1)}, f32[1,3,3,16,4]{3,4,2,1,0:T(4,128)S(1)}, u32[]{:S(2)}, u32[]{:S(2)}) collective-permute-start(f32[1,3,3,16,4]{3,4,2,1,0:T(4,128)S(1)} %slice_bitcast_fusion.21), channel_id=1, source_target_pairs={{0,1},{1,2},{2,3},{3,0},{4,5},{5,6},{6,7},{7,4},{8,9},{9,10},{10,1... | collective-permute-start | bytes 6920 | tf_op jit(solution)/shard_map/ppermute | solution.py:57
  53.1 3.2 %collective-permute-start.9 = (f32[1,3,3,16,4]{3,4,2,1,0:T(4,128)S(1)}, f32[1,3,3,16,4]{3,4,2,1,0:T(4,128)S(1)}, u32[]{:S(2)}, u32[]{:S(2)}) collective-permute-start(f32[1,3,3,16,4]{3,4,2,1,0:T(4,128)S(1)} %slice_bitcast_fusion.10), channel_id=1, source_target_pairs={{0,3},{1,0},{2,1},{3,2},{4,7},{5,4},{6,5},{7,6},{8,11},{9,8},{10,9... | collective-permute-start | bytes 6920 | tf_op jit(solution)/shard_map/ppermute | solution.py:58

commit v14 on v13

--- a/solution.py
+++ b/solution.py
@@ -79,16 +79,17 @@
     return lax.slice_in_dim(plus, n - 1, n, axis=2 + d), lax.slice_in_dim(minus, 0, 1, axis=2 + d)
 
 
-def columns_kernel(a_ref, b_ref, out_ref):
-    _, sx, sy, sz = a_ref.shape
-    pairs = [(r, q, i) for r in (a_ref, b_ref) for q in range(27) for i in range(sx)]
+def columns_kernel(*refs):
+    fields, out_ref = refs[:-1], refs[-1]
+    _, sx, sy, sz = fields[0].shape
+    pairs = [(r, q, i) for r in fields for q in range(27) for i in range(sx)]
     per = 128 // sy
-    for g in range(len(pairs) // per):
-        block = jnp.concatenate([r[q, i] for r, q, i in pairs[g * per : (g + 1) * per]], axis=0)
-        flipped = block.T
+    for g in range(out_ref.shape[1]):
+        tiles = [r[q, i] for r, q, i in pairs[g * per : (g + 1) * per]]
+        tiles += [jnp.zeros((sy, sz), jnp.float32)] * (per - len(tiles))
+        flipped = jnp.concatenate(tiles, axis=0).T
         out_ref[0, pl.ds(g, 1), :] = flipped[sz - 1 : sz, :]
         out_ref[1, pl.ds(g, 1), :] = flipped[0:1, :]
-
 
 def halos(fields, signs):
     cubes = [f.reshape((3, 3, 3) + f.shape[1:]) for f in fields]
@@ -97,11 +98,12 @@
     xlo, xhi = halo_exchange(jnp.stack(x_up), jnp.stack(x_dn), "gx")
     both = jnp.stack(cubes)
     rows = jnp.concatenate([both[..., sy - 1 : sy, :], both[..., 0:1, :]], axis=5)
-    if len(fields) == 2 and sy * 8 == 128 and sz == 128:
+    if sy * 8 == 128 and sz == 128:
+        count = len(fields) * 27 * sx
         flat = pl.pallas_call(
-            columns_kernel, out_shape=jax.ShapeDtypeStruct((2, 2 * 27 * sx * sy // 128, 128), jnp.float32)
-        )(fields[0], fields[1])
-        cols = flat.reshape((2, 2, 3, 3, 3, sx, sy))
+            columns_kernel, out_shape=jax.ShapeDtypeStruct((2, -(-count // 8), 128), jnp.float32)
+        )(*fields)
+        cols = flat.reshape(2, -1)[:, : count * sy].reshape((2, len(fields), 3, 3, 3, sx, sy))
     else:
         cols = None
         edges = jnp.concatenate([both[..., sz - 1 : sz], both[..., 0:1]], axis=6)

time: 85.1 us -> 86.4 us (1.015)
  Pallas kernels: 11.7 us -> 13.8 us
    pallas_call x1 -> x2, Pallas kernels: 2.65 us -> 4.71 us  [halos(): pl.pallas_call(columns_kernel, out_shape=jax.ShapeDtypeStruct((2, -(-coun...]
    ppermute x4, waiting for transfers between devices: 1.37 us -> 0.32 us  [halo_exchange(): hi = lax.ppermute(down, axis, [(i, (i - 1) % size) for i in range(size)])]
    unnamed x47 -> x44, local copies, waits for them, and re-layouts: 3.59 us -> 2.91 us
where the time goes in v14:
time: 86.4 us; the launch traced here: 85.7 us
  blocking collectives  22.1 us (26%)
  starting transfers between devices  20.1 us (23%)
  local copies, waits for them, and re-layouts  16.5 us (19%)
  Pallas kernels  13.8 us (16%)
  other arithmetic  8.28 us (10%)
  waiting for transfers between devices  3.1 us (4%)
  between operations  1.84 us (2%)
    all_to_all x1, blocking collectives, shards(): lax.all_to_all(placed.reshape(devices, count // devices), ('gx', 'gy', 'g...  22.1 us
    pallas_call x2, Pallas kernels, run_stage(): pl.pallas_call(kernel, out_shape=(jax.ShapeDtypeStruct(shape, jnp.float32...  9.08 us
    ppermute x4, starting transfers between devices, halo_exchange(): lo = lax.ppermute(up, axis, [(i, (i + 1) % size) for i in range(size)])  8.88 us
    ppermute x2, starting transfers between devices, halo_exchange(): both = lax.ppermute(jnp.stack([up, down]), axis, [(0, 1), (1, 0)])  7.07 us
    pallas_call x2, Pallas kernels, halos(): pl.pallas_call(columns_kernel, out_shape=jax.ShapeDtypeStruct((2, -(-coun...  4.71 us
    ppermute x4, starting transfers between devices, halo_exchange(): hi = lax.ppermute(down, axis, [(i, (i - 1) % size) for i in range(size)])  4.18 us
    unnamed x44, local copies, waits for them, and re-layouts  2.91 us
    ppermute x2, waiting for transfers between devices, halo_exchange(): both = lax.ppermute(jnp.stack([up, down]), axis, [(0, 1), (1, 0)])  1.96 us
  transfers between devices with their start and end apart: 10, of which 5 were waited for; matrix products, arithmetic and copies ran while one was open for 11% of the time, Pallas kernels for 3%

profile of v14, /device:TPU:1, one launch (start us, length us, event | category | flops | bytes accessed | tf_op | source)
XLA Modules:
  0.0 85.7 jit_solution(4921716400201571876)
XLA Ops:
  0.7 1.2 %slice_reduce_fusion.4 = (f32[4,16,128]{2,1,0:T(8,128)S(1)}, f32[4,16,128]{2,1,0:T(8,128)S(1)}) fusion(f32[27,4,16,128]{3,2,1,0:T(8,128)} %f_ref.1), kind=kLoop, calls=%fused_computation.16 | loop fusion | flops 131072 | bytes 655360 | tf_op jit(solution)/shard_map/reduce_sum | solution.py:32
  1.9 1.1 %slice_reduce_fusion.2 = (f32[4,16,128]{2,1,0:T(8,128)S(1)}, f32[4,16,128]{2,1,0:T(8,128)S(1)}) fusion(f32[3,3,3,4,16,128]{5,4,3,2,1,0:T(8,128)} %bitcast.380), kind=kLoop, calls=%fused_computation.14 | loop fusion | flops 131072 | bytes 655360 | tf_op jit(solution)/shard_map/reduce_sum | solution.py:33
  3.0 1.1 %slice_reduce_fusion = (f32[4,16,128]{2,1,0:T(8,128)S(1)}, f32[4,16,128]{2,1,0:T(8,128)S(1)}) fusion(f32[3,3,3,4,16,128]{5,4,3,2,1,0:T(8,128)} %bitcast.381), kind=kLoop, calls=%fused_computation.12 | loop fusion | flops 131072 | bytes 655360 | tf_op jit(solution)/shard_map/reduce_sum | solution.py:34
  4.3 0.2 copy.426
  4.5 0.8 slice.663
  5.4 0.1 reshape.175
  5.5 0.6 gather_fusion
  6.0 0.1 copy.491
  6.2 0.1 broadcast_in_dim.8
  6.3 0.1 reshape.161
  6.6 1.4 %fusion.7.refs_0_.cf_ref = f32[27,4,16,128]{3,2,1,0:T(8,128)S(1)} fusion(f32[27,4,16,128]{3,2,1,0:T(8,128)S(1)} %copy-done, f32[4,16,128]{2,1,0:T(8,128)S(1)} %get-tuple-element.144.refs_7_, f32[4,16,128]{2,1,0:T(8,128)S(1)} %get-tuple-element.40, f32[4,16,128]{2,1,0:T(8,128)S(1)} %get-tuple-element.43, f32[27]{0:T(128)S(1)} %copy-done.15, ...), kind=kLoop, calls=%fused_computation.9 | loop fusion | flops 4202496 | bytes 2032048 | tf_op jit(solution)/shard_map/add | solution.py:47
  8.1 3.1 %collective-permute-start = (f32[2,3,3,1,16,128]{5,4,2,1,3,0:T(8,128)S(1)}, f32[2,3,3,1,16,128]{5,4,2,1,3,0:T(8,128)S(1)}, u32[]{:S(2)}, u32[]{:S(2)}) collective-permute-start(f32[2,3,3,1,16,128]{5,4,2,1,3,0:T(8,128)S(1)} %pad_maximum_fusion), channel_id=1, source_target_pairs={{0,8},{8,16},{16,24},{24,32},{32,40},{40,48},{48,56},{56,64},{64,7... | collective-permute-start | bytes 442376 | tf_op jit(solution)/shard_map/ppermute | solution.py:57
  11.3 2.6 %shard_map.122 = f32[2,27,128]{2,1,0:T(8,128)} custom-call(f32[27,4,16,128]{3,2,1,0:T(8,128)} %copy-done.1, f32[27,4,16,128]{3,2,1,0:T(8,128)} %ae_ref.1), custom_call_target="tpu_custom_call" | custom-call | tf_op jit(solution)/shard_map/pallas_call | solution.py:103
  14.0 1.5 %copy_dynamic-update-slice_fusion.1 = f32[2,3,3,3,4,16,128]{6,4,3,2,5,1,0:T(4,128)S(1)} fusion(f32[1,3,3,3,4,16,128]{6,5,4,3,2,1,0:T(8,128)} %bitcast.382), kind=kLoop, calls=%fused_computation.11 | loop fusion | bytes 1769472
  15.5 0.4 copy_dynamic-update-slice_fusion
  16.1 0.1 copy-done.10
  16.2 0.2 reshape_reshape.3
  16.6 0.1 copy.508
  16.7 0.1 copy.507
  16.8 0.1 copy.506
  16.9 0.3 collective-permute-done.1
  17.2 0.2 slice_reduce_fusion.10
  17.4 0.2 slice_reduce_fusion.11
  17.6 0.2 slice_reduce_fusion.12
  17.8 0.2 slice_reduce_fusion.13
  18.3 3.7 %collective-permute-start.2 = (f32[2,2,3,3,4,1,128]{6,4,3,2,5,1,0:T(4,128)S(1)}, f32[2,2,3,3,4,1,128]{6,4,3,2,5,1,0:T(4,128)S(1)}, u32[]{:S(2)}, u32[]{:S(2)}) collective-permute-start(f32[2,2,3,3,4,1,128]{6,4,3,2,5,1,0:T(4,128)S(1)} %pad_maximum_fusion.3), channel_id=1, source_target_pairs={{0,4},{4,0},{1,5},{5,1},{2,6},{6,2},{3,7},{7,3},{8,12},{12,8},{9,1... | collective-permute-start | bytes 221192 | tf_op jit(solution)/shard_map/ppermute | solution.py:55
  22.7 1.0 %collective-permute-done.2 = f32[2,2,3,3,4,1,128]{6,4,3,2,5,1,0:T(4,128)S(1)} collective-permute-done((f32[2,2,3,3,4,1,128]{6,4,3,2,5,1,0:T(4,128)S(1)}, f32[2,2,3,3,4,1,128]{6,4,3,2,5,1,0:T(4,128)S(1)}, u32[]{:S(2)}, u32[]{:S(2)}) %collective-permute-start.2) | collective-permute-done | bytes 73760 | tf_op jit(solution)/shard_map/ppermute | solution.py:55
  23.9 0.2 slice_reduce_fusion.18
  24.1 0.1 copy.451
  24.2 0.2 slice_reduce_fusion.19
  24.4 0.1 copy.450
  24.9 1.3 %collective-permute-start.3 = (f32[2,3,3,16,4]{3,4,1,2,0:T(4,128)S(1)}, f32[2,3,3,16,4]{3,4,1,2,0:T(4,128)S(1)}, u32[]{:S(2)}, u32[]{:S(2)}) collective-permute-start(f32[2,3,3,16,4]{3,4,1,2,0:T(4,128)S(1)} %pad_maximum_fusion.10), channel_id=1, source_target_pairs={{0,1},{1,2},{2,3},{3,0},{4,5},{5,6},{6,7},{7,4},{8,9},{9,10},{10,1... | collective-permute-start | bytes 13832 | tf_op jit(solution)/shard_map/ppermute | solution.py:57
  26.2 0.1 copy.460
  26.4 0.1 copy.459
  26.9 1.5 %collective-permute-start.4 = (f32[2,3,3,16,4]{3,4,1,2,0:T(4,128)S(1)}, f32[2,3,3,16,4]{3,4,1,2,0:T(4,128)S(1)}, u32[]{:S(2)}, u32[]{:S(2)}) collective-permute-start(f32[2,3,3,16,4]{3,4,1,2,0:T(4,128)S(1)} %pad_maximum_fusion.11), channel_id=1, source_target_pairs={{0,3},{1,0},{2,1},{3,2},{4,7},{5,4},{6,5},{7,6},{8,11},{9,8},{10,9... | collective-permute-start | bytes 13832 | tf_op jit(solution)/shard_map/ppermute | solution.py:58
  28.4 0.6 fusion.28
  29.0 0.8 copy.458
  29.9 0.8 copy.467
  30.7 4.8 %shard_map.123 = (f32[27,4,16,128]{3,2,1,0:T(8,128)}, f32[4,16,128]{2,1,0:T(8,128)}) custom-call(f32[27,4,16,128]{3,2,1,0:T(8,128)} %copy-done.1, f32[27,4,16,128]{3,2,1,0:T(8,128)} %ae_ref.1, f32[18,16,128]{2,1,0:T(8,128)} %bitcast.391, f32[18,16,128]{2,1,0:T(8,128)} %bitcast.392, f32[18,4,128]{2,1,0:T(4,128)} %bitcast.407, f32[18,4,128]{2,1,0:T(4,128)} %bitcast.406, ...), custom_call_target="tpu_custom_call" | custom-call | tf_op jit(solution)/shard_map/pallas_call | solution.py:266
  35.6 1.1 %fusion.25 = (f32[9,4,16,128]{3,2,1,0:T(8,128)S(1)}, f32[9,4,16,128]{3,2,1,0:T(8,128)S(1)}) fusion(f32[27,4,16,128]{3,2,1,0:T(8,128)} %get-tuple-element.6.refs_0_.an_ref), kind=kLoop, calls=%fused_computation.232 | loop fusion | bytes 1179648 | tf_op jit(solution)/shard_map/slice | solution.py:78
  36.7 2.1 %shard_map.124 = f32[2,14,128]{2,1,0:T(8,128)} custom-call(f32[27,4,16,128]{3,2,1,0:T(8,128)} %get-tuple-element.6.refs_0_.an_ref), custom_call_target="tpu_custom_call" | custom-call | tf_op jit(solution)/shard_map/pallas_call | solution.py:103
  38.8 3.2 %collective-permute-start.5 = (f32[1,3,3,1,16,128]{5,4,2,1,3,0:T(8,128)S(1)}, f32[1,3,3,1,16,128]{5,4,2,1,3,0:T(8,128)S(1)}, u32[]{:S(2)}, u32[]{:S(2)}) collective-permute-start(f32[1,3,3,1,16,128]{5,4,2,1,3,0:T(8,128)S(1)} %slice_bitcast_fusion.1), channel_id=1, source_target_pairs={{0,8},{8,16},{16,24},{24,32},{32,40},{40,48},{48,56},{56,64},{64,7... | collective-permute-start | bytes 221192 | tf_op jit(solution)/shard_map/ppermute | solution.py:57
  42.0 1.0 %collective-permute-start.6 = (f32[1,3,3,1,16,128]{5,4,2,1,3,0:T(8,128)S(1)}, f32[1,3,3,1,16,128]{5,4,2,1,3,0:T(8,128)S(1)}, u32[]{:S(2)}, u32[]{:S(2)}) collective-permute-start(f32[1,3,3,1,16,128]{5,4,2,1,3,0:T(8,128)S(1)} %slice_bitcast_fusion), channel_id=1, source_target_pairs={{0,120},{8,0},{16,8},{24,16},{32,24},{40,32},{48,40},{56,48},{64,5... | collective-permute-start | bytes 221192 | tf_op jit(solution)/shard_map/ppermute | solution.py:58
  43.0 1.2 %fusion.24 = (f32[1,3,3,3,4,1,128]{6,5,4,3,2,1,0:T(1,128)S(1)}, f32[1,3,3,3,4,1,128]{6,5,4,3,2,1,0:T(1,128)S(1)}) fusion(f32[1,3,3,3,4,16,128]{6,5,4,3,2,1,0:T(8,128)} %bitcast.384), kind=kLoop, calls=%fused_computation.231 | loop fusion | bytes 221184 | tf_op jit(solution)/shard_map/slice | solution.py:100
  44.4 0.7 copy.513
  45.1 0.1 slice_reduce_fusion.24
  45.8 0.2 slice_reduce_fusion.6
  46.0 0.2 slice_reduce_fusion.7
  46.3 3.4 %collective-permute-start.7 = (f32[2,1,3,3,4,1,128]{6,4,3,2,5,1,0:T(4,128)S(1)}, f32[2,1,3,3,4,1,128]{6,4,3,2,5,1,0:T(4,128)S(1)}, u32[]{:S(2)}, u32[]{:S(2)}) collective-permute-start(f32[2,1,3,3,4,1,128]{6,4,3,2,5,1,0:T(4,128)S(1)} %pad_maximum_fusion.12), channel_id=1, source_target_pairs={{0,4},{4,0},{1,5},{5,1},{2,6},{6,2},{3,7},{7,3},{8,12},{12,8},{9,1... | collective-permute-start | bytes 110600 | tf_op jit(solution)/shard_map/ppermute | solution.py:55
  50.1 1.0 %collective-permute-done.7 = f32[2,1,3,3,4,1,128]{6,4,3,2,5,1,0:T(4,128)S(1)} collective-permute-done((f32[2,1,3,3,4,1,128]{6,4,3,2,5,1,0:T(4,128)S(1)}, f32[2,1,3,3,4,1,128]{6,4,3,2,5,1,0:T(4,128)S(1)}, u32[]{:S(2)}, u32[]{:S(2)}) %collective-permute-start.7) | collective-permute-done | bytes 36896 | tf_op jit(solution)/shard_map/ppermute | solution.py:55
  51.1 0.6 slice_bitcast_fusion.80
  52.0 1.3 %collective-permute-start.8 = (f32[1,3,3,16,4]{3,4,1,2,0:T(4,128)S(1)}, f32[1,3,3,16,4]{3,4,1,2,0:T(4,128)S(1)}, u32[]{:S(2)}, u32[]{:S(2)}) collective-permute-start(f32[1,3,3,16,4]{3,4,1,2,0:T(4,128)S(1)} %fusion.12), channel_id=1, source_target_pairs={{0,1},{1,2},{2,3},{3,0},{4,5},{5,6},{6,7},{7,4},{8,9},{9,10},{10,1... | collective-permute-start | bytes 6920 | tf_op jit(solution)/shard_map/ppermute | solution.py:57
  53.5 1.5 %collective-permute-start.9 = (f32[1,3,3,16,4]{3,4,1,2,0:T(4,128)S(1)}, f32[1,3,3,16,4]{3,4,1,2,0:T(4,128)S(1)}, u32[]{:S(2)}, u32[]{:S(2)}) collective-permute-start(f32[1,3,3,16,4]{3,4,1,2,0:T(4,128)S(1)} %fusion.11), channel_id=1, source_target_pairs={{0,3},{1,0},{2,1},{3,2},{4,7},{5,4},{6,5},{7,6},{8,11},{9,8},{10,9... | collective-permute-start | bytes 6920 | tf_op jit(solution)/shard_map/ppermute | solution.py:58
  55.0 0.1 eq.15
  55.1 0.8 collective-permute-done.8
  55.9 0.8 copy.482
  56.7 0.8 copy.487
  57.4 4.2 %shard_map.125 = (f32[27,4,16,128]{3,2,1,0:T(8,128)}, f32[4,16,128]{2,1,0:T(8,128)}) custom-call(f32[27,4,16,128]{3,2,1,0:T(8,128)} %get-tuple-element.6.refs_0_.an_ref, f32[27,4,16,128]{3,2,1,0:T(8,128)} %f_ref.1, f32[9,16,128]{2,1,0:T(8,128)} %bitcast.387, f32[9,16,128]{2,1,0:T(8,128)} %bitcast.390, f32[9,4,128]{2,1,0:T(4,128)} %bitcast.427, ...), custom_call_target="tpu_custom_call" | custom-call | tf_op jit(solution)/shard_map/pallas_call | solution.py:266
  61.7 0.8 add_multiply_fusion
  62.4 0.1 reshape.172
  62.5 0.1 reduce_sum.106
  62.8 0.1 select_reduce_fusion
  63.0 22.1 %all_to_all.9 = f32[128,1,8]{2,1,0:T(1,128)S(1)} all-to-all(f32[128,1,8]{2,1,0:T(1,128)S(1)} %bitcast.403), channel_id=1, replica_groups=mesh['gx'=16,'gy'=2,'gz'=4] {'gx','gy','gz'}, dimensions={0} | all-to-all | bytes 8192 | tf_op jit(solution)/shard_map/all_to_all | solution.py:300
  85.0 0.7 reduce_sum.109
  (195 shorter events, 4.2 us)
Async XLA Ops:
  0.6 3.5 %copy-start = (f32[27,4,16,128]{3,2,1,0:T(8,128)S(1)}, f32[27,4,16,128]{3,2,1,0:T(8,128)}, u32[]{:S(2)}) copy-start(f32[27,4,16,128]{3,2,1,0:T(8,128)} %f_ref.1) | copy-start | bytes 2654212
  0.6 3.5 %copy-start.13 = (s32[1024]{0:T(1024)S(1)}, s32[1024]{0:T(1024)}, u32[]{:S(2)}) copy-start(s32[1024]{0:T(1024)} %param.17) | copy-start | bytes 12292
  0.7 3.6 %copy-start.14 = (f32[1024]{0:T(1024)S(1)}, f32[1024]{0:T(1024)}, u32[]{:S(2)}) copy-start(f32[1024]{0:T(1024)} %param.16) | copy-start | bytes 12292
  0.7 5.7 %copy-start.2 = (f32[27,4,16,128]{3,2,1,0:T(8,128)S(1)}, f32[27,4,16,128]{3,2,1,0:T(8,128)}, u32[]{:S(2)}) copy-start(f32[27,4,16,128]{3,2,1,0:T(8,128)} %ae_ref.1) | copy-start | bytes 2654212
  4.1 2.4 %copy-start.11 = (s32[4,16,128]{2,1,0:T(8,128)S(1)}, s32[4,16,128]{2,1,0:T(8,128)}, u32[]{:S(2)}) copy-start(s32[4,16,128]{2,1,0:T(8,128)} %param.14) | copy-start | bytes 98308
  4.2 2.3 %copy-start.9 = (f32[4,16,128]{2,1,0:T(8,128)S(1)}, f32[4,16,128]{2,1,0:T(8,128)}, u32[]{:S(2)}) copy-start(f32[4,16,128]{2,1,0:T(8,128)} %refs_6_.3) | copy-start | bytes 98308
  4.2 2.3 %copy-start.15 = (f32[27]{0:T(128)S(1)}, f32[27]{0:T(128)}, u32[]{:S(2)}) copy-start(f32[27]{0:T(128)} %constant.26.clone) | copy-start | bytes 328
  4.2 2.3 %copy-start.16 = (f32[27]{0:T(128)S(1)}, f32[27]{0:T(128)}, u32[]{:S(2)}) copy-start(f32[27]{0:T(128)} %constant.25.clone) | copy-start | bytes 328
  4.2 2.3 %copy-start.17 = (f32[27]{0:T(128)S(1)}, f32[27]{0:T(128)}, u32[]{:S(2)}) copy-start(f32[27]{0:T(128)} %constant.24.clone) | copy-start | bytes 328
  4.2 2.3 %copy-start.18 = (f32[27]{0:T(128)S(1)}, f32[27]{0:T(128)}, u32[]{:S(2)}) copy-start(f32[27]{0:T(128)} %constant.27.clone) | copy-start | bytes 328
  6.5 1.5 %copy-start.8 = (f32[4,16,128]{2,1,0:T(8,128)}, f32[4,16,128]{2,1,0:T(8,128)S(1)}, u32[]{:S(2)}) copy-start(f32[4,16,128]{2,1,0:T(8,128)S(1)} %get-tuple-element.144.refs_7_) | copy-start | bytes 98308
  8.0 3.4 %copy-start.1 = (f32[27,4,16,128]{3,2,1,0:T(8,128)}, f32[27,4,16,128]{3,2,1,0:T(8,128)S(1)}, u32[]{:S(2)}) copy-start(f32[27,4,16,128]{3,2,1,0:T(8,128)S(1)} %fusion.7.refs_0_.cf_ref) | copy-start | bytes 2654212
  8.1 9.3 %collective-permute-start = (f32[2,3,3,1,16,128]{5,4,2,1,3,0:T(8,128)S(1)}, f32[2,3,3,1,16,128]{5,4,2,1,3,0:T(8,128)S(1)}, u32[]{:S(2)}, u32[]{:S(2)}) collective-permute-start(f32[2,3,3,1,16,128]{5,4,2,1,3,0:T(8,128)S(1)} %pad_maximum_fusion), channel_id=1, source_target_pairs={{0,8},{8,16},{16,24},{24,32},{32,40},{40,48},{48,56},{56,64},{64,7... | collective-permute-start | bytes 442376 | tf_op jit(solution)/shard_map/ppermute | solution.py:57
  11.2 4.3 %copy-start.3 = (f32[27,4,16,128]{3,2,1,0:T(8,128)S(1)}, f32[27,4,16,128]{3,2,1,0:T(8,128)}, u32[]{:S(2)}) copy-start(f32[27,4,16,128]{3,2,1,0:T(8,128)} %ae_ref.1) | copy-start | bytes 2654212
  11.2 5.9 %collective-permute-start.1 = (f32[2,3,3,1,16,128]{5,4,2,1,3,0:T(8,128)S(1)}, f32[2,3,3,1,16,128]{5,4,2,1,3,0:T(8,128)S(1)}, u32[]{:S(2)}, u32[]{:S(2)}) collective-permute-start(f32[2,3,3,1,16,128]{5,4,2,1,3,0:T(8,128)S(1)} %pad_maximum_fusion.1), channel_id=1, source_target_pairs={{0,120},{8,0},{16,8},{24,16},{32,24},{40,32},{48,40},{56,48},{64,5... | collective-permute-start | bytes 442376 | tf_op jit(solution)/shard_map/ppermute | solution.py:58
  15.5 0.8 copy-start.10
  17.1 5.3 %copy-start.7 = (f32[2,3,3,1,16,128]{5,4,2,1,3,0:T(8,128)}, f32[2,3,3,1,16,128]{5,4,2,1,3,0:T(8,128)S(1)}, u32[]{:S(2)}) copy-start(f32[2,3,3,1,16,128]{5,4,2,1,3,0:T(8,128)S(1)} %collective-permute-done.1) | copy-start | bytes 442372
  17.4 6.5 %copy-start.6 = (f32[2,3,3,1,16,128]{5,4,2,1,3,0:T(8,128)}, f32[2,3,3,1,16,128]{5,4,2,1,3,0:T(8,128)S(1)}, u32[]{:S(2)}) copy-start(f32[2,3,3,1,16,128]{5,4,2,1,3,0:T(8,128)S(1)} %collective-permute-done) | copy-start | bytes 442372
  18.3 5.4 %collective-permute-start.2 = (f32[2,2,3,3,4,1,128]{6,4,3,2,5,1,0:T(4,128)S(1)}, f32[2,2,3,3,4,1,128]{6,4,3,2,5,1,0:T(4,128)S(1)}, u32[]{:S(2)}, u32[]{:S(2)}) collective-permute-start(f32[2,2,3,3,4,1,128]{6,4,3,2,5,1,0:T(4,128)S(1)} %pad_maximum_fusion.3), channel_id=1, source_target_pairs={{0,4},{4,0},{1,5},{5,1},{2,6},{6,2},{3,7},{7,3},{8,12},{12,8},{9,1... | collective-permute-start | bytes 221192 | tf_op jit(solution)/shard_map/ppermute | solution.py:55
  24.9 4.1 %collective-permute-start.3 = (f32[2,3,3,16,4]{3,4,1,2,0:T(4,128)S(1)}, f32[2,3,3,16,4]{3,4,1,2,0:T(4,128)S(1)}, u32[]{:S(2)}, u32[]{:S(2)}) collective-permute-start(f32[2,3,3,16,4]{3,4,1,2,0:T(4,128)S(1)} %pad_maximum_fusion.10), channel_id=1, source_target_pairs={{0,1},{1,2},{2,3},{3,0},{4,5},{5,6},{6,7},{7,4},{8,9},{9,10},{10,1... | collective-permute-start | bytes 13832 | tf_op jit(solution)/shard_map/ppermute | solution.py:57
  26.9 3.0 %collective-permute-start.4 = (f32[2,3,3,16,4]{3,4,1,2,0:T(4,128)S(1)}, f32[2,3,3,16,4]{3,4,1,2,0:T(4,128)S(1)}, u32[]{:S(2)}, u32[]{:S(2)}) collective-permute-start(f32[2,3,3,16,4]{3,4,1,2,0:T(4,128)S(1)} %pad_maximum_fusion.11), channel_id=1, source_target_pairs={{0,3},{1,0},{2,1},{3,2},{4,7},{5,4},{6,5},{7,6},{8,11},{9,8},{10,9... | collective-permute-start | bytes 13832 | tf_op jit(solution)/shard_map/ppermute | solution.py:58
  38.8 7.2 %collective-permute-start.5 = (f32[1,3,3,1,16,128]{5,4,2,1,3,0:T(8,128)S(1)}, f32[1,3,3,1,16,128]{5,4,2,1,3,0:T(8,128)S(1)}, u32[]{:S(2)}, u32[]{:S(2)}) collective-permute-start(f32[1,3,3,1,16,128]{5,4,2,1,3,0:T(8,128)S(1)} %slice_bitcast_fusion.1), channel_id=1, source_target_pairs={{0,8},{8,16},{16,24},{24,32},{32,40},{40,48},{48,56},{56,64},{64,7... | collective-permute-start | bytes 221192 | tf_op jit(solution)/shard_map/ppermute | solution.py:57
  42.0 3.8 %collective-permute-start.6 = (f32[1,3,3,1,16,128]{5,4,2,1,3,0:T(8,128)S(1)}, f32[1,3,3,1,16,128]{5,4,2,1,3,0:T(8,128)S(1)}, u32[]{:S(2)}, u32[]{:S(2)}) collective-permute-start(f32[1,3,3,1,16,128]{5,4,2,1,3,0:T(8,128)S(1)} %slice_bitcast_fusion), channel_id=1, source_target_pairs={{0,120},{8,0},{16,8},{24,16},{32,24},{40,32},{48,40},{56,48},{64,5... | collective-permute-start | bytes 221192 | tf_op jit(solution)/shard_map/ppermute | solution.py:58
  45.8 11.7 %copy-start.5 = (f32[1,3,3,1,16,128]{5,4,2,1,3,0:T(8,128)}, f32[1,3,3,1,16,128]{5,4,2,1,3,0:T(8,128)S(1)}, u32[]{:S(2)}) copy-start(f32[1,3,3,1,16,128]{5,4,2,1,3,0:T(8,128)S(1)} %collective-permute-done.6) | copy-start | bytes 221188
  46.0 11.4 %copy-start.4 = (f32[1,3,3,1,16,128]{5,4,2,1,3,0:T(8,128)}, f32[1,3,3,1,16,128]{5,4,2,1,3,0:T(8,128)S(1)}, u32[]{:S(2)}) copy-start(f32[1,3,3,1,16,128]{5,4,2,1,3,0:T(8,128)S(1)} %collective-permute-done.5) | copy-start | bytes 221188
  46.3 4.7 %collective-permute-start.7 = (f32[2,1,3,3,4,1,128]{6,4,3,2,5,1,0:T(4,128)S(1)}, f32[2,1,3,3,4,1,128]{6,4,3,2,5,1,0:T(4,128)S(1)}, u32[]{:S(2)}, u32[]{:S(2)}) collective-permute-start(f32[2,1,3,3,4,1,128]{6,4,3,2,5,1,0:T(4,128)S(1)} %pad_maximum_fusion.12), channel_id=1, source_target_pairs={{0,4},{4,0},{1,5},{5,1},{2,6},{6,2},{3,7},{7,3},{8,12},{12,8},{9,1... | collective-permute-start | bytes 110600 | tf_op jit(solution)/shard_map/ppermute | solution.py:55
  49.8 11.9 %copy-start.12 = (f32[4,16,128]{2,1,0:T(8,128)S(1)}, f32[4,16,128]{2,1,0:T(8,128)}, u32[]{:S(2)}) copy-start(f32[4,16,128]{2,1,0:T(8,128)} %get-tuple-element.8) | copy-start | bytes 98308
  52.0 3.9 %collective-permute-start.8 = (f32[1,3,3,16,4]{3,4,1,2,0:T(4,128)S(1)}, f32[1,3,3,16,4]{3,4,1,2,0:T(4,128)S(1)}, u32[]{:S(2)}, u32[]{:S(2)}) collective-permute-start(f32[1,3,3,16,4]{3,4,1,2,0:T(4,128)S(1)} %fusion.12), channel_id=1, source_target_pairs={{0,1},{1,2},{2,3},{3,0},{4,5},{5,6},{6,7},{7,4},{8,9},{9,10},{10,1... | collective-permute-start | bytes 6920 | tf_op jit(solution)/shard_map/ppermute | solution.py:57
  53.5 3.2 %collective-permute-start.9 = (f32[1,3,3,16,4]{3,4,1,2,0:T(4,128)S(1)}, f32[1,3,3,16,4]{3,4,1,2,0:T(4,128)S(1)}, u32[]{:S(2)}, u32[]{:S(2)}) collective-permute-start(f32[1,3,3,16,4]{3,4,1,2,0:T(4,128)S(1)} %fusion.11), channel_id=1, source_target_pairs={{0,3},{1,0},{2,1},{3,2},{4,7},{5,4},{6,5},{7,6},{8,11},{9,8},{10,9... | collective-permute-start | bytes 6920 | tf_op jit(solution)/shard_map/ppermute | solution.py:58

commit v15 on v13

--- a/solution.py
+++ b/solution.py
@@ -254,9 +254,25 @@
 
 def now_kernel(an_ref, f_ref, *refs):
     hal = refs[0:6]
-    rate_ref, gamma_ref, out_ref, sens_ref, as_ = refs[6:]
-    move_into(as_, an_ref, hal, -1, 0)
-    chunked_adjoint(f_ref, as_, rate_ref, gamma_ref, out_ref, sens_ref)
+    rate_ref, gamma_ref, moved_ref, sens_ref = refs[6:]
+    move_into(moved_ref, an_ref, hal, -1, 0)
+    _, sx, sy, sz = f_ref.shape
+    halves = sy // 8
+
+    def body(step, carry):
+        i = step // halves
+        h = pl.multiple_of((step % halves) * 8, 8)
+        F = [f_ref[q, i, pl.ds(h, 8), :] for q in range(27)]
+        A = [moved_ref[q, i, pl.ds(h, 8), :] for q in range(27)]
+        _, sens = adjoint_rows(F, A, rate_ref[i, pl.ds(h, 8), :], gamma_ref[i, pl.ds(h, 8), :])
+        sens_ref[i, pl.ds(h, 8), :] = sens
+        return carry
+
+    lax.fori_loop(0, sx * halves, body, 0)
+
+
+def start_kernel(f_ref, moved_ref, rate_ref, gamma_ref, out_ref, sens_ref):
+    chunked_adjoint(f_ref, moved_ref, rate_ref, gamma_ref, out_ref, sens_ref)
 
 
 def run_stage(kernel, args, shape, scratch):
@@ -286,7 +302,8 @@
         next_kernel, (post_now, adjoint_end) + hal + (relax_rate, gamma), shape, 2
     )
     hal_n = halos([adj_next], [-1])
-    adjoint_start, sens_now = run_stage(now_kernel, (adj_next, check_pops) + hal_n + (relax_rate, gamma), shape, 1)
+    post_adj, sens_now = run_stage(now_kernel, (adj_next, check_pops) + hal_n + (relax_rate, gamma), shape, 0)
+    adjoint_start, _ = run_stage(start_kernel, (check_pops, post_adj, relax_rate, gamma), shape, 0)
     density = walls * (sens_next + sens_now)
     boxes = density.reshape(sx, 2, sy // 2, 2, sz // 2).sum(axis=(2, 4))
     parts = jnp.stack([boxes[0], boxes[1 : sx - 1].sum(axis=0), boxes[sx - 1]])

time: 85.1 us -> 85.5 us (level)
  blocking collectives: 21.4 us -> 0 us
  starting transfers between devices: 20.2 us -> 31.9 us
  waiting for transfers between devices: 3.73 us -> 9.87 us
  Pallas kernels: 11.7 us -> 14.9 us
    all_to_all x1 -> x0, blocking collectives: 21.4 us -> none  [shards(): lax.all_to_all(placed.reshape(devices, count // devices), ('gx', 'gy', 'g...]
    all_to_all x0 -> x1, starting transfers between devices: none -> 11.7 us  [shards(): lax.all_to_all(placed.reshape(devices, count // devices), ('gx', 'gy', 'g...]
    all_to_all x0 -> x1, waiting for transfers between devices: none -> 6.13 us  [shards(): lax.all_to_all(placed.reshape(devices, count // devices), ('gx', 'gy', 'g...]
    pallas_call x2 -> x3, Pallas kernels: 9.08 us -> 12.3 us  [run_stage(): pl.pallas_call(kernel, out_shape=(jax.ShapeDtypeStruct(shape, jnp.float32...]
  transfers between devices with their start and end apart: 10 -> 11, of which waited for: 5 -> 6; matrix products, arithmetic and copies ran while one was open for 11% -> 11% of each run, Pallas kernels for 3% -> 7%
where the time goes in v15:
time: 85.5 us; the launch traced here: 84.9 us
  starting transfers between devices  31.9 us (37%)
  local copies, waits for them, and re-layouts  17.9 us (21%)
  Pallas kernels  14.9 us (17%)
  waiting for transfers between devices  9.87 us (12%)
  other arithmetic  8.4 us (10%)
  between operations  1.86 us (2%)
    pallas_call x3, Pallas kernels, run_stage(): pl.pallas_call(kernel, out_shape=(jax.ShapeDtypeStruct(shape, jnp.float32...  12.3 us
    all_to_all x1, starting transfers between devices, shards(): lax.all_to_all(placed.reshape(devices, count // devices), ('gx', 'gy', 'g...  11.7 us
    ppermute x4, starting transfers between devices, halo_exchange(): lo = lax.ppermute(up, axis, [(i, (i + 1) % size) for i in range(size)])  8.93 us
    ppermute x2, starting transfers between devices, halo_exchange(): both = lax.ppermute(jnp.stack([up, down]), axis, [(0, 1), (1, 0)])  7.07 us
    all_to_all x1, waiting for transfers between devices, shards(): lax.all_to_all(placed.reshape(devices, count // devices), ('gx', 'gy', 'g...  6.13 us
    ppermute x4, starting transfers between devices, halo_exchange(): hi = lax.ppermute(down, axis, [(i, (i - 1) % size) for i in range(size)])  4.19 us
    unnamed x47, local copies, waits for them, and re-layouts  3.59 us
    pallas_call x1, Pallas kernels, halos(): pl.pallas_call(columns_kernel, out_shape=jax.ShapeDtypeStruct((2, 2 * 27...  2.64 us
  transfers between devices with their start and end apart: 11, of which 6 were waited for; matrix products, arithmetic and copies ran while one was open for 11% of the time, Pallas kernels for 7%

profile of v15, /device:TPU:1, one launch (start us, length us, event | category | flops | bytes accessed | tf_op | source)
XLA Modules:
  0.0 84.9 jit_solution(486530158285898883)
XLA Ops:
  0.7 1.2 %slice_reduce_fusion.4 = (f32[4,16,128]{2,1,0:T(8,128)S(1)}, f32[4,16,128]{2,1,0:T(8,128)S(1)}) fusion(f32[27,4,16,128]{3,2,1,0:T(8,128)} %f_ref.3), kind=kLoop, calls=%fused_computation.16 | loop fusion | flops 131072 | bytes 655360 | tf_op jit(solution)/shard_map/reduce_sum | solution.py:32
  1.9 1.1 %slice_reduce_fusion.2 = (f32[4,16,128]{2,1,0:T(8,128)S(1)}, f32[4,16,128]{2,1,0:T(8,128)S(1)}) fusion(f32[3,3,3,4,16,128]{5,4,3,2,1,0:T(8,128)} %bitcast.410), kind=kLoop, calls=%fused_computation.14 | loop fusion | flops 131072 | bytes 655360 | tf_op jit(solution)/shard_map/reduce_sum | solution.py:33
  3.0 1.1 %slice_reduce_fusion = (f32[4,16,128]{2,1,0:T(8,128)S(1)}, f32[4,16,128]{2,1,0:T(8,128)S(1)}) fusion(f32[3,3,3,4,16,128]{5,4,3,2,1,0:T(8,128)} %bitcast.411), kind=kLoop, calls=%fused_computation.12 | loop fusion | flops 131072 | bytes 655360 | tf_op jit(solution)/shard_map/reduce_sum | solution.py:34
  4.3 0.2 copy.472
  4.5 0.8 slice.654
  5.5 0.6 gather_fusion
  6.0 0.1 copy.555
  6.3 0.1 reshape.146
  6.6 1.4 %fusion.7.a_ref.cf_ref = f32[27,4,16,128]{3,2,1,0:T(8,128)S(1)} fusion(f32[27,4,16,128]{3,2,1,0:T(8,128)S(1)} %copy-done, f32[4,16,128]{2,1,0:T(8,128)S(1)} %get-tuple-element.148.refs_7_.gamma_ref, f32[4,16,128]{2,1,0:T(8,128)S(1)} %get-tuple-element.32, f32[4,16,128]{2,1,0:T(8,128)S(1)} %get-tuple-element.35, f32[27]{0:T(128)S(1)} %copy-done.16, ...), kind=kLoop, calls=%fused_computation.9 | loop fusion | flops 4202496 | bytes 2032048 | tf_op jit(solution)/shard_map/add | solution.py:47
  8.1 3.1 %collective-permute-start = (f32[2,3,3,1,16,128]{5,4,2,1,3,0:T(8,128)S(1)}, f32[2,3,3,1,16,128]{5,4,2,1,3,0:T(8,128)S(1)}, u32[]{:S(2)}, u32[]{:S(2)}) collective-permute-start(f32[2,3,3,1,16,128]{5,4,2,1,3,0:T(8,128)S(1)} %pad_maximum_fusion), channel_id=1, source_target_pairs={{0,8},{8,16},{16,24},{24,32},{32,40},{40,48},{48,56},{56,64},{64,7... | collective-permute-start | bytes 442376 | tf_op jit(solution)/shard_map/ppermute | solution.py:57
  11.3 2.6 %shard_map.122 = f32[2,27,128]{2,1,0:T(8,128)} custom-call(f32[27,4,16,128]{3,2,1,0:T(8,128)} %copy-done.1, f32[27,4,16,128]{3,2,1,0:T(8,128)} %ae_ref.1), custom_call_target="tpu_custom_call" | custom-call | tf_op jit(solution)/shard_map/pallas_call | solution.py:101
  14.0 1.5 %copy_dynamic-update-slice_fusion.1 = f32[2,3,3,3,4,16,128]{6,4,3,2,5,1,0:T(4,128)S(1)} fusion(f32[1,3,3,3,4,16,128]{6,5,4,3,2,1,0:T(8,128)} %bitcast.412), kind=kLoop, calls=%fused_computation.11 | loop fusion | bytes 1769472
  15.5 0.4 copy_dynamic-update-slice_fusion
  16.1 0.1 copy-done.11
  16.2 0.2 reshape.150
  16.6 0.1 copy.570
  16.7 0.1 copy.569
  16.9 0.3 collective-permute-done.1
  17.2 0.2 slice_reduce_fusion.6
  17.4 0.2 slice_reduce_fusion.7
  17.6 0.2 slice_reduce_fusion.8
  17.8 0.2 slice_reduce_fusion.9
  18.3 3.7 %collective-permute-start.2 = (f32[2,2,3,3,4,1,128]{6,4,3,2,5,1,0:T(4,128)S(1)}, f32[2,2,3,3,4,1,128]{6,4,3,2,5,1,0:T(4,128)S(1)}, u32[]{:S(2)}, u32[]{:S(2)}) collective-permute-start(f32[2,2,3,3,4,1,128]{6,4,3,2,5,1,0:T(4,128)S(1)} %pad_maximum_fusion.3), channel_id=1, source_target_pairs={{0,4},{4,0},{1,5},{5,1},{2,6},{6,2},{3,7},{7,3},{8,12},{12,8},{9,1... | collective-permute-start | bytes 221192 | tf_op jit(solution)/shard_map/ppermute | solution.py:55
  22.7 1.0 %collective-permute-done.2 = f32[2,2,3,3,4,1,128]{6,4,3,2,5,1,0:T(4,128)S(1)} collective-permute-done((f32[2,2,3,3,4,1,128]{6,4,3,2,5,1,0:T(4,128)S(1)}, f32[2,2,3,3,4,1,128]{6,4,3,2,5,1,0:T(4,128)S(1)}, u32[]{:S(2)}, u32[]{:S(2)}) %collective-permute-start.2) | collective-permute-done | bytes 73760 | tf_op jit(solution)/shard_map/ppermute | solution.py:55
  23.9 0.2 slice_reduce_fusion.14
  24.1 0.1 copy.497
  24.2 0.2 slice_reduce_fusion.15
  24.4 0.1 copy.496
  24.9 1.3 %collective-permute-start.3 = (f32[2,3,3,16,4]{3,4,1,2,0:T(4,128)S(1)}, f32[2,3,3,16,4]{3,4,1,2,0:T(4,128)S(1)}, u32[]{:S(2)}, u32[]{:S(2)}) collective-permute-start(f32[2,3,3,16,4]{3,4,1,2,0:T(4,128)S(1)} %pad_maximum_fusion.10), channel_id=1, source_target_pairs={{0,1},{1,2},{2,3},{3,0},{4,5},{5,6},{6,7},{7,4},{8,9},{9,10},{10,1... | collective-permute-start | bytes 13832 | tf_op jit(solution)/shard_map/ppermute | solution.py:57
  26.2 0.1 copy.506
  26.4 0.1 copy.505
  26.9 1.5 %collective-permute-start.4 = (f32[2,3,3,16,4]{3,4,1,2,0:T(4,128)S(1)}, f32[2,3,3,16,4]{3,4,1,2,0:T(4,128)S(1)}, u32[]{:S(2)}, u32[]{:S(2)}) collective-permute-start(f32[2,3,3,16,4]{3,4,1,2,0:T(4,128)S(1)} %pad_maximum_fusion.11), channel_id=1, source_target_pairs={{0,3},{1,0},{2,1},{3,2},{4,7},{5,4},{6,5},{7,6},{8,11},{9,8},{10,9... | collective-permute-start | bytes 13832 | tf_op jit(solution)/shard_map/ppermute | solution.py:58
  28.4 0.6 fusion.29
  29.1 0.8 copy.504
  29.9 0.8 copy.513
  30.7 4.8 %shard_map.123 = (f32[27,4,16,128]{3,2,1,0:T(8,128)}, f32[4,16,128]{2,1,0:T(8,128)}) custom-call(f32[27,4,16,128]{3,2,1,0:T(8,128)} %copy-done.1, f32[27,4,16,128]{3,2,1,0:T(8,128)} %ae_ref.1, f32[18,16,128]{2,1,0:T(8,128)} %bitcast.422, f32[18,16,128]{2,1,0:T(8,128)} %bitcast.423, f32[18,4,128]{2,1,0:T(4,128)} %bitcast.437, f32[18,4,128]{2,1,0:T(4,128)} %bitcast.436, ...), custom_call_target="tpu_custom_call" | custom-call | tf_op jit(solution)/shard_map/pallas_call | solution.py:280
  35.6 1.2 %fusion.24 = (f32[9,4,16,128]{3,2,1,0:T(8,128)S(1)}, f32[9,4,16,128]{3,2,1,0:T(8,128)S(1)}) fusion(f32[27,4,16,128]{3,2,1,0:T(8,128)} %get-tuple-element.7.an_ref), kind=kLoop, calls=%fused_computation.231 | loop fusion | bytes 1179648 | tf_op jit(solution)/shard_map/slice | solution.py:78
  36.8 1.2 %fusion.23 = (f32[1,3,3,3,4,1,128]{6,5,4,3,2,1,0:T(1,128)S(1)}, f32[1,3,3,3,4,1,128]{6,5,4,3,2,1,0:T(1,128)S(1)}) fusion(f32[1,3,3,3,4,16,128]{6,5,4,3,2,1,0:T(8,128)} %bitcast.413), kind=kLoop, calls=%fused_computation.230 | loop fusion | bytes 221184 | tf_op jit(solution)/shard_map/slice | solution.py:99
  38.0 0.3 fusion.22
  38.4 3.3 %collective-permute-start.5 = (f32[1,3,3,1,16,128]{5,4,2,1,3,0:T(8,128)S(1)}, f32[1,3,3,1,16,128]{5,4,2,1,3,0:T(8,128)S(1)}, u32[]{:S(2)}, u32[]{:S(2)}) collective-permute-start(f32[1,3,3,1,16,128]{5,4,2,1,3,0:T(8,128)S(1)} %slice_bitcast_fusion.1), channel_id=1, source_target_pairs={{0,8},{8,16},{16,24},{24,32},{32,40},{40,48},{48,56},{56,64},{64,7... | collective-permute-start | bytes 221192 | tf_op jit(solution)/shard_map/ppermute | solution.py:57
  41.7 1.0 %collective-permute-start.6 = (f32[1,3,3,1,16,128]{5,4,2,1,3,0:T(8,128)S(1)}, f32[1,3,3,1,16,128]{5,4,2,1,3,0:T(8,128)S(1)}, u32[]{:S(2)}, u32[]{:S(2)}) collective-permute-start(f32[1,3,3,1,16,128]{5,4,2,1,3,0:T(8,128)S(1)} %slice_bitcast_fusion), channel_id=1, source_target_pairs={{0,120},{8,0},{16,8},{24,16},{32,24},{40,32},{48,40},{56,48},{64,5... | collective-permute-start | bytes 221192 | tf_op jit(solution)/shard_map/ppermute | solution.py:58
  42.7 0.7 copy.567
  43.4 0.7 copy.566
  44.3 1.1 %collective-permute-done.6 = f32[1,3,3,1,16,128]{5,4,2,1,3,0:T(8,128)S(1)} collective-permute-done((f32[1,3,3,1,16,128]{5,4,2,1,3,0:T(8,128)S(1)}, f32[1,3,3,1,16,128]{5,4,2,1,3,0:T(8,128)S(1)}, u32[]{:S(2)}, u32[]{:S(2)}) %collective-permute-start.6) | collective-permute-done | bytes 73760 | tf_op jit(solution)/shard_map/ppermute | solution.py:58
  45.8 3.4 %collective-permute-start.7 = (f32[2,1,3,3,4,1,128]{6,4,3,2,5,1,0:T(4,128)S(1)}, f32[2,1,3,3,4,1,128]{6,4,3,2,5,1,0:T(4,128)S(1)}, u32[]{:S(2)}, u32[]{:S(2)}) collective-permute-start(f32[2,1,3,3,4,1,128]{6,4,3,2,5,1,0:T(4,128)S(1)} %pad_maximum_fusion.12), channel_id=1, source_target_pairs={{0,4},{4,0},{1,5},{5,1},{2,6},{6,2},{3,7},{7,3},{8,12},{12,8},{9,1... | collective-permute-start | bytes 110600 | tf_op jit(solution)/shard_map/ppermute | solution.py:55
  49.2 0.1 copy.529
  49.3 0.1 copy.526
  49.6 0.1 copy.542
  49.7 0.1 copy.539
  50.0 0.6 collective-permute-done.7
  50.6 0.6 slice_bitcast_fusion.92
  51.6 1.3 %collective-permute-start.8 = (f32[1,3,3,16,4]{3,4,2,1,0:T(4,128)S(1)}, f32[1,3,3,16,4]{3,4,2,1,0:T(4,128)S(1)}, u32[]{:S(2)}, u32[]{:S(2)}) collective-permute-start(f32[1,3,3,16,4]{3,4,2,1,0:T(4,128)S(1)} %slice_bitcast_fusion.21), channel_id=1, source_target_pairs={{0,1},{1,2},{2,3},{3,0},{4,5},{5,6},{6,7},{7,4},{8,9},{9,10},{10,1... | collective-permute-start | bytes 6920 | tf_op jit(solution)/shard_map/ppermute | solution.py:57
  53.1 1.5 %collective-permute-start.9 = (f32[1,3,3,16,4]{3,4,2,1,0:T(4,128)S(1)}, f32[1,3,3,16,4]{3,4,2,1,0:T(4,128)S(1)}, u32[]{:S(2)}, u32[]{:S(2)}) collective-permute-start(f32[1,3,3,16,4]{3,4,2,1,0:T(4,128)S(1)} %slice_bitcast_fusion.10), channel_id=1, source_target_pairs={{0,3},{1,0},{2,1},{3,2},{4,7},{5,4},{6,5},{7,6},{8,11},{9,8},{10,9... | collective-permute-start | bytes 6920 | tf_op jit(solution)/shard_map/ppermute | solution.py:58
  54.7 0.8 collective-permute-done.8
  55.5 0.8 copy.538
  56.2 0.8 copy.551
  57.0 3.8 %shard_map.124 = (f32[27,4,16,128]{3,2,1,0:T(8,128)}, f32[4,16,128]{2,1,0:T(8,128)}) custom-call(f32[27,4,16,128]{3,2,1,0:T(8,128)} %get-tuple-element.7.an_ref, f32[27,4,16,128]{3,2,1,0:T(8,128)} %f_ref.3, f32[9,16,128]{2,1,0:T(8,128)} %bitcast.418, f32[9,16,128]{2,1,0:T(8,128)} %bitcast.421, f32[9,4,128]{2,1,0:T(4,128)} %bitcast.453, ...), custom_call_target="tpu_custom_call" | custom-call | tf_op jit(solution)/shard_map/pallas_call | solution.py:280
  60.8 0.8 add_multiply_fusion
  61.6 0.1 reduce_sum.106
  62.0 0.7 all_to_all.6
  62.7 11.7 %all-to-all-start = ((f32[128,1,8]{2,1,0:T(1,128)}), f32[128,1,8]{2,1,0:T(1,128)S(1)}, u32[]{:S(2)}, u32[]{:S(2)}) async-start(f32[128,1,8]{2,1,0:T(1,128)} %bitcast.204), calls=%async_computation | async-start | bytes 131072 | tf_op jit(solution)/shard_map/all_to_all | solution.py:315
  74.4 3.7 %shard_map.125 = (f32[27,4,16,128]{3,2,1,0:T(8,128)}, f32[4,16,128]{2,1,0:T(8,128)}) custom-call(f32[27,4,16,128]{3,2,1,0:T(8,128)} %f_ref.3, f32[27,4,16,128]{3,2,1,0:T(8,128)} %get-tuple-element.8.moved_ref, f32[4,16,128]{2,1,0:T(8,128)} %rate_ref.1, f32[4,16,128]{2,1,0:T(8,128)} %copy-done.5), custom_call_target="tpu_custom_call" | custom-call | tf_op jit(solution)/shard_map/pallas_call | solution.py:280
  78.1 6.1 %all-to-all-done = f32[128,1,8]{2,1,0:T(1,128)S(1)} async-done(((f32[128,1,8]{2,1,0:T(1,128)}), f32[128,1,8]{2,1,0:T(1,128)S(1)}, u32[]{:S(2)}, u32[]{:S(2)}) %all-to-all-start) | async-done | bytes 4128 | tf_op jit(solution)/shard_map/all_to_all | solution.py:315
  84.2 0.7 reduce_sum.109
  (201 shorter events, 4.4 us)
Async XLA Ops:
  0.6 3.5 %copy-start = (f32[27,4,16,128]{3,2,1,0:T(8,128)S(1)}, f32[27,4,16,128]{3,2,1,0:T(8,128)}, u32[]{:S(2)}) copy-start(f32[27,4,16,128]{3,2,1,0:T(8,128)} %f_ref.3) | copy-start | bytes 2654212
  0.6 3.5 %copy-start.14 = (s32[1024]{0:T(1024)S(1)}, s32[1024]{0:T(1024)}, u32[]{:S(2)}) copy-start(s32[1024]{0:T(1024)} %param.17) | copy-start | bytes 12292
  0.7 3.6 %copy-start.15 = (f32[1024]{0:T(1024)S(1)}, f32[1024]{0:T(1024)}, u32[]{:S(2)}) copy-start(f32[1024]{0:T(1024)} %param.16) | copy-start | bytes 12292
  0.7 5.7 %copy-start.3 = (f32[27,4,16,128]{3,2,1,0:T(8,128)S(1)}, f32[27,4,16,128]{3,2,1,0:T(8,128)}, u32[]{:S(2)}) copy-start(f32[27,4,16,128]{3,2,1,0:T(8,128)} %ae_ref.1) | copy-start | bytes 2654212
  4.1 2.4 %copy-start.12 = (s32[4,16,128]{2,1,0:T(8,128)S(1)}, s32[4,16,128]{2,1,0:T(8,128)}, u32[]{:S(2)}) copy-start(s32[4,16,128]{2,1,0:T(8,128)} %param.14) | copy-start | bytes 98308
  4.2 2.3 %copy-start.10 = (f32[4,16,128]{2,1,0:T(8,128)S(1)}, f32[4,16,128]{2,1,0:T(8,128)}, u32[]{:S(2)}) copy-start(f32[4,16,128]{2,1,0:T(8,128)} %rate_ref.1) | copy-start | bytes 98308
  4.2 2.3 %copy-start.16 = (f32[27]{0:T(128)S(1)}, f32[27]{0:T(128)}, u32[]{:S(2)}) copy-start(f32[27]{0:T(128)} %constant.26.clone) | copy-start | bytes 328
  4.2 2.3 %copy-start.17 = (f32[27]{0:T(128)S(1)}, f32[27]{0:T(128)}, u32[]{:S(2)}) copy-start(f32[27]{0:T(128)} %constant.25.clone) | copy-start | bytes 328
  4.2 2.3 %copy-start.18 = (f32[27]{0:T(128)S(1)}, f32[27]{0:T(128)}, u32[]{:S(2)}) copy-start(f32[27]{0:T(128)} %constant.24.clone) | copy-start | bytes 328
  4.2 2.3 %copy-start.19 = (f32[27]{0:T(128)S(1)}, f32[27]{0:T(128)}, u32[]{:S(2)}) copy-start(f32[27]{0:T(128)} %constant.27.clone) | copy-start | bytes 328
  6.5 1.5 %copy-start.5 = (f32[4,16,128]{2,1,0:T(8,128)}, f32[4,16,128]{2,1,0:T(8,128)S(1)}, u32[]{:S(2)}) copy-start(f32[4,16,128]{2,1,0:T(8,128)S(1)} %get-tuple-element.148.refs_7_.gamma_ref) | copy-start | bytes 98308
  8.0 3.4 %copy-start.1 = (f32[27,4,16,128]{3,2,1,0:T(8,128)}, f32[27,4,16,128]{3,2,1,0:T(8,128)S(1)}, u32[]{:S(2)}) copy-start(f32[27,4,16,128]{3,2,1,0:T(8,128)S(1)} %fusion.7.a_ref.cf_ref) | copy-start | bytes 2654212
  8.1 9.3 %collective-permute-start = (f32[2,3,3,1,16,128]{5,4,2,1,3,0:T(8,128)S(1)}, f32[2,3,3,1,16,128]{5,4,2,1,3,0:T(8,128)S(1)}, u32[]{:S(2)}, u32[]{:S(2)}) collective-permute-start(f32[2,3,3,1,16,128]{5,4,2,1,3,0:T(8,128)S(1)} %pad_maximum_fusion), channel_id=1, source_target_pairs={{0,8},{8,16},{16,24},{24,32},{32,40},{40,48},{48,56},{56,64},{64,7... | collective-permute-start | bytes 442376 | tf_op jit(solution)/shard_map/ppermute | solution.py:57
  11.2 4.3 %copy-start.4 = (f32[27,4,16,128]{3,2,1,0:T(8,128)S(1)}, f32[27,4,16,128]{3,2,1,0:T(8,128)}, u32[]{:S(2)}) copy-start(f32[27,4,16,128]{3,2,1,0:T(8,128)} %ae_ref.1) | copy-start | bytes 2654212
  11.2 5.9 %collective-permute-start.1 = (f32[2,3,3,1,16,128]{5,4,2,1,3,0:T(8,128)S(1)}, f32[2,3,3,1,16,128]{5,4,2,1,3,0:T(8,128)S(1)}, u32[]{:S(2)}, u32[]{:S(2)}) collective-permute-start(f32[2,3,3,1,16,128]{5,4,2,1,3,0:T(8,128)S(1)} %pad_maximum_fusion.1), channel_id=1, source_target_pairs={{0,120},{8,0},{16,8},{24,16},{32,24},{40,32},{48,40},{56,48},{64,5... | collective-permute-start | bytes 442376 | tf_op jit(solution)/shard_map/ppermute | solution.py:58
  15.5 0.8 copy-start.11
  17.2 5.3 %copy-start.9 = (f32[2,3,3,1,16,128]{5,4,2,1,3,0:T(8,128)}, f32[2,3,3,1,16,128]{5,4,2,1,3,0:T(8,128)S(1)}, u32[]{:S(2)}) copy-start(f32[2,3,3,1,16,128]{5,4,2,1,3,0:T(8,128)S(1)} %collective-permute-done.1) | copy-start | bytes 442372
  17.4 6.5 %copy-start.8 = (f32[2,3,3,1,16,128]{5,4,2,1,3,0:T(8,128)}, f32[2,3,3,1,16,128]{5,4,2,1,3,0:T(8,128)S(1)}, u32[]{:S(2)}) copy-start(f32[2,3,3,1,16,128]{5,4,2,1,3,0:T(8,128)S(1)} %collective-permute-done) | copy-start | bytes 442372
  18.3 5.4 %collective-permute-start.2 = (f32[2,2,3,3,4,1,128]{6,4,3,2,5,1,0:T(4,128)S(1)}, f32[2,2,3,3,4,1,128]{6,4,3,2,5,1,0:T(4,128)S(1)}, u32[]{:S(2)}, u32[]{:S(2)}) collective-permute-start(f32[2,2,3,3,4,1,128]{6,4,3,2,5,1,0:T(4,128)S(1)} %pad_maximum_fusion.3), channel_id=1, source_target_pairs={{0,4},{4,0},{1,5},{5,1},{2,6},{6,2},{3,7},{7,3},{8,12},{12,8},{9,1... | collective-permute-start | bytes 221192 | tf_op jit(solution)/shard_map/ppermute | solution.py:55
  24.9 4.1 %collective-permute-start.3 = (f32[2,3,3,16,4]{3,4,1,2,0:T(4,128)S(1)}, f32[2,3,3,16,4]{3,4,1,2,0:T(4,128)S(1)}, u32[]{:S(2)}, u32[]{:S(2)}) collective-permute-start(f32[2,3,3,16,4]{3,4,1,2,0:T(4,128)S(1)} %pad_maximum_fusion.10), channel_id=1, source_target_pairs={{0,1},{1,2},{2,3},{3,0},{4,5},{5,6},{6,7},{7,4},{8,9},{9,10},{10,1... | collective-permute-start | bytes 13832 | tf_op jit(solution)/shard_map/ppermute | solution.py:57
  26.9 3.0 %collective-permute-start.4 = (f32[2,3,3,16,4]{3,4,1,2,0:T(4,128)S(1)}, f32[2,3,3,16,4]{3,4,1,2,0:T(4,128)S(1)}, u32[]{:S(2)}, u32[]{:S(2)}) collective-permute-start(f32[2,3,3,16,4]{3,4,1,2,0:T(4,128)S(1)} %pad_maximum_fusion.11), channel_id=1, source_target_pairs={{0,3},{1,0},{2,1},{3,2},{4,7},{5,4},{6,5},{7,6},{8,11},{9,8},{10,9... | collective-permute-start | bytes 13832 | tf_op jit(solution)/shard_map/ppermute | solution.py:58
  35.6 2.4 %copy-start.2 = (f32[27,4,16,128]{3,2,1,0:T(8,128)S(1)}, f32[27,4,16,128]{3,2,1,0:T(8,128)}, u32[]{:S(2)}) copy-start(f32[27,4,16,128]{3,2,1,0:T(8,128)} %get-tuple-element.7.an_ref) | copy-start | bytes 2654212
  38.4 7.2 %collective-permute-start.5 = (f32[1,3,3,1,16,128]{5,4,2,1,3,0:T(8,128)S(1)}, f32[1,3,3,1,16,128]{5,4,2,1,3,0:T(8,128)S(1)}, u32[]{:S(2)}, u32[]{:S(2)}) collective-permute-start(f32[1,3,3,1,16,128]{5,4,2,1,3,0:T(8,128)S(1)} %slice_bitcast_fusion.1), channel_id=1, source_target_pairs={{0,8},{8,16},{16,24},{24,32},{32,40},{40,48},{48,56},{56,64},{64,7... | collective-permute-start | bytes 221192 | tf_op jit(solution)/shard_map/ppermute | solution.py:57
  41.7 3.8 %collective-permute-start.6 = (f32[1,3,3,1,16,128]{5,4,2,1,3,0:T(8,128)S(1)}, f32[1,3,3,1,16,128]{5,4,2,1,3,0:T(8,128)S(1)}, u32[]{:S(2)}, u32[]{:S(2)}) collective-permute-start(f32[1,3,3,1,16,128]{5,4,2,1,3,0:T(8,128)S(1)} %slice_bitcast_fusion), channel_id=1, source_target_pairs={{0,120},{8,0},{16,8},{24,16},{32,24},{40,32},{48,40},{56,48},{64,5... | collective-permute-start | bytes 221192 | tf_op jit(solution)/shard_map/ppermute | solution.py:58
  45.4 11.6 %copy-start.7 = (f32[1,3,3,1,16,128]{5,4,2,1,3,0:T(8,128)}, f32[1,3,3,1,16,128]{5,4,2,1,3,0:T(8,128)S(1)}, u32[]{:S(2)}) copy-start(f32[1,3,3,1,16,128]{5,4,2,1,3,0:T(8,128)S(1)} %collective-permute-done.6) | copy-start | bytes 221188
  45.5 11.5 %copy-start.6 = (f32[1,3,3,1,16,128]{5,4,2,1,3,0:T(8,128)}, f32[1,3,3,1,16,128]{5,4,2,1,3,0:T(8,128)S(1)}, u32[]{:S(2)}) copy-start(f32[1,3,3,1,16,128]{5,4,2,1,3,0:T(8,128)S(1)} %collective-permute-done.5) | copy-start | bytes 221188
  45.8 4.8 %collective-permute-start.7 = (f32[2,1,3,3,4,1,128]{6,4,3,2,5,1,0:T(4,128)S(1)}, f32[2,1,3,3,4,1,128]{6,4,3,2,5,1,0:T(4,128)S(1)}, u32[]{:S(2)}, u32[]{:S(2)}) collective-permute-start(f32[2,1,3,3,4,1,128]{6,4,3,2,5,1,0:T(4,128)S(1)} %pad_maximum_fusion.12), channel_id=1, source_target_pairs={{0,4},{4,0},{1,5},{5,1},{2,6},{6,2},{3,7},{7,3},{8,12},{12,8},{9,1... | collective-permute-start | bytes 110600 | tf_op jit(solution)/shard_map/ppermute | solution.py:55
  49.8 10.9 %copy-start.13 = (f32[4,16,128]{2,1,0:T(8,128)S(1)}, f32[4,16,128]{2,1,0:T(8,128)}, u32[]{:S(2)}) copy-start(f32[4,16,128]{2,1,0:T(8,128)} %get-tuple-element.10) | copy-start | bytes 98308
  51.6 3.9 %collective-permute-start.8 = (f32[1,3,3,16,4]{3,4,2,1,0:T(4,128)S(1)}, f32[1,3,3,16,4]{3,4,2,1,0:T(4,128)S(1)}, u32[]{:S(2)}, u32[]{:S(2)}) collective-permute-start(f32[1,3,3,16,4]{3,4,2,1,0:T(4,128)S(1)} %slice_bitcast_fusion.21), channel_id=1, source_target_pairs={{0,1},{1,2},{2,3},{3,0},{4,5},{5,6},{6,7},{7,4},{8,9},{9,10},{10,1... | collective-permute-start | bytes 6920 | tf_op jit(solution)/shard_map/ppermute | solution.py:57
  53.1 3.2 %collective-permute-start.9 = (f32[1,3,3,16,4]{3,4,2,1,0:T(4,128)S(1)}, f32[1,3,3,16,4]{3,4,2,1,0:T(4,128)S(1)}, u32[]{:S(2)}, u32[]{:S(2)}) collective-permute-start(f32[1,3,3,16,4]{3,4,2,1,0:T(4,128)S(1)} %slice_bitcast_fusion.10), channel_id=1, source_target_pairs={{0,3},{1,0},{2,1},{3,2},{4,7},{5,4},{6,5},{7,6},{8,11},{9,8},{10,9... | collective-permute-start | bytes 6920 | tf_op jit(solution)/shard_map/ppermute | solution.py:58
  62.7 21.6 %all-to-all-start = ((f32[128,1,8]{2,1,0:T(1,128)}), f32[128,1,8]{2,1,0:T(1,128)S(1)}, u32[]{:S(2)}, u32[]{:S(2)}) async-start(f32[128,1,8]{2,1,0:T(1,128)} %bitcast.204), calls=%async_computation | async-start | bytes 131072 | tf_op jit(solution)/shard_map/all_to_all | solution.py:315

commit v16 on v13

--- a/solution.py
+++ b/solution.py
@@ -79,10 +79,13 @@
     return lax.slice_in_dim(plus, n - 1, n, axis=2 + d), lax.slice_in_dim(minus, 0, 1, axis=2 + d)
 
 
-def columns_kernel(a_ref, b_ref, out_ref):
+def columns_kernel(a_ref, b_ref, out_ref, rows_ref):
     _, sx, sy, sz = a_ref.shape
     pairs = [(r, q, i) for r in (a_ref, b_ref) for q in range(27) for i in range(sx)]
     per = 128 // sy
+    for p, (r, q, i) in enumerate(pairs):
+        rows_ref[0, pl.ds(p, 1), :] = r[q, i, pl.ds(sy - 1, 1), :]
+        rows_ref[1, pl.ds(p, 1), :] = r[q, i, pl.ds(0, 1), :]
     for g in range(len(pairs) // per):
         block = jnp.concatenate([r[q, i] for r, q, i in pairs[g * per : (g + 1) * per]], axis=0)
         flipped = block.T
@@ -98,10 +101,16 @@
     both = jnp.stack(cubes)
     rows = jnp.concatenate([both[..., sy - 1 : sy, :], both[..., 0:1, :]], axis=5)
     if len(fields) == 2 and sy * 8 == 128 and sz == 128:
-        flat = pl.pallas_call(
-            columns_kernel, out_shape=jax.ShapeDtypeStruct((2, 2 * 27 * sx * sy // 128, 128), jnp.float32)
+        flat, edge_rows = pl.pallas_call(
+            columns_kernel,
+            out_shape=(
+                jax.ShapeDtypeStruct((2, 2 * 27 * sx * sy // 128, 128), jnp.float32),
+                jax.ShapeDtypeStruct((2, 2 * 27 * sx, sz), jnp.float32),
+            ),
         )(fields[0], fields[1])
         cols = flat.reshape((2, 2, 3, 3, 3, sx, sy))
+        edge_rows = edge_rows.reshape((2, 2, 3, 3, 3, sx, 1, sz))
+        rows = jnp.concatenate([edge_rows[0], edge_rows[1]], axis=5)
     else:
         cols = None
         edges = jnp.concatenate([both[..., sz - 1 : sz], both[..., 0:1]], axis=6)

time: 85.1 us -> 91.3 us (1.073)
  local copies, waits for them, and re-layouts: 17.3 us -> 22.3 us
  waiting for transfers between devices: 3.73 us -> 6.91 us
  other arithmetic: 8.4 us -> 7.27 us
    unnamed x47 -> x44, local copies, waits for them, and re-layouts: 3.59 us -> 9.41 us
    ppermute x4, waiting for transfers between devices: 0.78 us -> 4.12 us  [halo_exchange(): lo = lax.ppermute(up, axis, [(i, (i + 1) % size) for i in range(size)])]
    ppermute x4, starting transfers between devices: 8.92 us -> 6.08 us  [halo_exchange(): lo = lax.ppermute(up, axis, [(i, (i + 1) % size) for i in range(size)])]
    ppermute x4, starting transfers between devices: 4.19 us -> 6.64 us  [halo_exchange(): hi = lax.ppermute(down, axis, [(i, (i - 1) % size) for i in range(size)])]
    slice x2 -> x1, local copies, waits for them, and re-layouts: 1.26 us -> 0.08 us  [halos(): rows = jnp.concatenate([both[..., sy - 1:sy, :], both[..., 0:1, :]], axis=5)]
    reduce_sum x1, other arithmetic: 1.21 us -> 0.04 us  [collide(): mom_x = jnp.sum(cube[2], axis=(0, 1)) - jnp.sum(cube[0], axis=(0, 1))]
  transfers between devices with their start and end apart: 10 -> 10, of which waited for: 5 -> 6; matrix products, arithmetic and copies ran while one was open for 11% -> 7% of each run, Pallas kernels for 3% -> 3%
where the time goes in v16:
time: 91.3 us; the launch traced here: 90.5 us
  local copies, waits for them, and re-layouts  22.3 us (24%)
  blocking collectives  21 us (23%)
  starting transfers between devices  19.5 us (21%)
  Pallas kernels  11.8 us (13%)
  other arithmetic  7.27 us (8%)
  waiting for transfers between devices  6.91 us (8%)
  between operations  1.69 us (2%)
    all_to_all x1, blocking collectives, shards(): lax.all_to_all(placed.reshape(devices, count // devices), ('gx', 'gy', 'g...  21 us
    unnamed x44, local copies, waits for them, and re-layouts  9.41 us
    pallas_call x2, Pallas kernels, run_stage(): pl.pallas_call(kernel, out_shape=(jax.ShapeDtypeStruct(shape, jnp.float32...  9.08 us
    ppermute x2, starting transfers between devices, halo_exchange(): both = lax.ppermute(jnp.stack([up, down]), axis, [(0, 1), (1, 0)])  6.77 us
    ppermute x4, starting transfers between devices, halo_exchange(): hi = lax.ppermute(down, axis, [(i, (i - 1) % size) for i in range(size)])  6.64 us
    ppermute x4, starting transfers between devices, halo_exchange(): lo = lax.ppermute(up, axis, [(i, (i + 1) % size) for i in range(size)])  6.08 us
    ppermute x4, waiting for transfers between devices, halo_exchange(): lo = lax.ppermute(up, axis, [(i, (i + 1) % size) for i in range(size)])  4.12 us
    pallas_call x1, Pallas kernels, halos(): pl.pallas_call(columns_kernel, out_shape=(jax.ShapeDtypeStruct((2, 2 * 27...  2.72 us
  transfers between devices with their start and end apart: 10, of which 6 were waited for; matrix products, arithmetic and copies ran while one was open for 7% of the time, Pallas kernels for 3%

profile of v16, /device:TPU:1, one launch (start us, length us, event | category | flops | bytes accessed | tf_op | source)
XLA Modules:
  0.0 90.5 jit_solution(10759175946907405416)
XLA Ops:
  0.6 1.2 %slice_reduce_fusion.2 = (f32[4,16,128]{2,1,0:T(8,128)S(1)}, f32[4,16,128]{2,1,0:T(8,128)S(1)}) fusion(f32[3,3,3,4,16,128]{5,4,3,2,1,0:T(8,128)} %bitcast.414), kind=kLoop, calls=%fused_computation.12 | loop fusion | flops 131072 | bytes 655360 | tf_op jit(solution)/shard_map/reduce_sum | solution.py:33
  1.8 1.1 %slice_reduce_fusion = (f32[4,16,128]{2,1,0:T(8,128)S(1)}, f32[4,16,128]{2,1,0:T(8,128)S(1)}) fusion(f32[3,3,3,4,16,128]{5,4,3,2,1,0:T(8,128)} %bitcast.415), kind=kLoop, calls=%fused_computation.10 | loop fusion | flops 131072 | bytes 655360 | tf_op jit(solution)/shard_map/reduce_sum | solution.py:34
  3.0 0.6 copy-done.13
  3.6 0.7 copy-done.14
  4.3 0.2 copy.472
  4.5 0.8 slice.656
  5.5 0.6 gather_fusion
  6.1 0.1 copy.555
  6.5 0.7 copy-done.11
  7.2 0.7 copy-done.9
  7.9 1.4 %fusion.7.a_ref.cf_ref = f32[27,4,16,128]{3,2,1,0:T(8,128)S(1)} fusion(f32[27,4,16,128]{3,2,1,0:T(8,128)S(1)} %copy-done, f32[4,16,128]{2,1,0:T(8,128)S(1)} %get-tuple-element.150.refs_7_, f32[4,16,128]{2,1,0:T(8,128)S(1)} %get-tuple-element.34, f32[4,16,128]{2,1,0:T(8,128)S(1)} %get-tuple-element.37, f32[27]{0:T(128)S(1)} %copy-done.17, ...), kind=kLoop, calls=%fused_computation.9 | loop fusion | flops 4202496 | bytes 2032048 | tf_op jit(solution)/shard_map/add | solution.py:47
  9.4 1.4 %copy-done.3 = f32[27,4,16,128]{3,2,1,0:T(8,128)S(1)} copy-done((f32[27,4,16,128]{3,2,1,0:T(8,128)S(1)}, f32[27,4,16,128]{3,2,1,0:T(8,128)}, u32[]{:S(2)}) %copy-start.3) | copy-done | bytes 884760
  10.9 1.5 %collective-permute-start.1 = (f32[2,3,3,1,16,128]{5,4,2,1,3,0:T(8,128)S(1)}, f32[2,3,3,1,16,128]{5,4,2,1,3,0:T(8,128)S(1)}, u32[]{:S(2)}, u32[]{:S(2)}) collective-permute-start(f32[2,3,3,1,16,128]{5,4,2,1,3,0:T(8,128)S(1)} %pad_maximum_fusion.1), channel_id=1, source_target_pairs={{0,120},{8,0},{16,8},{24,16},{32,24},{40,32},{48,40},{56,48},{64,5... | collective-permute-start | bytes 442376 | tf_op jit(solution)/shard_map/ppermute | solution.py:58
  12.4 1.7 %collective-permute-start = (f32[2,3,3,1,16,128]{5,4,2,1,3,0:T(8,128)S(1)}, f32[2,3,3,1,16,128]{5,4,2,1,3,0:T(8,128)S(1)}, u32[]{:S(2)}, u32[]{:S(2)}) collective-permute-start(f32[2,3,3,1,16,128]{5,4,2,1,3,0:T(8,128)S(1)} %pad_maximum_fusion), channel_id=1, source_target_pairs={{0,8},{8,16},{16,24},{24,32},{32,40},{40,48},{48,56},{56,64},{64,7... | collective-permute-start | bytes 442376 | tf_op jit(solution)/shard_map/ppermute | solution.py:57
  14.2 2.7 %shard_map.122 = (f32[2,27,128]{2,1,0:T(8,128)}, f32[2,216,128]{2,1,0:T(8,128)}) custom-call(f32[27,4,16,128]{3,2,1,0:T(8,128)} %copy-done.2, f32[27,4,16,128]{3,2,1,0:T(8,128)} %ae_ref.1), custom_call_target="tpu_custom_call" | custom-call | tf_op jit(solution)/shard_map/pallas_call | solution.py:104
  16.9 0.9 %reshape.155 = f32[2,2,3,3,3,4,16]{6,5,4,3,2,1,0:T(4,128)S(1)} reshape(f32[2,27,128]{2,1,0:T(8,128)} %get-tuple-element.9) | data formatting | bytes 55296 | tf_op jit(solution)/shard_map/reshape | solution.py:111
  17.9 0.9 copy-done.10
  19.4 0.6 copy-done.6
  20.1 0.2 slice_reduce_fusion.9
  20.3 0.6 copy-done.7
  20.9 0.2 slice_reduce_fusion.8
  21.1 0.2 slice_reduce_fusion.6
  21.3 0.2 slice_reduce_fusion.7
  21.9 3.4 %collective-permute-start.2 = (f32[2,2,3,3,4,1,128]{6,4,3,2,5,1,0:T(4,128)S(1)}, f32[2,2,3,3,4,1,128]{6,4,3,2,5,1,0:T(4,128)S(1)}, u32[]{:S(2)}, u32[]{:S(2)}) collective-permute-start(f32[2,2,3,3,4,1,128]{6,4,3,2,5,1,0:T(4,128)S(1)} %pad_maximum_fusion.3), channel_id=1, source_target_pairs={{0,4},{4,0},{1,5},{5,1},{2,6},{6,2},{3,7},{7,3},{8,12},{12,8},{9,1... | collective-permute-start | bytes 221192 | tf_op jit(solution)/shard_map/ppermute | solution.py:55
  25.9 1.1 %collective-permute-done.2 = f32[2,2,3,3,4,1,128]{6,4,3,2,5,1,0:T(4,128)S(1)} collective-permute-done((f32[2,2,3,3,4,1,128]{6,4,3,2,5,1,0:T(4,128)S(1)}, f32[2,2,3,3,4,1,128]{6,4,3,2,5,1,0:T(4,128)S(1)}, u32[]{:S(2)}, u32[]{:S(2)}) %collective-permute-start.2) | collective-permute-done | bytes 73760 | tf_op jit(solution)/shard_map/ppermute | solution.py:55
  27.0 0.2 slice_reduce_fusion.15
  27.2 0.1 copy.505
  27.4 0.2 slice_reduce_fusion.14
  27.5 0.1 copy.506
  28.2 2.5 %collective-permute-start.4 = (f32[2,3,3,16,4]{3,4,1,2,0:T(4,128)S(1)}, f32[2,3,3,16,4]{3,4,1,2,0:T(4,128)S(1)}, u32[]{:S(2)}, u32[]{:S(2)}) collective-permute-start(f32[2,3,3,16,4]{3,4,1,2,0:T(4,128)S(1)} %pad_maximum_fusion.11), channel_id=1, source_target_pairs={{0,3},{1,0},{2,1},{3,2},{4,7},{5,4},{6,5},{7,6},{8,11},{9,8},{10,9... | collective-permute-start | bytes 13832 | tf_op jit(solution)/shard_map/ppermute | solution.py:58
  30.8 0.1 copy.496
  30.9 0.1 copy.497
  31.5 0.7 fusion.29
  32.2 0.8 copy.513
  33.0 2.5 %collective-permute-done.3 = f32[2,3,3,16,4]{3,4,1,2,0:T(4,128)S(1)} collective-permute-done((f32[2,3,3,16,4]{3,4,1,2,0:T(4,128)S(1)}, f32[2,3,3,16,4]{3,4,1,2,0:T(4,128)S(1)}, u32[]{:S(2)}, u32[]{:S(2)}) %collective-permute-start.3) | collective-permute-done | bytes 4640 | tf_op jit(solution)/shard_map/ppermute | solution.py:57
  35.5 0.8 copy.504
  36.4 4.8 %shard_map.123 = (f32[27,4,16,128]{3,2,1,0:T(8,128)}, f32[4,16,128]{2,1,0:T(8,128)}) custom-call(f32[27,4,16,128]{3,2,1,0:T(8,128)} %copy-done.2, f32[27,4,16,128]{3,2,1,0:T(8,128)} %ae_ref.1, f32[18,16,128]{2,1,0:T(8,128)} %bitcast.425, f32[18,16,128]{2,1,0:T(8,128)} %bitcast.424, f32[18,4,128]{2,1,0:T(4,128)} %bitcast.442, f32[18,4,128]{2,1,0:T(4,128)} %bitcast.441, ...), custom_call_target="tpu_custom_call" | custom-call | tf_op jit(solution)/shard_map/pallas_call | solution.py:273
  41.2 1.2 %fusion.23 = (f32[9,4,16,128]{3,2,1,0:T(8,128)S(1)}, f32[9,4,16,128]{3,2,1,0:T(8,128)S(1)}) fusion(f32[27,4,16,128]{3,2,1,0:T(8,128)} %get-tuple-element.10.an_ref), kind=kLoop, calls=%fused_computation.228 | loop fusion | bytes 1179648 | tf_op jit(solution)/shard_map/slice | solution.py:78
  42.4 0.2 copy-done.1
  42.6 0.3 fusion.21
  43.0 0.7 copy.566
  43.7 0.7 copy.567
  44.5 2.8 %collective-permute-start.5 = (f32[1,3,3,1,16,128]{5,4,2,1,3,0:T(8,128)S(1)}, f32[1,3,3,1,16,128]{5,4,2,1,3,0:T(8,128)S(1)}, u32[]{:S(2)}, u32[]{:S(2)}) collective-permute-start(f32[1,3,3,1,16,128]{5,4,2,1,3,0:T(8,128)S(1)} %slice_bitcast_fusion.1), channel_id=1, source_target_pairs={{0,8},{8,16},{16,24},{24,32},{32,40},{40,48},{48,56},{56,64},{64,7... | collective-permute-start | bytes 221192 | tf_op jit(solution)/shard_map/ppermute | solution.py:57
  47.3 2.5 %collective-permute-start.6 = (f32[1,3,3,1,16,128]{5,4,2,1,3,0:T(8,128)S(1)}, f32[1,3,3,1,16,128]{5,4,2,1,3,0:T(8,128)S(1)}, u32[]{:S(2)}, u32[]{:S(2)}) collective-permute-start(f32[1,3,3,1,16,128]{5,4,2,1,3,0:T(8,128)S(1)} %slice_bitcast_fusion), channel_id=1, source_target_pairs={{0,120},{8,0},{16,8},{24,16},{32,24},{40,32},{48,40},{56,48},{64,5... | collective-permute-start | bytes 221192 | tf_op jit(solution)/shard_map/ppermute | solution.py:58
  49.9 0.5 collective-permute-done.5
  50.6 0.5 copy-done.4
  51.2 0.6 copy-done.5
  51.8 0.1 copy.539
  51.9 0.1 copy.542
  52.3 3.4 %collective-permute-start.7 = (f32[2,1,3,3,4,1,128]{6,4,3,2,5,1,0:T(4,128)S(1)}, f32[2,1,3,3,4,1,128]{6,4,3,2,5,1,0:T(4,128)S(1)}, u32[]{:S(2)}, u32[]{:S(2)}) collective-permute-start(f32[2,1,3,3,4,1,128]{6,4,3,2,5,1,0:T(4,128)S(1)} %pad_maximum_fusion.12), channel_id=1, source_target_pairs={{0,4},{4,0},{1,5},{5,1},{2,6},{6,2},{3,7},{7,3},{8,12},{12,8},{9,1... | collective-permute-start | bytes 110600 | tf_op jit(solution)/shard_map/ppermute | solution.py:55
  55.9 0.1 copy.529
  56.2 0.8 collective-permute-done.7
  57.0 0.6 slice_bitcast_fusion.92
  58.0 0.1 collective-permute-start.9
  58.3 1.5 %collective-permute-start.8 = (f32[1,3,3,16,4]{3,4,2,1,0:T(4,128)S(1)}, f32[1,3,3,16,4]{3,4,2,1,0:T(4,128)S(1)}, u32[]{:S(2)}, u32[]{:S(2)}) collective-permute-start(f32[1,3,3,16,4]{3,4,2,1,0:T(4,128)S(1)} %slice_bitcast_fusion.21), channel_id=1, source_target_pairs={{0,1},{1,2},{2,3},{3,0},{4,5},{5,6},{6,7},{7,4},{8,9},{9,10},{10,1... | collective-permute-start | bytes 6920 | tf_op jit(solution)/shard_map/ppermute | solution.py:57
  59.9 0.8 collective-permute-done.9
  60.7 0.8 copy.551
  61.4 1.1 %collective-permute-done.8 = f32[1,3,3,16,4]{3,4,2,1,0:T(4,128)S(1)} collective-permute-done((f32[1,3,3,16,4]{3,4,2,1,0:T(4,128)S(1)}, f32[1,3,3,16,4]{3,4,2,1,0:T(4,128)S(1)}, u32[]{:S(2)}, u32[]{:S(2)}) %collective-permute-start.8) | collective-permute-done | bytes 2336 | tf_op jit(solution)/shard_map/ppermute | solution.py:57
  62.5 0.8 copy.538
  63.3 4.2 %shard_map.124 = (f32[27,4,16,128]{3,2,1,0:T(8,128)}, f32[4,16,128]{2,1,0:T(8,128)}) custom-call(f32[27,4,16,128]{3,2,1,0:T(8,128)} %get-tuple-element.10.an_ref, f32[27,4,16,128]{3,2,1,0:T(8,128)} %f_ref.1, f32[9,16,128]{2,1,0:T(8,128)} %bitcast.420, f32[9,16,128]{2,1,0:T(8,128)} %bitcast.423, f32[9,4,128]{2,1,0:T(4,128)} %bitcast.458, ...), custom_call_target="tpu_custom_call" | custom-call | tf_op jit(solution)/shard_map/pallas_call | solution.py:273
  67.5 0.8 add_multiply_fusion
  68.4 0.1 reduce_sum.106
  68.8 21.0 %all_to_all.9 = f32[128,1,8]{2,1,0:T(1,128)S(1)} all-to-all(f32[128,1,8]{2,1,0:T(1,128)S(1)} %bitcast.438), channel_id=1, replica_groups=mesh['gx'=16,'gy'=2,'gz'=4] {'gx','gy','gz'}, dimensions={0} | all-to-all | bytes 8192 | tf_op jit(solution)/shard_map/all_to_all | solution.py:307
  89.8 0.7 reduce_sum.109
  (195 shorter events, 5.0 us)
Async XLA Ops:
  0.6 2.3 %copy-start = (f32[27,4,16,128]{3,2,1,0:T(8,128)S(1)}, f32[27,4,16,128]{3,2,1,0:T(8,128)}, u32[]{:S(2)}) copy-start(f32[27,4,16,128]{3,2,1,0:T(8,128)} %f_ref.1) | copy-start | bytes 2654212
  2.9 0.7 copy-start.13
  3.6 0.7 copy-start.14
  6.4 0.8 copy-start.11
  7.2 0.8 copy-start.9
  7.2 0.8 copy-start.18
  7.2 2.1 %copy-start.8 = (f32[4,16,128]{2,1,0:T(8,128)}, f32[4,16,128]{2,1,0:T(8,128)S(1)}, u32[]{:S(2)}) copy-start(f32[4,16,128]{2,1,0:T(8,128)S(1)} %get-tuple-element.150.refs_7_) | copy-start | bytes 98308
  7.2 0.7 copy-start.15
  7.2 0.7 copy-start.16
  7.2 0.7 copy-start.17
  9.3 1.5 %copy-start.2 = (f32[27,4,16,128]{3,2,1,0:T(8,128)}, f32[27,4,16,128]{3,2,1,0:T(8,128)S(1)}, u32[]{:S(2)}) copy-start(f32[27,4,16,128]{3,2,1,0:T(8,128)S(1)} %fusion.7.a_ref.cf_ref) | copy-start | bytes 2654212
  9.3 1.5 %copy-start.3 = (f32[27,4,16,128]{3,2,1,0:T(8,128)S(1)}, f32[27,4,16,128]{3,2,1,0:T(8,128)}, u32[]{:S(2)}) copy-start(f32[27,4,16,128]{3,2,1,0:T(8,128)} %ae_ref.1) | copy-start | bytes 2654212
  10.9 8.5 %collective-permute-start.1 = (f32[2,3,3,1,16,128]{5,4,2,1,3,0:T(8,128)S(1)}, f32[2,3,3,1,16,128]{5,4,2,1,3,0:T(8,128)S(1)}, u32[]{:S(2)}, u32[]{:S(2)}) collective-permute-start(f32[2,3,3,1,16,128]{5,4,2,1,3,0:T(8,128)S(1)} %pad_maximum_fusion.1), channel_id=1, source_target_pairs={{0,120},{8,0},{16,8},{24,16},{32,24},{40,32},{48,40},{56,48},{64,5... | collective-permute-start | bytes 442376 | tf_op jit(solution)/shard_map/ppermute | solution.py:58
  12.4 7.8 %collective-permute-start = (f32[2,3,3,1,16,128]{5,4,2,1,3,0:T(8,128)S(1)}, f32[2,3,3,1,16,128]{5,4,2,1,3,0:T(8,128)S(1)}, u32[]{:S(2)}, u32[]{:S(2)}) collective-permute-start(f32[2,3,3,1,16,128]{5,4,2,1,3,0:T(8,128)S(1)} %pad_maximum_fusion), channel_id=1, source_target_pairs={{0,8},{8,16},{16,24},{24,32},{32,40},{40,48},{48,56},{56,64},{64,7... | collective-permute-start | bytes 442376 | tf_op jit(solution)/shard_map/ppermute | solution.py:57
  17.9 0.9 %copy-start.10 = (f32[2,216,128]{2,1,0:T(8,128)S(1)}, f32[2,216,128]{2,1,0:T(8,128)}, u32[]{:S(2)}) copy-start(f32[2,216,128]{2,1,0:T(8,128)} %get-tuple-element.8) | copy-start | bytes 663556
  19.4 0.7 copy-start.6
  20.3 0.6 copy-start.7
  21.9 5.1 %collective-permute-start.2 = (f32[2,2,3,3,4,1,128]{6,4,3,2,5,1,0:T(4,128)S(1)}, f32[2,2,3,3,4,1,128]{6,4,3,2,5,1,0:T(4,128)S(1)}, u32[]{:S(2)}, u32[]{:S(2)}) collective-permute-start(f32[2,2,3,3,4,1,128]{6,4,3,2,5,1,0:T(4,128)S(1)} %pad_maximum_fusion.3), channel_id=1, source_target_pairs={{0,4},{4,0},{1,5},{5,1},{2,6},{6,2},{3,7},{7,3},{8,12},{12,8},{9,1... | collective-permute-start | bytes 221192 | tf_op jit(solution)/shard_map/ppermute | solution.py:55
  28.2 4.0 %collective-permute-start.4 = (f32[2,3,3,16,4]{3,4,1,2,0:T(4,128)S(1)}, f32[2,3,3,16,4]{3,4,1,2,0:T(4,128)S(1)}, u32[]{:S(2)}, u32[]{:S(2)}) collective-permute-start(f32[2,3,3,16,4]{3,4,1,2,0:T(4,128)S(1)} %pad_maximum_fusion.11), channel_id=1, source_target_pairs={{0,3},{1,0},{2,1},{3,2},{4,7},{5,4},{6,5},{7,6},{8,11},{9,8},{10,9... | collective-permute-start | bytes 13832 | tf_op jit(solution)/shard_map/ppermute | solution.py:58
  31.5 4.1 %collective-permute-start.3 = (f32[2,3,3,16,4]{3,4,1,2,0:T(4,128)S(1)}, f32[2,3,3,16,4]{3,4,1,2,0:T(4,128)S(1)}, u32[]{:S(2)}, u32[]{:S(2)}) collective-permute-start(f32[2,3,3,16,4]{3,4,1,2,0:T(4,128)S(1)} %pad_maximum_fusion.10), channel_id=1, source_target_pairs={{0,1},{1,2},{2,3},{3,0},{4,5},{5,6},{6,7},{7,4},{8,9},{9,10},{10,1... | collective-permute-start | bytes 13832 | tf_op jit(solution)/shard_map/ppermute | solution.py:57
  41.2 1.3 %copy-start.1 = (f32[27,4,16,128]{3,2,1,0:T(8,128)S(1)}, f32[27,4,16,128]{3,2,1,0:T(8,128)}, u32[]{:S(2)}) copy-start(f32[27,4,16,128]{3,2,1,0:T(8,128)} %get-tuple-element.10.an_ref) | copy-start | bytes 2654212
  44.5 6.0 %collective-permute-start.5 = (f32[1,3,3,1,16,128]{5,4,2,1,3,0:T(8,128)S(1)}, f32[1,3,3,1,16,128]{5,4,2,1,3,0:T(8,128)S(1)}, u32[]{:S(2)}, u32[]{:S(2)}) collective-permute-start(f32[1,3,3,1,16,128]{5,4,2,1,3,0:T(8,128)S(1)} %slice_bitcast_fusion.1), channel_id=1, source_target_pairs={{0,8},{8,16},{16,24},{24,32},{32,40},{40,48},{48,56},{56,64},{64,7... | collective-permute-start | bytes 221192 | tf_op jit(solution)/shard_map/ppermute | solution.py:57
  47.3 3.8 %collective-permute-start.6 = (f32[1,3,3,1,16,128]{5,4,2,1,3,0:T(8,128)S(1)}, f32[1,3,3,1,16,128]{5,4,2,1,3,0:T(8,128)S(1)}, u32[]{:S(2)}, u32[]{:S(2)}) collective-permute-start(f32[1,3,3,1,16,128]{5,4,2,1,3,0:T(8,128)S(1)} %slice_bitcast_fusion), channel_id=1, source_target_pairs={{0,120},{8,0},{16,8},{24,16},{32,24},{40,32},{48,40},{56,48},{64,5... | collective-permute-start | bytes 221192 | tf_op jit(solution)/shard_map/ppermute | solution.py:58
  50.5 0.6 copy-start.4
  51.2 0.6 copy-start.5
  52.3 4.7 %collective-permute-start.7 = (f32[2,1,3,3,4,1,128]{6,4,3,2,5,1,0:T(4,128)S(1)}, f32[2,1,3,3,4,1,128]{6,4,3,2,5,1,0:T(4,128)S(1)}, u32[]{:S(2)}, u32[]{:S(2)}) collective-permute-start(f32[2,1,3,3,4,1,128]{6,4,3,2,5,1,0:T(4,128)S(1)} %pad_maximum_fusion.12), channel_id=1, source_target_pairs={{0,4},{4,0},{1,5},{5,1},{2,6},{6,2},{3,7},{7,3},{8,12},{12,8},{9,1... | collective-permute-start | bytes 110600 | tf_op jit(solution)/shard_map/ppermute | solution.py:55
  58.0 2.7 %collective-permute-start.9 = (f32[1,3,3,16,4]{3,4,2,1,0:T(4,128)S(1)}, f32[1,3,3,16,4]{3,4,2,1,0:T(4,128)S(1)}, u32[]{:S(2)}, u32[]{:S(2)}) collective-permute-start(f32[1,3,3,16,4]{3,4,2,1,0:T(4,128)S(1)} %slice_bitcast_fusion.10), channel_id=1, source_target_pairs={{0,3},{1,0},{2,1},{3,2},{4,7},{5,4},{6,5},{7,6},{8,11},{9,8},{10,9... | collective-permute-start | bytes 6920 | tf_op jit(solution)/shard_map/ppermute | solution.py:58
  58.3 4.2 %collective-permute-start.8 = (f32[1,3,3,16,4]{3,4,2,1,0:T(4,128)S(1)}, f32[1,3,3,16,4]{3,4,2,1,0:T(4,128)S(1)}, u32[]{:S(2)}, u32[]{:S(2)}) collective-permute-start(f32[1,3,3,16,4]{3,4,2,1,0:T(4,128)S(1)} %slice_bitcast_fusion.21), channel_id=1, source_target_pairs={{0,1},{1,2},{2,3},{3,0},{4,5},{5,6},{6,7},{7,4},{8,9},{9,10},{10,1... | collective-permute-start | bytes 6920 | tf_op jit(solution)/shard_map/ppermute | solution.py:57
  63.3 4.2 %copy-start.12 = (f32[4,16,128]{2,1,0:T(8,128)S(1)}, f32[4,16,128]{2,1,0:T(8,128)}, u32[]{:S(2)}) copy-start(f32[4,16,128]{2,1,0:T(8,128)} %get-tuple-element.12) | copy-start | bytes 98308
